TPU v7x, 32 devices: a whole 2x2x4 slice. The times are simulated.
32 devices in a mesh: grp: 4 (over y, core), blk: 8 (over z, x).
Axes of the slice: x: 2, y: 2, z: 4, core: 2. Of those that a mesh axis runs over, the one named last changes fastest.
Arguments:
- embeddings: bfloat16 [2048, 4096], P(('grp', 'blk'))
- cluster_ids: int32 [2048], P(('grp', 'blk')), may hold values from 0 to 3, as said below
- row_index: int32 [2048], P(('grp', 'blk')), may hold values from 0 to 2047, each once
Outputs:
- best_similarity: float32 [2048], P(('grp', 'blk'))
Inputs may be any that keep to these rules, and one draw needn't show every extreme that they name: The owner group of a row is cluster_ids mod 4 (the number of devices along grp). Among the rows of one device at most 38 have one owner group; in every draw some device has exactly 38 rows of one group, and for some index along blk all devices along grp have exactly 38 rows of the same group. `row_index`: each number appears once.
All inputs are finite; a program needn't handle non-finite values.
Results may differ from a plain program's by a relative error of at most 0.00038.
Values may be sent and summed in bfloat16 or wider, within the bound.
No kernel may reach another device: no remote copies, remote signals or barrier semaphores. Data moves between devices by JAX's collectives and lax.ppermute only.
A program may use at most 64 MiB of HBM per device.

v0:
```python
import math

import jax
import jax.numpy as jnp
from jax import lax
from jax.sharding import PartitionSpec as P

D = 4096
CAP = 38


def from_behind(value, axis, steps):
    count = lax.axis_size(axis)
    pairs = [(source, (source + steps) % count) for source in range(count)]
    return lax.ppermute(value, axis, pairs)


def similarity(left_rows, left_labels, right_rows, right_labels):
    scores = jnp.einsum("id,jd->ij", left_rows, right_rows, preferred_element_type=jnp.float32)
    left_cluster = left_labels[:, 0]
    right_cluster = right_labels[:, 0]
    left_order = left_labels[:, 1]
    right_order = right_labels[:, 1]
    same_cluster = (left_cluster[:, None] == right_cluster[None, :]) & (left_cluster[:, None] >= 0)
    row_pick = same_cluster & (right_order[None, :] < left_order[:, None])
    col_pick = same_cluster & (left_order[:, None] < right_order[None, :])
    row_best = jnp.max(jnp.where(row_pick, scores, jnp.float32(-1.0)), axis=1)
    col_best = jnp.max(jnp.where(col_pick, scores, jnp.float32(-1.0)), axis=0)
    return (row_best, col_best)


def per_device(embeddings, cluster_ids, row_index):
    group_count = lax.axis_size("grp")
    loop_len = lax.axis_size("blk")
    held_count = group_count * CAP
    widened = embeddings.astype(jnp.float32)
    square_sum = jnp.sum(widened * widened, axis=1, keepdims=True)
    unit_rows = (widened * lax.rsqrt(square_sum / D + 1e-06) / math.sqrt(D)).astype(jnp.bfloat16)
    owner = cluster_ids % group_count
    member = (owner[:, None] == jnp.arange(group_count)[None, :]).astype(jnp.int32)
    before = jnp.cumsum(member, axis=0) - member
    slot_of = owner * CAP + jnp.sum(before * member, axis=1)
    placed = slot_of[None, :] == jnp.arange(held_count)[:, None]
    filled = jnp.any(placed, axis=1)
    send_rows = jnp.dot(
        placed.astype(jnp.bfloat16), unit_rows, preferred_element_type=jnp.float32
    ).astype(jnp.bfloat16)
    labels = jnp.stack([cluster_ids, row_index], axis=1)
    send_labels = jnp.sum(jnp.where(placed[:, :, None], labels[None, :, :], 0), axis=1)
    send_labels = jnp.where(filled[:, None], send_labels, -1)
    own_rows, own_labels = (
        lax.all_to_all(send_rows, "grp", split_axis=0, concat_axis=0, tiled=True),
        lax.all_to_all(send_labels, "grp", split_axis=0, concat_axis=0, tiled=True),
    )
    best_sim = similarity(own_rows, own_labels, own_rows, own_labels)[0]

    def advance(turn_no, state_now):
        visit_rows, visit_labels, best_now = state_now
        visit_rows, visit_labels = from_behind((visit_rows, visit_labels), "blk", 1)
        row_best, unused_col = similarity(own_rows, own_labels, visit_rows, visit_labels)
        return (visit_rows, visit_labels, jnp.maximum(best_now, row_best))

    best_sim = lax.fori_loop(1, loop_len, advance, (own_rows, own_labels, best_sim))[2]
    returned = lax.all_to_all(best_sim, "grp", split_axis=0, concat_axis=0, tiled=True)
    return jnp.take(returned, slot_of)


def solution(mesh):
    return jax.shard_map(
        per_device,
        mesh=mesh,
        in_specs=(P(("grp", "blk"), None), P(("grp", "blk")), P(("grp", "blk"))),
        out_specs=P(("grp", "blk")),
        check_vma=False,
    )
```

profile of v0, /device:TPU:0, one launch (start us, length us, event | category | flops | bytes accessed | tf_op | source)
XLA Modules:
  0.0 264.0 jit_solution(13407448707476018552)
XLA Ops:
  0.0 0.7 and_select_fusion.1
  0.7 0.1 reduce_window_sum.11
  0.8 0.2 select_reduce_fusion.2
  1.0 0.7 compare_select_fusion
  1.8 0.7 pad_add_fusion
  2.5 0.1 select_reduce_fusion.1
  2.8 0.6 copy.12
  3.4 4.3 %all-to-all-start.1 = ((s32[4,38,2]{1,2,0:T(2,128)}), s32[4,38,2]{1,2,0:T(2,128)S(1)}, u32[]{:S(2)}, u32[]{:S(2)}) async-start(s32[4,38,2]{1,2,0:T(2,128)} %copy.12), calls=%async_computation.1 | async-start | bytes 8192 | tf_op jit(solution)/shard_map/all_to_all | solution.py:53
  7.6 1.2 fusion.1
  8.9 1.7 convolution_convert_fusion
  10.5 1.4 all_to_all.22
  11.9 3.5 %all-to-all-start = ((bf16[4,38,4096]{2,1,0:T(8,128)(2,1)}), bf16[4,38,4096]{2,1,0:T(8,128)(2,1)S(1)}, u32[]{:S(2)}, u32[]{:S(2)}) async-start(bf16[4,38,4096]{2,1,0:T(8,128)(2,1)} %all_to_all.22), calls=%async_computation | async-start | bytes 2621440 | tf_op jit(solution)/shard_map/all_to_all | solution.py:52
  15.6 17.1 %all-to-all-done = bf16[4,38,4096]{2,1,0:T(8,128)(2,1)S(1)} async-done(((bf16[4,38,4096]{2,1,0:T(8,128)(2,1)}), bf16[4,38,4096]{2,1,0:T(8,128)(2,1)S(1)}, u32[]{:S(2)}, u32[]{:S(2)}) %all-to-all-start) | async-done | bytes 1245216 | tf_op jit(solution)/shard_map/all_to_all | solution.py:52
  32.7 0.3 all_to_all.24
  33.1 1.0 copy.16
  34.1 0.5 fusion
  34.6 218.1 %while.14 = (s32[]{:T(128)}, bf16[152,4096]{1,0:T(8,128)(2,1)}, s32[152,2]{0,1:T(2,128)S(1)}, f32[152]{0:T(256)S(1)}, s32[152,2]{0,1:T(2,128)S(1)}, /*index=5*/bf16[152,4096]{1,0:T(8,128)(2,1)S(1)}, s32[]{:T(128)}) while((s32[]{:T(128)}, bf16[152,4096]{1,0:T(8,128)(2,1)}, s32[152,2]{0,1:T(2,128)S(1)}, f32[152]{0:T(256)S(1)}, ...), condition=%wide.region_8.9_spmd, body=%wide.region_6.8_spmd.sunk | while | flops 189406752 | bytes 9979565 | solution.py:63
  34.6 2.0 collective-permute-start
  36.6 1.6 collective-permute-start.1
  38.2 28.8 %collective-permute-done.1 = s32[152,2]{0,1:T(2,128)S(1)} collective-permute-done((s32[152,2]{0,1:T(2,128)S(1)}, s32[152,2]{0,1:T(2,128)S(1)}, u32[]{:S(2)}, u32[]{:S(2)}) %collective-permute-start.1) | collective-permute-done | bytes 1248 | tf_op jit(solution)/shard_map/while/body/eval_jaxpr/ppermute | solution.py:15
  67.0 0.6 select_reduce_fusion.4
  67.6 1.0 copy.24
  68.6 1.1 collective-permute-start.1
  69.8 30.0 %collective-permute-done.1 = s32[152,2]{0,1:T(2,128)S(1)} collective-permute-done((s32[152,2]{0,1:T(2,128)S(1)}, s32[152,2]{0,1:T(2,128)S(1)}, u32[]{:S(2)}, u32[]{:S(2)}) %collective-permute-start.1) | collective-permute-done | bytes 1248 | tf_op jit(solution)/shard_map/while/body/eval_jaxpr/ppermute | solution.py:15
  99.8 0.6 select_reduce_fusion.4
  100.4 1.0 copy.24
  101.5 30.3 %collective-permute-done.1 = s32[152,2]{0,1:T(2,128)S(1)} collective-permute-done((s32[152,2]{0,1:T(2,128)S(1)}, s32[152,2]{0,1:T(2,128)S(1)}, u32[]{:S(2)}, u32[]{:S(2)}) %collective-permute-start.1) | collective-permute-done | bytes 1248 | tf_op jit(solution)/shard_map/while/body/eval_jaxpr/ppermute | solution.py:15
  131.8 0.6 select_reduce_fusion.4
  132.4 1.0 copy.24
  133.4 29.4 %collective-permute-done.1 = s32[152,2]{0,1:T(2,128)S(1)} collective-permute-done((s32[152,2]{0,1:T(2,128)S(1)}, s32[152,2]{0,1:T(2,128)S(1)}, u32[]{:S(2)}, u32[]{:S(2)}) %collective-permute-start.1) | collective-permute-done | bytes 1248 | tf_op jit(solution)/shard_map/while/body/eval_jaxpr/ppermute | solution.py:15
  162.9 0.6 select_reduce_fusion.4
  163.5 1.0 copy.24
  164.5 28.6 %collective-permute-done.1 = s32[152,2]{0,1:T(2,128)S(1)} collective-permute-done((s32[152,2]{0,1:T(2,128)S(1)}, s32[152,2]{0,1:T(2,128)S(1)}, u32[]{:S(2)}, u32[]{:S(2)}) %collective-permute-start.1) | collective-permute-done | bytes 1248 | tf_op jit(solution)/shard_map/while/body/eval_jaxpr/ppermute | solution.py:15
  193.1 0.6 select_reduce_fusion.4
  193.7 1.0 copy.24
  194.8 27.7 %collective-permute-done.1 = s32[152,2]{0,1:T(2,128)S(1)} collective-permute-done((s32[152,2]{0,1:T(2,128)S(1)}, s32[152,2]{0,1:T(2,128)S(1)}, u32[]{:S(2)}, u32[]{:S(2)}) %collective-permute-start.1) | collective-permute-done | bytes 1248 | tf_op jit(solution)/shard_map/while/body/eval_jaxpr/ppermute | solution.py:15
  222.5 0.6 select_reduce_fusion.4
  223.1 1.0 copy.24
  224.2 26.9 %collective-permute-done.1 = s32[152,2]{0,1:T(2,128)S(1)} collective-permute-done((s32[152,2]{0,1:T(2,128)S(1)}, s32[152,2]{0,1:T(2,128)S(1)}, u32[]{:S(2)}, u32[]{:S(2)}) %collective-permute-start.1) | collective-permute-done | bytes 1248 | tf_op jit(solution)/shard_map/while/body/eval_jaxpr/ppermute | solution.py:15
  251.1 0.6 select_reduce_fusion.4
  251.7 1.0 copy.24
  252.7 0.7 all_to_all.27
  253.4 4.2 %all-to-all-start.2 = ((f32[4,38,1]{1,2,0:T(1,128)}), f32[4,38,1]{1,2,0:T(1,128)S(1)}, u32[]{:S(2)}, u32[]{:S(2)}) async-start(f32[4,38,1]{1,2,0:T(1,128)} %bitcast.8), calls=%async_computation.2 | async-start | bytes 4096 | tf_op jit(solution)/shard_map/all_to_all | solution.py:64
  257.6 3.8 %all-to-all-done.2 = f32[4,38,1]{1,2,0:T(1,128)S(1)} async-done(((f32[4,38,1]{1,2,0:T(1,128)}), f32[4,38,1]{1,2,0:T(1,128)S(1)}, u32[]{:S(2)}, u32[]{:S(2)}) %all-to-all-start.2) | async-done | bytes 640 | tf_op jit(solution)/shard_map/all_to_all | solution.py:64
  261.4 0.5 broadcast.65
  261.9 0.7 reduce.7
  262.7 0.8 gather_fusion
  263.4 0.5 and_select_fusion
  (67 shorter events, 0.9 us)
Async XLA Ops:
  3.4 8.6 %all-to-all-start.1 = ((s32[4,38,2]{1,2,0:T(2,128)}), s32[4,38,2]{1,2,0:T(2,128)S(1)}, u32[]{:S(2)}, u32[]{:S(2)}) async-start(s32[4,38,2]{1,2,0:T(2,128)} %copy.12), calls=%async_computation.1 | async-start | bytes 8192 | tf_op jit(solution)/shard_map/all_to_all | solution.py:53
  11.9 20.8 %all-to-all-start = ((bf16[4,38,4096]{2,1,0:T(8,128)(2,1)}), bf16[4,38,4096]{2,1,0:T(8,128)(2,1)S(1)}, u32[]{:S(2)}, u32[]{:S(2)}) async-start(bf16[4,38,4096]{2,1,0:T(8,128)(2,1)} %all_to_all.22), calls=%async_computation | async-start | bytes 2621440 | tf_op jit(solution)/shard_map/all_to_all | solution.py:52
  34.6 32.3 %collective-permute-start = (bf16[152,4096]{1,0:T(8,128)(2,1)}, bf16[152,4096]{1,0:T(8,128)(2,1)S(1)}, u32[]{:S(2)}, u32[]{:S(2)}) collective-permute-start(bf16[152,4096]{1,0:T(8,128)(2,1)} %get-tuple-element.113), channel_id=1, source_target_pairs={{0,1},{1,2},{2,3},{3,4},{4,5},{5,6},{6,7},{7,0},{8,9},{9,10},{10,1... | collective-permute-start | bytes 3735560 | tf_op jit(solution)/shard_map/while/body/eval_jaxpr/ppermute | solution.py:15
  36.6 30.4 %collective-permute-start.1 = (s32[152,2]{0,1:T(2,128)S(1)}, s32[152,2]{0,1:T(2,128)S(1)}, u32[]{:S(2)}, u32[]{:S(2)}) collective-permute-start(s32[152,2]{0,1:T(2,128)S(1)} %get-tuple-element.114), channel_id=1, source_target_pairs={{0,1},{1,2},{2,3},{3,4},{4,5},{5,6},{6,7},{7,0},{8,9},{9,10},{10,1... | collective-permute-start | bytes 3656 | tf_op jit(solution)/shard_map/while/body/eval_jaxpr/ppermute | solution.py:15
  68.6 31.2 %collective-permute-start = (bf16[152,4096]{1,0:T(8,128)(2,1)}, bf16[152,4096]{1,0:T(8,128)(2,1)S(1)}, u32[]{:S(2)}, u32[]{:S(2)}) collective-permute-start(bf16[152,4096]{1,0:T(8,128)(2,1)} %get-tuple-element.113), channel_id=1, source_target_pairs={{0,1},{1,2},{2,3},{3,4},{4,5},{5,6},{6,7},{7,0},{8,9},{9,10},{10,1... | collective-permute-start | bytes 3735560 | tf_op jit(solution)/shard_map/while/body/eval_jaxpr/ppermute | solution.py:15
  68.6 31.2 %collective-permute-start.1 = (s32[152,2]{0,1:T(2,128)S(1)}, s32[152,2]{0,1:T(2,128)S(1)}, u32[]{:S(2)}, u32[]{:S(2)}) collective-permute-start(s32[152,2]{0,1:T(2,128)S(1)} %get-tuple-element.114), channel_id=1, source_target_pairs={{0,1},{1,2},{2,3},{3,4},{4,5},{5,6},{6,7},{7,0},{8,9},{9,10},{10,1... | collective-permute-start | bytes 3656 | tf_op jit(solution)/shard_map/while/body/eval_jaxpr/ppermute | solution.py:15
  101.4 30.3 %collective-permute-start = (bf16[152,4096]{1,0:T(8,128)(2,1)}, bf16[152,4096]{1,0:T(8,128)(2,1)S(1)}, u32[]{:S(2)}, u32[]{:S(2)}) collective-permute-start(bf16[152,4096]{1,0:T(8,128)(2,1)} %get-tuple-element.113), channel_id=1, source_target_pairs={{0,1},{1,2},{2,3},{3,4},{4,5},{5,6},{6,7},{7,0},{8,9},{9,10},{10,1... | collective-permute-start | bytes 3735560 | tf_op jit(solution)/shard_map/while/body/eval_jaxpr/ppermute | solution.py:15
  101.4 30.3 %collective-permute-start.1 = (s32[152,2]{0,1:T(2,128)S(1)}, s32[152,2]{0,1:T(2,128)S(1)}, u32[]{:S(2)}, u32[]{:S(2)}) collective-permute-start(s32[152,2]{0,1:T(2,128)S(1)} %get-tuple-element.114), channel_id=1, source_target_pairs={{0,1},{1,2},{2,3},{3,4},{4,5},{5,6},{6,7},{7,0},{8,9},{9,10},{10,1... | collective-permute-start | bytes 3656 | tf_op jit(solution)/shard_map/while/body/eval_jaxpr/ppermute | solution.py:15
  133.4 29.5 %collective-permute-start = (bf16[152,4096]{1,0:T(8,128)(2,1)}, bf16[152,4096]{1,0:T(8,128)(2,1)S(1)}, u32[]{:S(2)}, u32[]{:S(2)}) collective-permute-start(bf16[152,4096]{1,0:T(8,128)(2,1)} %get-tuple-element.113), channel_id=1, source_target_pairs={{0,1},{1,2},{2,3},{3,4},{4,5},{5,6},{6,7},{7,0},{8,9},{9,10},{10,1... | collective-permute-start | bytes 3735560 | tf_op jit(solution)/shard_map/while/body/eval_jaxpr/ppermute | solution.py:15
  133.4 29.5 %collective-permute-start.1 = (s32[152,2]{0,1:T(2,128)S(1)}, s32[152,2]{0,1:T(2,128)S(1)}, u32[]{:S(2)}, u32[]{:S(2)}) collective-permute-start(s32[152,2]{0,1:T(2,128)S(1)} %get-tuple-element.114), channel_id=1, source_target_pairs={{0,1},{1,2},{2,3},{3,4},{4,5},{5,6},{6,7},{7,0},{8,9},{9,10},{10,1... | collective-permute-start | bytes 3656 | tf_op jit(solution)/shard_map/while/body/eval_jaxpr/ppermute | solution.py:15
  164.5 28.6 %collective-permute-start = (bf16[152,4096]{1,0:T(8,128)(2,1)}, bf16[152,4096]{1,0:T(8,128)(2,1)S(1)}, u32[]{:S(2)}, u32[]{:S(2)}) collective-permute-start(bf16[152,4096]{1,0:T(8,128)(2,1)} %get-tuple-element.113), channel_id=1, source_target_pairs={{0,1},{1,2},{2,3},{3,4},{4,5},{5,6},{6,7},{7,0},{8,9},{9,10},{10,1... | collective-permute-start | bytes 3735560 | tf_op jit(solution)/shard_map/while/body/eval_jaxpr/ppermute | solution.py:15
  164.5 28.6 %collective-permute-start.1 = (s32[152,2]{0,1:T(2,128)S(1)}, s32[152,2]{0,1:T(2,128)S(1)}, u32[]{:S(2)}, u32[]{:S(2)}) collective-permute-start(s32[152,2]{0,1:T(2,128)S(1)} %get-tuple-element.114), channel_id=1, source_target_pairs={{0,1},{1,2},{2,3},{3,4},{4,5},{5,6},{6,7},{7,0},{8,9},{9,10},{10,1... | collective-permute-start | bytes 3656 | tf_op jit(solution)/shard_map/while/body/eval_jaxpr/ppermute | solution.py:15
  194.8 27.8 %collective-permute-start = (bf16[152,4096]{1,0:T(8,128)(2,1)}, bf16[152,4096]{1,0:T(8,128)(2,1)S(1)}, u32[]{:S(2)}, u32[]{:S(2)}) collective-permute-start(bf16[152,4096]{1,0:T(8,128)(2,1)} %get-tuple-element.113), channel_id=1, source_target_pairs={{0,1},{1,2},{2,3},{3,4},{4,5},{5,6},{6,7},{7,0},{8,9},{9,10},{10,1... | collective-permute-start | bytes 3735560 | tf_op jit(solution)/shard_map/while/body/eval_jaxpr/ppermute | solution.py:15
  194.8 27.8 %collective-permute-start.1 = (s32[152,2]{0,1:T(2,128)S(1)}, s32[152,2]{0,1:T(2,128)S(1)}, u32[]{:S(2)}, u32[]{:S(2)}) collective-permute-start(s32[152,2]{0,1:T(2,128)S(1)} %get-tuple-element.114), channel_id=1, source_target_pairs={{0,1},{1,2},{2,3},{3,4},{4,5},{5,6},{6,7},{7,0},{8,9},{9,10},{10,1... | collective-permute-start | bytes 3656 | tf_op jit(solution)/shard_map/while/body/eval_jaxpr/ppermute | solution.py:15
  224.2 26.9 %collective-permute-start = (bf16[152,4096]{1,0:T(8,128)(2,1)}, bf16[152,4096]{1,0:T(8,128)(2,1)S(1)}, u32[]{:S(2)}, u32[]{:S(2)}) collective-permute-start(bf16[152,4096]{1,0:T(8,128)(2,1)} %get-tuple-element.113), channel_id=1, source_target_pairs={{0,1},{1,2},{2,3},{3,4},{4,5},{5,6},{6,7},{7,0},{8,9},{9,10},{10,1... | collective-permute-start | bytes 3735560 | tf_op jit(solution)/shard_map/while/body/eval_jaxpr/ppermute | solution.py:15
  224.2 26.9 %collective-permute-start.1 = (s32[152,2]{0,1:T(2,128)S(1)}, s32[152,2]{0,1:T(2,128)S(1)}, u32[]{:S(2)}, u32[]{:S(2)}) collective-permute-start(s32[152,2]{0,1:T(2,128)S(1)} %get-tuple-element.114), channel_id=1, source_target_pairs={{0,1},{1,2},{2,3},{3,4},{4,5},{5,6},{6,7},{7,0},{8,9},{9,10},{10,1... | collective-permute-start | bytes 3656 | tf_op jit(solution)/shard_map/while/body/eval_jaxpr/ppermute | solution.py:15
  253.4 8.0 %all-to-all-start.2 = ((f32[4,38,1]{1,2,0:T(1,128)}), f32[4,38,1]{1,2,0:T(1,128)S(1)}, u32[]{:S(2)}, u32[]{:S(2)}) async-start(f32[4,38,1]{1,2,0:T(1,128)} %bitcast.8), calls=%async_computation.2 | async-start | bytes 4096 | tf_op jit(solution)/shard_map/all_to_all | solution.py:64
where the time goes:
time: 264 us
  waiting for transfers between devices  223 us (84%)
  starting transfers between devices  16.7 us (6%)
  local copies, waits for them, and re-layouts  13.1 us (5%)
  matrix products  6.19 us (2%)
  other arithmetic  5.27 us (2%)
    ppermute x14, waiting for transfers between devices, from_behind(): return lax.ppermute(value, axis, pairs)  202 us
    all_to_all x1, waiting for transfers between devices, per_device(): lax.all_to_all(send_rows, 'grp', split_axis=0, concat_axis=0, tiled=True)  17.1 us
    while x14, local copies, waits for them, and re-layouts  7.28 us
  transfers between devices with their start and end apart: 17, of which 9 were waited for; matrix products, arithmetic and copies ran while one was open for 1% of the time, Pallas kernels for 0%

commit v1 on v0

v1 whole, which is shorter than its diff:
```python
import math

import jax
import jax.numpy as jnp
from jax import lax
from jax.sharding import PartitionSpec as P

D = 4096
LABEL_SHIFT = 65536


def per_device(embeddings, cluster_ids, row_index):
    group_count = lax.axis_size("grp")
    widened = embeddings.astype(jnp.float32)
    square_sum = jnp.sum(widened * widened, axis=1, keepdims=True)
    unit_rows = (widened * lax.rsqrt(square_sum / D + 1e-06) / math.sqrt(D)).astype(jnp.bfloat16)
    labels = cluster_ids * LABEL_SHIFT + row_index

    left_rows = lax.all_gather(unit_rows, "grp", axis=0, tiled=True)
    left_labels = lax.all_gather(labels, "grp", axis=0, tiled=True)
    right_rows = lax.all_gather(unit_rows, "blk", axis=0, tiled=True)
    right_labels = lax.all_gather(labels, "blk", axis=0, tiled=True)

    scores = jnp.einsum("id,jd->ij", left_rows, right_rows, preferred_element_type=jnp.float32)
    same_cluster = (left_labels[:, None] // LABEL_SHIFT) == (right_labels[None, :] // LABEL_SHIFT)
    earlier = same_cluster & (right_labels[None, :] < left_labels[:, None])
    partial = jnp.max(jnp.where(earlier, scores, jnp.float32(-1.0)), axis=1)

    partial = partial.reshape(group_count, -1)
    gathered = lax.all_to_all(partial, "grp", split_axis=0, concat_axis=0, tiled=True)
    return jnp.max(gathered, axis=0)


def solution(mesh):
    return jax.shard_map(
        per_device,
        mesh=mesh,
        in_specs=(P(("grp", "blk"), None), P(("grp", "blk")), P(("grp", "blk"))),
        out_specs=P(("grp", "blk")),
        check_vma=False,
    )
```

time: 264 us -> 129 us (0.49)
  waiting for transfers between devices: 223 us -> 77.5 us
  blocking collectives: 0 us -> 24.5 us
  starting transfers between devices: 16.7 us -> 0.04 us
  between operations: 0.07 us -> 14.8 us
  local copies, waits for them, and re-layouts: 13.1 us -> 2.65 us
    ppermute x14 -> x0, waiting for transfers between devices: 202 us -> none  [from_behind(): return lax.ppermute(value, axis, pairs)]
    all_gather x0 -> x2, waiting for transfers between devices: none -> 76.8 us  [the longest x1 75 us: per_device(): right_rows = lax.all_gather(unit_rows, 'blk', axis=0, tiled=True)]
    all_to_all x3 -> x0, waiting for transfers between devices: 20.9 us -> none  [the longest x1 17.1 us: per_device(): lax.all_to_all(send_rows, 'grp', split_axis=0, concat_axis=0, tiled=True)]
    unnamed x0 -> x2, blocking collectives: none -> 18.2 us
    all_to_all x3 -> x0, starting transfers between devices: 12 us -> none  [the longest x1 4.26 us: per_device(): lax.all_to_all(send_labels, 'grp', split_axis=0, concat_axis=0, tiled=True)]
    while x14 -> x0, local copies, waits for them, and re-layouts: 7.28 us -> none
    all_to_all x0 -> x1, blocking collectives: none -> 6.31 us  [per_device(): lax.all_to_all(partial, 'grp', split_axis=0, concat_axis=0, tiled=True)]
    ppermute x14 -> x0, starting transfers between devices: 4.69 us -> none  [from_behind(): return lax.ppermute(value, axis, pairs)]
  transfers between devices with their start and end apart: 17 -> 2, of which waited for: 9 -> 2; matrix products, arithmetic and copies ran while one was open for 1% -> 3% of each run, Pallas kernels for 0% -> 0%
where the time goes in v1:
time: 129 us; the launch traced here: 128 us
  waiting for transfers between devices  77.5 us (60%)
  blocking collectives  24.5 us (19%)
  between operations  14.8 us (11%)
  other arithmetic  4.62 us (4%)
  matrix products  4.21 us (3%)
  local copies, waits for them, and re-layouts  2.65 us (2%)
    all_gather x1, waiting for transfers between devices, per_device(): right_rows = lax.all_gather(unit_rows, 'blk', axis=0, tiled=True)  75 us
    unnamed x2, blocking collectives  18.2 us
    all_to_all x1, blocking collectives, per_device(): lax.all_to_all(partial, 'grp', split_axis=0, concat_axis=0, tiled=True)  6.31 us
    dot_general x1, matrix products, per_device(): jnp.einsum('id,jd->ij', left_rows, right_rows, preferred_element_type=jnp...  4.21 us
  transfers between devices with their start and end apart: 2, of which 2 were waited for; matrix products, arithmetic and copies ran while one was open for 3% of the time, Pallas kernels for 0%

profile of v1, /device:TPU:0, one launch (start us, length us, event | category | flops | bytes accessed | tf_op | source)
XLA Modules:
  0.0 128.3 jit_solution(7676768416157748371)
XLA Ops:
  6.5 0.0 all-gather.3.cloned.1.call-start
  6.5 1.2 fusion.1
  7.8 2.1 %fusion.3 = bf16[64,4096]{1,0:T(8,128)(2,1)} fusion(bf16[64,4096]{1,0:T(8,128)(2,1)} %param.3, f32[64]{0:T(128)S(1)} %add_rsqrt_fusion), kind=kLoop, calls=%fused_computation.6 | loop fusion | flops 1048576 | bytes 1048832 | tf_op jit(solution)/shard_map/convert_element_type | solution.py:16
  9.8 0.0 all-gather.3.cloned.1.call-update
  9.9 0.0 all-gather.5.cloned.1.call-start
  9.9 0.7 all-gather.5.cloned.1.call-update
  10.6 1.2 dynamic-slice
  11.9 1.3 %dynamic-slice.1 = u32[1]{0:T(128)} dynamic-slice(u32[32]{0:T(128)} %constant.48, u32[]{:T(128)S(6)} %add.21), dynamic_slice_sizes={1} | dynamic-slice | bytes 12
  14.6 0.8 fusion.7
  15.3 13.1 %all-reduce.1 = s32[512]{0:T(512)S(1)} all-reduce(s32[512]{0:T(512)S(1)} %get-tuple-element.6), channel_id=1, replica_groups=mesh['grp'=4,'blk'=8] {'blk'}, use_global_device_ids=true, to_apply=%add.1 | all-reduce | flops 512 | bytes 4096
  28.4 5.1 %all-reduce = s32[256]{0:T(256)S(1)} all-reduce(s32[256]{0:T(256)S(1)} %get-tuple-element.5), channel_id=1, replica_groups=mesh['grp'=4,'blk'=8] {'grp'}, use_global_device_ids=true, to_apply=%add | all-reduce | flops 256 | bytes 2048
  33.6 1.8 %all-gather.3.cloned.1.call-done = bf16[256,4096]{1,0:T(8,128)(2,1)} async-done(((bf16[64,4096]{1,0:T(8,128)(2,1)}), bf16[256,4096]{1,0:T(8,128)(2,1)}) %all-gather.3.cloned.1.call-update) | async-done | bytes 2097168 | tf_op jit(solution)/shard_map/all_gather | solution.py:19
  35.4 75.0 %all-gather.5.cloned.1.call-done = bf16[512,4096]{1,0:T(8,128)(2,1)} async-done(((bf16[64,4096]{1,0:T(8,128)(2,1)}), bf16[512,4096]{1,0:T(8,128)(2,1)}) %all-gather.5.cloned.1.call-update) | async-done | bytes 4194320 | tf_op jit(solution)/shard_map/all_gather | solution.py:21
  110.4 4.2 %fusion = f32[256]{0:T(256)S(1)} fusion(bf16[256,4096]{1,0:T(8,128)(2,1)} %all-gather.3.cloned.1.call-done, bf16[512,4096]{1,0:T(8,128)(2,1)} %all-gather.5.cloned.1.call-done, s32[512]{0:T(512)S(1)} %all-reduce.1, s32[512]{0:T(512)S(1)} %add_select_fusion, s32[256]{0:T(256)S(1)} %all-reduce, s32[256]{0:T(256)S(1)} %and_select_fusion), kind=kOutput, calls=%fused_computation.3 | convolution fusion | flops 1074396928 | bytes 6298624 | tf_op jit(solution)/shard_map/id,jd->ij/dot_general | solution.py:24
  114.6 0.1 all_to_all.6
  114.7 6.3 %all_to_all.9 = f32[4,1,64]{2,1,0:T(1,128)S(1)} all-to-all(f32[4,1,64]{2,1,0:T(1,128)S(1)} %all_to_all.6), channel_id=1, replica_groups=mesh['grp'=4,'blk'=8] {'grp'}, dimensions={0} | all-to-all | bytes 2048 | tf_op jit(solution)/shard_map/all_to_all | solution.py:30
  121.0 0.5 reduce_max.19
  (5 shorter events, 0.0 us)
Async XLA Ops:
  6.5 28.9 %all-gather.3.cloned.1.call-start = ((), (), s32[]{:S(2)}) async-start(), calls=%async_computation.1 | async-start | bytes 2621440 | tf_op jit(solution)/shard_map/all_gather | solution.py:19
  9.9 100.5 %all-gather.5.cloned.1.call-start = ((), (), s32[]{:S(2)}) async-start(), calls=%async_computation.2 | async-start | bytes 4718592 | tf_op jit(solution)/shard_map/all_gather | solution.py:21
Sparse Core Ops, SparseCore 0:
  10.0 25.3 all-gather.2
  37.5 72.7 all-gather.4

commit v2 on v1

--- a/solution.py
+++ b/solution.py
@@ -6,23 +6,42 @@
 from jax.sharding import PartitionSpec as P
 
 D = 4096
-LABEL_SHIFT = 65536
+LABEL_SHIFT = 65536.0
+
+
+def ring_order(count):
+    if count % 2:
+        return list(range(count))
+    return [2 * k for k in range(count // 2)] + [2 * k + 1 for k in reversed(range(count // 2))]
 
 
 def per_device(embeddings, cluster_ids, row_index):
     group_count = lax.axis_size("grp")
+    block_count = lax.axis_size("blk")
     widened = embeddings.astype(jnp.float32)
     square_sum = jnp.sum(widened * widened, axis=1, keepdims=True)
     unit_rows = (widened * lax.rsqrt(square_sum / D + 1e-06) / math.sqrt(D)).astype(jnp.bfloat16)
-    labels = cluster_ids * LABEL_SHIFT + row_index
+    labels = cluster_ids.astype(jnp.float32) * LABEL_SHIFT + row_index.astype(jnp.float32)
 
     left_rows = lax.all_gather(unit_rows, "grp", axis=0, tiled=True)
     left_labels = lax.all_gather(labels, "grp", axis=0, tiled=True)
-    right_rows = lax.all_gather(unit_rows, "blk", axis=0, tiled=True)
-    right_labels = lax.all_gather(labels, "blk", axis=0, tiled=True)
+
+    order = ring_order(block_count)
+    forward = [(order[i], order[(i + 1) % block_count]) for i in range(block_count)]
+    backward = [(dst, src) for src, dst in forward]
+    ahead, behind = (unit_rows, labels), (unit_rows, labels)
+    blocks = [(unit_rows, labels)]
+    for step in range(block_count // 2):
+        ahead = lax.ppermute(ahead, "blk", forward)
+        blocks.append(ahead)
+        if step < (block_count - 1) // 2:
+            behind = lax.ppermute(behind, "blk", backward)
+            blocks.append(behind)
+    right_rows = jnp.concatenate([rows for rows, _ in blocks], axis=0)
+    right_labels = jnp.concatenate([lab for _, lab in blocks], axis=0)
 
     scores = jnp.einsum("id,jd->ij", left_rows, right_rows, preferred_element_type=jnp.float32)
-    same_cluster = (left_labels[:, None] // LABEL_SHIFT) == (right_labels[None, :] // LABEL_SHIFT)
+    same_cluster = jnp.floor(left_labels[:, None] / LABEL_SHIFT) == jnp.floor(right_labels[None, :] / LABEL_SHIFT)
     earlier = same_cluster & (right_labels[None, :] < left_labels[:, None])
     partial = jnp.max(jnp.where(earlier, scores, jnp.float32(-1.0)), axis=1)
 

time: 129 us -> 95.9 us (0.74)
  waiting for transfers between devices: 77.5 us -> 35.2 us
  starting transfers between devices: 0.04 us -> 18 us
  blocking collectives: 24.5 us -> 12.3 us
  local copies, waits for them, and re-layouts: 2.65 us -> 7.26 us
    all_gather x1 -> x0, waiting for transfers between devices: 75 us -> none  [per_device(): right_rows = lax.all_gather(unit_rows, 'blk', axis=0, tiled=True)]
    ppermute x0 -> x14, waiting for transfers between devices: none -> 35.1 us  [the longest x8 30.6 us: per_device(): ahead = lax.ppermute(ahead, 'blk', forward)]
    ppermute x0 -> x14, starting transfers between devices: none -> 18 us  [the longest x8 14 us: per_device(): ahead = lax.ppermute(ahead, 'blk', forward)]
    unnamed x2 -> x1, blocking collectives: 18.2 us -> 5.92 us
    unnamed x4 -> x10, local copies, waits for them, and re-layouts: 2.57 us -> 6.27 us
    unnamed x1 -> x2, other arithmetic: 0.77 us -> 2.84 us
    convert_element_type x1 -> x0, other arithmetic: 2.05 us -> none  [per_device(): (widened * lax.rsqrt(square_sum / D + 1e-06) / math.sqrt(D)).astype(jnp.b...]
    all_gather x1, waiting for transfers between devices: 1.83 us -> 0.01 us  [per_device(): left_rows = lax.all_gather(unit_rows, 'grp', axis=0, tiled=True)]
  transfers between devices with their start and end apart: 2 -> 15, of which waited for: 2 -> 7; matrix products, arithmetic and copies ran while one was open for 3% -> 8% of each run, Pallas kernels for 0% -> 0%
where the time goes in v2:
time: 95.9 us; the launch traced here: 95.6 us
  waiting for transfers between devices  35.2 us (37%)
  starting transfers between devices  18 us (19%)
  between operations  14.1 us (15%)
  blocking collectives  12.3 us (13%)
  local copies, waits for them, and re-layouts  7.26 us (8%)
  other arithmetic  4.63 us (5%)
  matrix products  4.2 us (4%)
    ppermute x8, waiting for transfers between devices, per_device(): ahead = lax.ppermute(ahead, 'blk', forward)  30.6 us
    ppermute x8, starting transfers between devices, per_device(): ahead = lax.ppermute(ahead, 'blk', forward)  14 us
    all_to_all x1, blocking collectives, per_device(): lax.all_to_all(partial, 'grp', split_axis=0, concat_axis=0, tiled=True)  6.34 us
    unnamed x10, local copies, waits for them, and re-layouts  6.27 us
    unnamed x1, blocking collectives  5.92 us
    ppermute x6, waiting for transfers between devices, per_device(): behind = lax.ppermute(behind, 'blk', backward)  4.59 us
    dot_general x1, matrix products, per_device(): jnp.einsum('id,jd->ij', left_rows, right_rows, preferred_element_type=jnp...  4.2 us
    ppermute x6, starting transfers between devices, per_device(): behind = lax.ppermute(behind, 'blk', backward)  3.98 us
  transfers between devices with their start and end apart: 15, of which 7 were waited for; matrix products, arithmetic and copies ran while one was open for 8% of the time, Pallas kernels for 0%

profile of v2, /device:TPU:0, one launch (start us, length us, event | category | flops | bytes accessed | tf_op | source)
XLA Modules:
  0.0 95.6 jit_solution(13435145265011946408)
XLA Ops:
  6.5 0.0 all-gather.2.cloned.1.call-start
  6.5 1.2 %fusion = f32[64]{0:T(128)S(1)} fusion(bf16[64,4096]{1,0:T(8,128)(2,1)} %param.3), kind=kLoop, calls=%fused_computation.2 | loop fusion | flops 786368 | bytes 524544 | tf_op jit(solution)/shard_map/reduce_sum | solution.py:22
  7.8 2.1 %constant_dynamic-update-slice_fusion.7 = (bf16[512,4096]{1,0:T(8,128)(2,1)}, bf16[64,4096]{1,0:T(8,128)(2,1)S(1)}) fusion(f32[64]{0:T(128)S(1)} %add_rsqrt_fusion, bf16[64,4096]{1,0:T(8,128)(2,1)} %param.3), kind=kLoop, calls=%fused_computation.13 | loop fusion | flops 1048575 | bytes 1573120
  9.9 3.1 %collective-permute-start.7 = (bf16[64,4096]{1,0:T(8,128)(2,1)S(1)}, bf16[64,4096]{1,0:T(8,128)(2,1)S(1)}, u32[]{:S(2)}, u32[]{:S(2)}) collective-permute-start(bf16[64,4096]{1,0:T(8,128)(2,1)S(1)} %get-tuple-element.8), channel_id=1, source_target_pairs={{0,2},{2,4},{4,6},{6,7},{7,5},{5,3},{3,1},{1,0},{8,10},{10,12},{12... | collective-permute-start | bytes 1572872 | tf_op jit(solution)/shard_map/ppermute | solution.py:35
  12.9 1.2 %dynamic-slice = u32[1]{0:T(128)} dynamic-slice(u32[32]{0:T(128)} %constant.23, u32[]{:T(128)S(6)} %add.17), dynamic_slice_sizes={1} | dynamic-slice | bytes 12
  14.8 0.8 fusion.3
  15.6 1.6 %collective-permute-start = (f32[64]{0:T(128)S(1)}, f32[64]{0:T(128)S(1)}, u32[]{:S(2)}, u32[]{:S(2)}) collective-permute-start(f32[64]{0:T(128)S(1)} %get-tuple-element.6), channel_id=1, source_target_pairs={{0,2},{2,4},{4,6},{6,7},{7,5},{5,3},{3,1},{1,0},{8,10},{10,12},{12... | collective-permute-start | bytes 776 | tf_op jit(solution)/shard_map/ppermute | solution.py:35
  17.2 0.4 collective-permute-start.1
  17.6 7.2 %collective-permute-done = f32[64]{0:T(128)S(1)} collective-permute-done((f32[64]{0:T(128)S(1)}, f32[64]{0:T(128)S(1)}, u32[]{:S(2)}, u32[]{:S(2)}) %collective-permute-start) | collective-permute-done | bytes 288 | tf_op jit(solution)/shard_map/ppermute | solution.py:35
  24.9 1.8 %collective-permute-start.2 = (f32[64]{0:T(128)S(1)}, f32[64]{0:T(128)S(1)}, u32[]{:S(2)}, u32[]{:S(2)}) collective-permute-start(f32[64]{0:T(128)S(1)} %collective-permute-done), channel_id=1, source_target_pairs={{0,2},{2,4},{4,6},{6,7},{7,5},{5,3},{3,1},{1,0},{8,10},{10,12},{12... | collective-permute-start | bytes 776 | tf_op jit(solution)/shard_map/ppermute | solution.py:35
  26.7 0.2 collective-permute-start.8
  26.9 0.0 copy-done
  26.9 0.0 all-gather.2.cloned.1.call-update
  26.9 0.0 collective-permute-done.1
  26.9 1.8 %collective-permute-start.3 = (f32[64]{0:T(128)S(1)}, f32[64]{0:T(128)S(1)}, u32[]{:S(2)}, u32[]{:S(2)}) collective-permute-start(f32[64]{0:T(128)S(1)} %collective-permute-done.1), channel_id=1, source_target_pairs={{2,0},{4,2},{6,4},{7,6},{5,7},{3,5},{1,3},{0,1},{10,8},{12,10},{14... | collective-permute-start | bytes 776 | tf_op jit(solution)/shard_map/ppermute | solution.py:38
  28.7 0.0 collective-permute-done.2
  28.7 1.5 %collective-permute-start.4 = (f32[64]{0:T(128)S(1)}, f32[64]{0:T(128)S(1)}, u32[]{:S(2)}, u32[]{:S(2)}) collective-permute-start(f32[64]{0:T(128)S(1)} %collective-permute-done.2), channel_id=1, source_target_pairs={{0,2},{2,4},{4,6},{6,7},{7,5},{5,3},{3,1},{1,0},{8,10},{10,12},{12... | collective-permute-start | bytes 776 | tf_op jit(solution)/shard_map/ppermute | solution.py:35
  30.3 5.9 %all-reduce = f32[256]{0:T(256)S(1)} all-reduce(f32[256]{0:T(256)S(1)} %get-tuple-element.5), channel_id=1, replica_groups=mesh['grp'=4,'blk'=8] {'grp'}, use_global_device_ids=true, to_apply=%add | all-reduce | flops 256 | bytes 2048
  36.2 3.0 %collective-permute-done.3 = f32[64]{0:T(128)S(1)} collective-permute-done((f32[64]{0:T(128)S(1)}, f32[64]{0:T(128)S(1)}, u32[]{:S(2)}, u32[]{:S(2)}) %collective-permute-start.3) | collective-permute-done | bytes 288 | tf_op jit(solution)/shard_map/ppermute | solution.py:38
  39.2 0.5 collective-permute-start.5
  39.7 0.0 collective-permute-done.4
  39.7 1.5 %collective-permute-start.6 = (f32[64]{0:T(128)S(1)}, f32[64]{0:T(128)S(1)}, u32[]{:S(2)}, u32[]{:S(2)}) collective-permute-start(f32[64]{0:T(128)S(1)} %collective-permute-done.4), channel_id=1, source_target_pairs={{0,2},{2,4},{4,6},{6,7},{7,5},{5,3},{3,1},{1,0},{8,10},{10,12},{12... | collective-permute-start | bytes 776 | tf_op jit(solution)/shard_map/ppermute | solution.py:35
  41.3 1.5 %collective-permute-done.5 = f32[64]{0:T(128)S(1)} collective-permute-done((f32[64]{0:T(128)S(1)}, f32[64]{0:T(128)S(1)}, u32[]{:S(2)}, u32[]{:S(2)}) %collective-permute-start.5) | collective-permute-done | bytes 288 | tf_op jit(solution)/shard_map/ppermute | solution.py:38
  42.8 0.5 collective-permute-done.6
  43.3 0.1 concatenate.10
  43.4 0.0 collective-permute-done.7
  43.4 1.6 %collective-permute-start.9 = (bf16[64,4096]{1,0:T(8,128)(2,1)S(1)}, bf16[64,4096]{1,0:T(8,128)(2,1)S(1)}, u32[]{:S(2)}, u32[]{:S(2)}) collective-permute-start(bf16[64,4096]{1,0:T(8,128)(2,1)S(1)} %collective-permute-done.7), channel_id=1, source_target_pairs={{0,2},{2,4},{4,6},{6,7},{7,5},{5,3},{3,1},{1,0},{8,10},{10,12},{12... | collective-permute-start | bytes 1572872 | tf_op jit(solution)/shard_map/ppermute | solution.py:35
  45.0 0.8 constant_dynamic-update-slice_fusion.6
  45.8 0.0 collective-permute-done.8
  45.8 0.5 collective-permute-start.10
  46.3 0.8 constant_dynamic-update-slice_fusion.5
  47.1 8.4 %collective-permute-done.9 = bf16[64,4096]{1,0:T(8,128)(2,1)S(1)} collective-permute-done((bf16[64,4096]{1,0:T(8,128)(2,1)S(1)}, bf16[64,4096]{1,0:T(8,128)(2,1)S(1)}, u32[]{:S(2)}, u32[]{:S(2)}) %collective-permute-start.9) | collective-permute-done | bytes 524320 | tf_op jit(solution)/shard_map/ppermute | solution.py:35
  55.5 1.4 %collective-permute-start.11 = (bf16[64,4096]{1,0:T(8,128)(2,1)S(1)}, bf16[64,4096]{1,0:T(8,128)(2,1)S(1)}, u32[]{:S(2)}, u32[]{:S(2)}) collective-permute-start(bf16[64,4096]{1,0:T(8,128)(2,1)S(1)} %collective-permute-done.9), channel_id=1, source_target_pairs={{0,2},{2,4},{4,6},{6,7},{7,5},{5,3},{3,1},{1,0},{8,10},{10,12},{12... | collective-permute-start | bytes 1572872 | tf_op jit(solution)/shard_map/ppermute | solution.py:35
  56.9 0.8 constant_dynamic-update-slice_fusion.4
  57.8 0.0 collective-permute-done.10
  57.8 0.6 collective-permute-start.12
  58.4 0.8 constant_dynamic-update-slice_fusion.3
  59.2 8.4 %collective-permute-done.11 = bf16[64,4096]{1,0:T(8,128)(2,1)S(1)} collective-permute-done((bf16[64,4096]{1,0:T(8,128)(2,1)S(1)}, bf16[64,4096]{1,0:T(8,128)(2,1)S(1)}, u32[]{:S(2)}, u32[]{:S(2)}) %collective-permute-start.11) | collective-permute-done | bytes 524320 | tf_op jit(solution)/shard_map/ppermute | solution.py:35
  67.6 1.4 %collective-permute-start.13 = (bf16[64,4096]{1,0:T(8,128)(2,1)S(1)}, bf16[64,4096]{1,0:T(8,128)(2,1)S(1)}, u32[]{:S(2)}, u32[]{:S(2)}) collective-permute-start(bf16[64,4096]{1,0:T(8,128)(2,1)S(1)} %collective-permute-done.11), channel_id=1, source_target_pairs={{0,2},{2,4},{4,6},{6,7},{7,5},{5,3},{3,1},{1,0},{8,10},{10,12},{12... | collective-permute-start | bytes 1572872 | tf_op jit(solution)/shard_map/ppermute | solution.py:35
  69.0 0.8 constant_dynamic-update-slice_fusion.2
  69.9 0.0 collective-permute-done.12
  69.9 0.8 constant_dynamic-update-slice_fusion.1
  70.7 6.1 %collective-permute-done.13 = bf16[64,4096]{1,0:T(8,128)(2,1)S(1)} collective-permute-done((bf16[64,4096]{1,0:T(8,128)(2,1)S(1)}, bf16[64,4096]{1,0:T(8,128)(2,1)S(1)}, u32[]{:S(2)}, u32[]{:S(2)}) %collective-permute-start.13) | collective-permute-done | bytes 524320 | tf_op jit(solution)/shard_map/ppermute | solution.py:35
  76.8 0.8 constant_dynamic-update-slice_fusion
  77.6 4.2 %select_reduce_fusion = f32[256]{0:T(256)S(1)} fusion(f32[512]{0:T(512)S(1)} %concatenate.10, f32[512]{0:T(512)S(1)} %multiply_floor_fusion, f32[256]{0:T(256)S(1)} %all-reduce, f32[256]{0:T(256)S(1)} %multiply_floor_fusion.1, bf16[256,4096]{1,0:T(8,128)(2,1)} %all-gather.2.cloned.1.call-done, bf16[512,4096]{1,0:T(8,128)(2,1)} %constant_dynamic-update-slice_fusion), kind=kOutput, calls=%fused_computation.5 | convolution fusion | flops 1074396928 | bytes 6298624 | tf_op jit(solution)/shard_map/id,jd->ij/dot_general | solution.py:43
  81.8 0.1 all_to_all.6
  81.9 6.3 %all_to_all.9 = f32[4,1,64]{2,1,0:T(1,128)S(1)} all-to-all(f32[4,1,64]{2,1,0:T(1,128)S(1)} %all_to_all.6), channel_id=1, replica_groups=mesh['grp'=4,'blk'=8] {'grp'}, dimensions={0} | all-to-all | bytes 2048 | tf_op jit(solution)/shard_map/all_to_all | solution.py:49
  88.2 0.5 reduce_max.19
  (6 shorter events, 0.0 us)
Async XLA Ops:
  6.5 71.1 %all-gather.2.cloned.1.call-start = ((), (), s32[]{:S(2)}) async-start(), calls=%async_computation.1 | async-start | bytes 2621440 | tf_op jit(solution)/shard_map/all_gather | solution.py:26
  9.9 17.0 %copy-start = (bf16[64,4096]{1,0:T(8,128)(2,1)}, bf16[64,4096]{1,0:T(8,128)(2,1)S(1)}, u32[]{:S(2)}) copy-start(bf16[64,4096]{1,0:T(8,128)(2,1)S(1)} %get-tuple-element.8) | copy-start | bytes 1572868
  9.9 33.5 %collective-permute-start.7 = (bf16[64,4096]{1,0:T(8,128)(2,1)S(1)}, bf16[64,4096]{1,0:T(8,128)(2,1)S(1)}, u32[]{:S(2)}, u32[]{:S(2)}) collective-permute-start(bf16[64,4096]{1,0:T(8,128)(2,1)S(1)} %get-tuple-element.8), channel_id=1, source_target_pairs={{0,2},{2,4},{4,6},{6,7},{7,5},{5,3},{3,1},{1,0},{8,10},{10,12},{12... | collective-permute-start | bytes 1572872 | tf_op jit(solution)/shard_map/ppermute | solution.py:35
  15.6 9.3 %collective-permute-start = (f32[64]{0:T(128)S(1)}, f32[64]{0:T(128)S(1)}, u32[]{:S(2)}, u32[]{:S(2)}) collective-permute-start(f32[64]{0:T(128)S(1)} %get-tuple-element.6), channel_id=1, source_target_pairs={{0,2},{2,4},{4,6},{6,7},{7,5},{5,3},{3,1},{1,0},{8,10},{10,12},{12... | collective-permute-start | bytes 776 | tf_op jit(solution)/shard_map/ppermute | solution.py:35
  17.2 9.7 %collective-permute-start.1 = (f32[64]{0:T(128)S(1)}, f32[64]{0:T(128)S(1)}, u32[]{:S(2)}, u32[]{:S(2)}) collective-permute-start(f32[64]{0:T(128)S(1)} %get-tuple-element.6), channel_id=1, source_target_pairs={{2,0},{4,2},{6,4},{7,6},{5,7},{3,5},{1,3},{0,1},{10,8},{12,10},{14... | collective-permute-start | bytes 776 | tf_op jit(solution)/shard_map/ppermute | solution.py:38
  24.9 3.9 %collective-permute-start.2 = (f32[64]{0:T(128)S(1)}, f32[64]{0:T(128)S(1)}, u32[]{:S(2)}, u32[]{:S(2)}) collective-permute-start(f32[64]{0:T(128)S(1)} %collective-permute-done), channel_id=1, source_target_pairs={{0,2},{2,4},{4,6},{6,7},{7,5},{5,3},{3,1},{1,0},{8,10},{10,12},{12... | collective-permute-start | bytes 776 | tf_op jit(solution)/shard_map/ppermute | solution.py:35
  26.7 19.1 %collective-permute-start.8 = (bf16[64,4096]{1,0:T(8,128)(2,1)S(1)}, bf16[64,4096]{1,0:T(8,128)(2,1)S(1)}, u32[]{:S(2)}, u32[]{:S(2)}) collective-permute-start(bf16[64,4096]{1,0:T(8,128)(2,1)S(1)} %get-tuple-element.8), channel_id=1, source_target_pairs={{2,0},{4,2},{6,4},{7,6},{5,7},{3,5},{1,3},{0,1},{10,8},{12,10},{14... | collective-permute-start | bytes 1572872 | tf_op jit(solution)/shard_map/ppermute | solution.py:38
  26.9 12.3 %collective-permute-start.3 = (f32[64]{0:T(128)S(1)}, f32[64]{0:T(128)S(1)}, u32[]{:S(2)}, u32[]{:S(2)}) collective-permute-start(f32[64]{0:T(128)S(1)} %collective-permute-done.1), channel_id=1, source_target_pairs={{2,0},{4,2},{6,4},{7,6},{5,7},{3,5},{1,3},{0,1},{10,8},{12,10},{14... | collective-permute-start | bytes 776 | tf_op jit(solution)/shard_map/ppermute | solution.py:38
  28.7 11.0 %collective-permute-start.4 = (f32[64]{0:T(128)S(1)}, f32[64]{0:T(128)S(1)}, u32[]{:S(2)}, u32[]{:S(2)}) collective-permute-start(f32[64]{0:T(128)S(1)} %collective-permute-done.2), channel_id=1, source_target_pairs={{0,2},{2,4},{4,6},{6,7},{7,5},{5,3},{3,1},{1,0},{8,10},{10,12},{12... | collective-permute-start | bytes 776 | tf_op jit(solution)/shard_map/ppermute | solution.py:35
  39.2 3.6 %collective-permute-start.5 = (f32[64]{0:T(128)S(1)}, f32[64]{0:T(128)S(1)}, u32[]{:S(2)}, u32[]{:S(2)}) collective-permute-start(f32[64]{0:T(128)S(1)} %collective-permute-done.3), channel_id=1, source_target_pairs={{2,0},{4,2},{6,4},{7,6},{5,7},{3,5},{1,3},{0,1},{10,8},{12,10},{14... | collective-permute-start | bytes 776 | tf_op jit(solution)/shard_map/ppermute | solution.py:38
  39.7 3.6 %collective-permute-start.6 = (f32[64]{0:T(128)S(1)}, f32[64]{0:T(128)S(1)}, u32[]{:S(2)}, u32[]{:S(2)}) collective-permute-start(f32[64]{0:T(128)S(1)} %collective-permute-done.4), channel_id=1, source_target_pairs={{0,2},{2,4},{4,6},{6,7},{7,5},{5,3},{3,1},{1,0},{8,10},{10,12},{12... | collective-permute-start | bytes 776 | tf_op jit(solution)/shard_map/ppermute | solution.py:35
  43.4 12.1 %collective-permute-start.9 = (bf16[64,4096]{1,0:T(8,128)(2,1)S(1)}, bf16[64,4096]{1,0:T(8,128)(2,1)S(1)}, u32[]{:S(2)}, u32[]{:S(2)}) collective-permute-start(bf16[64,4096]{1,0:T(8,128)(2,1)S(1)} %collective-permute-done.7), channel_id=1, source_target_pairs={{0,2},{2,4},{4,6},{6,7},{7,5},{5,3},{3,1},{1,0},{8,10},{10,12},{12... | collective-permute-start | bytes 1572872 | tf_op jit(solution)/shard_map/ppermute | solution.py:35
  45.8 12.0 %collective-permute-start.10 = (bf16[64,4096]{1,0:T(8,128)(2,1)S(1)}, bf16[64,4096]{1,0:T(8,128)(2,1)S(1)}, u32[]{:S(2)}, u32[]{:S(2)}) collective-permute-start(bf16[64,4096]{1,0:T(8,128)(2,1)S(1)} %collective-permute-done.8), channel_id=1, source_target_pairs={{2,0},{4,2},{6,4},{7,6},{5,7},{3,5},{1,3},{0,1},{10,8},{12,10},{14... | collective-permute-start | bytes 1572872 | tf_op jit(solution)/shard_map/ppermute | solution.py:38
  55.5 12.1 %collective-permute-start.11 = (bf16[64,4096]{1,0:T(8,128)(2,1)S(1)}, bf16[64,4096]{1,0:T(8,128)(2,1)S(1)}, u32[]{:S(2)}, u32[]{:S(2)}) collective-permute-start(bf16[64,4096]{1,0:T(8,128)(2,1)S(1)} %collective-permute-done.9), channel_id=1, source_target_pairs={{0,2},{2,4},{4,6},{6,7},{7,5},{5,3},{3,1},{1,0},{8,10},{10,12},{12... | collective-permute-start | bytes 1572872 | tf_op jit(solution)/shard_map/ppermute | solution.py:35
  57.8 12.1 %collective-permute-start.12 = (bf16[64,4096]{1,0:T(8,128)(2,1)S(1)}, bf16[64,4096]{1,0:T(8,128)(2,1)S(1)}, u32[]{:S(2)}, u32[]{:S(2)}) collective-permute-start(bf16[64,4096]{1,0:T(8,128)(2,1)S(1)} %collective-permute-done.10), channel_id=1, source_target_pairs={{2,0},{4,2},{6,4},{7,6},{5,7},{3,5},{1,3},{0,1},{10,8},{12,10},{14... | collective-permute-start | bytes 1572872 | tf_op jit(solution)/shard_map/ppermute | solution.py:38
  67.6 9.2 %collective-permute-start.13 = (bf16[64,4096]{1,0:T(8,128)(2,1)S(1)}, bf16[64,4096]{1,0:T(8,128)(2,1)S(1)}, u32[]{:S(2)}, u32[]{:S(2)}) collective-permute-start(bf16[64,4096]{1,0:T(8,128)(2,1)S(1)} %collective-permute-done.11), channel_id=1, source_target_pairs={{0,2},{2,4},{4,6},{6,7},{7,5},{5,3},{3,1},{1,0},{8,10},{10,12},{12... | collective-permute-start | bytes 1572872 | tf_op jit(solution)/shard_map/ppermute | solution.py:35
Sparse Core Ops, SparseCore 0:
  27.0 24.0 all-gather.1

commit v3 on v2

v3 whole, which is shorter than its diff:
```python
import math

import jax
import jax.numpy as jnp
from jax import lax
from jax.sharding import PartitionSpec as P

D = 4096
LABEL_SHIFT = 65536.0


def ring_order(count):
    if count % 2:
        return list(range(count))
    return [2 * k for k in range(count // 2)] + [2 * k + 1 for k in reversed(range(count // 2))]


def block_best(left_rows, left_labels, right_rows, right_labels):
    scores = jnp.einsum("id,jd->ij", left_rows, right_rows, preferred_element_type=jnp.float32)
    same_cluster = jnp.floor(left_labels[:, None] / LABEL_SHIFT) == jnp.floor(right_labels[None, :] / LABEL_SHIFT)
    earlier = same_cluster & (right_labels[None, :] < left_labels[:, None])
    return jnp.max(jnp.where(earlier, scores, jnp.float32(-1.0)), axis=1)


def per_device(embeddings, cluster_ids, row_index):
    group_count = lax.axis_size("grp")
    block_count = lax.axis_size("blk")
    rows_here = embeddings.shape[0]
    widened = embeddings.astype(jnp.float32)
    square_sum = jnp.sum(widened * widened, axis=1, keepdims=True)
    unit_rows = (widened * lax.rsqrt(square_sum / D + 1e-06) / math.sqrt(D)).astype(jnp.bfloat16)
    labels = cluster_ids.astype(jnp.float32) * LABEL_SHIFT + row_index.astype(jnp.float32)

    all_labels = lax.all_gather(labels, ("grp", "blk"), axis=0, tiled=True)
    all_labels = all_labels.reshape(group_count, block_count, rows_here)
    my_grp = lax.axis_index("grp")
    my_blk = lax.axis_index("blk")
    left_labels = lax.dynamic_index_in_dim(all_labels, my_blk, axis=1, keepdims=False).reshape(-1)
    my_column = lax.dynamic_index_in_dim(all_labels, my_grp, axis=0, keepdims=False)
    left_rows = lax.all_gather(unit_rows, "grp", axis=0, tiled=True)

    order = ring_order(block_count)
    place = [0] * block_count
    for position, blk in enumerate(order):
        place[blk] = position
    order_table = jnp.array(order, jnp.int32)
    my_place = jnp.array(place, jnp.int32)[my_blk]

    def column_labels(shift):
        source = order_table[(my_place + shift) % block_count]
        return lax.dynamic_index_in_dim(my_column, source, axis=0, keepdims=False)

    forward = [(order[i], order[(i + 1) % block_count]) for i in range(block_count)]
    backward = [(dst, src) for src, dst in forward]
    best = block_best(left_rows, left_labels, unit_rows, labels)
    ahead, behind = unit_rows, unit_rows
    for step in range(1, block_count // 2 + 1):
        ahead = lax.ppermute(ahead, "blk", forward)
        best = jnp.maximum(best, block_best(left_rows, left_labels, ahead, column_labels(-step)))
        if step <= (block_count - 1) // 2:
            behind = lax.ppermute(behind, "blk", backward)
            best = jnp.maximum(best, block_best(left_rows, left_labels, behind, column_labels(step)))

    best = best.reshape(group_count, rows_here)
    result = lax.dynamic_index_in_dim(best, my_grp, axis=0, keepdims=False)
    for shift in range(1, group_count):
        target = (my_grp + shift) % group_count
        piece = lax.dynamic_index_in_dim(best, target, axis=0, keepdims=False)
        pairs = [(g, (g + shift) % group_count) for g in range(group_count)]
        result = jnp.maximum(result, lax.ppermute(piece, "grp", pairs))
    return result


def solution(mesh):
    return jax.shard_map(
        per_device,
        mesh=mesh,
        in_specs=(P(("grp", "blk"), None), P(("grp", "blk")), P(("grp", "blk"))),
        out_specs=P(("grp", "blk")),
        check_vma=False,
    )
```

time: 95.9 us -> 123 us (1.28)
  blocking collectives: 12.3 us -> 44.9 us
  between operations: 14.1 us -> 31.8 us
  waiting for transfers between devices: 35.2 us -> 18.8 us
  starting transfers between devices: 18 us -> 12.2 us
  local copies, waits for them, and re-layouts: 7.26 us -> 1.85 us
  matrix products: 4.2 us -> 9.09 us
    unnamed x1, blocking collectives: 5.92 us -> 44.9 us
    ppermute x8 -> x4, waiting for transfers between devices: 30.6 us -> 12.1 us  [per_device(): ahead = lax.ppermute(ahead, 'blk', forward)]
    ppermute x8 -> x4, starting transfers between devices: 14 us -> 6.76 us  [per_device(): ahead = lax.ppermute(ahead, 'blk', forward)]
    all_to_all x1 -> x0, blocking collectives: 6.34 us -> none  [per_device(): lax.all_to_all(partial, 'grp', split_axis=0, concat_axis=0, tiled=True)]
    unnamed x10 -> x12, local copies, waits for them, and re-layouts: 6.27 us -> 0.3 us
    dot_general x1 -> x8, matrix products: 4.2 us -> 9.09 us  [block_best(): jnp.einsum('id,jd->ij', left_rows, right_rows, preferred_element_type=jnp...]
    unnamed x2 -> x0, other arithmetic: 2.84 us -> none
    ppermute x0 -> x3, starting transfers between devices: none -> 2.8 us  [per_device(): result = jnp.maximum(result, lax.ppermute(piece, 'grp', pairs))]
  transfers between devices with their start and end apart: 15 -> 11, of which waited for: 7 -> 4; matrix products, arithmetic and copies ran while one was open for 8% -> 8% of each run, Pallas kernels for 0% -> 0%
where the time goes in v3:
time: 123 us; the launch traced here: 122 us
  blocking collectives  44.9 us (37%)
  between operations  31.8 us (26%)
  waiting for transfers between devices  18.8 us (15%)
  starting transfers between devices  12.2 us (10%)
  matrix products  9.09 us (7%)
  other arithmetic  3.86 us (3%)
  local copies, waits for them, and re-layouts  1.85 us (2%)
    unnamed x1, blocking collectives  44.9 us
    ppermute x4, waiting for transfers between devices, per_device(): ahead = lax.ppermute(ahead, 'blk', forward)  12.1 us
    dot_general x8, matrix products, block_best(): jnp.einsum('id,jd->ij', left_rows, right_rows, preferred_element_type=jnp...  9.09 us
    ppermute x4, starting transfers between devices, per_device(): ahead = lax.ppermute(ahead, 'blk', forward)  6.76 us
    ppermute x3, waiting for transfers between devices, per_device(): behind = lax.ppermute(behind, 'blk', backward)  4.13 us
    ppermute x3, starting transfers between devices, per_device(): result = jnp.maximum(result, lax.ppermute(piece, 'grp', pairs))  2.8 us
    ppermute x3, starting transfers between devices, per_device(): behind = lax.ppermute(behind, 'blk', backward)  2.59 us
    ppermute x3, waiting for transfers between devices, per_device(): result = jnp.maximum(result, lax.ppermute(piece, 'grp', pairs))  2.56 us
  transfers between devices with their start and end apart: 11, of which 4 were waited for; matrix products, arithmetic and copies ran while one was open for 8% of the time, Pallas kernels for 0%

profile of v3, /device:TPU:0, one launch (start us, length us, event | category | flops | bytes accessed | tf_op | source)
XLA Modules:
  0.0 122.4 jit_solution(10094979446064894586)
XLA Ops:
  6.5 0.0 copy-start.4
  6.5 0.0 copy-start.1
  6.5 0.0 all-gather.2.cloned.1.call-start
  6.6 1.3 %fusion.8 = f32[64]{0:T(128)S(1)} fusion(bf16[64,4096]{1,0:T(8,128)(2,1)} %param.5), kind=kLoop, calls=%fused_computation.18 | loop fusion | flops 786368 | bytes 524544 | tf_op jit(solution)/shard_map/reduce_sum | solution.py:30
  7.9 2.0 %fusion.10 = bf16[64,4096]{1,0:T(8,128)(2,1)} fusion(bf16[64,4096]{1,0:T(8,128)(2,1)} %param.5, f32[64]{0:T(128)S(1)} %add_rsqrt_fusion), kind=kLoop, calls=%fused_computation.20 | loop fusion | flops 1048576 | bytes 1048832 | tf_op jit(solution)/shard_map/convert_element_type | solution.py:31
  9.9 0.0 all-gather.2.cloned.1.call-update
  9.9 3.1 %collective-permute-start = (bf16[64,4096]{1,0:T(8,128)(2,1)}, bf16[64,4096]{1,0:T(8,128)(2,1)S(1)}, u32[]{:S(2)}, u32[]{:S(2)}) collective-permute-start(bf16[64,4096]{1,0:T(8,128)(2,1)} %fusion.10), channel_id=1, source_target_pairs={{0,2},{2,4},{4,6},{6,7},{7,5},{5,3},{3,1},{1,0},{8,10},{10,12},{12... | collective-permute-start | bytes 1572872 | tf_op jit(solution)/shard_map/ppermute | solution.py:58
  13.0 0.0 collective-permute-start.1
  13.0 12.0 %collective-permute-done = bf16[64,4096]{1,0:T(8,128)(2,1)S(1)} collective-permute-done((bf16[64,4096]{1,0:T(8,128)(2,1)}, bf16[64,4096]{1,0:T(8,128)(2,1)S(1)}, u32[]{:S(2)}, u32[]{:S(2)}) %collective-permute-start) | collective-permute-done | bytes 524320 | tf_op jit(solution)/shard_map/ppermute | solution.py:58
  25.1 1.8 %collective-permute-start.2 = (bf16[64,4096]{1,0:T(8,128)(2,1)S(1)}, bf16[64,4096]{1,0:T(8,128)(2,1)S(1)}, u32[]{:S(2)}, u32[]{:S(2)}) collective-permute-start(bf16[64,4096]{1,0:T(8,128)(2,1)S(1)} %collective-permute-done), channel_id=1, source_target_pairs={{0,2},{2,4},{4,6},{6,7},{7,5},{5,3},{3,1},{1,0},{8,10},{10,12},{12... | collective-permute-start | bytes 1572872 | tf_op jit(solution)/shard_map/ppermute | solution.py:58
  26.9 0.0 copy-done.4
  26.9 0.6 dynamic_slice.80
  32.2 0.0 copy-done.1
  32.2 0.7 fusion.33
  46.4 0.0 collective-permute-done.1
  46.4 0.3 collective-permute-start.3
  46.7 0.0 collective-permute-done.2
  46.7 1.8 %collective-permute-start.4 = (bf16[64,4096]{1,0:T(8,128)(2,1)S(1)}, bf16[64,4096]{1,0:T(8,128)(2,1)S(1)}, u32[]{:S(2)}, u32[]{:S(2)}) collective-permute-start(bf16[64,4096]{1,0:T(8,128)(2,1)S(1)} %collective-permute-done.2), channel_id=1, source_target_pairs={{0,2},{2,4},{4,6},{6,7},{7,5},{5,3},{3,1},{1,0},{8,10},{10,12},{12... | collective-permute-start | bytes 1572872 | tf_op jit(solution)/shard_map/ppermute | solution.py:58
  48.5 0.0 copy-done.2
  48.5 0.0 copy-done.3
  48.5 0.3 dynamic-update-slice
  48.8 44.9 %all-reduce = f32[2048]{0:T(1024)S(1)} all-reduce(f32[2048]{0:T(1024)S(1)} %dynamic-update-slice), channel_id=1, replica_groups=mesh['grp'=4,'blk'=8] {'grp','blk'}, use_global_device_ids=true, to_apply=%add | all-reduce | flops 2048 | bytes 16384
  93.7 0.1 reshape.130
  93.8 0.1 broadcast_in_dim_reshape.2
  93.9 0.0 collective-permute-done.3
  93.9 2.3 %collective-permute-start.5 = (bf16[64,4096]{1,0:T(8,128)(2,1)S(1)}, bf16[64,4096]{1,0:T(8,128)(2,1)}, u32[]{:S(2)}, u32[]{:S(2)}) collective-permute-start(bf16[64,4096]{1,0:T(8,128)(2,1)S(1)} %collective-permute-done.3), channel_id=1, source_target_pairs={{2,0},{4,2},{6,4},{7,6},{5,7},{3,5},{1,3},{0,1},{10,8},{12,10},{14... | collective-permute-start | bytes 1572872 | tf_op jit(solution)/shard_map/ppermute | solution.py:61
  96.3 0.0 collective-permute-done.4
  96.3 0.0 collective-permute-start.6
  96.3 0.0 copy-start
  96.3 2.6 %fusion = f32[256]{0:T(256)S(1)} fusion(bf16[256,4096]{1,0:T(8,128)(2,1)} %all-gather.2.cloned.1.call-done, bf16[64,4096]{1,0:T(8,128)(2,1)} %fusion.10, f32[256]{0:T(256)S(1)} %broadcast_in_dim_reshape.2, f32[256]{0:T(256)S(1)} %multiply_floor_fusion, f32[64]{0:T(128)S(1)} %get-tuple-element.8, f32[64]{0:T(128)S(1)} %get-tuple-element.7), kind=kOutput, calls=%fused_computation.10 | convolution fusion | flops 134299392 | bytes 2625024 | tf_op jit(solution)/shard_map/id,jd->ij/dot_general | solution.py:19
  98.9 0.0 copy-done
  98.9 0.8 fusion.2
  99.7 0.8 fusion.4
  100.5 0.8 fusion.1
  101.2 0.8 fusion.3
  102.0 0.8 fusion.5
  102.8 4.1 %collective-permute-done.5 = bf16[64,4096]{1,0:T(8,128)(2,1)} collective-permute-done((bf16[64,4096]{1,0:T(8,128)(2,1)S(1)}, bf16[64,4096]{1,0:T(8,128)(2,1)}, u32[]{:S(2)}, u32[]{:S(2)}) %collective-permute-start.5) | collective-permute-done | bytes 524320 | tf_op jit(solution)/shard_map/ppermute | solution.py:61
  106.9 1.8 %fusion.6 = f32[256]{0:T(256)S(1)} fusion(bf16[256,4096]{1,0:T(8,128)(2,1)S(1)} %copy-done, bf16[64,4096]{1,0:T(8,128)(2,1)} %collective-permute-done.5, f32[256]{0:T(256)S(1)} %broadcast_in_dim_reshape.2, f32[256]{0:T(256)S(1)} %multiply_floor_fusion, f32[64]{0:T(128)S(1)} %get-tuple-element.24, f32[64]{0:T(128)S(1)} %get-tuple-element.23), kind=kOutput, calls=%fused_computation.16 | convolution fusion | flops 134299392 | bytes 2625024 | tf_op jit(solution)/shard_map/id,jd->ij/dot_general | solution.py:19
  108.8 0.0 collective-permute-done.6
  108.8 0.8 fusion.7
  109.6 0.1 reshape.133
  109.7 0.1 collective-permute-start.7
  109.7 1.7 %collective-permute-start.9 = (f32[64]{0:T(128)S(1)}, f32[64]{0:T(128)S(1)}, u32[]{:S(2)}, u32[]{:S(2)}) collective-permute-start(f32[64]{0:T(128)S(1)} %get-tuple-element.34), channel_id=1, source_target_pairs={{0,24},{8,0},{16,8},{24,16},{1,25},{9,1},{17,9},{25,17},{2,26},{10... | collective-permute-start | bytes 776 | tf_op jit(solution)/shard_map/ppermute | solution.py:70
  111.5 1.0 collective-permute-start.8
  112.5 0.2 collective-permute-done.7
  112.7 0.0 collective-permute-done.9
  112.7 2.3 %collective-permute-done.8 = f32[64]{0:T(128)S(1)} collective-permute-done((f32[64]{0:T(128)S(1)}, f32[64]{0:T(128)S(1)}, u32[]{:S(2)}, u32[]{:S(2)}) %collective-permute-start.8) | collective-permute-done | bytes 288 | tf_op jit(solution)/shard_map/ppermute | solution.py:70
  115.0 0.5 fusion.22
  (11 shorter events, 0.1 us)
Async XLA Ops:
  6.5 20.4 %copy-start.4 = (s32[8]{0:T(128)S(1)}, s32[8]{0:T(128)}, u32[]{:S(2)}) copy-start(s32[8]{0:T(128)} %constant.266.clone) | copy-start | bytes 100
  6.5 25.6 %copy-start.1 = (s32[8]{0:T(128)S(1)}, s32[8]{0:T(128)}, u32[]{:S(2)}) copy-start(s32[8]{0:T(128)} %constant.265.clone) | copy-start | bytes 100
  6.5 42.0 %copy-start.2 = (s32[64]{0:T(128)S(1)}, s32[64]{0:T(128)}, u32[]{:S(2)}) copy-start(s32[64]{0:T(128)} %param.7) | copy-start | bytes 772
  6.5 42.0 %copy-start.3 = (s32[64]{0:T(128)S(1)}, s32[64]{0:T(128)}, u32[]{:S(2)}) copy-start(s32[64]{0:T(128)} %param.6) | copy-start | bytes 772
  6.5 89.7 %all-gather.2.cloned.1.call-start = ((), (), s32[]{:S(2)}) async-start(), calls=%async_computation | async-start | bytes 2621440 | tf_op jit(solution)/shard_map/all_gather | solution.py:40
  9.9 15.2 %collective-permute-start = (bf16[64,4096]{1,0:T(8,128)(2,1)}, bf16[64,4096]{1,0:T(8,128)(2,1)S(1)}, u32[]{:S(2)}, u32[]{:S(2)}) collective-permute-start(bf16[64,4096]{1,0:T(8,128)(2,1)} %fusion.10), channel_id=1, source_target_pairs={{0,2},{2,4},{4,6},{6,7},{7,5},{5,3},{3,1},{1,0},{8,10},{10,12},{12... | collective-permute-start | bytes 1572872 | tf_op jit(solution)/shard_map/ppermute | solution.py:58
  13.0 33.4 %collective-permute-start.1 = (bf16[64,4096]{1,0:T(8,128)(2,1)}, bf16[64,4096]{1,0:T(8,128)(2,1)S(1)}, u32[]{:S(2)}, u32[]{:S(2)}) collective-permute-start(bf16[64,4096]{1,0:T(8,128)(2,1)} %fusion.10), channel_id=1, source_target_pairs={{2,0},{4,2},{6,4},{7,6},{5,7},{3,5},{1,3},{0,1},{10,8},{12,10},{14... | collective-permute-start | bytes 1572872 | tf_op jit(solution)/shard_map/ppermute | solution.py:61
  25.1 21.6 %collective-permute-start.2 = (bf16[64,4096]{1,0:T(8,128)(2,1)S(1)}, bf16[64,4096]{1,0:T(8,128)(2,1)S(1)}, u32[]{:S(2)}, u32[]{:S(2)}) collective-permute-start(bf16[64,4096]{1,0:T(8,128)(2,1)S(1)} %collective-permute-done), channel_id=1, source_target_pairs={{0,2},{2,4},{4,6},{6,7},{7,5},{5,3},{3,1},{1,0},{8,10},{10,12},{12... | collective-permute-start | bytes 1572872 | tf_op jit(solution)/shard_map/ppermute | solution.py:58
  46.4 47.5 %collective-permute-start.3 = (bf16[64,4096]{1,0:T(8,128)(2,1)S(1)}, bf16[64,4096]{1,0:T(8,128)(2,1)S(1)}, u32[]{:S(2)}, u32[]{:S(2)}) collective-permute-start(bf16[64,4096]{1,0:T(8,128)(2,1)S(1)} %collective-permute-done.1), channel_id=1, source_target_pairs={{2,0},{4,2},{6,4},{7,6},{5,7},{3,5},{1,3},{0,1},{10,8},{12,10},{14... | collective-permute-start | bytes 1572872 | tf_op jit(solution)/shard_map/ppermute | solution.py:61
  46.7 49.6 %collective-permute-start.4 = (bf16[64,4096]{1,0:T(8,128)(2,1)S(1)}, bf16[64,4096]{1,0:T(8,128)(2,1)S(1)}, u32[]{:S(2)}, u32[]{:S(2)}) collective-permute-start(bf16[64,4096]{1,0:T(8,128)(2,1)S(1)} %collective-permute-done.2), channel_id=1, source_target_pairs={{0,2},{2,4},{4,6},{6,7},{7,5},{5,3},{3,1},{1,0},{8,10},{10,12},{12... | collective-permute-start | bytes 1572872 | tf_op jit(solution)/shard_map/ppermute | solution.py:58
  93.9 13.0 %collective-permute-start.5 = (bf16[64,4096]{1,0:T(8,128)(2,1)S(1)}, bf16[64,4096]{1,0:T(8,128)(2,1)}, u32[]{:S(2)}, u32[]{:S(2)}) collective-permute-start(bf16[64,4096]{1,0:T(8,128)(2,1)S(1)} %collective-permute-done.3), channel_id=1, source_target_pairs={{2,0},{4,2},{6,4},{7,6},{5,7},{3,5},{1,3},{0,1},{10,8},{12,10},{14... | collective-permute-start | bytes 1572872 | tf_op jit(solution)/shard_map/ppermute | solution.py:61
  96.3 12.5 %collective-permute-start.6 = (bf16[64,4096]{1,0:T(8,128)(2,1)S(1)}, bf16[64,4096]{1,0:T(8,128)(2,1)S(1)}, u32[]{:S(2)}, u32[]{:S(2)}) collective-permute-start(bf16[64,4096]{1,0:T(8,128)(2,1)S(1)} %collective-permute-done.4), channel_id=1, source_target_pairs={{0,2},{2,4},{4,6},{6,7},{7,5},{5,3},{3,1},{1,0},{8,10},{10,12},{12... | collective-permute-start | bytes 1572872 | tf_op jit(solution)/shard_map/ppermute | solution.py:58
  96.3 2.6 %copy-start = (bf16[256,4096]{1,0:T(8,128)(2,1)S(1)}, bf16[256,4096]{1,0:T(8,128)(2,1)}, u32[]{:S(2)}) copy-start(bf16[256,4096]{1,0:T(8,128)(2,1)} %all-gather.2.cloned.1.call-done) | copy-start | bytes 6291460
  109.7 3.0 %collective-permute-start.7 = (f32[64]{0:T(128)S(1)}, f32[64]{0:T(128)S(1)}, u32[]{:S(2)}, u32[]{:S(2)}) collective-permute-start(f32[64]{0:T(128)S(1)} %get-tuple-element.33), channel_id=1, source_target_pairs={{0,8},{8,16},{16,24},{24,0},{1,9},{9,17},{17,25},{25,1},{2,10},{10... | collective-permute-start | bytes 776 | tf_op jit(solution)/shard_map/ppermute | solution.py:70
  109.7 3.0 %collective-permute-start.9 = (f32[64]{0:T(128)S(1)}, f32[64]{0:T(128)S(1)}, u32[]{:S(2)}, u32[]{:S(2)}) collective-permute-start(f32[64]{0:T(128)S(1)} %get-tuple-element.34), channel_id=1, source_target_pairs={{0,24},{8,0},{16,8},{24,16},{1,25},{9,1},{17,9},{25,17},{2,26},{10... | collective-permute-start | bytes 776 | tf_op jit(solution)/shard_map/ppermute | solution.py:70
  111.5 3.6 %collective-permute-start.8 = (f32[64]{0:T(128)S(1)}, f32[64]{0:T(128)S(1)}, u32[]{:S(2)}, u32[]{:S(2)}) collective-permute-start(f32[64]{0:T(128)S(1)} %get-tuple-element.35), channel_id=1, source_target_pairs={{0,16},{8,24},{16,0},{24,8},{1,17},{9,25},{17,1},{25,9},{2,18},{10... | collective-permute-start | bytes 776 | tf_op jit(solution)/shard_map/ppermute | solution.py:70
Sparse Core Ops, SparseCore 0:
  10.0 25.2 all-gather.1

commit v4 on v3

v4 whole, which is shorter than its diff:
```python
import math

import jax
import jax.numpy as jnp
from jax import lax
from jax.sharding import PartitionSpec as P

D = 4096
TAG_WIDTH = 128
ORDER_SPAN = 8192.0


def ring_order(count):
    if count % 2:
        return list(range(count))
    return [2 * k for k in range(count // 2)] + [2 * k + 1 for k in reversed(range(count // 2))]


def tag_labels(payload):
    high = payload[:, D].astype(jnp.float32)
    low = payload[:, D + 1].astype(jnp.float32)
    return high * 128.0 + low


def block_best(left_rows, left_labels, payload):
    scores = jnp.einsum("id,jd->ij", left_rows, payload, preferred_element_type=jnp.float32)
    right_labels = tag_labels(payload)
    same_cluster = jnp.floor(left_labels[:, None] / ORDER_SPAN) == jnp.floor(right_labels[None, :] / ORDER_SPAN)
    earlier = same_cluster & (right_labels[None, :] < left_labels[:, None])
    return jnp.max(jnp.where(earlier, scores, jnp.float32(-1.0)), axis=1)


def per_device(embeddings, cluster_ids, row_index):
    group_count = lax.axis_size("grp")
    block_count = lax.axis_size("blk")
    rows_here = embeddings.shape[0]
    widened = embeddings.astype(jnp.float32)
    square_sum = jnp.sum(widened * widened, axis=1, keepdims=True)
    unit_rows = (widened * lax.rsqrt(square_sum / D + 1e-06) / math.sqrt(D)).astype(jnp.bfloat16)
    high = cluster_ids * 64 + row_index // 128
    low = row_index % 128
    column = jnp.arange(TAG_WIDTH)[None, :]
    tags = jnp.where(column == 0, high[:, None], jnp.where(column == 1, low[:, None], 0)).astype(jnp.bfloat16)
    payload = jnp.concatenate([unit_rows, tags], axis=1)

    left_payload = lax.all_gather(payload, "grp", axis=0, tiled=True)
    left_labels = tag_labels(left_payload)
    inside = jnp.arange(D + TAG_WIDTH)[None, :] < D
    left_rows = jnp.where(inside, left_payload, jnp.zeros_like(left_payload))

    order = ring_order(block_count)
    forward = [(order[i], order[(i + 1) % block_count]) for i in range(block_count)]
    backward = [(dst, src) for src, dst in forward]
    best = block_best(left_rows, left_labels, payload)
    ahead, behind = payload, payload
    for step in range(1, block_count // 2 + 1):
        ahead = lax.ppermute(ahead, "blk", forward)
        best = jnp.maximum(best, block_best(left_rows, left_labels, ahead))
        if step <= (block_count - 1) // 2:
            behind = lax.ppermute(behind, "blk", backward)
            best = jnp.maximum(best, block_best(left_rows, left_labels, behind))

    my_grp = lax.axis_index("grp")
    best = best.reshape(group_count, rows_here)
    result = lax.dynamic_index_in_dim(best, my_grp, axis=0, keepdims=False)
    for shift in range(1, group_count):
        target = (my_grp + shift) % group_count
        piece = lax.dynamic_index_in_dim(best, target, axis=0, keepdims=False)
        pairs = [(g, (g + shift) % group_count) for g in range(group_count)]
        result = jnp.maximum(result, lax.ppermute(piece, "grp", pairs))
    return result


def solution(mesh):
    return jax.shard_map(
        per_device,
        mesh=mesh,
        in_specs=(P(("grp", "blk"), None), P(("grp", "blk")), P(("grp", "blk"))),
        out_specs=P(("grp", "blk")),
        check_vma=False,
    )
```

time: 123 us -> 88.4 us (0.72)
  blocking collectives: 44.9 us -> 0 us
  waiting for transfers between devices: 18.8 us -> 46.4 us
  between operations: 31.8 us -> 13.6 us
  other arithmetic: 3.86 us -> 7.22 us
    unnamed x1 -> x0, blocking collectives: 44.9 us -> none
    ppermute x4, waiting for transfers between devices: 12.1 us -> 43.7 us  [per_device(): ahead = lax.ppermute(ahead, 'blk', forward)]
    ppermute x3, waiting for transfers between devices: 4.13 us -> 0.01 us  [per_device(): behind = lax.ppermute(behind, 'blk', backward)]
    add x0 -> x9, other arithmetic: none -> 2.1 us  [the longest x8 1.41 us: tag_labels(): return high * 128.0 + low]
    ppermute x3, starting transfers between devices: 2.59 us -> 0.68 us  [per_device(): behind = lax.ppermute(behind, 'blk', backward)]
    dynamic_slice x3 -> x0, local copies, waits for them, and re-layouts: 1.31 us -> none  [the longest x1 0.7 us: column_labels(): source = order_table[(my_place + shift) % block_count]]
  transfers between devices with their start and end apart: 11 -> 11, of which waited for: 4 -> 6; matrix products, arithmetic and copies ran while one was open for 8% -> 2% of each run, Pallas kernels for 0% -> 0%
where the time goes in v4:
time: 88.4 us; the launch traced here: 88 us
  waiting for transfers between devices  46.4 us (52%)
  between operations  13.6 us (15%)
  starting transfers between devices  11.2 us (13%)
  matrix products  8.24 us (9%)
  other arithmetic  7.22 us (8%)
  local copies, waits for them, and re-layouts  1.37 us (2%)
    ppermute x4, waiting for transfers between devices, per_device(): ahead = lax.ppermute(ahead, 'blk', forward)  43.7 us
    dot_general x8, matrix products, block_best(): jnp.einsum('id,jd->ij', left_rows, payload, preferred_element_type=jnp.fl...  8.24 us
    ppermute x4, starting transfers between devices, per_device(): ahead = lax.ppermute(ahead, 'blk', forward)  7.77 us
    ppermute x3, starting transfers between devices, per_device(): result = jnp.maximum(result, lax.ppermute(piece, 'grp', pairs))  2.74 us
    ppermute x3, waiting for transfers between devices, per_device(): result = jnp.maximum(result, lax.ppermute(piece, 'grp', pairs))  2.61 us
  transfers between devices with their start and end apart: 11, of which 6 were waited for; matrix products, arithmetic and copies ran while one was open for 2% of the time, Pallas kernels for 0%

profile of v4, /device:TPU:0, one launch (start us, length us, event | category | flops | bytes accessed | tf_op | source)
XLA Modules:
  0.0 88.0 jit_solution(7882567862838647717)
XLA Ops:
  6.5 1.2 %fusion.8 = f32[64]{0:T(128)S(1)} fusion(bf16[64,4096]{1,0:T(8,128)(2,1)} %param.3), kind=kLoop, calls=%fused_computation.19 | loop fusion | flops 786368 | bytes 524544 | tf_op jit(solution)/shard_map/reduce_sum | solution.py:38
  7.8 1.2 %fusion.10 = bf16[64,4096]{1,0:T(8,128)(2,1)S(1)} fusion(bf16[64,4096]{1,0:T(8,128)(2,1)} %param.3, f32[64]{0:T(128)S(1)} %add_rsqrt_fusion), kind=kLoop, calls=%fused_computation.21 | loop fusion | flops 1048576 | bytes 1048832 | tf_op jit(solution)/shard_map/convert_element_type | solution.py:39
  9.0 0.7 multiply_add_fusion
  9.7 0.1 select_convert_fusion
  9.8 0.8 pad_maximum_fusion
  10.7 0.0 all-gather.2.cloned.1.call-update
  10.7 3.1 %collective-permute-start = (bf16[64,4224]{1,0:T(8,128)(2,1)}, bf16[64,4224]{1,0:T(8,128)(2,1)S(1)}, u32[]{:S(2)}, u32[]{:S(2)}) collective-permute-start(bf16[64,4224]{1,0:T(8,128)(2,1)} %pad_maximum_fusion), channel_id=1, source_target_pairs={{0,2},{2,4},{4,6},{6,7},{7,5},{5,3},{3,1},{1,0},{8,10},{10,12},{12... | collective-permute-start | bytes 1622024 | tf_op jit(solution)/shard_map/ppermute | solution.py:57
  13.8 0.0 collective-permute-start.1
  13.8 0.2 add_reduce_fusion.7
  14.0 12.2 %collective-permute-done = bf16[64,4224]{1,0:T(8,128)(2,1)S(1)} collective-permute-done((bf16[64,4224]{1,0:T(8,128)(2,1)}, bf16[64,4224]{1,0:T(8,128)(2,1)S(1)}, u32[]{:S(2)}, u32[]{:S(2)}) %collective-permute-start) | collective-permute-done | bytes 540704 | tf_op jit(solution)/shard_map/ppermute | solution.py:57
  26.2 1.8 %collective-permute-start.2 = (bf16[64,4224]{1,0:T(8,128)(2,1)S(1)}, bf16[64,4224]{1,0:T(8,128)(2,1)S(1)}, u32[]{:S(2)}, u32[]{:S(2)}) collective-permute-start(bf16[64,4224]{1,0:T(8,128)(2,1)S(1)} %collective-permute-done), channel_id=1, source_target_pairs={{0,2},{2,4},{4,6},{6,7},{7,5},{5,3},{3,1},{1,0},{8,10},{10,12},{12... | collective-permute-start | bytes 1622024 | tf_op jit(solution)/shard_map/ppermute | solution.py:57
  28.0 0.0 collective-permute-done.1
  28.0 0.2 collective-permute-start.3
  28.2 0.2 add_reduce_fusion.6
  28.4 0.2 add_reduce_fusion.5
  28.6 11.1 %collective-permute-done.2 = bf16[64,4224]{1,0:T(8,128)(2,1)S(1)} collective-permute-done((bf16[64,4224]{1,0:T(8,128)(2,1)S(1)}, bf16[64,4224]{1,0:T(8,128)(2,1)S(1)}, u32[]{:S(2)}, u32[]{:S(2)}) %collective-permute-start.2) | collective-permute-done | bytes 540704 | tf_op jit(solution)/shard_map/ppermute | solution.py:57
  39.7 1.5 %collective-permute-start.4 = (bf16[64,4224]{1,0:T(8,128)(2,1)S(1)}, bf16[64,4224]{1,0:T(8,128)(2,1)S(1)}, u32[]{:S(2)}, u32[]{:S(2)}) collective-permute-start(bf16[64,4224]{1,0:T(8,128)(2,1)S(1)} %collective-permute-done.2), channel_id=1, source_target_pairs={{0,2},{2,4},{4,6},{6,7},{7,5},{5,3},{3,1},{1,0},{8,10},{10,12},{12... | collective-permute-start | bytes 1622024 | tf_op jit(solution)/shard_map/ppermute | solution.py:57
  41.3 0.0 collective-permute-done.3
  41.3 0.5 collective-permute-start.5
  41.8 0.2 add_reduce_fusion.4
  41.9 0.2 add_reduce_fusion.3
  42.1 10.3 %collective-permute-done.4 = bf16[64,4224]{1,0:T(8,128)(2,1)S(1)} collective-permute-done((bf16[64,4224]{1,0:T(8,128)(2,1)S(1)}, bf16[64,4224]{1,0:T(8,128)(2,1)S(1)}, u32[]{:S(2)}, u32[]{:S(2)}) %collective-permute-start.4) | collective-permute-done | bytes 540704 | tf_op jit(solution)/shard_map/ppermute | solution.py:57
  52.4 1.3 %collective-permute-start.6 = (bf16[64,4224]{1,0:T(8,128)(2,1)S(1)}, bf16[64,4224]{1,0:T(8,128)(2,1)S(1)}, u32[]{:S(2)}, u32[]{:S(2)}) collective-permute-start(bf16[64,4224]{1,0:T(8,128)(2,1)S(1)} %collective-permute-done.4), channel_id=1, source_target_pairs={{0,2},{2,4},{4,6},{6,7},{7,5},{5,3},{3,1},{1,0},{8,10},{10,12},{12... | collective-permute-start | bytes 1622024 | tf_op jit(solution)/shard_map/ppermute | solution.py:57
  53.7 0.2 add_reduce_fusion.2
  53.9 0.2 add_reduce_fusion.1
  54.1 10.1 %collective-permute-done.6 = bf16[64,4224]{1,0:T(8,128)(2,1)S(1)} collective-permute-done((bf16[64,4224]{1,0:T(8,128)(2,1)S(1)}, bf16[64,4224]{1,0:T(8,128)(2,1)S(1)}, u32[]{:S(2)}, u32[]{:S(2)}) %collective-permute-start.6) | collective-permute-done | bytes 540704 | tf_op jit(solution)/shard_map/ppermute | solution.py:57
  64.3 0.8 copy-done.3
  65.1 0.2 add_reduce_fusion
  65.3 0.0 all-gather.2.cloned.1.call-done
  65.3 1.1 %floor_reduce_fusion = (f32[256]{0:T(256)S(1)}, f32[256]{0:T(256)S(1)}) fusion(bf16[256,4224]{1,0:T(8,128)(2,1)} %all-gather.2.cloned.1.call-done), kind=kLoop, calls=%fused_computation.23 | loop fusion | flops 1536 | bytes 3072 | tf_op jit(solution)/shard_map/floor | solution.py:28
  66.4 2.6 %fusion = f32[256]{0:T(256)S(1)} fusion(bf16[256,4224]{1,0:T(8,128)(2,1)} %all-gather.2.cloned.1.call-done, pred[4224]{0:T(1024)(128)(4,1)S(1)} %iota_compare_fusion, f32[256]{0:T(256)S(1)} %get-tuple-element.6, f32[256]{0:T(256)S(1)} %get-tuple-element.5, f32[64]{0:T(128)S(1)} %add_reduce_fusion.7, f32[64]{0:T(128)S(1)} %multiply_floor_fusion.7, ...), kind=kOutput, calls=%fused_computation.11 | convolution fusion | flops 140656384 | bytes 2711168 | tf_op jit(solution)/shard_map/id,jd->ij/dot_general | solution.py:26
  69.0 0.8 fusion.1
  69.8 0.8 fusion.3
  70.7 0.2 copy-done.2
  70.9 0.8 fusion.5
  71.7 0.2 copy-done.4
  71.9 0.8 fusion.7
  72.7 0.8 fusion.2
  73.6 0.8 fusion.4
  74.4 0.8 fusion.6
  75.2 0.1 reshape.258
  75.3 0.1 collective-permute-start.7
  75.4 1.7 %collective-permute-start.9 = (f32[64]{0:T(128)S(1)}, f32[64]{0:T(128)S(1)}, u32[]{:S(2)}, u32[]{:S(2)}) collective-permute-start(f32[64]{0:T(128)S(1)} %get-tuple-element.8), channel_id=1, source_target_pairs={{0,24},{8,0},{16,8},{24,16},{1,25},{9,1},{17,9},{25,17},{2,26},{10... | collective-permute-start | bytes 776 | tf_op jit(solution)/shard_map/ppermute | solution.py:70
  77.1 1.0 %collective-permute-start.8 = (f32[64]{0:T(128)S(1)}, f32[64]{0:T(128)S(1)}, u32[]{:S(2)}, u32[]{:S(2)}) collective-permute-start(f32[64]{0:T(128)S(1)} %get-tuple-element.9), channel_id=1, source_target_pairs={{0,16},{8,24},{16,0},{24,8},{1,17},{9,25},{17,1},{25,9},{2,18},{10... | collective-permute-start | bytes 776 | tf_op jit(solution)/shard_map/ppermute | solution.py:70
  78.0 0.3 collective-permute-done.7
  78.3 0.0 collective-permute-done.9
  78.4 2.3 %collective-permute-done.8 = f32[64]{0:T(128)S(1)} collective-permute-done((f32[64]{0:T(128)S(1)}, f32[64]{0:T(128)S(1)}, u32[]{:S(2)}, u32[]{:S(2)}) %collective-permute-start.8) | collective-permute-done | bytes 288 | tf_op jit(solution)/shard_map/ppermute | solution.py:70
  80.7 0.5 fusion.15
  (22 shorter events, 0.1 us)
Async XLA Ops:
  6.5 58.7 %all-gather.2.cloned.1.call-start = ((), (), s32[]{:S(2)}) async-start(), calls=%async_computation | async-start | bytes 2703360 | tf_op jit(solution)/shard_map/all_gather | solution.py:46
  10.7 15.5 %collective-permute-start = (bf16[64,4224]{1,0:T(8,128)(2,1)}, bf16[64,4224]{1,0:T(8,128)(2,1)S(1)}, u32[]{:S(2)}, u32[]{:S(2)}) collective-permute-start(bf16[64,4224]{1,0:T(8,128)(2,1)} %pad_maximum_fusion), channel_id=1, source_target_pairs={{0,2},{2,4},{4,6},{6,7},{7,5},{5,3},{3,1},{1,0},{8,10},{10,12},{12... | collective-permute-start | bytes 1622024 | tf_op jit(solution)/shard_map/ppermute | solution.py:57
  13.8 14.2 %collective-permute-start.1 = (bf16[64,4224]{1,0:T(8,128)(2,1)}, bf16[64,4224]{1,0:T(8,128)(2,1)S(1)}, u32[]{:S(2)}, u32[]{:S(2)}) collective-permute-start(bf16[64,4224]{1,0:T(8,128)(2,1)} %pad_maximum_fusion), channel_id=1, source_target_pairs={{2,0},{4,2},{6,4},{7,6},{5,7},{3,5},{1,3},{0,1},{10,8},{12,10},{14... | collective-permute-start | bytes 1622024 | tf_op jit(solution)/shard_map/ppermute | solution.py:60
  26.2 13.5 %collective-permute-start.2 = (bf16[64,4224]{1,0:T(8,128)(2,1)S(1)}, bf16[64,4224]{1,0:T(8,128)(2,1)S(1)}, u32[]{:S(2)}, u32[]{:S(2)}) collective-permute-start(bf16[64,4224]{1,0:T(8,128)(2,1)S(1)} %collective-permute-done), channel_id=1, source_target_pairs={{0,2},{2,4},{4,6},{6,7},{7,5},{5,3},{3,1},{1,0},{8,10},{10,12},{12... | collective-permute-start | bytes 1622024 | tf_op jit(solution)/shard_map/ppermute | solution.py:57
  28.0 13.3 %collective-permute-start.3 = (bf16[64,4224]{1,0:T(8,128)(2,1)S(1)}, bf16[64,4224]{1,0:T(8,128)(2,1)S(1)}, u32[]{:S(2)}, u32[]{:S(2)}) collective-permute-start(bf16[64,4224]{1,0:T(8,128)(2,1)S(1)} %collective-permute-done.1), channel_id=1, source_target_pairs={{2,0},{4,2},{6,4},{7,6},{5,7},{3,5},{1,3},{0,1},{10,8},{12,10},{14... | collective-permute-start | bytes 1622024 | tf_op jit(solution)/shard_map/ppermute | solution.py:60
  39.7 12.7 %collective-permute-start.4 = (bf16[64,4224]{1,0:T(8,128)(2,1)S(1)}, bf16[64,4224]{1,0:T(8,128)(2,1)S(1)}, u32[]{:S(2)}, u32[]{:S(2)}) collective-permute-start(bf16[64,4224]{1,0:T(8,128)(2,1)S(1)} %collective-permute-done.2), channel_id=1, source_target_pairs={{0,2},{2,4},{4,6},{6,7},{7,5},{5,3},{3,1},{1,0},{8,10},{10,12},{12... | collective-permute-start | bytes 1622024 | tf_op jit(solution)/shard_map/ppermute | solution.py:57
  41.3 12.6 %collective-permute-start.5 = (bf16[64,4224]{1,0:T(8,128)(2,1)S(1)}, bf16[64,4224]{1,0:T(8,128)(2,1)S(1)}, u32[]{:S(2)}, u32[]{:S(2)}) collective-permute-start(bf16[64,4224]{1,0:T(8,128)(2,1)S(1)} %collective-permute-done.3), channel_id=1, source_target_pairs={{2,0},{4,2},{6,4},{7,6},{5,7},{3,5},{1,3},{0,1},{10,8},{12,10},{14... | collective-permute-start | bytes 1622024 | tf_op jit(solution)/shard_map/ppermute | solution.py:60
  52.4 1.5 %copy-start.1 = (bf16[64,4224]{1,0:T(8,128)(2,1)}, bf16[64,4224]{1,0:T(8,128)(2,1)S(1)}, u32[]{:S(2)}) copy-start(bf16[64,4224]{1,0:T(8,128)(2,1)S(1)} %collective-permute-done.4) | copy-start | bytes 1622020
  52.4 11.8 %collective-permute-start.6 = (bf16[64,4224]{1,0:T(8,128)(2,1)S(1)}, bf16[64,4224]{1,0:T(8,128)(2,1)S(1)}, u32[]{:S(2)}, u32[]{:S(2)}) collective-permute-start(bf16[64,4224]{1,0:T(8,128)(2,1)S(1)} %collective-permute-done.4), channel_id=1, source_target_pairs={{0,2},{2,4},{4,6},{6,7},{7,5},{5,3},{3,1},{1,0},{8,10},{10,12},{12... | collective-permute-start | bytes 1622024 | tf_op jit(solution)/shard_map/ppermute | solution.py:57
  64.3 0.8 copy-start.3
  66.4 2.6 %copy-start = (bf16[256,4224]{1,0:T(8,128)(2,1)S(1)}, bf16[256,4224]{1,0:T(8,128)(2,1)}, u32[]{:S(2)}) copy-start(bf16[256,4224]{1,0:T(8,128)(2,1)} %all-gather.2.cloned.1.call-done) | copy-start | bytes 6488068
  69.8 1.0 %copy-start.2 = (bf16[64,4224]{1,0:T(8,128)(2,1)S(1)}, bf16[64,4224]{1,0:T(8,128)(2,1)}, u32[]{:S(2)}) copy-start(bf16[64,4224]{1,0:T(8,128)(2,1)} %copy-done.1) | copy-start | bytes 1622020
  70.9 1.0 %copy-start.4 = (bf16[64,4224]{1,0:T(8,128)(2,1)S(1)}, bf16[64,4224]{1,0:T(8,128)(2,1)}, u32[]{:S(2)}) copy-start(bf16[64,4224]{1,0:T(8,128)(2,1)} %copy-done.3) | copy-start | bytes 1622020
  75.3 3.0 %collective-permute-start.7 = (f32[64]{0:T(128)S(1)}, f32[64]{0:T(128)S(1)}, u32[]{:S(2)}, u32[]{:S(2)}) collective-permute-start(f32[64]{0:T(128)S(1)} %get-tuple-element.7), channel_id=1, source_target_pairs={{0,8},{8,16},{16,24},{24,0},{1,9},{9,17},{17,25},{25,1},{2,10},{10... | collective-permute-start | bytes 776 | tf_op jit(solution)/shard_map/ppermute | solution.py:70
  75.4 3.0 %collective-permute-start.9 = (f32[64]{0:T(128)S(1)}, f32[64]{0:T(128)S(1)}, u32[]{:S(2)}, u32[]{:S(2)}) collective-permute-start(f32[64]{0:T(128)S(1)} %get-tuple-element.8), channel_id=1, source_target_pairs={{0,24},{8,0},{16,8},{24,16},{1,25},{9,1},{17,9},{25,17},{2,26},{10... | collective-permute-start | bytes 776 | tf_op jit(solution)/shard_map/ppermute | solution.py:70
  77.1 3.6 %collective-permute-start.8 = (f32[64]{0:T(128)S(1)}, f32[64]{0:T(128)S(1)}, u32[]{:S(2)}, u32[]{:S(2)}) collective-permute-start(f32[64]{0:T(128)S(1)} %get-tuple-element.9), channel_id=1, source_target_pairs={{0,16},{8,24},{16,0},{24,8},{1,17},{9,25},{17,1},{25,9},{2,18},{10... | collective-permute-start | bytes 776 | tf_op jit(solution)/shard_map/ppermute | solution.py:70
Sparse Core Ops, SparseCore 0:
  10.8 25.6 all-gather.1

commit v5 on v4

--- a/solution.py
+++ b/solution.py
@@ -30,6 +30,10 @@
     return jnp.max(jnp.where(earlier, scores, jnp.float32(-1.0)), axis=1)
 
 
+def partner_pairs(group_count, mask):
+    return [(g, g ^ mask) for g in range(group_count)]
+
+
 def per_device(embeddings, cluster_ids, row_index):
     group_count = lax.axis_size("grp")
     block_count = lax.axis_size("blk")
@@ -43,7 +47,17 @@
     tags = jnp.where(column == 0, high[:, None], jnp.where(column == 1, low[:, None], 0)).astype(jnp.bfloat16)
     payload = jnp.concatenate([unit_rows, tags], axis=1)
 
-    left_payload = lax.all_gather(payload, "grp", axis=0, tiled=True)
+    if group_count == 4:
+        across = lax.ppermute(payload, "grp", partner_pairs(group_count, 2))
+        beside = lax.ppermute(payload, "grp", partner_pairs(group_count, 1))
+        diagonal = lax.ppermute(across, "grp", partner_pairs(group_count, 1))
+        segment_pairs = [partner_pairs(group_count, k) for k in range(1, 4)]
+        left_payload = jnp.concatenate([payload, beside, across, diagonal], axis=0)
+    else:
+        shifted = [lax.ppermute(payload, "grp", [(g, (g + k) % group_count) for g in range(group_count)])
+                   for k in range(1, group_count)]
+        segment_pairs = [[(g, (g - k) % group_count) for g in range(group_count)] for k in range(1, group_count)]
+        left_payload = jnp.concatenate([payload] + shifted, axis=0)
     left_labels = tag_labels(left_payload)
     inside = jnp.arange(D + TAG_WIDTH)[None, :] < D
     left_rows = jnp.where(inside, left_payload, jnp.zeros_like(left_payload))
@@ -51,23 +65,33 @@
     order = ring_order(block_count)
     forward = [(order[i], order[(i + 1) % block_count]) for i in range(block_count)]
     backward = [(dst, src) for src, dst in forward]
-    best = block_best(left_rows, left_labels, payload)
+    best = None
+    pending = [payload]
     ahead, behind = payload, payload
     for step in range(1, block_count // 2 + 1):
         ahead = lax.ppermute(ahead, "blk", forward)
-        best = jnp.maximum(best, block_best(left_rows, left_labels, ahead))
+        stepped = [ahead]
         if step <= (block_count - 1) // 2:
             behind = lax.ppermute(behind, "blk", backward)
-            best = jnp.maximum(best, block_best(left_rows, left_labels, behind))
+            stepped.append(behind)
+        if step >= 2:
+            for block in pending:
+                tile = block_best(left_rows, left_labels, block)
+                best = tile if best is None else jnp.maximum(best, tile)
+            pending = []
+            stepped, best = lax.optimization_barrier((stepped, best))
+            ahead = stepped[0]
+            if len(stepped) > 1:
+                behind = stepped[1]
+        pending.extend(stepped)
+    for block in pending:
+        tile = block_best(left_rows, left_labels, block)
+        best = tile if best is None else jnp.maximum(best, tile)
 
-    my_grp = lax.axis_index("grp")
     best = best.reshape(group_count, rows_here)
-    result = lax.dynamic_index_in_dim(best, my_grp, axis=0, keepdims=False)
-    for shift in range(1, group_count):
-        target = (my_grp + shift) % group_count
-        piece = lax.dynamic_index_in_dim(best, target, axis=0, keepdims=False)
-        pairs = [(g, (g + shift) % group_count) for g in range(group_count)]
-        result = jnp.maximum(result, lax.ppermute(piece, "grp", pairs))
+    result = best[0]
+    for k, pairs in enumerate(segment_pairs, start=1):
+        result = jnp.maximum(result, lax.ppermute(best[k], "grp", pairs))
     return result
 
 

time: 88.4 us -> 68.8 us (0.78)
  between operations: 13.6 us -> 0.2 us
  waiting for transfers between devices: 46.4 us -> 41.1 us
  matrix products: 8.24 us -> 6.5 us
  starting transfers between devices: 11.2 us -> 12.7 us
  local copies, waits for them, and re-layouts: 1.37 us -> 0.07 us
    ppermute x4, waiting for transfers between devices: 43.7 us -> 23.8 us  [per_device(): ahead = lax.ppermute(ahead, 'blk', forward)]
    ppermute x3 -> x6, waiting for transfers between devices: 2.61 us -> 11.8 us  [the longest x1 10.1 us: per_device(): across = lax.ppermute(payload, 'grp', partner_pairs(group_count, 2))]
    ppermute x3, waiting for transfers between devices: 0.01 us -> 5.43 us  [per_device(): behind = lax.ppermute(behind, 'blk', backward)]
    concatenate x0 -> x1, other arithmetic: none -> 2.48 us  [per_device(): left_payload = jnp.concatenate([payload, beside, across, diagonal], axis=0)]
    ppermute x3 -> x6, starting transfers between devices: 2.74 us -> 4.93 us  [the longest x1 3.06 us: per_device(): across = lax.ppermute(payload, 'grp', partner_pairs(group_count, 2))]
    dot_general x8, matrix products: 8.24 us -> 6.5 us  [block_best(): jnp.einsum('id,jd->ij', left_rows, payload, preferred_element_type=jnp.fl...]
    ppermute x4, starting transfers between devices: 7.77 us -> 6.41 us  [per_device(): ahead = lax.ppermute(ahead, 'blk', forward)]
    unnamed x10 -> x0, local copies, waits for them, and re-layouts: 1.28 us -> none
  transfers between devices with their start and end apart: 11 -> 13, of which waited for: 6 -> 9; matrix products, arithmetic and copies ran while one was open for 2% -> 14% of each run, Pallas kernels for 0% -> 0%
where the time goes in v5:
time: 68.8 us; the launch traced here: 68.6 us
  waiting for transfers between devices  41.1 us (60%)
  starting transfers between devices  12.7 us (18%)
  other arithmetic  7.97 us (12%)
  matrix products  6.5 us (9%)
    ppermute x4, waiting for transfers between devices, per_device(): ahead = lax.ppermute(ahead, 'blk', forward)  23.8 us
    ppermute x1, waiting for transfers between devices, per_device(): across = lax.ppermute(payload, 'grp', partner_pairs(group_count, 2))  10.1 us
    dot_general x8, matrix products, block_best(): jnp.einsum('id,jd->ij', left_rows, payload, preferred_element_type=jnp.fl...  6.5 us
    ppermute x4, starting transfers between devices, per_device(): ahead = lax.ppermute(ahead, 'blk', forward)  6.41 us
    ppermute x3, waiting for transfers between devices, per_device(): behind = lax.ppermute(behind, 'blk', backward)  5.43 us
    ppermute x1, starting transfers between devices, per_device(): across = lax.ppermute(payload, 'grp', partner_pairs(group_count, 2))  3.06 us
    concatenate x1, other arithmetic, per_device(): left_payload = jnp.concatenate([payload, beside, across, diagonal], axis=0)  2.48 us
    ppermute x3, starting transfers between devices, per_device(): result = jnp.maximum(result, lax.ppermute(best[k], 'grp', pairs))  1.86 us
  transfers between devices with their start and end apart: 13, of which 9 were waited for; matrix products, arithmetic and copies ran while one was open for 14% of the time, Pallas kernels for 0%

profile of v5, /device:TPU:0, one launch (start us, length us, event | category | flops | bytes accessed | tf_op | source)
XLA Modules:
  0.0 68.6 jit_solution(10498678410486524617)
XLA Ops:
  0.0 1.2 %fusion.8 = f32[64]{0:T(128)S(1)} fusion(bf16[64,4096]{1,0:T(8,128)(2,1)} %param.3), kind=kLoop, calls=%fused_computation.20 | loop fusion | flops 786368 | bytes 524544 | tf_op jit(solution)/shard_map/reduce_sum | solution.py:42
  1.3 1.2 %fusion.10 = bf16[64,4096]{1,0:T(8,128)(2,1)S(1)} fusion(bf16[64,4096]{1,0:T(8,128)(2,1)} %param.3, f32[64]{0:T(128)S(1)} %add_rsqrt_fusion), kind=kLoop, calls=%fused_computation.22 | loop fusion | flops 1048576 | bytes 1048832 | tf_op jit(solution)/shard_map/convert_element_type | solution.py:43
  2.5 0.7 multiply_add_fusion
  3.2 0.1 select_convert_fusion
  3.3 3.1 %collective-permute-start.5 = (bf16[64,4224]{1,0:T(8,128)(2,1)S(1)}, bf16[64,4224]{1,0:T(8,128)(2,1)S(1)}, u32[]{:S(2)}, u32[]{:S(2)}) collective-permute-start(bf16[64,4224]{1,0:T(8,128)(2,1)S(1)} %pad_maximum_fusion.1), channel_id=1, source_target_pairs={{0,16},{8,24},{16,0},{24,8},{1,17},{9,25},{17,1},{25,9},{2,18},{10... | collective-permute-start | bytes 1622024 | tf_op jit(solution)/shard_map/ppermute | solution.py:51
  6.4 1.6 %collective-permute-start = (bf16[64,4224]{1,0:T(8,128)(2,1)S(1)}, bf16[64,4224]{1,0:T(8,128)(2,1)S(1)}, u32[]{:S(2)}, u32[]{:S(2)}) collective-permute-start(bf16[64,4224]{1,0:T(8,128)(2,1)S(1)} %pad_maximum_fusion.1), channel_id=1, source_target_pairs={{0,2},{2,4},{4,6},{6,7},{7,5},{5,3},{3,1},{1,0},{8,10},{10,12},{12... | collective-permute-start | bytes 1622024 | tf_op jit(solution)/shard_map/ppermute | solution.py:72
  8.0 0.0 collective-permute-start.4
  8.0 0.4 collective-permute-start.2
  8.4 0.2 add_reduce_fusion.7
  8.6 10.1 %collective-permute-done.5 = bf16[64,4224]{1,0:T(8,128)(2,1)S(1)} collective-permute-done((bf16[64,4224]{1,0:T(8,128)(2,1)S(1)}, bf16[64,4224]{1,0:T(8,128)(2,1)S(1)}, u32[]{:S(2)}, u32[]{:S(2)}) %collective-permute-start.5) | collective-permute-done | bytes 540704 | tf_op jit(solution)/shard_map/ppermute | solution.py:51
  18.7 0.0 collective-permute-start.6
  18.7 1.5 %collective-permute-done = bf16[64,4224]{1,0:T(8,128)(2,1)S(1)} collective-permute-done((bf16[64,4224]{1,0:T(8,128)(2,1)S(1)}, bf16[64,4224]{1,0:T(8,128)(2,1)S(1)}, u32[]{:S(2)}, u32[]{:S(2)}) %collective-permute-start) | collective-permute-done | bytes 540704 | tf_op jit(solution)/shard_map/ppermute | solution.py:72
  20.1 1.6 %collective-permute-start.1 = (bf16[64,4224]{1,0:T(8,128)(2,1)S(1)}, bf16[64,4224]{1,0:T(8,128)(2,1)S(1)}, u32[]{:S(2)}, u32[]{:S(2)}) collective-permute-start(bf16[64,4224]{1,0:T(8,128)(2,1)S(1)} %collective-permute-done), channel_id=1, source_target_pairs={{0,2},{2,4},{4,6},{6,7},{7,5},{5,3},{3,1},{1,0},{8,10},{10,12},{12... | collective-permute-start | bytes 1622024 | tf_op jit(solution)/shard_map/ppermute | solution.py:72
  21.7 0.2 add_reduce_fusion.6
  21.9 0.8 %collective-permute-done.2 = bf16[64,4224]{1,0:T(8,128)(2,1)S(1)} collective-permute-done((bf16[64,4224]{1,0:T(8,128)(2,1)S(1)}, bf16[64,4224]{1,0:T(8,128)(2,1)S(1)}, u32[]{:S(2)}, u32[]{:S(2)}) %collective-permute-start.2) | collective-permute-done | bytes 540704 | tf_op jit(solution)/shard_map/ppermute | solution.py:75
  22.7 0.4 collective-permute-start.3
  23.1 0.2 add_reduce_fusion.5
  23.3 0.0 collective-permute-done.4
  23.3 2.5 %pad_maximum_fusion = bf16[256,4224]{1,0:T(8,128)(2,1)S(1)} fusion(bf16[64,4224]{1,0:T(8,128)(2,1)S(1)} %collective-permute-done.6, bf16[64,4224]{1,0:T(8,128)(2,1)S(1)} %collective-permute-done.5, bf16[64,4224]{1,0:T(8,128)(2,1)S(1)} %collective-permute-done.4, bf16[64,128]{1,0:T(8,128)(2,1)S(1)} %select_convert_fusion, bf16[64,4096]{1,0:T(8,128)(2,1)S(1)} %fusion.10), kind=kLoop, calls=%fused_computation | loop fusion | flops 10813440 | bytes 4325376 | tf_op jit(solution)/shard_map/concatenate | solution.py:55
  25.8 0.2 floor_reduce_fusion
  26.0 0.8 %fusion.1 = f32[256]{0:T(256)S(1)} fusion(bf16[64,4224]{1,0:T(8,128)(2,1)S(1)} %collective-permute-done, bf16[256,4224]{1,0:T(8,128)(2,1)S(1)} %pad_maximum_fusion, pred[4224]{0:T(1024)(128)(4,1)S(1)} %iota_compare_fusion, f32[256]{0:T(256)S(1)} %get-tuple-element.22, f32[256]{0:T(256)S(1)} %get-tuple-element.21, f32[64]{0:T(128)S(1)} %add_reduce_fusion.6, ...), kind=kOutput, calls=%fused_computation.13 | convolution fusion | flops 139575040 | bytes 2711168 | tf_op jit(solution)/shard_map/id,jd->ij/dot_general | solution.py:26
  26.9 0.8 %fusion = f32[256]{0:T(256)S(1)} fusion(bf16[256,4224]{1,0:T(8,128)(2,1)S(1)} %pad_maximum_fusion, pred[4224]{0:T(1024)(128)(4,1)S(1)} %iota_compare_fusion, f32[256]{0:T(256)S(1)} %get-tuple-element.22, f32[256]{0:T(256)S(1)} %get-tuple-element.21, f32[64]{0:T(128)S(1)} %add_reduce_fusion.7, f32[64]{0:T(128)S(1)} %multiply_floor_fusion.7, ...), kind=kOutput, calls=%fused_computation.12 | convolution fusion | flops 140656384 | bytes 2711168 | tf_op jit(solution)/shard_map/id,jd->ij/dot_general | solution.py:26
  27.7 0.8 %fusion.2 = f32[256]{0:T(256)S(1)} fusion(bf16[64,4224]{1,0:T(8,128)(2,1)S(1)} %collective-permute-done.2, bf16[256,4224]{1,0:T(8,128)(2,1)S(1)} %pad_maximum_fusion, pred[4224]{0:T(1024)(128)(4,1)S(1)} %iota_compare_fusion, f32[256]{0:T(256)S(1)} %get-tuple-element.22, f32[256]{0:T(256)S(1)} %get-tuple-element.21, f32[64]{0:T(128)S(1)} %add_reduce_fusion.5, ...), kind=kOutput, calls=%fused_computation.14 | convolution fusion | flops 139575040 | bytes 2711168 | tf_op jit(solution)/shard_map/id,jd->ij/dot_general | solution.py:26
  28.5 4.9 %collective-permute-done.1 = bf16[64,4224]{1,0:T(8,128)(2,1)S(1)} collective-permute-done((bf16[64,4224]{1,0:T(8,128)(2,1)S(1)}, bf16[64,4224]{1,0:T(8,128)(2,1)S(1)}, u32[]{:S(2)}, u32[]{:S(2)}) %collective-permute-start.1) | collective-permute-done | bytes 540704 | tf_op jit(solution)/shard_map/ppermute | solution.py:72
  33.4 3.1 %collective-permute-done.3 = bf16[64,4224]{1,0:T(8,128)(2,1)S(1)} collective-permute-done((bf16[64,4224]{1,0:T(8,128)(2,1)S(1)}, bf16[64,4224]{1,0:T(8,128)(2,1)S(1)}, u32[]{:S(2)}, u32[]{:S(2)}) %collective-permute-start.3) | collective-permute-done | bytes 540704 | tf_op jit(solution)/shard_map/ppermute | solution.py:75
  36.5 0.2 add_reduce_fusion.4
  36.7 1.6 %collective-permute-start.7 = (bf16[64,4224]{1,0:T(8,128)(2,1)S(1)}, bf16[64,4224]{1,0:T(8,128)(2,1)S(1)}, u32[]{:S(2)}, u32[]{:S(2)}) collective-permute-start(bf16[64,4224]{1,0:T(8,128)(2,1)S(1)} %collective-permute-done.1), channel_id=1, source_target_pairs={{0,2},{2,4},{4,6},{6,7},{7,5},{5,3},{3,1},{1,0},{8,10},{10,12},{12... | collective-permute-start | bytes 1622024 | tf_op jit(solution)/shard_map/ppermute | solution.py:72
  38.3 0.2 add_reduce_fusion.3
  38.5 0.5 collective-permute-start.8
  39.0 0.8 %fusion.3 = f32[256]{0:T(256)S(1)} fusion(bf16[64,4224]{1,0:T(8,128)(2,1)S(1)} %collective-permute-done.1, bf16[256,4224]{1,0:T(8,128)(2,1)S(1)} %pad_maximum_fusion, pred[4224]{0:T(1024)(128)(4,1)S(1)} %iota_compare_fusion, f32[256]{0:T(256)S(1)} %get-tuple-element.22, f32[256]{0:T(256)S(1)} %get-tuple-element.21, f32[64]{0:T(128)S(1)} %add_reduce_fusion.4, ...), kind=kOutput, calls=%fused_computation.15 | convolution fusion | flops 139575040 | bytes 2711168 | tf_op jit(solution)/shard_map/id,jd->ij/dot_general | solution.py:26
  39.8 0.8 %fusion.4 = f32[256]{0:T(256)S(1)} fusion(bf16[64,4224]{1,0:T(8,128)(2,1)S(1)} %collective-permute-done.3, bf16[256,4224]{1,0:T(8,128)(2,1)S(1)} %pad_maximum_fusion, pred[4224]{0:T(1024)(128)(4,1)S(1)} %iota_compare_fusion, f32[256]{0:T(256)S(1)} %get-tuple-element.22, f32[256]{0:T(256)S(1)} %get-tuple-element.21, f32[64]{0:T(128)S(1)} %add_reduce_fusion.3, ...), kind=kOutput, calls=%fused_computation.16 | convolution fusion | flops 139575040 | bytes 2711168 | tf_op jit(solution)/shard_map/id,jd->ij/dot_general | solution.py:26
  40.6 9.1 %collective-permute-done.7 = bf16[64,4224]{1,0:T(8,128)(2,1)S(1)} collective-permute-done((bf16[64,4224]{1,0:T(8,128)(2,1)S(1)}, bf16[64,4224]{1,0:T(8,128)(2,1)S(1)}, u32[]{:S(2)}, u32[]{:S(2)}) %collective-permute-start.7) | collective-permute-done | bytes 540704 | tf_op jit(solution)/shard_map/ppermute | solution.py:72
  49.7 1.5 %collective-permute-done.8 = bf16[64,4224]{1,0:T(8,128)(2,1)S(1)} collective-permute-done((bf16[64,4224]{1,0:T(8,128)(2,1)S(1)}, bf16[64,4224]{1,0:T(8,128)(2,1)S(1)}, u32[]{:S(2)}, u32[]{:S(2)}) %collective-permute-start.8) | collective-permute-done | bytes 540704 | tf_op jit(solution)/shard_map/ppermute | solution.py:75
  51.2 0.2 add_reduce_fusion.2
  51.4 1.6 %collective-permute-start.9 = (bf16[64,4224]{1,0:T(8,128)(2,1)S(1)}, bf16[64,4224]{1,0:T(8,128)(2,1)S(1)}, u32[]{:S(2)}, u32[]{:S(2)}) collective-permute-start(bf16[64,4224]{1,0:T(8,128)(2,1)S(1)} %collective-permute-done.7), channel_id=1, source_target_pairs={{0,2},{2,4},{4,6},{6,7},{7,5},{5,3},{3,1},{1,0},{8,10},{10,12},{12... | collective-permute-start | bytes 1622024 | tf_op jit(solution)/shard_map/ppermute | solution.py:72
  53.0 0.8 %fusion.5 = f32[256]{0:T(256)S(1)} fusion(bf16[64,4224]{1,0:T(8,128)(2,1)S(1)} %collective-permute-done.7, bf16[256,4224]{1,0:T(8,128)(2,1)S(1)} %pad_maximum_fusion, pred[4224]{0:T(1024)(128)(4,1)S(1)} %iota_compare_fusion, f32[256]{0:T(256)S(1)} %get-tuple-element.22, f32[256]{0:T(256)S(1)} %get-tuple-element.21, f32[64]{0:T(128)S(1)} %add_reduce_fusion.2, ...), kind=kOutput, calls=%fused_computation.17 | convolution fusion | flops 139575040 | bytes 2711168 | tf_op jit(solution)/shard_map/id,jd->ij/dot_general | solution.py:26
  53.8 0.2 add_reduce_fusion.1
  54.0 0.8 %fusion.6 = f32[256]{0:T(256)S(1)} fusion(bf16[64,4224]{1,0:T(8,128)(2,1)S(1)} %collective-permute-done.8, bf16[256,4224]{1,0:T(8,128)(2,1)S(1)} %pad_maximum_fusion, pred[4224]{0:T(1024)(128)(4,1)S(1)} %iota_compare_fusion, f32[256]{0:T(256)S(1)} %get-tuple-element.22, f32[256]{0:T(256)S(1)} %get-tuple-element.21, f32[64]{0:T(128)S(1)} %add_reduce_fusion.1, ...), kind=kOutput, calls=%fused_computation.18 | convolution fusion | flops 139575040 | bytes 2711168 | tf_op jit(solution)/shard_map/id,jd->ij/dot_general | solution.py:26
  54.9 8.4 %collective-permute-done.9 = bf16[64,4224]{1,0:T(8,128)(2,1)S(1)} collective-permute-done((bf16[64,4224]{1,0:T(8,128)(2,1)S(1)}, bf16[64,4224]{1,0:T(8,128)(2,1)S(1)}, u32[]{:S(2)}, u32[]{:S(2)}) %collective-permute-start.9) | collective-permute-done | bytes 540704 | tf_op jit(solution)/shard_map/ppermute | solution.py:72
  63.3 0.2 add_reduce_fusion
  63.5 0.8 %fusion.7 = f32[256]{0:T(256)S(1)} fusion(bf16[64,4224]{1,0:T(8,128)(2,1)S(1)} %collective-permute-done.9, bf16[256,4224]{1,0:T(8,128)(2,1)S(1)} %pad_maximum_fusion, pred[4224]{0:T(1024)(128)(4,1)S(1)} %iota_compare_fusion, f32[256]{0:T(256)S(1)} %get-tuple-element.22, f32[256]{0:T(256)S(1)} %get-tuple-element.21, f32[64]{0:T(128)S(1)} %add_reduce_fusion, ...), kind=kOutput, calls=%fused_computation.19 | convolution fusion | flops 139575040 | bytes 2711168 | tf_op jit(solution)/shard_map/id,jd->ij/dot_general | solution.py:26
  64.3 0.1 fusion.20
  64.4 0.0 collective-permute-start.10
  64.4 0.6 collective-permute-start.11
  65.0 1.3 %collective-permute-start.12 = (f32[64]{0:T(128)S(1)}, f32[64]{0:T(128)S(1)}, u32[]{:S(2)}, u32[]{:S(2)}) collective-permute-start(f32[64]{0:T(128)S(1)} %get-tuple-element.24), channel_id=1, source_target_pairs={{0,24},{8,16},{16,8},{24,0},{1,25},{9,17},{17,9},{25,1},{2,26},{10... | collective-permute-start | bytes 776 | tf_op jit(solution)/shard_map/ppermute | solution.py:94
  66.2 0.0 collective-permute-done.10
  66.2 1.8 %collective-permute-done.11 = f32[64]{0:T(128)S(1)} collective-permute-done((f32[64]{0:T(128)S(1)}, f32[64]{0:T(128)S(1)}, u32[]{:S(2)}, u32[]{:S(2)}) %collective-permute-start.11) | collective-permute-done | bytes 288 | tf_op jit(solution)/shard_map/ppermute | solution.py:94
  68.0 0.5 maximum_maximum_fusion.3
  (18 shorter events, 0.1 us)
Async XLA Ops:
  3.3 15.3 %collective-permute-start.5 = (bf16[64,4224]{1,0:T(8,128)(2,1)S(1)}, bf16[64,4224]{1,0:T(8,128)(2,1)S(1)}, u32[]{:S(2)}, u32[]{:S(2)}) collective-permute-start(bf16[64,4224]{1,0:T(8,128)(2,1)S(1)} %pad_maximum_fusion.1), channel_id=1, source_target_pairs={{0,16},{8,24},{16,0},{24,8},{1,17},{9,25},{17,1},{25,9},{2,18},{10... | collective-permute-start | bytes 1622024 | tf_op jit(solution)/shard_map/ppermute | solution.py:51
  6.4 13.7 %collective-permute-start = (bf16[64,4224]{1,0:T(8,128)(2,1)S(1)}, bf16[64,4224]{1,0:T(8,128)(2,1)S(1)}, u32[]{:S(2)}, u32[]{:S(2)}) collective-permute-start(bf16[64,4224]{1,0:T(8,128)(2,1)S(1)} %pad_maximum_fusion.1), channel_id=1, source_target_pairs={{0,2},{2,4},{4,6},{6,7},{7,5},{5,3},{3,1},{1,0},{8,10},{10,12},{12... | collective-permute-start | bytes 1622024 | tf_op jit(solution)/shard_map/ppermute | solution.py:72
  8.0 15.3 %collective-permute-start.4 = (bf16[64,4224]{1,0:T(8,128)(2,1)S(1)}, bf16[64,4224]{1,0:T(8,128)(2,1)S(1)}, u32[]{:S(2)}, u32[]{:S(2)}) collective-permute-start(bf16[64,4224]{1,0:T(8,128)(2,1)S(1)} %pad_maximum_fusion.1), channel_id=1, source_target_pairs={{0,8},{8,0},{16,24},{24,16},{1,9},{9,1},{17,25},{25,17},{2,10},{10... | collective-permute-start | bytes 1622024 | tf_op jit(solution)/shard_map/ppermute | solution.py:52
  8.0 14.7 %collective-permute-start.2 = (bf16[64,4224]{1,0:T(8,128)(2,1)S(1)}, bf16[64,4224]{1,0:T(8,128)(2,1)S(1)}, u32[]{:S(2)}, u32[]{:S(2)}) collective-permute-start(bf16[64,4224]{1,0:T(8,128)(2,1)S(1)} %pad_maximum_fusion.1), channel_id=1, source_target_pairs={{2,0},{4,2},{6,4},{7,6},{5,7},{3,5},{1,3},{0,1},{10,8},{12,10},{14... | collective-permute-start | bytes 1622024 | tf_op jit(solution)/shard_map/ppermute | solution.py:75
  18.7 4.7 %collective-permute-start.6 = (bf16[64,4224]{1,0:T(8,128)(2,1)S(1)}, bf16[64,4224]{1,0:T(8,128)(2,1)S(1)}, u32[]{:S(2)}, u32[]{:S(2)}) collective-permute-start(bf16[64,4224]{1,0:T(8,128)(2,1)S(1)} %collective-permute-done.5), channel_id=1, source_target_pairs={{0,8},{8,0},{16,24},{24,16},{1,9},{9,1},{17,25},{25,17},{2,10},{10... | collective-permute-start | bytes 1622024 | tf_op jit(solution)/shard_map/ppermute | solution.py:53
  20.1 13.2 %collective-permute-start.1 = (bf16[64,4224]{1,0:T(8,128)(2,1)S(1)}, bf16[64,4224]{1,0:T(8,128)(2,1)S(1)}, u32[]{:S(2)}, u32[]{:S(2)}) collective-permute-start(bf16[64,4224]{1,0:T(8,128)(2,1)S(1)} %collective-permute-done), channel_id=1, source_target_pairs={{0,2},{2,4},{4,6},{6,7},{7,5},{5,3},{3,1},{1,0},{8,10},{10,12},{12... | collective-permute-start | bytes 1622024 | tf_op jit(solution)/shard_map/ppermute | solution.py:72
  22.7 13.8 %collective-permute-start.3 = (bf16[64,4224]{1,0:T(8,128)(2,1)S(1)}, bf16[64,4224]{1,0:T(8,128)(2,1)S(1)}, u32[]{:S(2)}, u32[]{:S(2)}) collective-permute-start(bf16[64,4224]{1,0:T(8,128)(2,1)S(1)} %collective-permute-done.2), channel_id=1, source_target_pairs={{2,0},{4,2},{6,4},{7,6},{5,7},{3,5},{1,3},{0,1},{10,8},{12,10},{14... | collective-permute-start | bytes 1622024 | tf_op jit(solution)/shard_map/ppermute | solution.py:75
  36.7 13.0 %collective-permute-start.7 = (bf16[64,4224]{1,0:T(8,128)(2,1)S(1)}, bf16[64,4224]{1,0:T(8,128)(2,1)S(1)}, u32[]{:S(2)}, u32[]{:S(2)}) collective-permute-start(bf16[64,4224]{1,0:T(8,128)(2,1)S(1)} %collective-permute-done.1), channel_id=1, source_target_pairs={{0,2},{2,4},{4,6},{6,7},{7,5},{5,3},{3,1},{1,0},{8,10},{10,12},{12... | collective-permute-start | bytes 1622024 | tf_op jit(solution)/shard_map/ppermute | solution.py:72
  38.5 12.7 %collective-permute-start.8 = (bf16[64,4224]{1,0:T(8,128)(2,1)S(1)}, bf16[64,4224]{1,0:T(8,128)(2,1)S(1)}, u32[]{:S(2)}, u32[]{:S(2)}) collective-permute-start(bf16[64,4224]{1,0:T(8,128)(2,1)S(1)} %collective-permute-done.3), channel_id=1, source_target_pairs={{2,0},{4,2},{6,4},{7,6},{5,7},{3,5},{1,3},{0,1},{10,8},{12,10},{14... | collective-permute-start | bytes 1622024 | tf_op jit(solution)/shard_map/ppermute | solution.py:75
  51.4 11.9 %collective-permute-start.9 = (bf16[64,4224]{1,0:T(8,128)(2,1)S(1)}, bf16[64,4224]{1,0:T(8,128)(2,1)S(1)}, u32[]{:S(2)}, u32[]{:S(2)}) collective-permute-start(bf16[64,4224]{1,0:T(8,128)(2,1)S(1)} %collective-permute-done.7), channel_id=1, source_target_pairs={{0,2},{2,4},{4,6},{6,7},{7,5},{5,3},{3,1},{1,0},{8,10},{10,12},{12... | collective-permute-start | bytes 1622024 | tf_op jit(solution)/shard_map/ppermute | solution.py:72
  64.4 1.9 %collective-permute-start.10 = (f32[64]{0:T(128)S(1)}, f32[64]{0:T(128)S(1)}, u32[]{:S(2)}, u32[]{:S(2)}) collective-permute-start(f32[64]{0:T(128)S(1)} %get-tuple-element.23), channel_id=1, source_target_pairs={{0,8},{8,0},{16,24},{24,16},{1,9},{9,1},{17,25},{25,17},{2,10},{10... | collective-permute-start | bytes 776 | tf_op jit(solution)/shard_map/ppermute | solution.py:94
  64.4 3.6 %collective-permute-start.11 = (f32[64]{0:T(128)S(1)}, f32[64]{0:T(128)S(1)}, u32[]{:S(2)}, u32[]{:S(2)}) collective-permute-start(f32[64]{0:T(128)S(1)} %get-tuple-element.25), channel_id=1, source_target_pairs={{0,16},{8,24},{16,0},{24,8},{1,17},{9,25},{17,1},{25,9},{2,18},{10... | collective-permute-start | bytes 776 | tf_op jit(solution)/shard_map/ppermute | solution.py:94
  65.0 3.1 %collective-permute-start.12 = (f32[64]{0:T(128)S(1)}, f32[64]{0:T(128)S(1)}, u32[]{:S(2)}, u32[]{:S(2)}) collective-permute-start(f32[64]{0:T(128)S(1)} %get-tuple-element.24), channel_id=1, source_target_pairs={{0,24},{8,16},{16,8},{24,0},{1,25},{9,17},{17,9},{25,1},{2,26},{10... | collective-permute-start | bytes 776 | tf_op jit(solution)/shard_map/ppermute | solution.py:94

commit v6 on v5

--- a/solution.py
+++ b/solution.py
@@ -65,28 +65,33 @@
     order = ring_order(block_count)
     forward = [(order[i], order[(i + 1) % block_count]) for i in range(block_count)]
     backward = [(dst, src) for src, dst in forward]
+    half = rows_here // 2
+
+    def fold(best, blocks):
+        for block in blocks:
+            tile = block_best(left_rows, left_labels, block)
+            best = tile if best is None else jnp.maximum(best, tile)
+        return best
+
+    chains = [[payload, forward, None, [payload]], [payload, backward, None, []]]
+    steps = block_count // 2
+    for step in range(1, steps + 1):
+        for which, chain in enumerate(chains):
+            visiting, pairs, best, pending = chain
+            if step == steps and block_count % 2 == 0:
+                visiting = visiting[:half] if which == 0 else visiting[half:]
+            visiting = lax.ppermute(visiting, "blk", pairs)
+            if step >= 2:
+                best = fold(best, pending)
+                pending = []
+                visiting, best = lax.optimization_barrier((visiting, best))
+            pending.append(visiting)
+            chain[0], chain[2], chain[3] = visiting, best, pending
     best = None
-    pending = [payload]
-    ahead, behind = payload, payload
-    for step in range(1, block_count // 2 + 1):
-        ahead = lax.ppermute(ahead, "blk", forward)
-        stepped = [ahead]
-        if step <= (block_count - 1) // 2:
-            behind = lax.ppermute(behind, "blk", backward)
-            stepped.append(behind)
-        if step >= 2:
-            for block in pending:
-                tile = block_best(left_rows, left_labels, block)
-                best = tile if best is None else jnp.maximum(best, tile)
-            pending = []
-            stepped, best = lax.optimization_barrier((stepped, best))
-            ahead = stepped[0]
-            if len(stepped) > 1:
-                behind = stepped[1]
-        pending.extend(stepped)
-    for block in pending:
-        tile = block_best(left_rows, left_labels, block)
-        best = tile if best is None else jnp.maximum(best, tile)
+    for _, _, chain_best, pending in chains:
+        chain_best = fold(chain_best, pending)
+        if chain_best is not None:
+            best = chain_best if best is None else jnp.maximum(best, chain_best)
 
     best = best.reshape(group_count, rows_here)
     result = best[0]

time: 68.8 us -> 65.3 us (0.949)
  waiting for transfers between devices: 41.1 us -> 35.9 us
  matrix products: 6.5 us -> 7.27 us
  starting transfers between devices: 12.7 us -> 13.4 us
    ppermute x7 -> x8, waiting for transfers between devices: 29.2 us -> 23.1 us  [per_device(): visiting = lax.ppermute(visiting, 'blk', pairs)]
    ppermute x3, waiting for transfers between devices: 1.79 us -> 2.76 us  [per_device(): result = jnp.maximum(result, lax.ppermute(best[k], 'grp', pairs))]
    dot_general x8 -> x9, matrix products: 6.5 us -> 7.27 us  [block_best(): jnp.einsum('id,jd->ij', left_rows, payload, preferred_element_type=jnp.fl...]
    ppermute x7 -> x8, starting transfers between devices: 7.81 us -> 8.43 us  [per_device(): visiting = lax.ppermute(visiting, 'blk', pairs)]
    add x8 -> x9, other arithmetic: 1.39 us -> 1.57 us  [tag_labels(): return high * 128.0 + low]
  transfers between devices with their start and end apart: 13 -> 14, of which waited for: 9 -> 11; matrix products, arithmetic and copies ran while one was open for 14% -> 15% of each run, Pallas kernels for 0% -> 0%
where the time goes in v6:
time: 65.3 us; the launch traced here: 65 us
  waiting for transfers between devices  35.9 us (55%)
  starting transfers between devices  13.4 us (21%)
  other arithmetic  8.17 us (13%)
  matrix products  7.27 us (11%)
    ppermute x8, waiting for transfers between devices, per_device(): visiting = lax.ppermute(visiting, 'blk', pairs)  23.1 us
    ppermute x1, waiting for transfers between devices, per_device(): across = lax.ppermute(payload, 'grp', partner_pairs(group_count, 2))  10.1 us
    ppermute x8, starting transfers between devices, per_device(): visiting = lax.ppermute(visiting, 'blk', pairs)  8.43 us
    dot_general x9, matrix products, block_best(): jnp.einsum('id,jd->ij', left_rows, payload, preferred_element_type=jnp.fl...  7.27 us
    ppermute x1, starting transfers between devices, per_device(): across = lax.ppermute(payload, 'grp', partner_pairs(group_count, 2))  3.06 us
    ppermute x3, waiting for transfers between devices, per_device(): result = jnp.maximum(result, lax.ppermute(best[k], 'grp', pairs))  2.76 us
    concatenate x1, other arithmetic, per_device(): left_payload = jnp.concatenate([payload, beside, across, diagonal], axis=0)  2.48 us
    ppermute x3, starting transfers between devices, per_device(): result = jnp.maximum(result, lax.ppermute(best[k], 'grp', pairs))  1.86 us
  transfers between devices with their start and end apart: 14, of which 11 were waited for; matrix products, arithmetic and copies ran while one was open for 15% of the time, Pallas kernels for 0%

profile of v6, /device:TPU:0, one launch (start us, length us, event | category | flops | bytes accessed | tf_op | source)
XLA Modules:
  0.0 65.0 jit_solution(5444457683721960534)
XLA Ops:
  0.0 1.2 %fusion.9 = f32[64]{0:T(128)S(1)} fusion(bf16[64,4096]{1,0:T(8,128)(2,1)} %param.3), kind=kLoop, calls=%fused_computation.22 | loop fusion | flops 786368 | bytes 524544 | tf_op jit(solution)/shard_map/reduce_sum | solution.py:42
  1.3 1.2 %fusion.11 = bf16[64,4096]{1,0:T(8,128)(2,1)S(1)} fusion(bf16[64,4096]{1,0:T(8,128)(2,1)} %param.3, f32[64]{0:T(128)S(1)} %add_rsqrt_fusion), kind=kLoop, calls=%fused_computation.24 | loop fusion | flops 1048576 | bytes 1048832 | tf_op jit(solution)/shard_map/convert_element_type | solution.py:43
  2.5 0.7 %multiply_add_fusion = (s32[64]{0:T(128)S(1)}, s32[64]{0:T(128)S(1)}) fusion(s32[64]{0:T(128)} %param.4, s32[64]{0:T(128)} %param.5), kind=kLoop, calls=%fused_computation.57 | loop fusion | flops 1344 | bytes 1024 | tf_op jit(solution)/shard_map/add | solution.py:44
  3.2 0.1 select_convert_fusion
  3.3 3.1 %collective-permute-start.3 = (bf16[64,4224]{1,0:T(8,128)(2,1)S(1)}, bf16[64,4224]{1,0:T(8,128)(2,1)S(1)}, u32[]{:S(2)}, u32[]{:S(2)}) collective-permute-start(bf16[64,4224]{1,0:T(8,128)(2,1)S(1)} %pad_maximum_fusion.1), channel_id=1, source_target_pairs={{0,16},{8,24},{16,0},{24,8},{1,17},{9,25},{17,1},{25,9},{2,18},{10... | collective-permute-start | bytes 1622024 | tf_op jit(solution)/shard_map/ppermute | solution.py:51
  6.4 1.6 %collective-permute-start = (bf16[64,4224]{1,0:T(8,128)(2,1)S(1)}, bf16[64,4224]{1,0:T(8,128)(2,1)S(1)}, u32[]{:S(2)}, u32[]{:S(2)}) collective-permute-start(bf16[64,4224]{1,0:T(8,128)(2,1)S(1)} %pad_maximum_fusion.1), channel_id=1, source_target_pairs={{0,2},{2,4},{4,6},{6,7},{7,5},{5,3},{3,1},{1,0},{8,10},{10,12},{12... | collective-permute-start | bytes 1622024 | tf_op jit(solution)/shard_map/ppermute | solution.py:83
  8.0 0.4 collective-permute-start.7
  8.4 0.2 add_reduce_fusion.6
  8.6 10.1 %collective-permute-done.3 = bf16[64,4224]{1,0:T(8,128)(2,1)S(1)} collective-permute-done((bf16[64,4224]{1,0:T(8,128)(2,1)S(1)}, bf16[64,4224]{1,0:T(8,128)(2,1)S(1)}, u32[]{:S(2)}, u32[]{:S(2)}) %collective-permute-start.3) | collective-permute-done | bytes 540704 | tf_op jit(solution)/shard_map/ppermute | solution.py:51
  18.7 1.5 %collective-permute-done = bf16[64,4224]{1,0:T(8,128)(2,1)S(1)} collective-permute-done((bf16[64,4224]{1,0:T(8,128)(2,1)S(1)}, bf16[64,4224]{1,0:T(8,128)(2,1)S(1)}, u32[]{:S(2)}, u32[]{:S(2)}) %collective-permute-start) | collective-permute-done | bytes 540704 | tf_op jit(solution)/shard_map/ppermute | solution.py:83
  20.1 1.6 %collective-permute-start.1 = (bf16[64,4224]{1,0:T(8,128)(2,1)S(1)}, bf16[64,4224]{1,0:T(8,128)(2,1)S(1)}, u32[]{:S(2)}, u32[]{:S(2)}) collective-permute-start(bf16[64,4224]{1,0:T(8,128)(2,1)S(1)} %collective-permute-done), channel_id=1, source_target_pairs={{0,2},{2,4},{4,6},{6,7},{7,5},{5,3},{3,1},{1,0},{8,10},{10,12},{12... | collective-permute-start | bytes 1622024 | tf_op jit(solution)/shard_map/ppermute | solution.py:83
  21.7 0.2 add_reduce_fusion.5
  21.9 0.8 %collective-permute-done.7 = bf16[64,4224]{1,0:T(8,128)(2,1)S(1)} collective-permute-done((bf16[64,4224]{1,0:T(8,128)(2,1)S(1)}, bf16[64,4224]{1,0:T(8,128)(2,1)S(1)}, u32[]{:S(2)}, u32[]{:S(2)}) %collective-permute-start.7) | collective-permute-done | bytes 540704 | tf_op jit(solution)/shard_map/ppermute | solution.py:83
  22.7 0.4 collective-permute-start.8
  23.1 0.2 add_reduce_fusion.2
  23.3 2.5 %pad_maximum_fusion = bf16[256,4224]{1,0:T(8,128)(2,1)S(1)} fusion(bf16[64,4224]{1,0:T(8,128)(2,1)S(1)} %collective-permute-done.4, bf16[64,4224]{1,0:T(8,128)(2,1)S(1)} %collective-permute-done.3, bf16[64,4224]{1,0:T(8,128)(2,1)S(1)} %collective-permute-done.2, bf16[64,128]{1,0:T(8,128)(2,1)S(1)} %select_convert_fusion, bf16[64,4096]{1,0:T(8,128)(2,1)S(1)} %fusion.11), kind=kLoop, calls=%fused_computation | loop fusion | flops 10813440 | bytes 4325376 | tf_op jit(solution)/shard_map/concatenate | solution.py:55
  25.8 0.2 floor_reduce_fusion
  26.0 0.8 %fusion.1 = f32[256]{0:T(256)S(1)} fusion(bf16[64,4224]{1,0:T(8,128)(2,1)S(1)} %collective-permute-done, bf16[256,4224]{1,0:T(8,128)(2,1)S(1)} %pad_maximum_fusion, pred[4224]{0:T(1024)(128)(4,1)S(1)} %iota_compare_fusion, f32[256]{0:T(256)S(1)} %get-tuple-element.30, f32[256]{0:T(256)S(1)} %get-tuple-element.29, f32[64]{0:T(128)S(1)} %add_reduce_fusion.5, ...), kind=kOutput, calls=%fused_computation.12 | convolution fusion | flops 139575040 | bytes 2711168 | tf_op jit(solution)/shard_map/id,jd->ij/dot_general | solution.py:26
  26.9 0.8 %fusion = f32[256]{0:T(256)S(1)} fusion(bf16[256,4224]{1,0:T(8,128)(2,1)S(1)} %pad_maximum_fusion, pred[4224]{0:T(1024)(128)(4,1)S(1)} %iota_compare_fusion, f32[256]{0:T(256)S(1)} %get-tuple-element.30, f32[256]{0:T(256)S(1)} %get-tuple-element.29, f32[64]{0:T(128)S(1)} %add_reduce_fusion.6, f32[64]{0:T(128)S(1)} %multiply_floor_fusion.8, ...), kind=kOutput, calls=%fused_computation.11 | convolution fusion | flops 140656384 | bytes 2711168 | tf_op jit(solution)/shard_map/id,jd->ij/dot_general | solution.py:26
  27.7 5.7 %collective-permute-done.1 = bf16[64,4224]{1,0:T(8,128)(2,1)S(1)} collective-permute-done((bf16[64,4224]{1,0:T(8,128)(2,1)S(1)}, bf16[64,4224]{1,0:T(8,128)(2,1)S(1)}, u32[]{:S(2)}, u32[]{:S(2)}) %collective-permute-start.1) | collective-permute-done | bytes 540704 | tf_op jit(solution)/shard_map/ppermute | solution.py:83
  33.4 1.8 %collective-permute-start.5 = (bf16[64,4224]{1,0:T(8,128)(2,1)S(1)}, bf16[64,4224]{1,0:T(8,128)(2,1)S(1)}, u32[]{:S(2)}, u32[]{:S(2)}) collective-permute-start(bf16[64,4224]{1,0:T(8,128)(2,1)S(1)} %collective-permute-done.1), channel_id=1, source_target_pairs={{0,2},{2,4},{4,6},{6,7},{7,5},{5,3},{3,1},{1,0},{8,10},{10,12},{12... | collective-permute-start | bytes 1622024 | tf_op jit(solution)/shard_map/ppermute | solution.py:83
  35.2 0.2 add_reduce_fusion.4
  35.3 0.8 %fusion.4 = f32[256]{0:T(256)S(1)} fusion(bf16[64,4224]{1,0:T(8,128)(2,1)S(1)} %collective-permute-done.7, bf16[256,4224]{1,0:T(8,128)(2,1)S(1)} %pad_maximum_fusion, pred[4224]{0:T(1024)(128)(4,1)S(1)} %iota_compare_fusion, f32[256]{0:T(256)S(1)} %get-tuple-element.30, f32[256]{0:T(256)S(1)} %get-tuple-element.29, f32[64]{0:T(128)S(1)} %add_reduce_fusion.2, ...), kind=kOutput, calls=%fused_computation.15 | convolution fusion | flops 139575040 | bytes 2711168 | tf_op jit(solution)/shard_map/id,jd->ij/dot_general | solution.py:26
  36.2 0.3 collective-permute-done.8
  36.5 0.2 add_reduce_fusion.1
  36.7 0.5 collective-permute-start.9
  37.2 0.8 %fusion.2 = f32[256]{0:T(256)S(1)} fusion(bf16[64,4224]{1,0:T(8,128)(2,1)S(1)} %collective-permute-done.1, bf16[256,4224]{1,0:T(8,128)(2,1)S(1)} %pad_maximum_fusion, pred[4224]{0:T(1024)(128)(4,1)S(1)} %iota_compare_fusion, f32[256]{0:T(256)S(1)} %get-tuple-element.30, f32[256]{0:T(256)S(1)} %get-tuple-element.29, f32[64]{0:T(128)S(1)} %add_reduce_fusion.4, ...), kind=kOutput, calls=%fused_computation.13 | convolution fusion | flops 139575040 | bytes 2711168 | tf_op jit(solution)/shard_map/id,jd->ij/dot_general | solution.py:26
  38.0 0.8 %fusion.5 = f32[256]{0:T(256)S(1)} fusion(bf16[64,4224]{1,0:T(8,128)(2,1)S(1)} %collective-permute-done.8, bf16[256,4224]{1,0:T(8,128)(2,1)S(1)} %pad_maximum_fusion, pred[4224]{0:T(1024)(128)(4,1)S(1)} %iota_compare_fusion, f32[256]{0:T(256)S(1)} %get-tuple-element.30, f32[256]{0:T(256)S(1)} %get-tuple-element.29, f32[64]{0:T(128)S(1)} %add_reduce_fusion.1, ...), kind=kOutput, calls=%fused_computation.16 | convolution fusion | flops 139575040 | bytes 2711168 | tf_op jit(solution)/shard_map/id,jd->ij/dot_general | solution.py:26
  38.8 7.1 %collective-permute-done.5 = bf16[64,4224]{1,0:T(8,128)(2,1)S(1)} collective-permute-done((bf16[64,4224]{1,0:T(8,128)(2,1)S(1)}, bf16[64,4224]{1,0:T(8,128)(2,1)S(1)}, u32[]{:S(2)}, u32[]{:S(2)}) %collective-permute-start.5) | collective-permute-done | bytes 540704 | tf_op jit(solution)/shard_map/ppermute | solution.py:83
  45.9 0.2 add_reduce_fusion.3
  46.1 3.6 %collective-permute-done.9 = bf16[64,4224]{1,0:T(8,128)(2,1)S(1)} collective-permute-done((bf16[64,4224]{1,0:T(8,128)(2,1)S(1)}, bf16[64,4224]{1,0:T(8,128)(2,1)S(1)}, u32[]{:S(2)}, u32[]{:S(2)}) %collective-permute-start.9) | collective-permute-done | bytes 540704 | tf_op jit(solution)/shard_map/ppermute | solution.py:83
  49.7 0.2 add_reduce_fusion
  49.9 0.8 %fusion.3 = f32[256]{0:T(256)S(1)} fusion(bf16[64,4224]{1,0:T(8,128)(2,1)S(1)} %collective-permute-done.5, bf16[256,4224]{1,0:T(8,128)(2,1)S(1)} %pad_maximum_fusion, pred[4224]{0:T(1024)(128)(4,1)S(1)} %iota_compare_fusion, f32[256]{0:T(256)S(1)} %get-tuple-element.30, f32[256]{0:T(256)S(1)} %get-tuple-element.29, f32[64]{0:T(128)S(1)} %add_reduce_fusion.3, ...), kind=kOutput, calls=%fused_computation.14 | convolution fusion | flops 139575040 | bytes 2711168 | tf_op jit(solution)/shard_map/id,jd->ij/dot_general | solution.py:26
  50.7 1.6 %collective-permute-start.6 = (bf16[32,4224]{1,0:T(8,128)(2,1)S(1)}, bf16[32,4224]{1,0:T(8,128)(2,1)S(1)}, u32[]{:S(2)}, u32[]{:S(2)}) collective-permute-start(bf16[32,4224]{1,0:T(8,128)(2,1)S(1)} %slice.90), channel_id=1, source_target_pairs={{0,2},{2,4},{4,6},{6,7},{7,5},{5,3},{3,1},{1,0},{8,10},{10,12},{12... | collective-permute-start | bytes 811016 | tf_op jit(solution)/shard_map/ppermute | solution.py:83
  52.4 0.4 collective-permute-start.10
  52.8 0.8 %fusion.6 = f32[256]{0:T(256)S(1)} fusion(bf16[64,4224]{1,0:T(8,128)(2,1)S(1)} %collective-permute-done.9, bf16[256,4224]{1,0:T(8,128)(2,1)S(1)} %pad_maximum_fusion, pred[4224]{0:T(1024)(128)(4,1)S(1)} %iota_compare_fusion, f32[256]{0:T(256)S(1)} %get-tuple-element.30, f32[256]{0:T(256)S(1)} %get-tuple-element.29, f32[64]{0:T(128)S(1)} %add_reduce_fusion, ...), kind=kOutput, calls=%fused_computation.17 | convolution fusion | flops 139575040 | bytes 2711168 | tf_op jit(solution)/shard_map/id,jd->ij/dot_general | solution.py:26
  53.6 3.6 %collective-permute-done.6 = bf16[32,4224]{1,0:T(8,128)(2,1)S(1)} collective-permute-done((bf16[32,4224]{1,0:T(8,128)(2,1)S(1)}, bf16[32,4224]{1,0:T(8,128)(2,1)S(1)}, u32[]{:S(2)}, u32[]{:S(2)}) %collective-permute-start.6) | collective-permute-done | bytes 270368 | tf_op jit(solution)/shard_map/ppermute | solution.py:83
  57.2 0.2 add_reduce_fusion.8
  57.4 0.8 %fusion.7 = f32[256]{0:T(256)S(1)} fusion(bf16[32,4224]{1,0:T(8,128)(2,1)S(1)} %collective-permute-done.6, bf16[256,4224]{1,0:T(8,128)(2,1)S(1)} %pad_maximum_fusion, pred[4224]{0:T(1024)(128)(4,1)S(1)} %iota_compare_fusion, f32[256]{0:T(256)S(1)} %get-tuple-element.30, f32[256]{0:T(256)S(1)} %get-tuple-element.29, f32[32]{0:T(128)S(1)} %add_reduce_fusion.8, ...), kind=kOutput, calls=%fused_computation.20 | convolution fusion | flops 70328064 | bytes 2440576 | tf_op jit(solution)/shard_map/id,jd->ij/dot_general | solution.py:26
  58.2 0.6 collective-permute-done.10
  58.8 0.2 add_reduce_fusion.7
  59.0 0.8 %fusion.8 = f32[256]{0:T(256)S(1)} fusion(bf16[32,4224]{1,0:T(8,128)(2,1)S(1)} %collective-permute-done.10, bf16[256,4224]{1,0:T(8,128)(2,1)S(1)} %pad_maximum_fusion, pred[4224]{0:T(1024)(128)(4,1)S(1)} %iota_compare_fusion, f32[256]{0:T(256)S(1)} %get-tuple-element.30, f32[256]{0:T(256)S(1)} %get-tuple-element.29, f32[32]{0:T(128)S(1)} %add_reduce_fusion.7, ...), kind=kOutput, calls=%fused_computation.21 | convolution fusion | flops 70328064 | bytes 2440576 | tf_op jit(solution)/shard_map/id,jd->ij/dot_general | solution.py:26
  59.8 0.1 fusion.22
  59.9 1.6 %collective-permute-start.12 = (f32[64]{0:T(128)S(1)}, f32[64]{0:T(128)S(1)}, u32[]{:S(2)}, u32[]{:S(2)}) collective-permute-start(f32[64]{0:T(128)S(1)} %get-tuple-element.33), channel_id=1, source_target_pairs={{0,16},{8,24},{16,0},{24,8},{1,17},{9,25},{17,1},{25,9},{2,18},{10... | collective-permute-start | bytes 776 | tf_op jit(solution)/shard_map/ppermute | solution.py:99
  61.5 0.2 collective-permute-start.13
  61.8 1.8 %collective-permute-done.12 = f32[64]{0:T(128)S(1)} collective-permute-done((f32[64]{0:T(128)S(1)}, f32[64]{0:T(128)S(1)}, u32[]{:S(2)}, u32[]{:S(2)}) %collective-permute-start.12) | collective-permute-done | bytes 288 | tf_op jit(solution)/shard_map/ppermute | solution.py:99
  63.5 1.0 %collective-permute-done.13 = f32[64]{0:T(128)S(1)} collective-permute-done((f32[64]{0:T(128)S(1)}, f32[64]{0:T(128)S(1)}, u32[]{:S(2)}, u32[]{:S(2)}) %collective-permute-start.13) | collective-permute-done | bytes 288 | tf_op jit(solution)/shard_map/ppermute | solution.py:99
  64.5 0.5 maximum_maximum_fusion.1
  (27 shorter events, 0.2 us)
Async XLA Ops:
  3.3 15.3 %collective-permute-start.3 = (bf16[64,4224]{1,0:T(8,128)(2,1)S(1)}, bf16[64,4224]{1,0:T(8,128)(2,1)S(1)}, u32[]{:S(2)}, u32[]{:S(2)}) collective-permute-start(bf16[64,4224]{1,0:T(8,128)(2,1)S(1)} %pad_maximum_fusion.1), channel_id=1, source_target_pairs={{0,16},{8,24},{16,0},{24,8},{1,17},{9,25},{17,1},{25,9},{2,18},{10... | collective-permute-start | bytes 1622024 | tf_op jit(solution)/shard_map/ppermute | solution.py:51
  6.4 13.7 %collective-permute-start = (bf16[64,4224]{1,0:T(8,128)(2,1)S(1)}, bf16[64,4224]{1,0:T(8,128)(2,1)S(1)}, u32[]{:S(2)}, u32[]{:S(2)}) collective-permute-start(bf16[64,4224]{1,0:T(8,128)(2,1)S(1)} %pad_maximum_fusion.1), channel_id=1, source_target_pairs={{0,2},{2,4},{4,6},{6,7},{7,5},{5,3},{3,1},{1,0},{8,10},{10,12},{12... | collective-permute-start | bytes 1622024 | tf_op jit(solution)/shard_map/ppermute | solution.py:83
  8.0 15.3 %collective-permute-start.2 = (bf16[64,4224]{1,0:T(8,128)(2,1)S(1)}, bf16[64,4224]{1,0:T(8,128)(2,1)S(1)}, u32[]{:S(2)}, u32[]{:S(2)}) collective-permute-start(bf16[64,4224]{1,0:T(8,128)(2,1)S(1)} %pad_maximum_fusion.1), channel_id=1, source_target_pairs={{0,8},{8,0},{16,24},{24,16},{1,9},{9,1},{17,25},{25,17},{2,10},{10... | collective-permute-start | bytes 1622024 | tf_op jit(solution)/shard_map/ppermute | solution.py:52
  8.0 14.7 %collective-permute-start.7 = (bf16[64,4224]{1,0:T(8,128)(2,1)S(1)}, bf16[64,4224]{1,0:T(8,128)(2,1)S(1)}, u32[]{:S(2)}, u32[]{:S(2)}) collective-permute-start(bf16[64,4224]{1,0:T(8,128)(2,1)S(1)} %pad_maximum_fusion.1), channel_id=1, source_target_pairs={{2,0},{4,2},{6,4},{7,6},{5,7},{3,5},{1,3},{0,1},{10,8},{12,10},{14... | collective-permute-start | bytes 1622024 | tf_op jit(solution)/shard_map/ppermute | solution.py:83
  18.7 4.7 %collective-permute-start.4 = (bf16[64,4224]{1,0:T(8,128)(2,1)S(1)}, bf16[64,4224]{1,0:T(8,128)(2,1)S(1)}, u32[]{:S(2)}, u32[]{:S(2)}) collective-permute-start(bf16[64,4224]{1,0:T(8,128)(2,1)S(1)} %collective-permute-done.3), channel_id=1, source_target_pairs={{0,8},{8,0},{16,24},{24,16},{1,9},{9,1},{17,25},{25,17},{2,10},{10... | collective-permute-start | bytes 1622024 | tf_op jit(solution)/shard_map/ppermute | solution.py:53
  20.1 13.2 %collective-permute-start.1 = (bf16[64,4224]{1,0:T(8,128)(2,1)S(1)}, bf16[64,4224]{1,0:T(8,128)(2,1)S(1)}, u32[]{:S(2)}, u32[]{:S(2)}) collective-permute-start(bf16[64,4224]{1,0:T(8,128)(2,1)S(1)} %collective-permute-done), channel_id=1, source_target_pairs={{0,2},{2,4},{4,6},{6,7},{7,5},{5,3},{3,1},{1,0},{8,10},{10,12},{12... | collective-permute-start | bytes 1622024 | tf_op jit(solution)/shard_map/ppermute | solution.py:83
  22.7 13.8 %collective-permute-start.8 = (bf16[64,4224]{1,0:T(8,128)(2,1)S(1)}, bf16[64,4224]{1,0:T(8,128)(2,1)S(1)}, u32[]{:S(2)}, u32[]{:S(2)}) collective-permute-start(bf16[64,4224]{1,0:T(8,128)(2,1)S(1)} %collective-permute-done.7), channel_id=1, source_target_pairs={{2,0},{4,2},{6,4},{7,6},{5,7},{3,5},{1,3},{0,1},{10,8},{12,10},{14... | collective-permute-start | bytes 1622024 | tf_op jit(solution)/shard_map/ppermute | solution.py:83
  33.4 12.6 %collective-permute-start.5 = (bf16[64,4224]{1,0:T(8,128)(2,1)S(1)}, bf16[64,4224]{1,0:T(8,128)(2,1)S(1)}, u32[]{:S(2)}, u32[]{:S(2)}) collective-permute-start(bf16[64,4224]{1,0:T(8,128)(2,1)S(1)} %collective-permute-done.1), channel_id=1, source_target_pairs={{0,2},{2,4},{4,6},{6,7},{7,5},{5,3},{3,1},{1,0},{8,10},{10,12},{12... | collective-permute-start | bytes 1622024 | tf_op jit(solution)/shard_map/ppermute | solution.py:83
  36.7 13.0 %collective-permute-start.9 = (bf16[64,4224]{1,0:T(8,128)(2,1)S(1)}, bf16[64,4224]{1,0:T(8,128)(2,1)S(1)}, u32[]{:S(2)}, u32[]{:S(2)}) collective-permute-start(bf16[64,4224]{1,0:T(8,128)(2,1)S(1)} %collective-permute-done.8), channel_id=1, source_target_pairs={{2,0},{4,2},{6,4},{7,6},{5,7},{3,5},{1,3},{0,1},{10,8},{12,10},{14... | collective-permute-start | bytes 1622024 | tf_op jit(solution)/shard_map/ppermute | solution.py:83
  50.7 6.5 %collective-permute-start.6 = (bf16[32,4224]{1,0:T(8,128)(2,1)S(1)}, bf16[32,4224]{1,0:T(8,128)(2,1)S(1)}, u32[]{:S(2)}, u32[]{:S(2)}) collective-permute-start(bf16[32,4224]{1,0:T(8,128)(2,1)S(1)} %slice.90), channel_id=1, source_target_pairs={{0,2},{2,4},{4,6},{6,7},{7,5},{5,3},{3,1},{1,0},{8,10},{10,12},{12... | collective-permute-start | bytes 811016 | tf_op jit(solution)/shard_map/ppermute | solution.py:83
  52.4 6.5 %collective-permute-start.10 = (bf16[32,4224]{1,0:T(8,128)(2,1)S(1)}, bf16[32,4224]{1,0:T(8,128)(2,1)S(1)}, u32[]{:S(2)}, u32[]{:S(2)}) collective-permute-start(bf16[32,4224]{1,0:T(8,128)(2,1)S(1)} %slice.99), channel_id=1, source_target_pairs={{2,0},{4,2},{6,4},{7,6},{5,7},{3,5},{1,3},{0,1},{10,8},{12,10},{14... | collective-permute-start | bytes 811016 | tf_op jit(solution)/shard_map/ppermute | solution.py:83
  59.9 1.9 %collective-permute-start.11 = (f32[64]{0:T(128)S(1)}, f32[64]{0:T(128)S(1)}, u32[]{:S(2)}, u32[]{:S(2)}) collective-permute-start(f32[64]{0:T(128)S(1)} %get-tuple-element.31), channel_id=1, source_target_pairs={{0,8},{8,0},{16,24},{24,16},{1,9},{9,1},{17,25},{25,17},{2,10},{10... | collective-permute-start | bytes 776 | tf_op jit(solution)/shard_map/ppermute | solution.py:99
  59.9 3.6 %collective-permute-start.12 = (f32[64]{0:T(128)S(1)}, f32[64]{0:T(128)S(1)}, u32[]{:S(2)}, u32[]{:S(2)}) collective-permute-start(f32[64]{0:T(128)S(1)} %get-tuple-element.33), channel_id=1, source_target_pairs={{0,16},{8,24},{16,0},{24,8},{1,17},{9,25},{17,1},{25,9},{2,18},{10... | collective-permute-start | bytes 776 | tf_op jit(solution)/shard_map/ppermute | solution.py:99
  61.5 3.0 %collective-permute-start.13 = (f32[64]{0:T(128)S(1)}, f32[64]{0:T(128)S(1)}, u32[]{:S(2)}, u32[]{:S(2)}) collective-permute-start(f32[64]{0:T(128)S(1)} %get-tuple-element.32), channel_id=1, source_target_pairs={{0,24},{8,16},{16,8},{24,0},{1,25},{9,17},{17,9},{25,1},{2,26},{10... | collective-permute-start | bytes 776 | tf_op jit(solution)/shard_map/ppermute | solution.py:99

commit v7 on v6

--- a/solution.py
+++ b/solution.py
@@ -23,7 +23,7 @@
 
 
 def block_best(left_rows, left_labels, payload):
-    scores = jnp.einsum("id,jd->ij", left_rows, payload, preferred_element_type=jnp.float32)
+    scores = jnp.einsum("id,jd->ij", left_rows, payload[:, :D], preferred_element_type=jnp.float32)
     right_labels = tag_labels(payload)
     same_cluster = jnp.floor(left_labels[:, None] / ORDER_SPAN) == jnp.floor(right_labels[None, :] / ORDER_SPAN)
     earlier = same_cluster & (right_labels[None, :] < left_labels[:, None])
@@ -40,12 +40,30 @@
     rows_here = embeddings.shape[0]
     widened = embeddings.astype(jnp.float32)
     square_sum = jnp.sum(widened * widened, axis=1, keepdims=True)
-    unit_rows = (widened * lax.rsqrt(square_sum / D + 1e-06) / math.sqrt(D)).astype(jnp.bfloat16)
-    high = cluster_ids * 64 + row_index // 128
-    low = row_index % 128
-    column = jnp.arange(TAG_WIDTH)[None, :]
-    tags = jnp.where(column == 0, high[:, None], jnp.where(column == 1, low[:, None], 0)).astype(jnp.bfloat16)
-    payload = jnp.concatenate([unit_rows, tags], axis=1)
+    scale = lax.rsqrt(square_sum / D + 1e-06)
+    high = (cluster_ids * 64 + row_index // 128).astype(jnp.float32)[:, None]
+    low = (row_index % 128).astype(jnp.float32)[:, None]
+    column = jnp.arange(D + TAG_WIDTH)[None, :]
+    padded = jnp.pad(widened, ((0, 0), (0, TAG_WIDTH)))
+    tags = jnp.where(column == D, high, jnp.where(column == D + 1, low, 0.0))
+    payload = jnp.where(column < D, padded * scale / math.sqrt(D), tags).astype(jnp.bfloat16)
+
+    order = ring_order(block_count)
+    forward = [(order[i], order[(i + 1) % block_count]) for i in range(block_count)]
+    backward = [(dst, src) for src, dst in forward]
+    half = rows_here // 2
+    steps = block_count // 2
+
+    def send(which, visiting, step):
+        if step == steps and block_count % 2 == 0:
+            visiting = visiting[:half] if which == 0 else visiting[half:]
+        return lax.ppermute(visiting, "blk", forward if which == 0 else backward)
+
+    chains = [[payload, None, [payload]], [payload, None, []]]
+    if steps >= 1:
+        for which, chain in enumerate(chains):
+            chain[0] = send(which, chain[0], 1)
+            chain[2].append(chain[0])
 
     if group_count == 4:
         across = lax.ppermute(payload, "grp", partner_pairs(group_count, 2))
@@ -59,13 +77,7 @@
         segment_pairs = [[(g, (g - k) % group_count) for g in range(group_count)] for k in range(1, group_count)]
         left_payload = jnp.concatenate([payload] + shifted, axis=0)
     left_labels = tag_labels(left_payload)
-    inside = jnp.arange(D + TAG_WIDTH)[None, :] < D
-    left_rows = jnp.where(inside, left_payload, jnp.zeros_like(left_payload))
-
-    order = ring_order(block_count)
-    forward = [(order[i], order[(i + 1) % block_count]) for i in range(block_count)]
-    backward = [(dst, src) for src, dst in forward]
-    half = rows_here // 2
+    left_rows = left_payload[:, :D]
 
     def fold(best, blocks):
         for block in blocks:
@@ -73,22 +85,15 @@
             best = tile if best is None else jnp.maximum(best, tile)
         return best
 
-    chains = [[payload, forward, None, [payload]], [payload, backward, None, []]]
-    steps = block_count // 2
-    for step in range(1, steps + 1):
+    for step in range(2, steps + 1):
         for which, chain in enumerate(chains):
-            visiting, pairs, best, pending = chain
-            if step == steps and block_count % 2 == 0:
-                visiting = visiting[:half] if which == 0 else visiting[half:]
-            visiting = lax.ppermute(visiting, "blk", pairs)
-            if step >= 2:
-                best = fold(best, pending)
-                pending = []
-                visiting, best = lax.optimization_barrier((visiting, best))
-            pending.append(visiting)
-            chain[0], chain[2], chain[3] = visiting, best, pending
+            visiting, best, pending = chain
+            visiting = send(which, visiting, step)
+            best = fold(best, pending)
+            visiting, best = lax.optimization_barrier((visiting, best))
+            chain[0], chain[1], chain[2] = visiting, best, [visiting]
     best = None
-    for _, _, chain_best, pending in chains:
+    for _, chain_best, pending in chains:
         chain_best = fold(chain_best, pending)
         if chain_best is not None:
             best = chain_best if best is None else jnp.maximum(best, chain_best)

time: 65.3 us -> 63 us (0.965)
  other arithmetic: 8.17 us -> 5.33 us
  starting transfers between devices: 13.4 us -> 14.4 us
    concatenate x1, other arithmetic: 2.48 us -> 0.24 us  [per_device(): left_payload = jnp.concatenate([payload, beside, across, diagonal], axis=0)]
    ppermute x3, starting transfers between devices: 1.86 us -> 2.87 us  [per_device(): result = jnp.maximum(result, lax.ppermute(best[k], 'grp', pairs))]
    add x1 -> x0, other arithmetic: 0.69 us -> none  [per_device(): high = cluster_ids * 64 + row_index // 128]
    convert_element_type x2 -> x3, other arithmetic: 1.32 us -> 1.42 us  [the longest x1 1.12 us: per_device(): widened = embeddings.astype(jnp.float32)]
  transfers between devices with their start and end apart: 14 -> 14, of which waited for: 11 -> 9; matrix products, arithmetic and copies ran while one was open for 15% -> 13% of each run, Pallas kernels for 0% -> 0%
where the time goes in v7:
time: 63 us; the launch traced here: 62.9 us
  waiting for transfers between devices  35.8 us (57%)
  starting transfers between devices  14.4 us (23%)
  matrix products  6.96 us (11%)
  other arithmetic  5.33 us (8%)
    ppermute x8, waiting for transfers between devices, send(): return lax.ppermute(visiting, 'blk', forward if which == 0 else backward)  22.8 us
    ppermute x1, waiting for transfers between devices, per_device(): across = lax.ppermute(payload, 'grp', partner_pairs(group_count, 2))  10.1 us
    ppermute x8, starting transfers between devices, send(): return lax.ppermute(visiting, 'blk', forward if which == 0 else backward)  8.45 us
    dot_general x9, matrix products, block_best(): jnp.einsum('id,jd->ij', left_rows, payload[:, :D], preferred_element_type...  6.96 us
    ppermute x1, starting transfers between devices, per_device(): across = lax.ppermute(payload, 'grp', partner_pairs(group_count, 2))  3.06 us
    ppermute x3, waiting for transfers between devices, per_device(): result = jnp.maximum(result, lax.ppermute(best[k], 'grp', pairs))  2.95 us
    ppermute x3, starting transfers between devices, per_device(): result = jnp.maximum(result, lax.ppermute(best[k], 'grp', pairs))  2.87 us
    add x9, other arithmetic, tag_labels(): return high * 128.0 + low  1.57 us
  transfers between devices with their start and end apart: 14, of which 9 were waited for; matrix products, arithmetic and copies ran while one was open for 13% of the time, Pallas kernels for 0%

profile of v7, /device:TPU:0, one launch (start us, length us, event | category | flops | bytes accessed | tf_op | source)
XLA Modules:
  0.0 62.9 jit_solution(4011949494502168330)
XLA Ops:
  0.0 1.1 %convert_element_type.222 = f32[64,4096]{1,0:T(8,128)S(1)} convert(bf16[64,4096]{1,0:T(8,128)(2,1)} %param.3) | non-fusion elementwise | flops 262144 | bytes 1572864 | tf_op jit(solution)/shard_map/convert_element_type | solution.py:41
  1.1 1.2 %multiply_reduce_fusion = f32[64]{0:T(128)S(1)} fusion(bf16[64,4096]{1,0:T(8,128)(2,1)} %param.3), kind=kLoop, calls=%fused_computation.22 | loop fusion | flops 786368 | bytes 524544 | tf_op jit(solution)/shard_map/reduce_sum | solution.py:42
  2.4 0.3 select_convert_fusion
  2.7 3.1 %collective-permute-start.3 = (bf16[64,4224]{1,0:T(8,128)(2,1)S(1)}, bf16[64,4224]{1,0:T(8,128)(2,1)S(1)}, u32[]{:S(2)}, u32[]{:S(2)}) collective-permute-start(bf16[64,4224]{1,0:T(8,128)(2,1)S(1)} %select_convert_fusion), channel_id=1, source_target_pairs={{0,16},{8,24},{16,0},{24,8},{1,17},{9,25},{17,1},{25,9},{2,18},{10... | collective-permute-start | bytes 1622024 | tf_op jit(solution)/shard_map/ppermute | solution.py:69
  5.8 1.6 %collective-permute-start = (bf16[64,4224]{1,0:T(8,128)(2,1)S(1)}, bf16[64,4224]{1,0:T(8,128)(2,1)S(1)}, u32[]{:S(2)}, u32[]{:S(2)}) collective-permute-start(bf16[64,4224]{1,0:T(8,128)(2,1)S(1)} %select_convert_fusion), channel_id=1, source_target_pairs={{0,2},{2,4},{4,6},{6,7},{7,5},{5,3},{3,1},{1,0},{8,10},{10,12},{12... | collective-permute-start | bytes 1622024 | tf_op jit(solution)/shard_map/ppermute | solution.py:60
  7.4 0.4 collective-permute-start.7
  7.8 0.2 add_reduce_fusion.6
  8.0 10.1 %collective-permute-done.3 = bf16[64,4224]{1,0:T(8,128)(2,1)S(1)} collective-permute-done((bf16[64,4224]{1,0:T(8,128)(2,1)S(1)}, bf16[64,4224]{1,0:T(8,128)(2,1)S(1)}, u32[]{:S(2)}, u32[]{:S(2)}) %collective-permute-start.3) | collective-permute-done | bytes 540704 | tf_op jit(solution)/shard_map/ppermute | solution.py:69
  18.1 0.0 collective-permute-start.4
  18.1 1.5 %collective-permute-done = bf16[64,4224]{1,0:T(8,128)(2,1)S(1)} collective-permute-done((bf16[64,4224]{1,0:T(8,128)(2,1)S(1)}, bf16[64,4224]{1,0:T(8,128)(2,1)S(1)}, u32[]{:S(2)}, u32[]{:S(2)}) %collective-permute-start) | collective-permute-done | bytes 540704 | tf_op jit(solution)/shard_map/ppermute | solution.py:60
  19.5 1.6 %collective-permute-start.1 = (bf16[64,4224]{1,0:T(8,128)(2,1)S(1)}, bf16[64,4224]{1,0:T(8,128)(2,1)S(1)}, u32[]{:S(2)}, u32[]{:S(2)}) collective-permute-start(bf16[64,4224]{1,0:T(8,128)(2,1)S(1)} %collective-permute-done), channel_id=1, source_target_pairs={{0,2},{2,4},{4,6},{6,7},{7,5},{5,3},{3,1},{1,0},{8,10},{10,12},{12... | collective-permute-start | bytes 1622024 | tf_op jit(solution)/shard_map/ppermute | solution.py:60
  21.1 0.2 add_reduce_fusion.5
  21.3 0.5 collective-permute-start.8
  21.8 0.2 add_reduce_fusion.2
  22.0 0.1 pad_maximum_fusion.4
  22.1 0.2 pad_maximum_fusion
  22.4 0.2 floor_reduce_fusion
  22.5 0.8 %fusion = f32[256]{0:T(256)S(1)} fusion(bf16[256,4096]{1,0:T(8,128)(2,1)S(1)} %pad_maximum_fusion, bf16[64,4224]{1,0:T(8,128)(2,1)S(1)} %select_convert_fusion, f32[256]{0:T(256)S(1)} %get-tuple-element.30, f32[256]{0:T(256)S(1)} %get-tuple-element.29, f32[64]{0:T(128)S(1)} %add_reduce_fusion.6, f32[64]{0:T(128)S(1)} %multiply_floor_fusion.8), kind=kOutput, calls=%fused_computation.10 | convolution fusion | flops 134299392 | bytes 2625536 | tf_op jit(solution)/shard_map/id,jd->ij/dot_general | solution.py:26
  23.3 0.8 %fusion.1 = f32[256]{0:T(256)S(1)} fusion(bf16[256,4096]{1,0:T(8,128)(2,1)S(1)} %pad_maximum_fusion, bf16[64,4224]{1,0:T(8,128)(2,1)S(1)} %collective-permute-done, f32[256]{0:T(256)S(1)} %get-tuple-element.30, f32[256]{0:T(256)S(1)} %get-tuple-element.29, f32[64]{0:T(128)S(1)} %add_reduce_fusion.5, f32[64]{0:T(128)S(1)} %multiply_floor_fusion.7), kind=kOutput, calls=%fused_computation.11 | convolution fusion | flops 134299392 | bytes 2625536 | tf_op jit(solution)/shard_map/id,jd->ij/dot_general | solution.py:26
  24.1 8.7 %collective-permute-done.1 = bf16[64,4224]{1,0:T(8,128)(2,1)S(1)} collective-permute-done((bf16[64,4224]{1,0:T(8,128)(2,1)S(1)}, bf16[64,4224]{1,0:T(8,128)(2,1)S(1)}, u32[]{:S(2)}, u32[]{:S(2)}) %collective-permute-start.1) | collective-permute-done | bytes 540704 | tf_op jit(solution)/shard_map/ppermute | solution.py:60
  32.8 0.2 add_reduce_fusion.4
  33.0 1.8 %collective-permute-start.5 = (bf16[64,4224]{1,0:T(8,128)(2,1)S(1)}, bf16[64,4224]{1,0:T(8,128)(2,1)S(1)}, u32[]{:S(2)}, u32[]{:S(2)}) collective-permute-start(bf16[64,4224]{1,0:T(8,128)(2,1)S(1)} %collective-permute-done.1), channel_id=1, source_target_pairs={{0,2},{2,4},{4,6},{6,7},{7,5},{5,3},{3,1},{1,0},{8,10},{10,12},{12... | collective-permute-start | bytes 1622024 | tf_op jit(solution)/shard_map/ppermute | solution.py:60
  34.8 0.8 %fusion.2 = f32[256]{0:T(256)S(1)} fusion(bf16[256,4096]{1,0:T(8,128)(2,1)S(1)} %pad_maximum_fusion, bf16[64,4224]{1,0:T(8,128)(2,1)S(1)} %collective-permute-done.1, f32[256]{0:T(256)S(1)} %get-tuple-element.30, f32[256]{0:T(256)S(1)} %get-tuple-element.29, f32[64]{0:T(128)S(1)} %add_reduce_fusion.4, f32[64]{0:T(128)S(1)} %multiply_floor_fusion.6), kind=kOutput, calls=%fused_computation.12 | convolution fusion | flops 134299392 | bytes 2625536 | tf_op jit(solution)/shard_map/id,jd->ij/dot_general | solution.py:26
  35.6 0.8 %fusion.4 = f32[256]{0:T(256)S(1)} fusion(bf16[256,4096]{1,0:T(8,128)(2,1)S(1)} %pad_maximum_fusion, bf16[64,4224]{1,0:T(8,128)(2,1)S(1)} %collective-permute-done.7, f32[256]{0:T(256)S(1)} %get-tuple-element.30, f32[256]{0:T(256)S(1)} %get-tuple-element.29, f32[64]{0:T(128)S(1)} %add_reduce_fusion.2, f32[64]{0:T(128)S(1)} %multiply_floor_fusion.3), kind=kOutput, calls=%fused_computation.14 | convolution fusion | flops 134299392 | bytes 2625536 | tf_op jit(solution)/shard_map/id,jd->ij/dot_general | solution.py:26
  36.4 0.3 collective-permute-start.9
  36.7 0.2 add_reduce_fusion.1
  36.9 0.8 %fusion.5 = f32[256]{0:T(256)S(1)} fusion(bf16[256,4096]{1,0:T(8,128)(2,1)S(1)} %pad_maximum_fusion, bf16[64,4224]{1,0:T(8,128)(2,1)S(1)} %collective-permute-done.8, f32[256]{0:T(256)S(1)} %get-tuple-element.30, f32[256]{0:T(256)S(1)} %get-tuple-element.29, f32[64]{0:T(128)S(1)} %add_reduce_fusion.1, f32[64]{0:T(128)S(1)} %multiply_floor_fusion.2), kind=kOutput, calls=%fused_computation.15 | convolution fusion | flops 134299392 | bytes 2625536 | tf_op jit(solution)/shard_map/id,jd->ij/dot_general | solution.py:26
  37.6 7.9 %collective-permute-done.5 = bf16[64,4224]{1,0:T(8,128)(2,1)S(1)} collective-permute-done((bf16[64,4224]{1,0:T(8,128)(2,1)S(1)}, bf16[64,4224]{1,0:T(8,128)(2,1)S(1)}, u32[]{:S(2)}, u32[]{:S(2)}) %collective-permute-start.5) | collective-permute-done | bytes 540704 | tf_op jit(solution)/shard_map/ppermute | solution.py:60
  45.6 1.9 %collective-permute-start.6 = (bf16[32,4224]{1,0:T(8,128)(2,1)S(1)}, bf16[32,4224]{1,0:T(8,128)(2,1)S(1)}, u32[]{:S(2)}, u32[]{:S(2)}) collective-permute-start(bf16[32,4224]{1,0:T(8,128)(2,1)S(1)} %slice.124), channel_id=1, source_target_pairs={{0,2},{2,4},{4,6},{6,7},{7,5},{5,3},{3,1},{1,0},{8,10},{10,12},{12... | collective-permute-start | bytes 811016 | tf_op jit(solution)/shard_map/ppermute | solution.py:60
  47.5 0.2 add_reduce_fusion.3
  47.7 0.8 %fusion.3 = f32[256]{0:T(256)S(1)} fusion(bf16[256,4096]{1,0:T(8,128)(2,1)S(1)} %pad_maximum_fusion, bf16[64,4224]{1,0:T(8,128)(2,1)S(1)} %collective-permute-done.5, f32[256]{0:T(256)S(1)} %get-tuple-element.30, f32[256]{0:T(256)S(1)} %get-tuple-element.29, f32[64]{0:T(128)S(1)} %add_reduce_fusion.3, f32[64]{0:T(128)S(1)} %multiply_floor_fusion.5), kind=kOutput, calls=%fused_computation.13 | convolution fusion | flops 134299392 | bytes 2625536 | tf_op jit(solution)/shard_map/id,jd->ij/dot_general | solution.py:26
  48.4 0.3 collective-permute-done.9
  48.7 0.2 add_reduce_fusion
  49.0 0.3 collective-permute-start.10
  49.3 0.8 %fusion.6 = f32[256]{0:T(256)S(1)} fusion(bf16[256,4096]{1,0:T(8,128)(2,1)S(1)} %pad_maximum_fusion, bf16[64,4224]{1,0:T(8,128)(2,1)S(1)} %collective-permute-done.9, f32[256]{0:T(256)S(1)} %get-tuple-element.30, f32[256]{0:T(256)S(1)} %get-tuple-element.29, f32[64]{0:T(128)S(1)} %add_reduce_fusion, f32[64]{0:T(128)S(1)} %multiply_floor_fusion.1), kind=kOutput, calls=%fused_computation.16 | convolution fusion | flops 134299392 | bytes 2625536 | tf_op jit(solution)/shard_map/id,jd->ij/dot_general | solution.py:26
  50.1 2.0 %collective-permute-done.6 = bf16[32,4224]{1,0:T(8,128)(2,1)S(1)} collective-permute-done((bf16[32,4224]{1,0:T(8,128)(2,1)S(1)}, bf16[32,4224]{1,0:T(8,128)(2,1)S(1)}, u32[]{:S(2)}, u32[]{:S(2)}) %collective-permute-start.6) | collective-permute-done | bytes 270368 | tf_op jit(solution)/shard_map/ppermute | solution.py:60
  52.1 0.2 add_reduce_fusion.8
  52.3 0.8 %fusion.7 = f32[256]{0:T(256)S(1)} fusion(bf16[256,4096]{1,0:T(8,128)(2,1)S(1)} %pad_maximum_fusion, bf16[32,4224]{1,0:T(8,128)(2,1)S(1)} %collective-permute-done.6, f32[256]{0:T(256)S(1)} %get-tuple-element.30, f32[256]{0:T(256)S(1)} %get-tuple-element.29, f32[32]{0:T(128)S(1)} %add_reduce_fusion.8, f32[32]{0:T(128)S(1)} %multiply_floor_fusion.4), kind=kOutput, calls=%fused_computation.19 | convolution fusion | flops 67149568 | bytes 2363392 | tf_op jit(solution)/shard_map/id,jd->ij/dot_general | solution.py:26
  53.1 2.4 %collective-permute-done.10 = bf16[32,4224]{1,0:T(8,128)(2,1)S(1)} collective-permute-done((bf16[32,4224]{1,0:T(8,128)(2,1)S(1)}, bf16[32,4224]{1,0:T(8,128)(2,1)S(1)}, u32[]{:S(2)}, u32[]{:S(2)}) %collective-permute-start.10) | collective-permute-done | bytes 270368 | tf_op jit(solution)/shard_map/ppermute | solution.py:60
  55.5 0.2 add_reduce_fusion.7
  55.7 0.8 %fusion.8 = f32[256]{0:T(256)S(1)} fusion(bf16[256,4096]{1,0:T(8,128)(2,1)S(1)} %pad_maximum_fusion, bf16[32,4224]{1,0:T(8,128)(2,1)S(1)} %collective-permute-done.10, f32[256]{0:T(256)S(1)} %get-tuple-element.30, f32[256]{0:T(256)S(1)} %get-tuple-element.29, f32[32]{0:T(128)S(1)} %add_reduce_fusion.7, f32[32]{0:T(128)S(1)} %multiply_floor_fusion), kind=kOutput, calls=%fused_computation.20 | convolution fusion | flops 67149568 | bytes 2363392 | tf_op jit(solution)/shard_map/id,jd->ij/dot_general | solution.py:26
  56.4 0.1 fusion.20
  56.5 0.0 collective-permute-start.11
  56.5 2.8 %collective-permute-start.12 = (f32[64]{0:T(128)S(1)}, f32[64]{0:T(128)S(1)}, u32[]{:S(2)}, u32[]{:S(2)}) collective-permute-start(f32[64]{0:T(128)S(1)} %get-tuple-element.35), channel_id=1, source_target_pairs={{0,16},{8,24},{16,0},{24,8},{1,17},{9,25},{17,1},{25,9},{2,18},{10... | collective-permute-start | bytes 776 | tf_op jit(solution)/shard_map/ppermute | solution.py:104
  59.3 0.0 collective-permute-start.13
  59.4 1.5 %collective-permute-done.12 = f32[64]{0:T(128)S(1)} collective-permute-done((f32[64]{0:T(128)S(1)}, f32[64]{0:T(128)S(1)}, u32[]{:S(2)}, u32[]{:S(2)}) %collective-permute-start.12) | collective-permute-done | bytes 288 | tf_op jit(solution)/shard_map/ppermute | solution.py:104
  60.9 1.4 %collective-permute-done.13 = f32[64]{0:T(128)S(1)} collective-permute-done((f32[64]{0:T(128)S(1)}, f32[64]{0:T(128)S(1)}, u32[]{:S(2)}, u32[]{:S(2)}) %collective-permute-start.13) | collective-permute-done | bytes 288 | tf_op jit(solution)/shard_map/ppermute | solution.py:104
  62.3 0.5 maximum_maximum_fusion.1
  (31 shorter events, 0.2 us)
Async XLA Ops:
  0.0 2.4 %copy-start = (s32[64]{0:T(128)S(1)}, s32[64]{0:T(128)}, u32[]{:S(2)}) copy-start(s32[64]{0:T(128)} %param.4) | copy-start | bytes 772
  0.0 2.4 %copy-start.1 = (s32[64]{0:T(128)S(1)}, s32[64]{0:T(128)}, u32[]{:S(2)}) copy-start(s32[64]{0:T(128)} %param.5) | copy-start | bytes 772
  2.7 15.3 %collective-permute-start.3 = (bf16[64,4224]{1,0:T(8,128)(2,1)S(1)}, bf16[64,4224]{1,0:T(8,128)(2,1)S(1)}, u32[]{:S(2)}, u32[]{:S(2)}) collective-permute-start(bf16[64,4224]{1,0:T(8,128)(2,1)S(1)} %select_convert_fusion), channel_id=1, source_target_pairs={{0,16},{8,24},{16,0},{24,8},{1,17},{9,25},{17,1},{25,9},{2,18},{10... | collective-permute-start | bytes 1622024 | tf_op jit(solution)/shard_map/ppermute | solution.py:69
  5.8 13.7 %collective-permute-start = (bf16[64,4224]{1,0:T(8,128)(2,1)S(1)}, bf16[64,4224]{1,0:T(8,128)(2,1)S(1)}, u32[]{:S(2)}, u32[]{:S(2)}) collective-permute-start(bf16[64,4224]{1,0:T(8,128)(2,1)S(1)} %select_convert_fusion), channel_id=1, source_target_pairs={{0,2},{2,4},{4,6},{6,7},{7,5},{5,3},{3,1},{1,0},{8,10},{10,12},{12... | collective-permute-start | bytes 1622024 | tf_op jit(solution)/shard_map/ppermute | solution.py:60
  7.4 13.9 %collective-permute-start.7 = (bf16[64,4224]{1,0:T(8,128)(2,1)S(1)}, bf16[64,4224]{1,0:T(8,128)(2,1)S(1)}, u32[]{:S(2)}, u32[]{:S(2)}) collective-permute-start(bf16[64,4224]{1,0:T(8,128)(2,1)S(1)} %select_convert_fusion), channel_id=1, source_target_pairs={{2,0},{4,2},{6,4},{7,6},{5,7},{3,5},{1,3},{0,1},{10,8},{12,10},{14... | collective-permute-start | bytes 1622024 | tf_op jit(solution)/shard_map/ppermute | solution.py:60
  7.8 14.2 %collective-permute-start.2 = (bf16[64,4224]{1,0:T(8,128)(2,1)S(1)}, bf16[64,4224]{1,0:T(8,128)(2,1)S(1)}, u32[]{:S(2)}, u32[]{:S(2)}) collective-permute-start(bf16[64,4224]{1,0:T(8,128)(2,1)S(1)} %select_convert_fusion), channel_id=1, source_target_pairs={{0,8},{8,0},{16,24},{24,16},{1,9},{9,1},{17,25},{25,17},{2,10},{10... | collective-permute-start | bytes 1622024 | tf_op jit(solution)/shard_map/ppermute | solution.py:70
  18.1 3.9 %collective-permute-start.4 = (bf16[64,4224]{1,0:T(8,128)(2,1)S(1)}, bf16[64,4224]{1,0:T(8,128)(2,1)S(1)}, u32[]{:S(2)}, u32[]{:S(2)}) collective-permute-start(bf16[64,4224]{1,0:T(8,128)(2,1)S(1)} %collective-permute-done.3), channel_id=1, source_target_pairs={{0,8},{8,0},{16,24},{24,16},{1,9},{9,1},{17,25},{25,17},{2,10},{10... | collective-permute-start | bytes 1622024 | tf_op jit(solution)/shard_map/ppermute | solution.py:71
  19.5 13.2 %collective-permute-start.1 = (bf16[64,4224]{1,0:T(8,128)(2,1)S(1)}, bf16[64,4224]{1,0:T(8,128)(2,1)S(1)}, u32[]{:S(2)}, u32[]{:S(2)}) collective-permute-start(bf16[64,4224]{1,0:T(8,128)(2,1)S(1)} %collective-permute-done), channel_id=1, source_target_pairs={{0,2},{2,4},{4,6},{6,7},{7,5},{5,3},{3,1},{1,0},{8,10},{10,12},{12... | collective-permute-start | bytes 1622024 | tf_op jit(solution)/shard_map/ppermute | solution.py:60
  21.3 15.1 %collective-permute-start.8 = (bf16[64,4224]{1,0:T(8,128)(2,1)S(1)}, bf16[64,4224]{1,0:T(8,128)(2,1)S(1)}, u32[]{:S(2)}, u32[]{:S(2)}) collective-permute-start(bf16[64,4224]{1,0:T(8,128)(2,1)S(1)} %collective-permute-done.7), channel_id=1, source_target_pairs={{2,0},{4,2},{6,4},{7,6},{5,7},{3,5},{1,3},{0,1},{10,8},{12,10},{14... | collective-permute-start | bytes 1622024 | tf_op jit(solution)/shard_map/ppermute | solution.py:60
  33.0 12.6 %collective-permute-start.5 = (bf16[64,4224]{1,0:T(8,128)(2,1)S(1)}, bf16[64,4224]{1,0:T(8,128)(2,1)S(1)}, u32[]{:S(2)}, u32[]{:S(2)}) collective-permute-start(bf16[64,4224]{1,0:T(8,128)(2,1)S(1)} %collective-permute-done.1), channel_id=1, source_target_pairs={{0,2},{2,4},{4,6},{6,7},{7,5},{5,3},{3,1},{1,0},{8,10},{10,12},{12... | collective-permute-start | bytes 1622024 | tf_op jit(solution)/shard_map/ppermute | solution.py:60
  36.4 12.4 %collective-permute-start.9 = (bf16[64,4224]{1,0:T(8,128)(2,1)S(1)}, bf16[64,4224]{1,0:T(8,128)(2,1)S(1)}, u32[]{:S(2)}, u32[]{:S(2)}) collective-permute-start(bf16[64,4224]{1,0:T(8,128)(2,1)S(1)} %collective-permute-done.8), channel_id=1, source_target_pairs={{2,0},{4,2},{6,4},{7,6},{5,7},{3,5},{1,3},{0,1},{10,8},{12,10},{14... | collective-permute-start | bytes 1622024 | tf_op jit(solution)/shard_map/ppermute | solution.py:60
  45.6 6.5 %collective-permute-start.6 = (bf16[32,4224]{1,0:T(8,128)(2,1)S(1)}, bf16[32,4224]{1,0:T(8,128)(2,1)S(1)}, u32[]{:S(2)}, u32[]{:S(2)}) collective-permute-start(bf16[32,4224]{1,0:T(8,128)(2,1)S(1)} %slice.124), channel_id=1, source_target_pairs={{0,2},{2,4},{4,6},{6,7},{7,5},{5,3},{3,1},{1,0},{8,10},{10,12},{12... | collective-permute-start | bytes 811016 | tf_op jit(solution)/shard_map/ppermute | solution.py:60
  49.0 6.5 %collective-permute-start.10 = (bf16[32,4224]{1,0:T(8,128)(2,1)S(1)}, bf16[32,4224]{1,0:T(8,128)(2,1)S(1)}, u32[]{:S(2)}, u32[]{:S(2)}) collective-permute-start(bf16[32,4224]{1,0:T(8,128)(2,1)S(1)} %slice.137), channel_id=1, source_target_pairs={{2,0},{4,2},{6,4},{7,6},{5,7},{3,5},{1,3},{0,1},{10,8},{12,10},{14... | collective-permute-start | bytes 811016 | tf_op jit(solution)/shard_map/ppermute | solution.py:60
  56.5 2.9 %collective-permute-start.11 = (f32[64]{0:T(128)S(1)}, f32[64]{0:T(128)S(1)}, u32[]{:S(2)}, u32[]{:S(2)}) collective-permute-start(f32[64]{0:T(128)S(1)} %get-tuple-element.33), channel_id=1, source_target_pairs={{0,8},{8,0},{16,24},{24,16},{1,9},{9,1},{17,25},{25,17},{2,10},{10... | collective-permute-start | bytes 776 | tf_op jit(solution)/shard_map/ppermute | solution.py:104
  56.5 4.4 %collective-permute-start.12 = (f32[64]{0:T(128)S(1)}, f32[64]{0:T(128)S(1)}, u32[]{:S(2)}, u32[]{:S(2)}) collective-permute-start(f32[64]{0:T(128)S(1)} %get-tuple-element.35), channel_id=1, source_target_pairs={{0,16},{8,24},{16,0},{24,8},{1,17},{9,25},{17,1},{25,9},{2,18},{10... | collective-permute-start | bytes 776 | tf_op jit(solution)/shard_map/ppermute | solution.py:104
  59.3 3.0 %collective-permute-start.13 = (f32[64]{0:T(128)S(1)}, f32[64]{0:T(128)S(1)}, u32[]{:S(2)}, u32[]{:S(2)}) collective-permute-start(f32[64]{0:T(128)S(1)} %get-tuple-element.34), channel_id=1, source_target_pairs={{0,24},{8,16},{16,8},{24,0},{1,25},{9,17},{17,9},{25,1},{2,26},{10... | collective-permute-start | bytes 776 | tf_op jit(solution)/shard_map/ppermute | solution.py:104

commit v8 on v7

--- a/solution.py
+++ b/solution.py
@@ -44,7 +44,7 @@
     high = (cluster_ids * 64 + row_index // 128).astype(jnp.float32)[:, None]
     low = (row_index % 128).astype(jnp.float32)[:, None]
     column = jnp.arange(D + TAG_WIDTH)[None, :]
-    padded = jnp.pad(widened, ((0, 0), (0, TAG_WIDTH)))
+    padded = jnp.pad(embeddings, ((0, 0), (0, TAG_WIDTH))).astype(jnp.float32)
     tags = jnp.where(column == D, high, jnp.where(column == D + 1, low, 0.0))
     payload = jnp.where(column < D, padded * scale / math.sqrt(D), tags).astype(jnp.bfloat16)
 
@@ -53,16 +53,25 @@
     backward = [(dst, src) for src, dst in forward]
     half = rows_here // 2
     steps = block_count // 2
+    lanes = [(0, 0), (0, 1), (1, 0), (1, 1)]
 
-    def send(which, visiting, step):
-        if step == steps and block_count % 2 == 0:
-            visiting = visiting[:half] if which == 0 else visiting[half:]
+    def lane_steps(lane):
+        which, part = lane
+        if block_count % 2 == 0 and which != part:
+            return steps - 1
+        return steps
+
+    def send(lane, visiting):
+        which, _ = lane
         return lax.ppermute(visiting, "blk", forward if which == 0 else backward)
 
-    chains = [[payload, None, [payload]], [payload, None, []]]
-    if steps >= 1:
-        for which, chain in enumerate(chains):
-            chain[0] = send(which, chain[0], 1)
+    chains = []
+    for lane in lanes:
+        piece = payload[:half] if lane[1] == 0 else payload[half:]
+        chains.append([piece, None, [piece] if lane[0] == 0 else []])
+    for lane, chain in zip(lanes, chains):
+        if lane_steps(lane) >= 1:
+            chain[0] = send(lane, chain[0])
             chain[2].append(chain[0])
 
     if group_count == 4:
@@ -86,14 +95,16 @@
         return best
 
     for step in range(2, steps + 1):
-        for which, chain in enumerate(chains):
+        for lane, chain in zip(lanes, chains):
+            if step > lane_steps(lane):
+                continue
             visiting, best, pending = chain
-            visiting = send(which, visiting, step)
+            visiting = send(lane, visiting)
             best = fold(best, pending)
             visiting, best = lax.optimization_barrier((visiting, best))
             chain[0], chain[1], chain[2] = visiting, best, [visiting]
     best = None
-    for _, chain_best, pending in chains:
+    for chain_best, pending in [(c[1], c[2]) for c in chains]:
         chain_best = fold(chain_best, pending)
         if chain_best is not None:
             best = chain_best if best is None else jnp.maximum(best, chain_best)

time: 63 us -> 63.5 us (level)
  waiting for transfers between devices: 35.8 us -> 22.8 us
  starting transfers between devices: 14.4 us -> 20.9 us
  matrix products: 6.96 us -> 12.1 us
  other arithmetic: 5.33 us -> 7.13 us
    ppermute x1, waiting for transfers between devices: 10.1 us -> 0.01 us  [per_device(): across = lax.ppermute(payload, 'grp', partner_pairs(group_count, 2))]
    ppermute x8 -> x14, starting transfers between devices: 8.45 us -> 15.9 us  [send(): return lax.ppermute(visiting, 'blk', forward if which == 0 else backward)]
    dot_general x9 -> x16, matrix products: 6.96 us -> 12.1 us  [block_best(): jnp.einsum('id,jd->ij', left_rows, payload[:, :D], preferred_element_type...]
    ppermute x8 -> x14, waiting for transfers between devices: 22.8 us -> 20.5 us  [send(): return lax.ppermute(visiting, 'blk', forward if which == 0 else backward)]
    ppermute x3, waiting for transfers between devices: 2.95 us -> 1.79 us  [per_device(): result = jnp.maximum(result, lax.ppermute(best[k], 'grp', pairs))]
    convert_element_type x1 -> x0, other arithmetic: 1.12 us -> none  [per_device(): widened = embeddings.astype(jnp.float32)]
    add x9 -> x15, other arithmetic: 1.57 us -> 2.68 us  [tag_labels(): return high * 128.0 + low]
    convert_element_type x1, other arithmetic: 0.29 us -> 1.36 us  [per_device(): jnp.where(column < D, padded * scale / math.sqrt(D), tags)]
  transfers between devices with their start and end apart: 14 -> 20, of which waited for: 9 -> 9; matrix products, arithmetic and copies ran while one was open for 13% -> 23% of each run, Pallas kernels for 0% -> 0%
where the time goes in v8:
time: 63.5 us; the launch traced here: 63.3 us
  waiting for transfers between devices  22.8 us (36%)
  starting transfers between devices  20.9 us (33%)
  matrix products  12.1 us (19%)
  other arithmetic  7.13 us (11%)
    ppermute x14, waiting for transfers between devices, send(): return lax.ppermute(visiting, 'blk', forward if which == 0 else backward)  20.5 us
    ppermute x14, starting transfers between devices, send(): return lax.ppermute(visiting, 'blk', forward if which == 0 else backward)  15.9 us
    dot_general x16, matrix products, block_best(): jnp.einsum('id,jd->ij', left_rows, payload[:, :D], preferred_element_type...  12.1 us
    ppermute x1, starting transfers between devices, per_device(): across = lax.ppermute(payload, 'grp', partner_pairs(group_count, 2))  3.07 us
    add x15, other arithmetic, tag_labels(): return high * 128.0 + low  2.68 us
    ppermute x3, starting transfers between devices, per_device(): result = jnp.maximum(result, lax.ppermute(best[k], 'grp', pairs))  1.86 us
    ppermute x3, waiting for transfers between devices, per_device(): result = jnp.maximum(result, lax.ppermute(best[k], 'grp', pairs))  1.79 us
    convert_element_type x1, other arithmetic, per_device(): jnp.where(column < D, padded * scale / math.sqrt(D), tags)  1.36 us
  transfers between devices with their start and end apart: 20, of which 9 were waited for; matrix products, arithmetic and copies ran while one was open for 23% of the time, Pallas kernels for 0%

profile of v8, /device:TPU:0, one launch (start us, length us, event | category | flops | bytes accessed | tf_op | source)
XLA Modules:
  0.0 63.3 jit_solution(5340379615462545013)
XLA Ops:
  0.0 1.2 %multiply_reduce_fusion = f32[64]{0:T(128)S(1)} fusion(bf16[64,4096]{1,0:T(8,128)(2,1)} %param.3), kind=kLoop, calls=%fused_computation.36 | loop fusion | flops 786368 | bytes 524544 | tf_op jit(solution)/shard_map/reduce_sum | solution.py:42
  1.3 0.7 %add_convert_fusion = (bf16[64]{0:T(256)(128)(2,1)S(1)}, bf16[64]{0:T(256)(128)(2,1)S(1)}) fusion(s32[64]{0:T(128)} %param.4, s32[64]{0:T(128)} %param.5), kind=kLoop, calls=%fused_computation.101 | loop fusion | flops 1472 | bytes 768 | tf_op jit(solution)/shard_map/convert_element_type | solution.py:44
  2.0 1.4 %select_convert_fusion = bf16[64,4224]{1,0:T(8,128)(2,1)S(1)} fusion(bf16[64]{0:T(256)(128)(2,1)S(1)} %get-tuple-element.57, bf16[64]{0:T(256)(128)(2,1)S(1)} %get-tuple-element.56, f32[64]{0:T(128)S(1)} %add_rsqrt_fusion, bf16[64,4096]{1,0:T(8,128)(2,1)} %param.3, pred[4224]{0:T(1024)(128)(4,1)S(1)} %get-tuple-element.58, ...), kind=kLoop, calls=%fused_computation.35 | loop fusion | flops 1622016 | bytes 1078144 | tf_op jit(solution)/shard_map/convert_element_type | solution.py:49
  3.3 3.1 %collective-permute-start.3 = (bf16[64,4224]{1,0:T(8,128)(2,1)S(1)}, bf16[64,4224]{1,0:T(8,128)(2,1)S(1)}, u32[]{:S(2)}, u32[]{:S(2)}) collective-permute-start(bf16[64,4224]{1,0:T(8,128)(2,1)S(1)} %select_convert_fusion), channel_id=1, source_target_pairs={{0,16},{8,24},{16,0},{24,8},{1,17},{9,25},{17,1},{25,9},{2,18},{10... | collective-permute-start | bytes 1622024 | tf_op jit(solution)/shard_map/ppermute | solution.py:78
  6.5 1.6 %collective-permute-start = (bf16[32,4224]{1,0:T(8,128)(2,1)S(1)}, bf16[32,4224]{1,0:T(8,128)(2,1)S(1)}, u32[]{:S(2)}, u32[]{:S(2)}) collective-permute-start(bf16[32,4224]{1,0:T(8,128)(2,1)S(1)} %get-tuple-element.51), channel_id=1, source_target_pairs={{0,2},{2,4},{4,6},{6,7},{7,5},{5,3},{3,1},{1,0},{8,10},{10,12},{12... | collective-permute-start | bytes 811016 | tf_op jit(solution)/shard_map/ppermute | solution.py:66
  8.1 0.4 collective-permute-start.10
  8.5 1.6 %collective-permute-start.7 = (bf16[32,4224]{1,0:T(8,128)(2,1)S(1)}, bf16[32,4224]{1,0:T(8,128)(2,1)S(1)}, u32[]{:S(2)}, u32[]{:S(2)}) collective-permute-start(bf16[32,4224]{1,0:T(8,128)(2,1)S(1)} %get-tuple-element.52), channel_id=1, source_target_pairs={{0,2},{2,4},{4,6},{6,7},{7,5},{5,3},{3,1},{1,0},{8,10},{10,12},{12... | collective-permute-start | bytes 811016 | tf_op jit(solution)/shard_map/ppermute | solution.py:66
  10.1 0.2 add_reduce_fusion.15
  10.3 5.6 %collective-permute-done = bf16[32,4224]{1,0:T(8,128)(2,1)S(1)} collective-permute-done((bf16[32,4224]{1,0:T(8,128)(2,1)S(1)}, bf16[32,4224]{1,0:T(8,128)(2,1)S(1)}, u32[]{:S(2)}, u32[]{:S(2)}) %collective-permute-start) | collective-permute-done | bytes 270368 | tf_op jit(solution)/shard_map/ppermute | solution.py:66
  15.9 1.5 %collective-permute-start.13 = (bf16[32,4224]{1,0:T(8,128)(2,1)S(1)}, bf16[32,4224]{1,0:T(8,128)(2,1)S(1)}, u32[]{:S(2)}, u32[]{:S(2)}) collective-permute-start(bf16[32,4224]{1,0:T(8,128)(2,1)S(1)} %get-tuple-element.52), channel_id=1, source_target_pairs={{2,0},{4,2},{6,4},{7,6},{5,7},{3,5},{1,3},{0,1},{10,8},{12,10},{14... | collective-permute-start | bytes 811016 | tf_op jit(solution)/shard_map/ppermute | solution.py:66
  17.5 3.7 %collective-permute-done.7 = bf16[32,4224]{1,0:T(8,128)(2,1)S(1)} collective-permute-done((bf16[32,4224]{1,0:T(8,128)(2,1)S(1)}, bf16[32,4224]{1,0:T(8,128)(2,1)S(1)}, u32[]{:S(2)}, u32[]{:S(2)}) %collective-permute-start.7) | collective-permute-done | bytes 270368 | tf_op jit(solution)/shard_map/ppermute | solution.py:66
  21.2 1.6 %collective-permute-start.1 = (bf16[32,4224]{1,0:T(8,128)(2,1)S(1)}, bf16[32,4224]{1,0:T(8,128)(2,1)S(1)}, u32[]{:S(2)}, u32[]{:S(2)}) collective-permute-start(bf16[32,4224]{1,0:T(8,128)(2,1)S(1)} %collective-permute-done), channel_id=1, source_target_pairs={{0,2},{2,4},{4,6},{6,7},{7,5},{5,3},{3,1},{1,0},{8,10},{10,12},{12... | collective-permute-start | bytes 811016 | tf_op jit(solution)/shard_map/ppermute | solution.py:66
  23.0 1.6 %collective-permute-start.8 = (bf16[32,4224]{1,0:T(8,128)(2,1)S(1)}, bf16[32,4224]{1,0:T(8,128)(2,1)S(1)}, u32[]{:S(2)}, u32[]{:S(2)}) collective-permute-start(bf16[32,4224]{1,0:T(8,128)(2,1)S(1)} %collective-permute-done.7), channel_id=1, source_target_pairs={{0,2},{2,4},{4,6},{6,7},{7,5},{5,3},{3,1},{1,0},{8,10},{10,12},{12... | collective-permute-start | bytes 811016 | tf_op jit(solution)/shard_map/ppermute | solution.py:66
  24.8 0.5 collective-permute-start.11
  25.5 1.3 %collective-permute-start.14 = (bf16[32,4224]{1,0:T(8,128)(2,1)S(1)}, bf16[32,4224]{1,0:T(8,128)(2,1)S(1)}, u32[]{:S(2)}, u32[]{:S(2)}) collective-permute-start(bf16[32,4224]{1,0:T(8,128)(2,1)S(1)} %collective-permute-done.13), channel_id=1, source_target_pairs={{2,0},{4,2},{6,4},{7,6},{5,7},{3,5},{1,3},{0,1},{10,8},{12,10},{14... | collective-permute-start | bytes 811016 | tf_op jit(solution)/shard_map/ppermute | solution.py:66
  26.8 0.5 collective-permute-done.4
  27.5 0.2 pad_maximum_fusion
  27.7 0.8 %fusion = f32[256]{0:T(256)S(1)} fusion(bf16[256,4096]{1,0:T(8,128)(2,1)S(1)} %pad_maximum_fusion, bf16[64,4224]{1,0:T(8,128)(2,1)S(1)} %select_convert_fusion, f32[256]{0:T(256)S(1)} %get-tuple-element.48, f32[256]{0:T(256)S(1)} %get-tuple-element.47, f32[32]{0:T(128)S(1)} %get-tuple-element.45, f32[32]{0:T(128)S(1)} %multiply_floor_fusion.15), kind=kOutput, calls=%fused_computation.19 | convolution fusion | flops 67149568 | bytes 2363392 | tf_op jit(solution)/shard_map/id,jd->ij/dot_general | solution.py:26
  28.5 0.8 %fusion.1 = f32[256]{0:T(256)S(1)} fusion(bf16[256,4096]{1,0:T(8,128)(2,1)S(1)} %pad_maximum_fusion, bf16[32,4224]{1,0:T(8,128)(2,1)S(1)} %collective-permute-done, f32[256]{0:T(256)S(1)} %get-tuple-element.48, f32[256]{0:T(256)S(1)} %get-tuple-element.47, f32[32]{0:T(128)S(1)} %add_reduce_fusion.14, f32[32]{0:T(128)S(1)} %multiply_floor_fusion.14), kind=kOutput, calls=%fused_computation.20 | convolution fusion | flops 67149568 | bytes 2363392 | tf_op jit(solution)/shard_map/id,jd->ij/dot_general | solution.py:26
  29.3 1.3 %collective-permute-done.1 = bf16[32,4224]{1,0:T(8,128)(2,1)S(1)} collective-permute-done((bf16[32,4224]{1,0:T(8,128)(2,1)S(1)}, bf16[32,4224]{1,0:T(8,128)(2,1)S(1)}, u32[]{:S(2)}, u32[]{:S(2)}) %collective-permute-start.1) | collective-permute-done | bytes 270368 | tf_op jit(solution)/shard_map/ppermute | solution.py:66
  30.5 1.6 %collective-permute-start.5 = (bf16[32,4224]{1,0:T(8,128)(2,1)S(1)}, bf16[32,4224]{1,0:T(8,128)(2,1)S(1)}, u32[]{:S(2)}, u32[]{:S(2)}) collective-permute-start(bf16[32,4224]{1,0:T(8,128)(2,1)S(1)} %collective-permute-done.1), channel_id=1, source_target_pairs={{0,2},{2,4},{4,6},{6,7},{7,5},{5,3},{3,1},{1,0},{8,10},{10,12},{12... | collective-permute-start | bytes 811016 | tf_op jit(solution)/shard_map/ppermute | solution.py:66
  32.1 0.7 %fusion.5 = f32[256]{0:T(256)S(1)} fusion(bf16[256,4096]{1,0:T(8,128)(2,1)S(1)} %pad_maximum_fusion, bf16[64,4224]{1,0:T(8,128)(2,1)S(1)} %select_convert_fusion, f32[256]{0:T(256)S(1)} %get-tuple-element.48, f32[256]{0:T(256)S(1)} %get-tuple-element.47, f32[32]{0:T(128)S(1)} %get-tuple-element.46, f32[32]{0:T(128)S(1)} %multiply_floor_fusion.10), kind=kOutput, calls=%fused_computation.24 | convolution fusion | flops 67149568 | bytes 2363392 | tf_op jit(solution)/shard_map/id,jd->ij/dot_general | solution.py:26
  32.9 0.8 %fusion.6 = f32[256]{0:T(256)S(1)} fusion(bf16[256,4096]{1,0:T(8,128)(2,1)S(1)} %pad_maximum_fusion, bf16[32,4224]{1,0:T(8,128)(2,1)S(1)} %collective-permute-done.7, f32[256]{0:T(256)S(1)} %get-tuple-element.48, f32[256]{0:T(256)S(1)} %get-tuple-element.47, f32[32]{0:T(128)S(1)} %add_reduce_fusion.9, f32[32]{0:T(128)S(1)} %multiply_floor_fusion.9), kind=kOutput, calls=%fused_computation.25 | convolution fusion | flops 67149568 | bytes 2363392 | tf_op jit(solution)/shard_map/id,jd->ij/dot_general | solution.py:26
  33.6 0.2 add_reduce_fusion.13
  33.8 2.5 %collective-permute-done.8 = bf16[32,4224]{1,0:T(8,128)(2,1)S(1)} collective-permute-done((bf16[32,4224]{1,0:T(8,128)(2,1)S(1)}, bf16[32,4224]{1,0:T(8,128)(2,1)S(1)}, u32[]{:S(2)}, u32[]{:S(2)}) %collective-permute-start.8) | collective-permute-done | bytes 270368 | tf_op jit(solution)/shard_map/ppermute | solution.py:66
  36.5 1.6 %collective-permute-start.9 = (bf16[32,4224]{1,0:T(8,128)(2,1)S(1)}, bf16[32,4224]{1,0:T(8,128)(2,1)S(1)}, u32[]{:S(2)}, u32[]{:S(2)}) collective-permute-start(bf16[32,4224]{1,0:T(8,128)(2,1)S(1)} %collective-permute-done.8), channel_id=1, source_target_pairs={{0,2},{2,4},{4,6},{6,7},{7,5},{5,3},{3,1},{1,0},{8,10},{10,12},{12... | collective-permute-start | bytes 811016 | tf_op jit(solution)/shard_map/ppermute | solution.py:66
  38.1 0.8 %fusion.9 = f32[256]{0:T(256)S(1)} fusion(bf16[256,4096]{1,0:T(8,128)(2,1)S(1)} %pad_maximum_fusion, bf16[32,4224]{1,0:T(8,128)(2,1)S(1)} %collective-permute-done.10, f32[256]{0:T(256)S(1)} %get-tuple-element.48, f32[256]{0:T(256)S(1)} %get-tuple-element.47, f32[32]{0:T(128)S(1)} %add_reduce_fusion.6, f32[32]{0:T(128)S(1)} %multiply_floor_fusion.6), kind=kOutput, calls=%fused_computation.28 | convolution fusion | flops 67149568 | bytes 2363392 | tf_op jit(solution)/shard_map/id,jd->ij/dot_general | solution.py:26
  39.1 0.5 collective-permute-start.12
  39.6 0.7 %fusion.12 = f32[256]{0:T(256)S(1)} fusion(bf16[256,4096]{1,0:T(8,128)(2,1)S(1)} %pad_maximum_fusion, bf16[32,4224]{1,0:T(8,128)(2,1)S(1)} %collective-permute-done.13, f32[256]{0:T(256)S(1)} %get-tuple-element.48, f32[256]{0:T(256)S(1)} %get-tuple-element.47, f32[32]{0:T(128)S(1)} %add_reduce_fusion.3, f32[32]{0:T(128)S(1)} %multiply_floor_fusion.3), kind=kOutput, calls=%fused_computation.31 | convolution fusion | flops 67149568 | bytes 2363392 | tf_op jit(solution)/shard_map/id,jd->ij/dot_general | solution.py:26
  40.5 1.5 %collective-permute-start.15 = (bf16[32,4224]{1,0:T(8,128)(2,1)S(1)}, bf16[32,4224]{1,0:T(8,128)(2,1)S(1)}, u32[]{:S(2)}, u32[]{:S(2)}) collective-permute-start(bf16[32,4224]{1,0:T(8,128)(2,1)S(1)} %collective-permute-done.14), channel_id=1, source_target_pairs={{2,0},{4,2},{6,4},{7,6},{5,7},{3,5},{1,3},{0,1},{10,8},{12,10},{14... | collective-permute-start | bytes 811016 | tf_op jit(solution)/shard_map/ppermute | solution.py:66
  42.1 0.8 %fusion.2 = f32[256]{0:T(256)S(1)} fusion(bf16[256,4096]{1,0:T(8,128)(2,1)S(1)} %pad_maximum_fusion, bf16[32,4224]{1,0:T(8,128)(2,1)S(1)} %collective-permute-done.1, f32[256]{0:T(256)S(1)} %get-tuple-element.48, f32[256]{0:T(256)S(1)} %get-tuple-element.47, f32[32]{0:T(128)S(1)} %add_reduce_fusion.13, f32[32]{0:T(128)S(1)} %multiply_floor_fusion.13), kind=kOutput, calls=%fused_computation.21 | convolution fusion | flops 67149568 | bytes 2363392 | tf_op jit(solution)/shard_map/id,jd->ij/dot_general | solution.py:26
  42.8 0.8 %fusion.7 = f32[256]{0:T(256)S(1)} fusion(bf16[256,4096]{1,0:T(8,128)(2,1)S(1)} %pad_maximum_fusion, bf16[32,4224]{1,0:T(8,128)(2,1)S(1)} %collective-permute-done.8, f32[256]{0:T(256)S(1)} %get-tuple-element.48, f32[256]{0:T(256)S(1)} %get-tuple-element.47, f32[32]{0:T(128)S(1)} %add_reduce_fusion.8, f32[32]{0:T(128)S(1)} %multiply_floor_fusion.8), kind=kOutput, calls=%fused_computation.26 | convolution fusion | flops 67149568 | bytes 2363392 | tf_op jit(solution)/shard_map/id,jd->ij/dot_general | solution.py:26
  43.6 0.8 %fusion.10 = f32[256]{0:T(256)S(1)} fusion(bf16[256,4096]{1,0:T(8,128)(2,1)S(1)} %pad_maximum_fusion, bf16[32,4224]{1,0:T(8,128)(2,1)S(1)} %collective-permute-done.11, f32[256]{0:T(256)S(1)} %get-tuple-element.48, f32[256]{0:T(256)S(1)} %get-tuple-element.47, f32[32]{0:T(128)S(1)} %add_reduce_fusion.5, f32[32]{0:T(128)S(1)} %multiply_floor_fusion.5), kind=kOutput, calls=%fused_computation.29 | convolution fusion | flops 67149568 | bytes 2363392 | tf_op jit(solution)/shard_map/id,jd->ij/dot_general | solution.py:26
  44.4 0.8 %fusion.13 = f32[256]{0:T(256)S(1)} fusion(bf16[256,4096]{1,0:T(8,128)(2,1)S(1)} %pad_maximum_fusion, bf16[32,4224]{1,0:T(8,128)(2,1)S(1)} %collective-permute-done.14, f32[256]{0:T(256)S(1)} %get-tuple-element.48, f32[256]{0:T(256)S(1)} %get-tuple-element.47, f32[32]{0:T(128)S(1)} %add_reduce_fusion.2, f32[32]{0:T(128)S(1)} %multiply_floor_fusion.2), kind=kOutput, calls=%fused_computation.32 | convolution fusion | flops 67149568 | bytes 2363392 | tf_op jit(solution)/shard_map/id,jd->ij/dot_general | solution.py:26
  45.4 0.6 collective-permute-start.6
  46.0 2.0 %collective-permute-done.9 = bf16[32,4224]{1,0:T(8,128)(2,1)S(1)} collective-permute-done((bf16[32,4224]{1,0:T(8,128)(2,1)S(1)}, bf16[32,4224]{1,0:T(8,128)(2,1)S(1)}, u32[]{:S(2)}, u32[]{:S(2)}) %collective-permute-start.9) | collective-permute-done | bytes 270368 | tf_op jit(solution)/shard_map/ppermute | solution.py:66
  48.1 0.8 %fusion.3 = f32[256]{0:T(256)S(1)} fusion(bf16[256,4096]{1,0:T(8,128)(2,1)S(1)} %pad_maximum_fusion, bf16[32,4224]{1,0:T(8,128)(2,1)S(1)} %collective-permute-done.5, f32[256]{0:T(256)S(1)} %get-tuple-element.48, f32[256]{0:T(256)S(1)} %get-tuple-element.47, f32[32]{0:T(128)S(1)} %add_reduce_fusion.12, f32[32]{0:T(128)S(1)} %multiply_floor_fusion.12), kind=kOutput, calls=%fused_computation.22 | convolution fusion | flops 67149568 | bytes 2363392 | tf_op jit(solution)/shard_map/id,jd->ij/dot_general | solution.py:26
  48.9 2.7 %collective-permute-done.15 = bf16[32,4224]{1,0:T(8,128)(2,1)S(1)} collective-permute-done((bf16[32,4224]{1,0:T(8,128)(2,1)S(1)}, bf16[32,4224]{1,0:T(8,128)(2,1)S(1)}, u32[]{:S(2)}, u32[]{:S(2)}) %collective-permute-start.15) | collective-permute-done | bytes 270368 | tf_op jit(solution)/shard_map/ppermute | solution.py:66
  51.8 0.8 %fusion.8 = f32[256]{0:T(256)S(1)} fusion(bf16[256,4096]{1,0:T(8,128)(2,1)S(1)} %pad_maximum_fusion, bf16[32,4224]{1,0:T(8,128)(2,1)S(1)} %collective-permute-done.9, f32[256]{0:T(256)S(1)} %get-tuple-element.48, f32[256]{0:T(256)S(1)} %get-tuple-element.47, f32[32]{0:T(128)S(1)} %add_reduce_fusion.7, f32[32]{0:T(128)S(1)} %multiply_floor_fusion.7), kind=kOutput, calls=%fused_computation.27 | convolution fusion | flops 67149568 | bytes 2363392 | tf_op jit(solution)/shard_map/id,jd->ij/dot_general | solution.py:26
  52.7 0.8 %fusion.14 = f32[256]{0:T(256)S(1)} fusion(bf16[256,4096]{1,0:T(8,128)(2,1)S(1)} %pad_maximum_fusion, bf16[32,4224]{1,0:T(8,128)(2,1)S(1)} %collective-permute-done.15, f32[256]{0:T(256)S(1)} %get-tuple-element.48, f32[256]{0:T(256)S(1)} %get-tuple-element.47, f32[32]{0:T(128)S(1)} %add_reduce_fusion.1, f32[32]{0:T(128)S(1)} %multiply_floor_fusion.1), kind=kOutput, calls=%fused_computation.33 | convolution fusion | flops 67149568 | bytes 2363392 | tf_op jit(solution)/shard_map/id,jd->ij/dot_general | solution.py:26
  53.5 0.8 %fusion.11 = f32[256]{0:T(256)S(1)} fusion(bf16[256,4096]{1,0:T(8,128)(2,1)S(1)} %pad_maximum_fusion, bf16[32,4224]{1,0:T(8,128)(2,1)S(1)} %collective-permute-done.12, f32[256]{0:T(256)S(1)} %get-tuple-element.48, f32[256]{0:T(256)S(1)} %get-tuple-element.47, f32[32]{0:T(128)S(1)} %add_reduce_fusion.4, f32[32]{0:T(128)S(1)} %multiply_floor_fusion.4), kind=kOutput, calls=%fused_computation.30 | convolution fusion | flops 67149568 | bytes 2363392 | tf_op jit(solution)/shard_map/id,jd->ij/dot_general | solution.py:26
  54.5 0.8 %fusion.4 = f32[256]{0:T(256)S(1)} fusion(bf16[256,4096]{1,0:T(8,128)(2,1)S(1)} %pad_maximum_fusion, bf16[32,4224]{1,0:T(8,128)(2,1)S(1)} %collective-permute-done.6, f32[256]{0:T(256)S(1)} %get-tuple-element.48, f32[256]{0:T(256)S(1)} %get-tuple-element.47, f32[32]{0:T(128)S(1)} %add_reduce_fusion.11, f32[32]{0:T(128)S(1)} %multiply_floor_fusion.11), kind=kOutput, calls=%fused_computation.23 | convolution fusion | flops 67149568 | bytes 2363392 | tf_op jit(solution)/shard_map/id,jd->ij/dot_general | solution.py:26
  55.2 2.8 %collective-permute-done.16 = bf16[32,4224]{1,0:T(8,128)(2,1)S(1)} collective-permute-done((bf16[32,4224]{1,0:T(8,128)(2,1)S(1)}, bf16[32,4224]{1,0:T(8,128)(2,1)S(1)}, u32[]{:S(2)}, u32[]{:S(2)}) %collective-permute-start.16) | collective-permute-done | bytes 270368 | tf_op jit(solution)/shard_map/ppermute | solution.py:66
  58.2 0.8 %fusion.15 = f32[256]{0:T(256)S(1)} fusion(bf16[256,4096]{1,0:T(8,128)(2,1)S(1)} %pad_maximum_fusion, bf16[32,4224]{1,0:T(8,128)(2,1)S(1)} %collective-permute-done.16, f32[256]{0:T(256)S(1)} %get-tuple-element.48, f32[256]{0:T(256)S(1)} %get-tuple-element.47, f32[32]{0:T(128)S(1)} %add_reduce_fusion, f32[32]{0:T(128)S(1)} %multiply_floor_fusion), kind=kOutput, calls=%fused_computation.34 | convolution fusion | flops 67149568 | bytes 2363392 | tf_op jit(solution)/shard_map/id,jd->ij/dot_general | solution.py:26
  59.1 0.6 collective-permute-start.18
  59.7 1.3 %collective-permute-start.19 = (f32[64]{0:T(128)S(1)}, f32[64]{0:T(128)S(1)}, u32[]{:S(2)}, u32[]{:S(2)}) collective-permute-start(f32[64]{0:T(128)S(1)} %get-tuple-element.54), channel_id=1, source_target_pairs={{0,24},{8,16},{16,8},{24,0},{1,25},{9,17},{17,9},{25,1},{2,26},{10... | collective-permute-start | bytes 776 | tf_op jit(solution)/shard_map/ppermute | solution.py:115
  60.9 1.8 %collective-permute-done.18 = f32[64]{0:T(128)S(1)} collective-permute-done((f32[64]{0:T(128)S(1)}, f32[64]{0:T(128)S(1)}, u32[]{:S(2)}, u32[]{:S(2)}) %collective-permute-start.18) | collective-permute-done | bytes 288 | tf_op jit(solution)/shard_map/ppermute | solution.py:115
  62.7 0.5 maximum_maximum_fusion.1
  (60 shorter events, 2.9 us)
Async XLA Ops:
  3.3 22.0 %collective-permute-start.3 = (bf16[64,4224]{1,0:T(8,128)(2,1)S(1)}, bf16[64,4224]{1,0:T(8,128)(2,1)S(1)}, u32[]{:S(2)}, u32[]{:S(2)}) collective-permute-start(bf16[64,4224]{1,0:T(8,128)(2,1)S(1)} %select_convert_fusion), channel_id=1, source_target_pairs={{0,16},{8,24},{16,0},{24,8},{1,17},{9,25},{17,1},{25,9},{2,18},{10... | collective-permute-start | bytes 1622024 | tf_op jit(solution)/shard_map/ppermute | solution.py:78
  6.4 19.1 %collective-permute-start.2 = (bf16[64,4224]{1,0:T(8,128)(2,1)S(1)}, bf16[64,4224]{1,0:T(8,128)(2,1)S(1)}, u32[]{:S(2)}, u32[]{:S(2)}) collective-permute-start(bf16[64,4224]{1,0:T(8,128)(2,1)S(1)} %select_convert_fusion), channel_id=1, source_target_pairs={{0,8},{8,0},{16,24},{24,16},{1,9},{9,1},{17,25},{25,17},{2,10},{10... | collective-permute-start | bytes 1622024 | tf_op jit(solution)/shard_map/ppermute | solution.py:79
  6.5 9.4 %collective-permute-start = (bf16[32,4224]{1,0:T(8,128)(2,1)S(1)}, bf16[32,4224]{1,0:T(8,128)(2,1)S(1)}, u32[]{:S(2)}, u32[]{:S(2)}) collective-permute-start(bf16[32,4224]{1,0:T(8,128)(2,1)S(1)} %get-tuple-element.51), channel_id=1, source_target_pairs={{0,2},{2,4},{4,6},{6,7},{7,5},{5,3},{3,1},{1,0},{8,10},{10,12},{12... | collective-permute-start | bytes 811016 | tf_op jit(solution)/shard_map/ppermute | solution.py:66
  8.1 14.9 %collective-permute-start.10 = (bf16[32,4224]{1,0:T(8,128)(2,1)S(1)}, bf16[32,4224]{1,0:T(8,128)(2,1)S(1)}, u32[]{:S(2)}, u32[]{:S(2)}) collective-permute-start(bf16[32,4224]{1,0:T(8,128)(2,1)S(1)} %get-tuple-element.51), channel_id=1, source_target_pairs={{2,0},{4,2},{6,4},{7,6},{5,7},{3,5},{1,3},{0,1},{10,8},{12,10},{14... | collective-permute-start | bytes 811016 | tf_op jit(solution)/shard_map/ppermute | solution.py:66
  8.5 12.7 %collective-permute-start.7 = (bf16[32,4224]{1,0:T(8,128)(2,1)S(1)}, bf16[32,4224]{1,0:T(8,128)(2,1)S(1)}, u32[]{:S(2)}, u32[]{:S(2)}) collective-permute-start(bf16[32,4224]{1,0:T(8,128)(2,1)S(1)} %get-tuple-element.52), channel_id=1, source_target_pairs={{0,2},{2,4},{4,6},{6,7},{7,5},{5,3},{3,1},{1,0},{8,10},{10,12},{12... | collective-permute-start | bytes 811016 | tf_op jit(solution)/shard_map/ppermute | solution.py:66
  15.9 8.9 %collective-permute-start.13 = (bf16[32,4224]{1,0:T(8,128)(2,1)S(1)}, bf16[32,4224]{1,0:T(8,128)(2,1)S(1)}, u32[]{:S(2)}, u32[]{:S(2)}) collective-permute-start(bf16[32,4224]{1,0:T(8,128)(2,1)S(1)} %get-tuple-element.52), channel_id=1, source_target_pairs={{2,0},{4,2},{6,4},{7,6},{5,7},{3,5},{1,3},{0,1},{10,8},{12,10},{14... | collective-permute-start | bytes 811016 | tf_op jit(solution)/shard_map/ppermute | solution.py:66
  21.2 9.4 %collective-permute-start.1 = (bf16[32,4224]{1,0:T(8,128)(2,1)S(1)}, bf16[32,4224]{1,0:T(8,128)(2,1)S(1)}, u32[]{:S(2)}, u32[]{:S(2)}) collective-permute-start(bf16[32,4224]{1,0:T(8,128)(2,1)S(1)} %collective-permute-done), channel_id=1, source_target_pairs={{0,2},{2,4},{4,6},{6,7},{7,5},{5,3},{3,1},{1,0},{8,10},{10,12},{12... | collective-permute-start | bytes 811016 | tf_op jit(solution)/shard_map/ppermute | solution.py:66
  23.0 13.4 %collective-permute-start.8 = (bf16[32,4224]{1,0:T(8,128)(2,1)S(1)}, bf16[32,4224]{1,0:T(8,128)(2,1)S(1)}, u32[]{:S(2)}, u32[]{:S(2)}) collective-permute-start(bf16[32,4224]{1,0:T(8,128)(2,1)S(1)} %collective-permute-done.7), channel_id=1, source_target_pairs={{0,2},{2,4},{4,6},{6,7},{7,5},{5,3},{3,1},{1,0},{8,10},{10,12},{12... | collective-permute-start | bytes 811016 | tf_op jit(solution)/shard_map/ppermute | solution.py:66
  24.8 14.1 %collective-permute-start.11 = (bf16[32,4224]{1,0:T(8,128)(2,1)S(1)}, bf16[32,4224]{1,0:T(8,128)(2,1)S(1)}, u32[]{:S(2)}, u32[]{:S(2)}) collective-permute-start(bf16[32,4224]{1,0:T(8,128)(2,1)S(1)} %collective-permute-done.10), channel_id=1, source_target_pairs={{2,0},{4,2},{6,4},{7,6},{5,7},{3,5},{1,3},{0,1},{10,8},{12,10},{14... | collective-permute-start | bytes 811016 | tf_op jit(solution)/shard_map/ppermute | solution.py:66
  25.3 1.9 %collective-permute-start.4 = (bf16[64,4224]{1,0:T(8,128)(2,1)S(1)}, bf16[64,4224]{1,0:T(8,128)(2,1)S(1)}, u32[]{:S(2)}, u32[]{:S(2)}) collective-permute-start(bf16[64,4224]{1,0:T(8,128)(2,1)S(1)} %collective-permute-done.3), channel_id=1, source_target_pairs={{0,8},{8,0},{16,24},{24,16},{1,9},{9,1},{17,25},{25,17},{2,10},{10... | collective-permute-start | bytes 1622024 | tf_op jit(solution)/shard_map/ppermute | solution.py:80
  25.5 14.8 %collective-permute-start.14 = (bf16[32,4224]{1,0:T(8,128)(2,1)S(1)}, bf16[32,4224]{1,0:T(8,128)(2,1)S(1)}, u32[]{:S(2)}, u32[]{:S(2)}) collective-permute-start(bf16[32,4224]{1,0:T(8,128)(2,1)S(1)} %collective-permute-done.13), channel_id=1, source_target_pairs={{2,0},{4,2},{6,4},{7,6},{5,7},{3,5},{1,3},{0,1},{10,8},{12,10},{14... | collective-permute-start | bytes 811016 | tf_op jit(solution)/shard_map/ppermute | solution.py:66
  30.5 14.6 %collective-permute-start.5 = (bf16[32,4224]{1,0:T(8,128)(2,1)S(1)}, bf16[32,4224]{1,0:T(8,128)(2,1)S(1)}, u32[]{:S(2)}, u32[]{:S(2)}) collective-permute-start(bf16[32,4224]{1,0:T(8,128)(2,1)S(1)} %collective-permute-done.1), channel_id=1, source_target_pairs={{0,2},{2,4},{4,6},{6,7},{7,5},{5,3},{3,1},{1,0},{8,10},{10,12},{12... | collective-permute-start | bytes 811016 | tf_op jit(solution)/shard_map/ppermute | solution.py:66
  36.5 11.4 %collective-permute-start.9 = (bf16[32,4224]{1,0:T(8,128)(2,1)S(1)}, bf16[32,4224]{1,0:T(8,128)(2,1)S(1)}, u32[]{:S(2)}, u32[]{:S(2)}) collective-permute-start(bf16[32,4224]{1,0:T(8,128)(2,1)S(1)} %collective-permute-done.8), channel_id=1, source_target_pairs={{0,2},{2,4},{4,6},{6,7},{7,5},{5,3},{3,1},{1,0},{8,10},{10,12},{12... | collective-permute-start | bytes 811016 | tf_op jit(solution)/shard_map/ppermute | solution.py:66
  39.1 13.4 %collective-permute-start.12 = (bf16[32,4224]{1,0:T(8,128)(2,1)S(1)}, bf16[32,4224]{1,0:T(8,128)(2,1)S(1)}, u32[]{:S(2)}, u32[]{:S(2)}) collective-permute-start(bf16[32,4224]{1,0:T(8,128)(2,1)S(1)} %collective-permute-done.11), channel_id=1, source_target_pairs={{2,0},{4,2},{6,4},{7,6},{5,7},{3,5},{1,3},{0,1},{10,8},{12,10},{14... | collective-permute-start | bytes 811016 | tf_op jit(solution)/shard_map/ppermute | solution.py:66
  40.5 11.0 %collective-permute-start.15 = (bf16[32,4224]{1,0:T(8,128)(2,1)S(1)}, bf16[32,4224]{1,0:T(8,128)(2,1)S(1)}, u32[]{:S(2)}, u32[]{:S(2)}) collective-permute-start(bf16[32,4224]{1,0:T(8,128)(2,1)S(1)} %collective-permute-done.14), channel_id=1, source_target_pairs={{2,0},{4,2},{6,4},{7,6},{5,7},{3,5},{1,3},{0,1},{10,8},{12,10},{14... | collective-permute-start | bytes 811016 | tf_op jit(solution)/shard_map/ppermute | solution.py:66
  45.4 8.9 %collective-permute-start.6 = (bf16[32,4224]{1,0:T(8,128)(2,1)S(1)}, bf16[32,4224]{1,0:T(8,128)(2,1)S(1)}, u32[]{:S(2)}, u32[]{:S(2)}) collective-permute-start(bf16[32,4224]{1,0:T(8,128)(2,1)S(1)} %collective-permute-done.5), channel_id=1, source_target_pairs={{0,2},{2,4},{4,6},{6,7},{7,5},{5,3},{3,1},{1,0},{8,10},{10,12},{12... | collective-permute-start | bytes 811016 | tf_op jit(solution)/shard_map/ppermute | solution.py:66
  51.6 6.5 %collective-permute-start.16 = (bf16[32,4224]{1,0:T(8,128)(2,1)S(1)}, bf16[32,4224]{1,0:T(8,128)(2,1)S(1)}, u32[]{:S(2)}, u32[]{:S(2)}) collective-permute-start(bf16[32,4224]{1,0:T(8,128)(2,1)S(1)} %collective-permute-done.15), channel_id=1, source_target_pairs={{2,0},{4,2},{6,4},{7,6},{5,7},{3,5},{1,3},{0,1},{10,8},{12,10},{14... | collective-permute-start | bytes 811016 | tf_op jit(solution)/shard_map/ppermute | solution.py:66
  59.1 1.9 %collective-permute-start.17 = (f32[64]{0:T(128)S(1)}, f32[64]{0:T(128)S(1)}, u32[]{:S(2)}, u32[]{:S(2)}) collective-permute-start(f32[64]{0:T(128)S(1)} %get-tuple-element.53), channel_id=1, source_target_pairs={{0,8},{8,0},{16,24},{24,16},{1,9},{9,1},{17,25},{25,17},{2,10},{10... | collective-permute-start | bytes 776 | tf_op jit(solution)/shard_map/ppermute | solution.py:115
  59.1 3.6 %collective-permute-start.18 = (f32[64]{0:T(128)S(1)}, f32[64]{0:T(128)S(1)}, u32[]{:S(2)}, u32[]{:S(2)}) collective-permute-start(f32[64]{0:T(128)S(1)} %get-tuple-element.55), channel_id=1, source_target_pairs={{0,16},{8,24},{16,0},{24,8},{1,17},{9,25},{17,1},{25,9},{2,18},{10... | collective-permute-start | bytes 776 | tf_op jit(solution)/shard_map/ppermute | solution.py:115
  59.7 3.1 %collective-permute-start.19 = (f32[64]{0:T(128)S(1)}, f32[64]{0:T(128)S(1)}, u32[]{:S(2)}, u32[]{:S(2)}) collective-permute-start(f32[64]{0:T(128)S(1)} %get-tuple-element.54), channel_id=1, source_target_pairs={{0,24},{8,16},{16,8},{24,0},{1,25},{9,17},{17,9},{25,1},{2,26},{10... | collective-permute-start | bytes 776 | tf_op jit(solution)/shard_map/ppermute | solution.py:115

commit v9 on v7

--- a/solution.py
+++ b/solution.py
@@ -59,9 +59,10 @@
             visiting = visiting[:half] if which == 0 else visiting[half:]
         return lax.ppermute(visiting, "blk", forward if which == 0 else backward)
 
-    chains = [[payload, None, [payload]], [payload, None, []]]
+    chains = [[payload, None, []], [payload, None, [payload]]]
+    directions = [1, 0]
     if steps >= 1:
-        for which, chain in enumerate(chains):
+        for which, chain in zip(directions, chains):
             chain[0] = send(which, chain[0], 1)
             chain[2].append(chain[0])
 
@@ -86,7 +87,7 @@
         return best
 
     for step in range(2, steps + 1):
-        for which, chain in enumerate(chains):
+        for which, chain in zip(directions, chains):
             visiting, best, pending = chain
             visiting = send(which, visiting, step)
             best = fold(best, pending)

time: 63 us -> 63.7 us (1.011)
  waiting for transfers between devices: 35.8 us -> 36.6 us
    ppermute x8, waiting for transfers between devices: 22.8 us -> 23.6 us  [send(): return lax.ppermute(visiting, 'blk', forward if which == 0 else backward)]
where the time goes in v9:
time: 63.7 us; the launch traced here: 63.5 us
  waiting for transfers between devices  36.6 us (57%)
  starting transfers between devices  14.2 us (22%)
  matrix products  6.97 us (11%)
  other arithmetic  5.33 us (8%)
    ppermute x8, waiting for transfers between devices, send(): return lax.ppermute(visiting, 'blk', forward if which == 0 else backward)  23.6 us
    ppermute x1, waiting for transfers between devices, per_device(): across = lax.ppermute(payload, 'grp', partner_pairs(group_count, 2))  10.1 us
    ppermute x8, starting transfers between devices, send(): return lax.ppermute(visiting, 'blk', forward if which == 0 else backward)  8.31 us
    dot_general x9, matrix products, block_best(): jnp.einsum('id,jd->ij', left_rows, payload[:, :D], preferred_element_type...  6.97 us
    ppermute x1, starting transfers between devices, per_device(): across = lax.ppermute(payload, 'grp', partner_pairs(group_count, 2))  3.06 us
    ppermute x3, waiting for transfers between devices, per_device(): result = jnp.maximum(result, lax.ppermute(best[k], 'grp', pairs))  2.95 us
    ppermute x3, starting transfers between devices, per_device(): result = jnp.maximum(result, lax.ppermute(best[k], 'grp', pairs))  2.86 us
    add x9, other arithmetic, tag_labels(): return high * 128.0 + low  1.57 us
  transfers between devices with their start and end apart: 14, of which 9 were waited for; matrix products, arithmetic and copies ran while one was open for 13% of the time, Pallas kernels for 0%

profile of v9, /device:TPU:0, one launch (start us, length us, event | category | flops | bytes accessed | tf_op | source)
XLA Modules:
  0.0 63.5 jit_solution(14614913042232935708)
XLA Ops:
  0.0 1.1 %convert_element_type.222 = f32[64,4096]{1,0:T(8,128)S(1)} convert(bf16[64,4096]{1,0:T(8,128)(2,1)} %param.3) | non-fusion elementwise | flops 262144 | bytes 1572864 | tf_op jit(solution)/shard_map/convert_element_type | solution.py:41
  1.1 1.2 %multiply_reduce_fusion = f32[64]{0:T(128)S(1)} fusion(bf16[64,4096]{1,0:T(8,128)(2,1)} %param.3), kind=kLoop, calls=%fused_computation.22 | loop fusion | flops 786368 | bytes 524544 | tf_op jit(solution)/shard_map/reduce_sum | solution.py:42
  2.4 0.3 select_convert_fusion
  2.7 3.1 %collective-permute-start.3 = (bf16[64,4224]{1,0:T(8,128)(2,1)S(1)}, bf16[64,4224]{1,0:T(8,128)(2,1)S(1)}, u32[]{:S(2)}, u32[]{:S(2)}) collective-permute-start(bf16[64,4224]{1,0:T(8,128)(2,1)S(1)} %select_convert_fusion), channel_id=1, source_target_pairs={{0,16},{8,24},{16,0},{24,8},{1,17},{9,25},{17,1},{25,9},{2,18},{10... | collective-permute-start | bytes 1622024 | tf_op jit(solution)/shard_map/ppermute | solution.py:70
  5.8 1.5 %collective-permute-start = (bf16[64,4224]{1,0:T(8,128)(2,1)S(1)}, bf16[64,4224]{1,0:T(8,128)(2,1)S(1)}, u32[]{:S(2)}, u32[]{:S(2)}) collective-permute-start(bf16[64,4224]{1,0:T(8,128)(2,1)S(1)} %select_convert_fusion), channel_id=1, source_target_pairs={{2,0},{4,2},{6,4},{7,6},{5,7},{3,5},{1,3},{0,1},{10,8},{12,10},{14... | collective-permute-start | bytes 1622024 | tf_op jit(solution)/shard_map/ppermute | solution.py:60
  7.3 0.5 collective-permute-start.7
  7.8 0.0 collective-permute-start.2
  7.8 0.2 add_reduce_fusion.3
  8.0 10.1 %collective-permute-done.3 = bf16[64,4224]{1,0:T(8,128)(2,1)S(1)} collective-permute-done((bf16[64,4224]{1,0:T(8,128)(2,1)S(1)}, bf16[64,4224]{1,0:T(8,128)(2,1)S(1)}, u32[]{:S(2)}, u32[]{:S(2)}) %collective-permute-start.3) | collective-permute-done | bytes 540704 | tf_op jit(solution)/shard_map/ppermute | solution.py:70
  18.1 1.5 %collective-permute-done = bf16[64,4224]{1,0:T(8,128)(2,1)S(1)} collective-permute-done((bf16[64,4224]{1,0:T(8,128)(2,1)S(1)}, bf16[64,4224]{1,0:T(8,128)(2,1)S(1)}, u32[]{:S(2)}, u32[]{:S(2)}) %collective-permute-start) | collective-permute-done | bytes 540704 | tf_op jit(solution)/shard_map/ppermute | solution.py:60
  19.5 1.5 %collective-permute-start.1 = (bf16[64,4224]{1,0:T(8,128)(2,1)S(1)}, bf16[64,4224]{1,0:T(8,128)(2,1)S(1)}, u32[]{:S(2)}, u32[]{:S(2)}) collective-permute-start(bf16[64,4224]{1,0:T(8,128)(2,1)S(1)} %collective-permute-done), channel_id=1, source_target_pairs={{2,0},{4,2},{6,4},{7,6},{5,7},{3,5},{1,3},{0,1},{10,8},{12,10},{14... | collective-permute-start | bytes 1622024 | tf_op jit(solution)/shard_map/ppermute | solution.py:60
  21.0 0.2 add_reduce_fusion.6
  21.2 0.6 collective-permute-start.8
  21.8 0.2 add_reduce_fusion.2
  22.0 0.2 pad_maximum_fusion
  22.3 0.1 pad_maximum_fusion.4
  22.4 0.2 floor_reduce_fusion
  22.5 0.8 %fusion = f32[256]{0:T(256)S(1)} fusion(bf16[256,4096]{1,0:T(8,128)(2,1)S(1)} %pad_maximum_fusion, bf16[64,4224]{1,0:T(8,128)(2,1)S(1)} %collective-permute-done, f32[256]{0:T(256)S(1)} %get-tuple-element.30, f32[256]{0:T(256)S(1)} %get-tuple-element.29, f32[64]{0:T(128)S(1)} %add_reduce_fusion.6, f32[64]{0:T(128)S(1)} %multiply_floor_fusion.8), kind=kOutput, calls=%fused_computation.10 | convolution fusion | flops 134299392 | bytes 2625536 | tf_op jit(solution)/shard_map/id,jd->ij/dot_general | solution.py:26
  23.3 9.5 %collective-permute-done.1 = bf16[64,4224]{1,0:T(8,128)(2,1)S(1)} collective-permute-done((bf16[64,4224]{1,0:T(8,128)(2,1)S(1)}, bf16[64,4224]{1,0:T(8,128)(2,1)S(1)}, u32[]{:S(2)}, u32[]{:S(2)}) %collective-permute-start.1) | collective-permute-done | bytes 540704 | tf_op jit(solution)/shard_map/ppermute | solution.py:60
  32.8 1.7 %collective-permute-start.5 = (bf16[64,4224]{1,0:T(8,128)(2,1)S(1)}, bf16[64,4224]{1,0:T(8,128)(2,1)S(1)}, u32[]{:S(2)}, u32[]{:S(2)}) collective-permute-start(bf16[64,4224]{1,0:T(8,128)(2,1)S(1)} %collective-permute-done.1), channel_id=1, source_target_pairs={{2,0},{4,2},{6,4},{7,6},{5,7},{3,5},{1,3},{0,1},{10,8},{12,10},{14... | collective-permute-start | bytes 1622024 | tf_op jit(solution)/shard_map/ppermute | solution.py:60
  34.5 0.8 %fusion.3 = f32[256]{0:T(256)S(1)} fusion(bf16[256,4096]{1,0:T(8,128)(2,1)S(1)} %pad_maximum_fusion, bf16[64,4224]{1,0:T(8,128)(2,1)S(1)} %select_convert_fusion, f32[256]{0:T(256)S(1)} %get-tuple-element.30, f32[256]{0:T(256)S(1)} %get-tuple-element.29, f32[64]{0:T(128)S(1)} %add_reduce_fusion.3, f32[64]{0:T(128)S(1)} %multiply_floor_fusion.4), kind=kOutput, calls=%fused_computation.13 | convolution fusion | flops 134299392 | bytes 2625536 | tf_op jit(solution)/shard_map/id,jd->ij/dot_general | solution.py:26
  35.3 0.8 %fusion.4 = f32[256]{0:T(256)S(1)} fusion(bf16[256,4096]{1,0:T(8,128)(2,1)S(1)} %pad_maximum_fusion, bf16[64,4224]{1,0:T(8,128)(2,1)S(1)} %collective-permute-done.7, f32[256]{0:T(256)S(1)} %get-tuple-element.30, f32[256]{0:T(256)S(1)} %get-tuple-element.29, f32[64]{0:T(128)S(1)} %add_reduce_fusion.2, f32[64]{0:T(128)S(1)} %multiply_floor_fusion.3), kind=kOutput, calls=%fused_computation.14 | convolution fusion | flops 134299392 | bytes 2625536 | tf_op jit(solution)/shard_map/id,jd->ij/dot_general | solution.py:26
  36.1 0.2 add_reduce_fusion.5
  36.3 0.8 %fusion.1 = f32[256]{0:T(256)S(1)} fusion(bf16[256,4096]{1,0:T(8,128)(2,1)S(1)} %pad_maximum_fusion, bf16[64,4224]{1,0:T(8,128)(2,1)S(1)} %collective-permute-done.1, f32[256]{0:T(256)S(1)} %get-tuple-element.30, f32[256]{0:T(256)S(1)} %get-tuple-element.29, f32[64]{0:T(128)S(1)} %add_reduce_fusion.5, f32[64]{0:T(128)S(1)} %multiply_floor_fusion.7), kind=kOutput, calls=%fused_computation.11 | convolution fusion | flops 134299392 | bytes 2625536 | tf_op jit(solution)/shard_map/id,jd->ij/dot_general | solution.py:26
  37.0 0.4 collective-permute-start.9
  37.5 0.2 add_reduce_fusion.1
  37.7 0.8 %fusion.5 = f32[256]{0:T(256)S(1)} fusion(bf16[256,4096]{1,0:T(8,128)(2,1)S(1)} %pad_maximum_fusion, bf16[64,4224]{1,0:T(8,128)(2,1)S(1)} %collective-permute-done.8, f32[256]{0:T(256)S(1)} %get-tuple-element.30, f32[256]{0:T(256)S(1)} %get-tuple-element.29, f32[64]{0:T(128)S(1)} %add_reduce_fusion.1, f32[64]{0:T(128)S(1)} %multiply_floor_fusion.2), kind=kOutput, calls=%fused_computation.15 | convolution fusion | flops 134299392 | bytes 2625536 | tf_op jit(solution)/shard_map/id,jd->ij/dot_general | solution.py:26
  38.5 7.0 %collective-permute-done.5 = bf16[64,4224]{1,0:T(8,128)(2,1)S(1)} collective-permute-done((bf16[64,4224]{1,0:T(8,128)(2,1)S(1)}, bf16[64,4224]{1,0:T(8,128)(2,1)S(1)}, u32[]{:S(2)}, u32[]{:S(2)}) %collective-permute-start.5) | collective-permute-done | bytes 540704 | tf_op jit(solution)/shard_map/ppermute | solution.py:60
  45.4 1.7 %collective-permute-start.6 = (bf16[32,4224]{1,0:T(8,128)(2,1)S(1)}, bf16[32,4224]{1,0:T(8,128)(2,1)S(1)}, u32[]{:S(2)}, u32[]{:S(2)}) collective-permute-start(bf16[32,4224]{1,0:T(8,128)(2,1)S(1)} %slice.121), channel_id=1, source_target_pairs={{2,0},{4,2},{6,4},{7,6},{5,7},{3,5},{1,3},{0,1},{10,8},{12,10},{14... | collective-permute-start | bytes 811016 | tf_op jit(solution)/shard_map/ppermute | solution.py:60
  47.2 0.2 add_reduce_fusion.4
  47.3 0.8 %fusion.2 = f32[256]{0:T(256)S(1)} fusion(bf16[256,4096]{1,0:T(8,128)(2,1)S(1)} %pad_maximum_fusion, bf16[64,4224]{1,0:T(8,128)(2,1)S(1)} %collective-permute-done.5, f32[256]{0:T(256)S(1)} %get-tuple-element.30, f32[256]{0:T(256)S(1)} %get-tuple-element.29, f32[64]{0:T(128)S(1)} %add_reduce_fusion.4, f32[64]{0:T(128)S(1)} %multiply_floor_fusion.6), kind=kOutput, calls=%fused_computation.12 | convolution fusion | flops 134299392 | bytes 2625536 | tf_op jit(solution)/shard_map/id,jd->ij/dot_general | solution.py:26
  48.1 1.3 %collective-permute-done.9 = bf16[64,4224]{1,0:T(8,128)(2,1)S(1)} collective-permute-done((bf16[64,4224]{1,0:T(8,128)(2,1)S(1)}, bf16[64,4224]{1,0:T(8,128)(2,1)S(1)}, u32[]{:S(2)}, u32[]{:S(2)}) %collective-permute-start.9) | collective-permute-done | bytes 540704 | tf_op jit(solution)/shard_map/ppermute | solution.py:60
  49.4 0.2 add_reduce_fusion
  49.6 0.4 collective-permute-start.10
  50.1 0.8 %fusion.6 = f32[256]{0:T(256)S(1)} fusion(bf16[256,4096]{1,0:T(8,128)(2,1)S(1)} %pad_maximum_fusion, bf16[64,4224]{1,0:T(8,128)(2,1)S(1)} %collective-permute-done.9, f32[256]{0:T(256)S(1)} %get-tuple-element.30, f32[256]{0:T(256)S(1)} %get-tuple-element.29, f32[64]{0:T(128)S(1)} %add_reduce_fusion, f32[64]{0:T(128)S(1)} %multiply_floor_fusion.1), kind=kOutput, calls=%fused_computation.16 | convolution fusion | flops 134299392 | bytes 2625536 | tf_op jit(solution)/shard_map/id,jd->ij/dot_general | solution.py:26
  50.8 1.1 %collective-permute-done.6 = bf16[32,4224]{1,0:T(8,128)(2,1)S(1)} collective-permute-done((bf16[32,4224]{1,0:T(8,128)(2,1)S(1)}, bf16[32,4224]{1,0:T(8,128)(2,1)S(1)}, u32[]{:S(2)}, u32[]{:S(2)}) %collective-permute-start.6) | collective-permute-done | bytes 270368 | tf_op jit(solution)/shard_map/ppermute | solution.py:60
  52.0 0.2 add_reduce_fusion.8
  52.1 0.8 %fusion.7 = f32[256]{0:T(256)S(1)} fusion(bf16[256,4096]{1,0:T(8,128)(2,1)S(1)} %pad_maximum_fusion, bf16[32,4224]{1,0:T(8,128)(2,1)S(1)} %collective-permute-done.6, f32[256]{0:T(256)S(1)} %get-tuple-element.30, f32[256]{0:T(256)S(1)} %get-tuple-element.29, f32[32]{0:T(128)S(1)} %add_reduce_fusion.8, f32[32]{0:T(128)S(1)} %multiply_floor_fusion.5), kind=kOutput, calls=%fused_computation.19 | convolution fusion | flops 67149568 | bytes 2363392 | tf_op jit(solution)/shard_map/id,jd->ij/dot_general | solution.py:26
  52.9 3.2 %collective-permute-done.10 = bf16[32,4224]{1,0:T(8,128)(2,1)S(1)} collective-permute-done((bf16[32,4224]{1,0:T(8,128)(2,1)S(1)}, bf16[32,4224]{1,0:T(8,128)(2,1)S(1)}, u32[]{:S(2)}, u32[]{:S(2)}) %collective-permute-start.10) | collective-permute-done | bytes 270368 | tf_op jit(solution)/shard_map/ppermute | solution.py:60
  56.1 0.2 add_reduce_fusion.7
  56.3 0.8 %fusion.8 = f32[256]{0:T(256)S(1)} fusion(bf16[256,4096]{1,0:T(8,128)(2,1)S(1)} %pad_maximum_fusion, bf16[32,4224]{1,0:T(8,128)(2,1)S(1)} %collective-permute-done.10, f32[256]{0:T(256)S(1)} %get-tuple-element.30, f32[256]{0:T(256)S(1)} %get-tuple-element.29, f32[32]{0:T(128)S(1)} %add_reduce_fusion.7, f32[32]{0:T(128)S(1)} %multiply_floor_fusion), kind=kOutput, calls=%fused_computation.20 | convolution fusion | flops 67149568 | bytes 2363392 | tf_op jit(solution)/shard_map/id,jd->ij/dot_general | solution.py:26
  57.1 0.1 fusion.20
  57.2 0.0 collective-permute-start.11
  57.2 2.8 %collective-permute-start.12 = (f32[64]{0:T(128)S(1)}, f32[64]{0:T(128)S(1)}, u32[]{:S(2)}, u32[]{:S(2)}) collective-permute-start(f32[64]{0:T(128)S(1)} %get-tuple-element.35), channel_id=1, source_target_pairs={{0,16},{8,24},{16,0},{24,8},{1,17},{9,25},{17,1},{25,9},{2,18},{10... | collective-permute-start | bytes 776 | tf_op jit(solution)/shard_map/ppermute | solution.py:105
  60.0 0.0 collective-permute-start.13
  60.1 1.5 %collective-permute-done.12 = f32[64]{0:T(128)S(1)} collective-permute-done((f32[64]{0:T(128)S(1)}, f32[64]{0:T(128)S(1)}, u32[]{:S(2)}, u32[]{:S(2)}) %collective-permute-start.12) | collective-permute-done | bytes 288 | tf_op jit(solution)/shard_map/ppermute | solution.py:105
  61.6 1.4 %collective-permute-done.13 = f32[64]{0:T(128)S(1)} collective-permute-done((f32[64]{0:T(128)S(1)}, f32[64]{0:T(128)S(1)}, u32[]{:S(2)}, u32[]{:S(2)}) %collective-permute-start.13) | collective-permute-done | bytes 288 | tf_op jit(solution)/shard_map/ppermute | solution.py:105
  63.0 0.5 maximum_maximum_fusion.1
  (31 shorter events, 0.2 us)
Async XLA Ops:
  0.0 2.4 %copy-start = (s32[64]{0:T(128)S(1)}, s32[64]{0:T(128)}, u32[]{:S(2)}) copy-start(s32[64]{0:T(128)} %param.4) | copy-start | bytes 772
  0.0 2.4 %copy-start.1 = (s32[64]{0:T(128)S(1)}, s32[64]{0:T(128)}, u32[]{:S(2)}) copy-start(s32[64]{0:T(128)} %param.5) | copy-start | bytes 772
  2.7 15.3 %collective-permute-start.3 = (bf16[64,4224]{1,0:T(8,128)(2,1)S(1)}, bf16[64,4224]{1,0:T(8,128)(2,1)S(1)}, u32[]{:S(2)}, u32[]{:S(2)}) collective-permute-start(bf16[64,4224]{1,0:T(8,128)(2,1)S(1)} %select_convert_fusion), channel_id=1, source_target_pairs={{0,16},{8,24},{16,0},{24,8},{1,17},{9,25},{17,1},{25,9},{2,18},{10... | collective-permute-start | bytes 1622024 | tf_op jit(solution)/shard_map/ppermute | solution.py:70
  5.8 13.7 %collective-permute-start = (bf16[64,4224]{1,0:T(8,128)(2,1)S(1)}, bf16[64,4224]{1,0:T(8,128)(2,1)S(1)}, u32[]{:S(2)}, u32[]{:S(2)}) collective-permute-start(bf16[64,4224]{1,0:T(8,128)(2,1)S(1)} %select_convert_fusion), channel_id=1, source_target_pairs={{2,0},{4,2},{6,4},{7,6},{5,7},{3,5},{1,3},{0,1},{10,8},{12,10},{14... | collective-permute-start | bytes 1622024 | tf_op jit(solution)/shard_map/ppermute | solution.py:60
  7.3 13.9 %collective-permute-start.7 = (bf16[64,4224]{1,0:T(8,128)(2,1)S(1)}, bf16[64,4224]{1,0:T(8,128)(2,1)S(1)}, u32[]{:S(2)}, u32[]{:S(2)}) collective-permute-start(bf16[64,4224]{1,0:T(8,128)(2,1)S(1)} %select_convert_fusion), channel_id=1, source_target_pairs={{0,2},{2,4},{4,6},{6,7},{7,5},{5,3},{3,1},{1,0},{8,10},{10,12},{12... | collective-permute-start | bytes 1622024 | tf_op jit(solution)/shard_map/ppermute | solution.py:60
  7.8 14.2 %collective-permute-start.2 = (bf16[64,4224]{1,0:T(8,128)(2,1)S(1)}, bf16[64,4224]{1,0:T(8,128)(2,1)S(1)}, u32[]{:S(2)}, u32[]{:S(2)}) collective-permute-start(bf16[64,4224]{1,0:T(8,128)(2,1)S(1)} %select_convert_fusion), channel_id=1, source_target_pairs={{0,8},{8,0},{16,24},{24,16},{1,9},{9,1},{17,25},{25,17},{2,10},{10... | collective-permute-start | bytes 1622024 | tf_op jit(solution)/shard_map/ppermute | solution.py:71
  18.1 3.9 %collective-permute-start.4 = (bf16[64,4224]{1,0:T(8,128)(2,1)S(1)}, bf16[64,4224]{1,0:T(8,128)(2,1)S(1)}, u32[]{:S(2)}, u32[]{:S(2)}) collective-permute-start(bf16[64,4224]{1,0:T(8,128)(2,1)S(1)} %collective-permute-done.3), channel_id=1, source_target_pairs={{0,8},{8,0},{16,24},{24,16},{1,9},{9,1},{17,25},{25,17},{2,10},{10... | collective-permute-start | bytes 1622024 | tf_op jit(solution)/shard_map/ppermute | solution.py:72
  19.5 13.3 %collective-permute-start.1 = (bf16[64,4224]{1,0:T(8,128)(2,1)S(1)}, bf16[64,4224]{1,0:T(8,128)(2,1)S(1)}, u32[]{:S(2)}, u32[]{:S(2)}) collective-permute-start(bf16[64,4224]{1,0:T(8,128)(2,1)S(1)} %collective-permute-done), channel_id=1, source_target_pairs={{2,0},{4,2},{6,4},{7,6},{5,7},{3,5},{1,3},{0,1},{10,8},{12,10},{14... | collective-permute-start | bytes 1622024 | tf_op jit(solution)/shard_map/ppermute | solution.py:60
  21.2 15.8 %collective-permute-start.8 = (bf16[64,4224]{1,0:T(8,128)(2,1)S(1)}, bf16[64,4224]{1,0:T(8,128)(2,1)S(1)}, u32[]{:S(2)}, u32[]{:S(2)}) collective-permute-start(bf16[64,4224]{1,0:T(8,128)(2,1)S(1)} %collective-permute-done.7), channel_id=1, source_target_pairs={{0,2},{2,4},{4,6},{6,7},{7,5},{5,3},{3,1},{1,0},{8,10},{10,12},{12... | collective-permute-start | bytes 1622024 | tf_op jit(solution)/shard_map/ppermute | solution.py:60
  32.8 12.6 %collective-permute-start.5 = (bf16[64,4224]{1,0:T(8,128)(2,1)S(1)}, bf16[64,4224]{1,0:T(8,128)(2,1)S(1)}, u32[]{:S(2)}, u32[]{:S(2)}) collective-permute-start(bf16[64,4224]{1,0:T(8,128)(2,1)S(1)} %collective-permute-done.1), channel_id=1, source_target_pairs={{2,0},{4,2},{6,4},{7,6},{5,7},{3,5},{1,3},{0,1},{10,8},{12,10},{14... | collective-permute-start | bytes 1622024 | tf_op jit(solution)/shard_map/ppermute | solution.py:60
  37.0 12.4 %collective-permute-start.9 = (bf16[64,4224]{1,0:T(8,128)(2,1)S(1)}, bf16[64,4224]{1,0:T(8,128)(2,1)S(1)}, u32[]{:S(2)}, u32[]{:S(2)}) collective-permute-start(bf16[64,4224]{1,0:T(8,128)(2,1)S(1)} %collective-permute-done.8), channel_id=1, source_target_pairs={{0,2},{2,4},{4,6},{6,7},{7,5},{5,3},{3,1},{1,0},{8,10},{10,12},{12... | collective-permute-start | bytes 1622024 | tf_op jit(solution)/shard_map/ppermute | solution.py:60
  45.4 6.5 %collective-permute-start.6 = (bf16[32,4224]{1,0:T(8,128)(2,1)S(1)}, bf16[32,4224]{1,0:T(8,128)(2,1)S(1)}, u32[]{:S(2)}, u32[]{:S(2)}) collective-permute-start(bf16[32,4224]{1,0:T(8,128)(2,1)S(1)} %slice.121), channel_id=1, source_target_pairs={{2,0},{4,2},{6,4},{7,6},{5,7},{3,5},{1,3},{0,1},{10,8},{12,10},{14... | collective-permute-start | bytes 811016 | tf_op jit(solution)/shard_map/ppermute | solution.py:60
  49.6 6.5 %collective-permute-start.10 = (bf16[32,4224]{1,0:T(8,128)(2,1)S(1)}, bf16[32,4224]{1,0:T(8,128)(2,1)S(1)}, u32[]{:S(2)}, u32[]{:S(2)}) collective-permute-start(bf16[32,4224]{1,0:T(8,128)(2,1)S(1)} %slice.137), channel_id=1, source_target_pairs={{0,2},{2,4},{4,6},{6,7},{7,5},{5,3},{3,1},{1,0},{8,10},{10,12},{12... | collective-permute-start | bytes 811016 | tf_op jit(solution)/shard_map/ppermute | solution.py:60
  57.2 2.9 %collective-permute-start.11 = (f32[64]{0:T(128)S(1)}, f32[64]{0:T(128)S(1)}, u32[]{:S(2)}, u32[]{:S(2)}) collective-permute-start(f32[64]{0:T(128)S(1)} %get-tuple-element.33), channel_id=1, source_target_pairs={{0,8},{8,0},{16,24},{24,16},{1,9},{9,1},{17,25},{25,17},{2,10},{10... | collective-permute-start | bytes 776 | tf_op jit(solution)/shard_map/ppermute | solution.py:105
  57.2 4.4 %collective-permute-start.12 = (f32[64]{0:T(128)S(1)}, f32[64]{0:T(128)S(1)}, u32[]{:S(2)}, u32[]{:S(2)}) collective-permute-start(f32[64]{0:T(128)S(1)} %get-tuple-element.35), channel_id=1, source_target_pairs={{0,16},{8,24},{16,0},{24,8},{1,17},{9,25},{17,1},{25,9},{2,18},{10... | collective-permute-start | bytes 776 | tf_op jit(solution)/shard_map/ppermute | solution.py:105
  60.0 3.0 %collective-permute-start.13 = (f32[64]{0:T(128)S(1)}, f32[64]{0:T(128)S(1)}, u32[]{:S(2)}, u32[]{:S(2)}) collective-permute-start(f32[64]{0:T(128)S(1)} %get-tuple-element.34), channel_id=1, source_target_pairs={{0,24},{8,16},{16,8},{24,0},{1,25},{9,17},{17,9},{25,1},{2,26},{10... | collective-permute-start | bytes 776 | tf_op jit(solution)/shard_map/ppermute | solution.py:105

commit v10 on v7

--- a/solution.py
+++ b/solution.py
@@ -44,7 +44,7 @@
     high = (cluster_ids * 64 + row_index // 128).astype(jnp.float32)[:, None]
     low = (row_index % 128).astype(jnp.float32)[:, None]
     column = jnp.arange(D + TAG_WIDTH)[None, :]
-    padded = jnp.pad(widened, ((0, 0), (0, TAG_WIDTH)))
+    padded = jnp.pad(embeddings, ((0, 0), (0, TAG_WIDTH))).astype(jnp.float32)
     tags = jnp.where(column == D, high, jnp.where(column == D + 1, low, 0.0))
     payload = jnp.where(column < D, padded * scale / math.sqrt(D), tags).astype(jnp.bfloat16)
 
@@ -99,6 +99,10 @@
             best = chain_best if best is None else jnp.maximum(best, chain_best)
 
     best = best.reshape(group_count, rows_here)
+    if group_count == 4:
+        far = lax.ppermute(best[2:], "grp", partner_pairs(group_count, 2))
+        near = jnp.maximum(best[:2], far)
+        return jnp.maximum(near[0], lax.ppermute(near[1], "grp", partner_pairs(group_count, 1)))
     result = best[0]
     for k, pairs in enumerate(segment_pairs, start=1):
         result = jnp.maximum(result, lax.ppermute(best[k], "grp", pairs))

time: 63 us -> 63.3 us (level)
  other arithmetic: 5.33 us -> 5.97 us
    convert_element_type x1 -> x0, other arithmetic: 1.12 us -> none  [per_device(): widened = embeddings.astype(jnp.float32)]
    convert_element_type x1, other arithmetic: 0.29 us -> 1.36 us  [per_device(): jnp.where(column < D, padded * scale / math.sqrt(D), tags)]
    convert_element_type x1, other arithmetic: 0.01 us -> 0.69 us  [per_device(): high = (cluster_ids * 64 + row_index // 128).astype(jnp.float32)[:, None]]
    ppermute x3 -> x2, waiting for transfers between devices: 2.95 us -> 2.63 us  [the longest x1 1.47 us: per_device(): far = lax.ppermute(best[2:], 'grp', partner_pairs(group_count, 2))]
    ppermute x3 -> x2, starting transfers between devices: 2.87 us -> 2.75 us  [the longest x1 2.75 us: per_device(): far = lax.ppermute(best[2:], 'grp', partner_pairs(group_count, 2))]
  transfers between devices with their start and end apart: 14 -> 13, of which waited for: 9 -> 9; matrix products, arithmetic and copies ran while one was open for 13% -> 13% of each run, Pallas kernels for 0% -> 0%
where the time goes in v10:
time: 63.3 us; the launch traced here: 63.1 us
  waiting for transfers between devices  35.5 us (56%)
  starting transfers between devices  14.3 us (23%)
  matrix products  6.96 us (11%)
  other arithmetic  5.97 us (9%)
    ppermute x8, waiting for transfers between devices, send(): return lax.ppermute(visiting, 'blk', forward if which == 0 else backward)  22.8 us
    ppermute x1, waiting for transfers between devices, per_device(): across = lax.ppermute(payload, 'grp', partner_pairs(group_count, 2))  10.1 us
    ppermute x8, starting transfers between devices, send(): return lax.ppermute(visiting, 'blk', forward if which == 0 else backward)  8.45 us
    dot_general x9, matrix products, block_best(): jnp.einsum('id,jd->ij', left_rows, payload[:, :D], preferred_element_type...  6.96 us
    ppermute x1, starting transfers between devices, per_device(): across = lax.ppermute(payload, 'grp', partner_pairs(group_count, 2))  3.07 us
    ppermute x1, starting transfers between devices, per_device(): far = lax.ppermute(best[2:], 'grp', partner_pairs(group_count, 2))  2.75 us
    add x9, other arithmetic, tag_labels(): return high * 128.0 + low  1.57 us
    ppermute x1, waiting for transfers between devices, per_device(): far = lax.ppermute(best[2:], 'grp', partner_pairs(group_count, 2))  1.47 us
  transfers between devices with their start and end apart: 13, of which 9 were waited for; matrix products, arithmetic and copies ran while one was open for 13% of the time, Pallas kernels for 0%

profile of v10, /device:TPU:0, one launch (start us, length us, event | category | flops | bytes accessed | tf_op | source)
XLA Modules:
  0.0 63.1 jit_solution(8297567416703871484)
XLA Ops:
  0.0 1.2 %multiply_reduce_fusion = f32[64]{0:T(128)S(1)} fusion(bf16[64,4096]{1,0:T(8,128)(2,1)} %param.3), kind=kLoop, calls=%fused_computation.22 | loop fusion | flops 786368 | bytes 524544 | tf_op jit(solution)/shard_map/reduce_sum | solution.py:42
  1.3 0.7 %add_convert_fusion = (bf16[64]{0:T(256)(128)(2,1)S(1)}, bf16[64]{0:T(256)(128)(2,1)S(1)}) fusion(s32[64]{0:T(128)} %param.4, s32[64]{0:T(128)} %param.5), kind=kLoop, calls=%fused_computation.67 | loop fusion | flops 1472 | bytes 768 | tf_op jit(solution)/shard_map/convert_element_type | solution.py:44
  2.0 1.4 %select_convert_fusion = bf16[64,4224]{1,0:T(8,128)(2,1)S(1)} fusion(bf16[64]{0:T(256)(128)(2,1)S(1)} %get-tuple-element.36, bf16[64]{0:T(256)(128)(2,1)S(1)} %get-tuple-element.35, f32[64]{0:T(128)S(1)} %add_rsqrt_fusion, bf16[64,4096]{1,0:T(8,128)(2,1)} %param.3, pred[4224]{0:T(1024)(128)(4,1)S(1)} %get-tuple-element.37, ...), kind=kLoop, calls=%fused_computation.21 | loop fusion | flops 1622016 | bytes 1078144 | tf_op jit(solution)/shard_map/convert_element_type | solution.py:49
  3.3 3.1 %collective-permute-start.3 = (bf16[64,4224]{1,0:T(8,128)(2,1)S(1)}, bf16[64,4224]{1,0:T(8,128)(2,1)S(1)}, u32[]{:S(2)}, u32[]{:S(2)}) collective-permute-start(bf16[64,4224]{1,0:T(8,128)(2,1)S(1)} %select_convert_fusion), channel_id=1, source_target_pairs={{0,16},{8,24},{16,0},{24,8},{1,17},{9,25},{17,1},{25,9},{2,18},{10... | collective-permute-start | bytes 1622024 | tf_op jit(solution)/shard_map/ppermute | solution.py:69
  6.4 1.6 %collective-permute-start = (bf16[64,4224]{1,0:T(8,128)(2,1)S(1)}, bf16[64,4224]{1,0:T(8,128)(2,1)S(1)}, u32[]{:S(2)}, u32[]{:S(2)}) collective-permute-start(bf16[64,4224]{1,0:T(8,128)(2,1)S(1)} %select_convert_fusion), channel_id=1, source_target_pairs={{0,2},{2,4},{4,6},{6,7},{7,5},{5,3},{3,1},{1,0},{8,10},{10,12},{12... | collective-permute-start | bytes 1622024 | tf_op jit(solution)/shard_map/ppermute | solution.py:60
  8.0 0.4 collective-permute-start.7
  8.4 0.0 collective-permute-start.2
  8.4 0.2 add_reduce_fusion.6
  8.6 10.1 %collective-permute-done.3 = bf16[64,4224]{1,0:T(8,128)(2,1)S(1)} collective-permute-done((bf16[64,4224]{1,0:T(8,128)(2,1)S(1)}, bf16[64,4224]{1,0:T(8,128)(2,1)S(1)}, u32[]{:S(2)}, u32[]{:S(2)}) %collective-permute-start.3) | collective-permute-done | bytes 540704 | tf_op jit(solution)/shard_map/ppermute | solution.py:69
  18.7 1.5 %collective-permute-done = bf16[64,4224]{1,0:T(8,128)(2,1)S(1)} collective-permute-done((bf16[64,4224]{1,0:T(8,128)(2,1)S(1)}, bf16[64,4224]{1,0:T(8,128)(2,1)S(1)}, u32[]{:S(2)}, u32[]{:S(2)}) %collective-permute-start) | collective-permute-done | bytes 540704 | tf_op jit(solution)/shard_map/ppermute | solution.py:60
  20.1 1.6 %collective-permute-start.1 = (bf16[64,4224]{1,0:T(8,128)(2,1)S(1)}, bf16[64,4224]{1,0:T(8,128)(2,1)S(1)}, u32[]{:S(2)}, u32[]{:S(2)}) collective-permute-start(bf16[64,4224]{1,0:T(8,128)(2,1)S(1)} %collective-permute-done), channel_id=1, source_target_pairs={{0,2},{2,4},{4,6},{6,7},{7,5},{5,3},{3,1},{1,0},{8,10},{10,12},{12... | collective-permute-start | bytes 1622024 | tf_op jit(solution)/shard_map/ppermute | solution.py:60
  21.7 0.2 add_reduce_fusion.5
  21.9 0.5 collective-permute-start.8
  22.4 0.2 add_reduce_fusion.2
  22.6 0.0 collective-permute-done.4
  22.6 0.1 pad_maximum_fusion.4
  22.7 0.2 pad_maximum_fusion
  23.0 0.2 floor_reduce_fusion
  23.1 0.8 %fusion = f32[256]{0:T(256)S(1)} fusion(bf16[256,4096]{1,0:T(8,128)(2,1)S(1)} %pad_maximum_fusion, bf16[64,4224]{1,0:T(8,128)(2,1)S(1)} %select_convert_fusion, f32[256]{0:T(256)S(1)} %get-tuple-element.30, f32[256]{0:T(256)S(1)} %get-tuple-element.29, f32[64]{0:T(128)S(1)} %add_reduce_fusion.6, f32[64]{0:T(128)S(1)} %multiply_floor_fusion.8), kind=kOutput, calls=%fused_computation.10 | convolution fusion | flops 134299392 | bytes 2625536 | tf_op jit(solution)/shard_map/id,jd->ij/dot_general | solution.py:26
  23.9 0.8 %fusion.1 = f32[256]{0:T(256)S(1)} fusion(bf16[256,4096]{1,0:T(8,128)(2,1)S(1)} %pad_maximum_fusion, bf16[64,4224]{1,0:T(8,128)(2,1)S(1)} %collective-permute-done, f32[256]{0:T(256)S(1)} %get-tuple-element.30, f32[256]{0:T(256)S(1)} %get-tuple-element.29, f32[64]{0:T(128)S(1)} %add_reduce_fusion.5, f32[64]{0:T(128)S(1)} %multiply_floor_fusion.7), kind=kOutput, calls=%fused_computation.11 | convolution fusion | flops 134299392 | bytes 2625536 | tf_op jit(solution)/shard_map/id,jd->ij/dot_general | solution.py:26
  24.7 8.7 %collective-permute-done.1 = bf16[64,4224]{1,0:T(8,128)(2,1)S(1)} collective-permute-done((bf16[64,4224]{1,0:T(8,128)(2,1)S(1)}, bf16[64,4224]{1,0:T(8,128)(2,1)S(1)}, u32[]{:S(2)}, u32[]{:S(2)}) %collective-permute-start.1) | collective-permute-done | bytes 540704 | tf_op jit(solution)/shard_map/ppermute | solution.py:60
  33.4 0.2 add_reduce_fusion.4
  33.6 1.8 %collective-permute-start.5 = (bf16[64,4224]{1,0:T(8,128)(2,1)S(1)}, bf16[64,4224]{1,0:T(8,128)(2,1)S(1)}, u32[]{:S(2)}, u32[]{:S(2)}) collective-permute-start(bf16[64,4224]{1,0:T(8,128)(2,1)S(1)} %collective-permute-done.1), channel_id=1, source_target_pairs={{0,2},{2,4},{4,6},{6,7},{7,5},{5,3},{3,1},{1,0},{8,10},{10,12},{12... | collective-permute-start | bytes 1622024 | tf_op jit(solution)/shard_map/ppermute | solution.py:60
  35.4 0.8 %fusion.2 = f32[256]{0:T(256)S(1)} fusion(bf16[256,4096]{1,0:T(8,128)(2,1)S(1)} %pad_maximum_fusion, bf16[64,4224]{1,0:T(8,128)(2,1)S(1)} %collective-permute-done.1, f32[256]{0:T(256)S(1)} %get-tuple-element.30, f32[256]{0:T(256)S(1)} %get-tuple-element.29, f32[64]{0:T(128)S(1)} %add_reduce_fusion.4, f32[64]{0:T(128)S(1)} %multiply_floor_fusion.6), kind=kOutput, calls=%fused_computation.12 | convolution fusion | flops 134299392 | bytes 2625536 | tf_op jit(solution)/shard_map/id,jd->ij/dot_general | solution.py:26
  36.2 0.8 %fusion.4 = f32[256]{0:T(256)S(1)} fusion(bf16[256,4096]{1,0:T(8,128)(2,1)S(1)} %pad_maximum_fusion, bf16[64,4224]{1,0:T(8,128)(2,1)S(1)} %collective-permute-done.7, f32[256]{0:T(256)S(1)} %get-tuple-element.30, f32[256]{0:T(256)S(1)} %get-tuple-element.29, f32[64]{0:T(128)S(1)} %add_reduce_fusion.2, f32[64]{0:T(128)S(1)} %multiply_floor_fusion.3), kind=kOutput, calls=%fused_computation.14 | convolution fusion | flops 134299392 | bytes 2625536 | tf_op jit(solution)/shard_map/id,jd->ij/dot_general | solution.py:26
  37.0 0.3 collective-permute-start.9
  37.3 0.2 add_reduce_fusion.1
  37.5 0.8 %fusion.5 = f32[256]{0:T(256)S(1)} fusion(bf16[256,4096]{1,0:T(8,128)(2,1)S(1)} %pad_maximum_fusion, bf16[64,4224]{1,0:T(8,128)(2,1)S(1)} %collective-permute-done.8, f32[256]{0:T(256)S(1)} %get-tuple-element.30, f32[256]{0:T(256)S(1)} %get-tuple-element.29, f32[64]{0:T(128)S(1)} %add_reduce_fusion.1, f32[64]{0:T(128)S(1)} %multiply_floor_fusion.2), kind=kOutput, calls=%fused_computation.15 | convolution fusion | flops 134299392 | bytes 2625536 | tf_op jit(solution)/shard_map/id,jd->ij/dot_general | solution.py:26
  38.2 7.9 %collective-permute-done.5 = bf16[64,4224]{1,0:T(8,128)(2,1)S(1)} collective-permute-done((bf16[64,4224]{1,0:T(8,128)(2,1)S(1)}, bf16[64,4224]{1,0:T(8,128)(2,1)S(1)}, u32[]{:S(2)}, u32[]{:S(2)}) %collective-permute-start.5) | collective-permute-done | bytes 540704 | tf_op jit(solution)/shard_map/ppermute | solution.py:60
  46.2 1.9 %collective-permute-start.6 = (bf16[32,4224]{1,0:T(8,128)(2,1)S(1)}, bf16[32,4224]{1,0:T(8,128)(2,1)S(1)}, u32[]{:S(2)}, u32[]{:S(2)}) collective-permute-start(bf16[32,4224]{1,0:T(8,128)(2,1)S(1)} %slice.142), channel_id=1, source_target_pairs={{0,2},{2,4},{4,6},{6,7},{7,5},{5,3},{3,1},{1,0},{8,10},{10,12},{12... | collective-permute-start | bytes 811016 | tf_op jit(solution)/shard_map/ppermute | solution.py:60
  48.1 0.2 add_reduce_fusion.3
  48.3 0.8 %fusion.3 = f32[256]{0:T(256)S(1)} fusion(bf16[256,4096]{1,0:T(8,128)(2,1)S(1)} %pad_maximum_fusion, bf16[64,4224]{1,0:T(8,128)(2,1)S(1)} %collective-permute-done.5, f32[256]{0:T(256)S(1)} %get-tuple-element.30, f32[256]{0:T(256)S(1)} %get-tuple-element.29, f32[64]{0:T(128)S(1)} %add_reduce_fusion.3, f32[64]{0:T(128)S(1)} %multiply_floor_fusion.5), kind=kOutput, calls=%fused_computation.13 | convolution fusion | flops 134299392 | bytes 2625536 | tf_op jit(solution)/shard_map/id,jd->ij/dot_general | solution.py:26
  49.0 0.3 collective-permute-done.9
  49.3 0.2 add_reduce_fusion
  49.6 0.3 collective-permute-start.10
  49.9 0.8 %fusion.6 = f32[256]{0:T(256)S(1)} fusion(bf16[256,4096]{1,0:T(8,128)(2,1)S(1)} %pad_maximum_fusion, bf16[64,4224]{1,0:T(8,128)(2,1)S(1)} %collective-permute-done.9, f32[256]{0:T(256)S(1)} %get-tuple-element.30, f32[256]{0:T(256)S(1)} %get-tuple-element.29, f32[64]{0:T(128)S(1)} %add_reduce_fusion, f32[64]{0:T(128)S(1)} %multiply_floor_fusion.1), kind=kOutput, calls=%fused_computation.16 | convolution fusion | flops 134299392 | bytes 2625536 | tf_op jit(solution)/shard_map/id,jd->ij/dot_general | solution.py:26
  50.7 2.0 %collective-permute-done.6 = bf16[32,4224]{1,0:T(8,128)(2,1)S(1)} collective-permute-done((bf16[32,4224]{1,0:T(8,128)(2,1)S(1)}, bf16[32,4224]{1,0:T(8,128)(2,1)S(1)}, u32[]{:S(2)}, u32[]{:S(2)}) %collective-permute-start.6) | collective-permute-done | bytes 270368 | tf_op jit(solution)/shard_map/ppermute | solution.py:60
  52.7 0.2 add_reduce_fusion.8
  52.9 0.8 %fusion.7 = f32[256]{0:T(256)S(1)} fusion(bf16[256,4096]{1,0:T(8,128)(2,1)S(1)} %pad_maximum_fusion, bf16[32,4224]{1,0:T(8,128)(2,1)S(1)} %collective-permute-done.6, f32[256]{0:T(256)S(1)} %get-tuple-element.30, f32[256]{0:T(256)S(1)} %get-tuple-element.29, f32[32]{0:T(128)S(1)} %add_reduce_fusion.8, f32[32]{0:T(128)S(1)} %multiply_floor_fusion.4), kind=kOutput, calls=%fused_computation.19 | convolution fusion | flops 67149568 | bytes 2363392 | tf_op jit(solution)/shard_map/id,jd->ij/dot_general | solution.py:26
  53.7 2.4 %collective-permute-done.10 = bf16[32,4224]{1,0:T(8,128)(2,1)S(1)} collective-permute-done((bf16[32,4224]{1,0:T(8,128)(2,1)S(1)}, bf16[32,4224]{1,0:T(8,128)(2,1)S(1)}, u32[]{:S(2)}, u32[]{:S(2)}) %collective-permute-start.10) | collective-permute-done | bytes 270368 | tf_op jit(solution)/shard_map/ppermute | solution.py:60
  56.1 0.2 add_reduce_fusion.7
  56.3 0.8 %fusion.8 = f32[256]{0:T(256)S(1)} fusion(bf16[256,4096]{1,0:T(8,128)(2,1)S(1)} %pad_maximum_fusion, bf16[32,4224]{1,0:T(8,128)(2,1)S(1)} %collective-permute-done.10, f32[256]{0:T(256)S(1)} %get-tuple-element.30, f32[256]{0:T(256)S(1)} %get-tuple-element.29, f32[32]{0:T(128)S(1)} %add_reduce_fusion.7, f32[32]{0:T(128)S(1)} %multiply_floor_fusion), kind=kOutput, calls=%fused_computation.20 | convolution fusion | flops 67149568 | bytes 2363392 | tf_op jit(solution)/shard_map/id,jd->ij/dot_general | solution.py:26
  57.0 0.1 slice.165
  57.1 2.7 %collective-permute-start.11 = (f32[2,64]{1,0:T(2,128)S(1)}, f32[2,64]{1,0:T(2,128)S(1)}, u32[]{:S(2)}, u32[]{:S(2)}) collective-permute-start(f32[2,64]{1,0:T(2,128)S(1)} %slice.165), channel_id=1, source_target_pairs={{0,16},{8,24},{16,0},{24,8},{1,17},{9,25},{17,1},{25,9},{2,18},{10... | collective-permute-start | bytes 1544 | tf_op jit(solution)/shard_map/ppermute | solution.py:103
  59.9 0.1 slice.163
  60.0 1.5 %collective-permute-done.11 = f32[2,64]{1,0:T(2,128)S(1)} collective-permute-done((f32[2,64]{1,0:T(2,128)S(1)}, f32[2,64]{1,0:T(2,128)S(1)}, u32[]{:S(2)}, u32[]{:S(2)}) %collective-permute-start.11) | collective-permute-done | bytes 544 | tf_op jit(solution)/shard_map/ppermute | solution.py:103
  61.4 1.2 %collective-permute-done.12 = f32[64]{0:T(128)S(1)} collective-permute-done((f32[64]{0:T(128)S(1)}, f32[64]{0:T(128)S(1)}, u32[]{:S(2)}, u32[]{:S(2)}) %collective-permute-start.12) | collective-permute-done | bytes 288 | tf_op jit(solution)/shard_map/ppermute | solution.py:105
  62.6 0.5 bitcast_maximum_fusion
  (28 shorter events, 0.2 us)
Async XLA Ops:
  3.3 15.3 %collective-permute-start.3 = (bf16[64,4224]{1,0:T(8,128)(2,1)S(1)}, bf16[64,4224]{1,0:T(8,128)(2,1)S(1)}, u32[]{:S(2)}, u32[]{:S(2)}) collective-permute-start(bf16[64,4224]{1,0:T(8,128)(2,1)S(1)} %select_convert_fusion), channel_id=1, source_target_pairs={{0,16},{8,24},{16,0},{24,8},{1,17},{9,25},{17,1},{25,9},{2,18},{10... | collective-permute-start | bytes 1622024 | tf_op jit(solution)/shard_map/ppermute | solution.py:69
  6.4 13.7 %collective-permute-start = (bf16[64,4224]{1,0:T(8,128)(2,1)S(1)}, bf16[64,4224]{1,0:T(8,128)(2,1)S(1)}, u32[]{:S(2)}, u32[]{:S(2)}) collective-permute-start(bf16[64,4224]{1,0:T(8,128)(2,1)S(1)} %select_convert_fusion), channel_id=1, source_target_pairs={{0,2},{2,4},{4,6},{6,7},{7,5},{5,3},{3,1},{1,0},{8,10},{10,12},{12... | collective-permute-start | bytes 1622024 | tf_op jit(solution)/shard_map/ppermute | solution.py:60
  8.0 13.9 %collective-permute-start.7 = (bf16[64,4224]{1,0:T(8,128)(2,1)S(1)}, bf16[64,4224]{1,0:T(8,128)(2,1)S(1)}, u32[]{:S(2)}, u32[]{:S(2)}) collective-permute-start(bf16[64,4224]{1,0:T(8,128)(2,1)S(1)} %select_convert_fusion), channel_id=1, source_target_pairs={{2,0},{4,2},{6,4},{7,6},{5,7},{3,5},{1,3},{0,1},{10,8},{12,10},{14... | collective-permute-start | bytes 1622024 | tf_op jit(solution)/shard_map/ppermute | solution.py:60
  8.4 14.2 %collective-permute-start.2 = (bf16[64,4224]{1,0:T(8,128)(2,1)S(1)}, bf16[64,4224]{1,0:T(8,128)(2,1)S(1)}, u32[]{:S(2)}, u32[]{:S(2)}) collective-permute-start(bf16[64,4224]{1,0:T(8,128)(2,1)S(1)} %select_convert_fusion), channel_id=1, source_target_pairs={{0,8},{8,0},{16,24},{24,16},{1,9},{9,1},{17,25},{25,17},{2,10},{10... | collective-permute-start | bytes 1622024 | tf_op jit(solution)/shard_map/ppermute | solution.py:70
  18.7 3.9 %collective-permute-start.4 = (bf16[64,4224]{1,0:T(8,128)(2,1)S(1)}, bf16[64,4224]{1,0:T(8,128)(2,1)S(1)}, u32[]{:S(2)}, u32[]{:S(2)}) collective-permute-start(bf16[64,4224]{1,0:T(8,128)(2,1)S(1)} %collective-permute-done.3), channel_id=1, source_target_pairs={{0,8},{8,0},{16,24},{24,16},{1,9},{9,1},{17,25},{25,17},{2,10},{10... | collective-permute-start | bytes 1622024 | tf_op jit(solution)/shard_map/ppermute | solution.py:71
  20.1 13.2 %collective-permute-start.1 = (bf16[64,4224]{1,0:T(8,128)(2,1)S(1)}, bf16[64,4224]{1,0:T(8,128)(2,1)S(1)}, u32[]{:S(2)}, u32[]{:S(2)}) collective-permute-start(bf16[64,4224]{1,0:T(8,128)(2,1)S(1)} %collective-permute-done), channel_id=1, source_target_pairs={{0,2},{2,4},{4,6},{6,7},{7,5},{5,3},{3,1},{1,0},{8,10},{10,12},{12... | collective-permute-start | bytes 1622024 | tf_op jit(solution)/shard_map/ppermute | solution.py:60
  21.9 15.1 %collective-permute-start.8 = (bf16[64,4224]{1,0:T(8,128)(2,1)S(1)}, bf16[64,4224]{1,0:T(8,128)(2,1)S(1)}, u32[]{:S(2)}, u32[]{:S(2)}) collective-permute-start(bf16[64,4224]{1,0:T(8,128)(2,1)S(1)} %collective-permute-done.7), channel_id=1, source_target_pairs={{2,0},{4,2},{6,4},{7,6},{5,7},{3,5},{1,3},{0,1},{10,8},{12,10},{14... | collective-permute-start | bytes 1622024 | tf_op jit(solution)/shard_map/ppermute | solution.py:60
  33.6 12.6 %collective-permute-start.5 = (bf16[64,4224]{1,0:T(8,128)(2,1)S(1)}, bf16[64,4224]{1,0:T(8,128)(2,1)S(1)}, u32[]{:S(2)}, u32[]{:S(2)}) collective-permute-start(bf16[64,4224]{1,0:T(8,128)(2,1)S(1)} %collective-permute-done.1), channel_id=1, source_target_pairs={{0,2},{2,4},{4,6},{6,7},{7,5},{5,3},{3,1},{1,0},{8,10},{10,12},{12... | collective-permute-start | bytes 1622024 | tf_op jit(solution)/shard_map/ppermute | solution.py:60
  37.0 12.4 %collective-permute-start.9 = (bf16[64,4224]{1,0:T(8,128)(2,1)S(1)}, bf16[64,4224]{1,0:T(8,128)(2,1)S(1)}, u32[]{:S(2)}, u32[]{:S(2)}) collective-permute-start(bf16[64,4224]{1,0:T(8,128)(2,1)S(1)} %collective-permute-done.8), channel_id=1, source_target_pairs={{2,0},{4,2},{6,4},{7,6},{5,7},{3,5},{1,3},{0,1},{10,8},{12,10},{14... | collective-permute-start | bytes 1622024 | tf_op jit(solution)/shard_map/ppermute | solution.py:60
  46.2 6.5 %collective-permute-start.6 = (bf16[32,4224]{1,0:T(8,128)(2,1)S(1)}, bf16[32,4224]{1,0:T(8,128)(2,1)S(1)}, u32[]{:S(2)}, u32[]{:S(2)}) collective-permute-start(bf16[32,4224]{1,0:T(8,128)(2,1)S(1)} %slice.142), channel_id=1, source_target_pairs={{0,2},{2,4},{4,6},{6,7},{7,5},{5,3},{3,1},{1,0},{8,10},{10,12},{12... | collective-permute-start | bytes 811016 | tf_op jit(solution)/shard_map/ppermute | solution.py:60
  49.6 6.5 %collective-permute-start.10 = (bf16[32,4224]{1,0:T(8,128)(2,1)S(1)}, bf16[32,4224]{1,0:T(8,128)(2,1)S(1)}, u32[]{:S(2)}, u32[]{:S(2)}) collective-permute-start(bf16[32,4224]{1,0:T(8,128)(2,1)S(1)} %slice.155), channel_id=1, source_target_pairs={{2,0},{4,2},{6,4},{7,6},{5,7},{3,5},{1,3},{0,1},{10,8},{12,10},{14... | collective-permute-start | bytes 811016 | tf_op jit(solution)/shard_map/ppermute | solution.py:60
  57.1 4.3 %collective-permute-start.11 = (f32[2,64]{1,0:T(2,128)S(1)}, f32[2,64]{1,0:T(2,128)S(1)}, u32[]{:S(2)}, u32[]{:S(2)}) collective-permute-start(f32[2,64]{1,0:T(2,128)S(1)} %slice.165), channel_id=1, source_target_pairs={{0,16},{8,24},{16,0},{24,8},{1,17},{9,25},{17,1},{25,9},{2,18},{10... | collective-permute-start | bytes 1544 | tf_op jit(solution)/shard_map/ppermute | solution.py:103
  61.4 1.2 %collective-permute-start.12 = (f32[64]{0:T(128)S(1)}, f32[64]{0:T(128)S(1)}, u32[]{:S(2)}, u32[]{:S(2)}) collective-permute-start(f32[64]{0:T(128)S(1)} %slice_bitcast_fusion), channel_id=1, source_target_pairs={{0,8},{8,0},{16,24},{24,16},{1,9},{9,1},{17,25},{25,17},{2,10},{10... | collective-permute-start | bytes 776 | tf_op jit(solution)/shard_map/ppermute | solution.py:105

commit v11 on v7

--- a/solution.py
+++ b/solution.py
@@ -51,12 +51,12 @@
     order = ring_order(block_count)
     forward = [(order[i], order[(i + 1) % block_count]) for i in range(block_count)]
     backward = [(dst, src) for src, dst in forward]
-    half = rows_here // 2
+    split = min(rows_here, max(0, (rows_here * 5 // 8) // 8 * 8))
     steps = block_count // 2
 
     def send(which, visiting, step):
         if step == steps and block_count % 2 == 0:
-            visiting = visiting[:half] if which == 0 else visiting[half:]
+            visiting = visiting[:split] if which == 0 else visiting[split:]
         return lax.ppermute(visiting, "blk", forward if which == 0 else backward)
 
     chains = [[payload, None, [payload]], [payload, None, []]]

time: 63 us -> 65.4 us (1.038)
  waiting for transfers between devices: 35.8 us -> 38.5 us
    ppermute x8, waiting for transfers between devices: 22.8 us -> 25.5 us  [send(): return lax.ppermute(visiting, 'blk', forward if which == 0 else backward)]
  transfers between devices with their start and end apart: 14 -> 14, of which waited for: 9 -> 8; matrix products, arithmetic and copies ran while one was open for 13% -> 11% of each run, Pallas kernels for 0% -> 0%
where the time goes in v11:
time: 65.4 us; the launch traced here: 65.2 us
  waiting for transfers between devices  38.5 us (59%)
  starting transfers between devices  14 us (21%)
  matrix products  6.91 us (11%)
  other arithmetic  5.33 us (8%)
    ppermute x8, waiting for transfers between devices, send(): return lax.ppermute(visiting, 'blk', forward if which == 0 else backward)  25.5 us
    ppermute x1, waiting for transfers between devices, per_device(): across = lax.ppermute(payload, 'grp', partner_pairs(group_count, 2))  10.1 us
    ppermute x8, starting transfers between devices, send(): return lax.ppermute(visiting, 'blk', forward if which == 0 else backward)  8.32 us
    dot_general x9, matrix products, block_best(): jnp.einsum('id,jd->ij', left_rows, payload[:, :D], preferred_element_type...  6.91 us
    ppermute x1, starting transfers between devices, per_device(): across = lax.ppermute(payload, 'grp', partner_pairs(group_count, 2))  3.06 us
    ppermute x3, waiting for transfers between devices, per_device(): result = jnp.maximum(result, lax.ppermute(best[k], 'grp', pairs))  2.95 us
    ppermute x3, starting transfers between devices, per_device(): result = jnp.maximum(result, lax.ppermute(best[k], 'grp', pairs))  2.65 us
    add x9, other arithmetic, tag_labels(): return high * 128.0 + low  1.57 us
  transfers between devices with their start and end apart: 14, of which 8 were waited for; matrix products, arithmetic and copies ran while one was open for 11% of the time, Pallas kernels for 0%

profile of v11, /device:TPU:0, one launch (start us, length us, event | category | flops | bytes accessed | tf_op | source)
XLA Modules:
  0.0 65.2 jit_solution(8233499061583233447)
XLA Ops:
  0.0 1.1 %convert_element_type.222 = f32[64,4096]{1,0:T(8,128)S(1)} convert(bf16[64,4096]{1,0:T(8,128)(2,1)} %param.3) | non-fusion elementwise | flops 262144 | bytes 1572864 | tf_op jit(solution)/shard_map/convert_element_type | solution.py:41
  1.1 1.2 %multiply_reduce_fusion = f32[64]{0:T(128)S(1)} fusion(bf16[64,4096]{1,0:T(8,128)(2,1)} %param.3), kind=kLoop, calls=%fused_computation.22 | loop fusion | flops 786368 | bytes 524544 | tf_op jit(solution)/shard_map/reduce_sum | solution.py:42
  2.4 0.3 select_convert_fusion
  2.7 3.1 %collective-permute-start.3 = (bf16[64,4224]{1,0:T(8,128)(2,1)S(1)}, bf16[64,4224]{1,0:T(8,128)(2,1)S(1)}, u32[]{:S(2)}, u32[]{:S(2)}) collective-permute-start(bf16[64,4224]{1,0:T(8,128)(2,1)S(1)} %select_convert_fusion), channel_id=1, source_target_pairs={{0,16},{8,24},{16,0},{24,8},{1,17},{9,25},{17,1},{25,9},{2,18},{10... | collective-permute-start | bytes 1622024 | tf_op jit(solution)/shard_map/ppermute | solution.py:69
  5.8 1.6 %collective-permute-start = (bf16[64,4224]{1,0:T(8,128)(2,1)S(1)}, bf16[64,4224]{1,0:T(8,128)(2,1)S(1)}, u32[]{:S(2)}, u32[]{:S(2)}) collective-permute-start(bf16[64,4224]{1,0:T(8,128)(2,1)S(1)} %select_convert_fusion), channel_id=1, source_target_pairs={{0,2},{2,4},{4,6},{6,7},{7,5},{5,3},{3,1},{1,0},{8,10},{10,12},{12... | collective-permute-start | bytes 1622024 | tf_op jit(solution)/shard_map/ppermute | solution.py:60
  7.4 0.4 collective-permute-start.7
  7.8 0.0 collective-permute-start.2
  7.8 0.2 add_reduce_fusion.6
  8.0 10.1 %collective-permute-done.3 = bf16[64,4224]{1,0:T(8,128)(2,1)S(1)} collective-permute-done((bf16[64,4224]{1,0:T(8,128)(2,1)S(1)}, bf16[64,4224]{1,0:T(8,128)(2,1)S(1)}, u32[]{:S(2)}, u32[]{:S(2)}) %collective-permute-start.3) | collective-permute-done | bytes 540704 | tf_op jit(solution)/shard_map/ppermute | solution.py:69
  18.1 1.5 %collective-permute-done = bf16[64,4224]{1,0:T(8,128)(2,1)S(1)} collective-permute-done((bf16[64,4224]{1,0:T(8,128)(2,1)S(1)}, bf16[64,4224]{1,0:T(8,128)(2,1)S(1)}, u32[]{:S(2)}, u32[]{:S(2)}) %collective-permute-start) | collective-permute-done | bytes 540704 | tf_op jit(solution)/shard_map/ppermute | solution.py:60
  19.5 1.6 %collective-permute-start.1 = (bf16[64,4224]{1,0:T(8,128)(2,1)S(1)}, bf16[64,4224]{1,0:T(8,128)(2,1)S(1)}, u32[]{:S(2)}, u32[]{:S(2)}) collective-permute-start(bf16[64,4224]{1,0:T(8,128)(2,1)S(1)} %collective-permute-done), channel_id=1, source_target_pairs={{0,2},{2,4},{4,6},{6,7},{7,5},{5,3},{3,1},{1,0},{8,10},{10,12},{12... | collective-permute-start | bytes 1622024 | tf_op jit(solution)/shard_map/ppermute | solution.py:60
  21.1 0.2 add_reduce_fusion.5
  21.3 0.5 collective-permute-start.8
  21.8 0.2 add_reduce_fusion.2
  22.0 0.0 collective-permute-done.4
  22.0 0.1 pad_maximum_fusion.4
  22.1 0.2 pad_maximum_fusion
  22.4 0.2 floor_reduce_fusion
  22.5 0.8 %fusion = f32[256]{0:T(256)S(1)} fusion(bf16[256,4096]{1,0:T(8,128)(2,1)S(1)} %pad_maximum_fusion, bf16[64,4224]{1,0:T(8,128)(2,1)S(1)} %select_convert_fusion, f32[256]{0:T(256)S(1)} %get-tuple-element.30, f32[256]{0:T(256)S(1)} %get-tuple-element.29, f32[64]{0:T(128)S(1)} %add_reduce_fusion.6, f32[64]{0:T(128)S(1)} %multiply_floor_fusion.8), kind=kOutput, calls=%fused_computation.11 | convolution fusion | flops 134299392 | bytes 2625536 | tf_op jit(solution)/shard_map/id,jd->ij/dot_general | solution.py:26
  23.3 0.8 %fusion.1 = f32[256]{0:T(256)S(1)} fusion(bf16[256,4096]{1,0:T(8,128)(2,1)S(1)} %pad_maximum_fusion, bf16[64,4224]{1,0:T(8,128)(2,1)S(1)} %collective-permute-done, f32[256]{0:T(256)S(1)} %get-tuple-element.30, f32[256]{0:T(256)S(1)} %get-tuple-element.29, f32[64]{0:T(128)S(1)} %add_reduce_fusion.5, f32[64]{0:T(128)S(1)} %multiply_floor_fusion.7), kind=kOutput, calls=%fused_computation.12 | convolution fusion | flops 134299392 | bytes 2625536 | tf_op jit(solution)/shard_map/id,jd->ij/dot_general | solution.py:26
  24.1 8.7 %collective-permute-done.1 = bf16[64,4224]{1,0:T(8,128)(2,1)S(1)} collective-permute-done((bf16[64,4224]{1,0:T(8,128)(2,1)S(1)}, bf16[64,4224]{1,0:T(8,128)(2,1)S(1)}, u32[]{:S(2)}, u32[]{:S(2)}) %collective-permute-start.1) | collective-permute-done | bytes 540704 | tf_op jit(solution)/shard_map/ppermute | solution.py:60
  32.8 0.2 add_reduce_fusion.4
  33.0 1.8 %collective-permute-start.5 = (bf16[64,4224]{1,0:T(8,128)(2,1)S(1)}, bf16[64,4224]{1,0:T(8,128)(2,1)S(1)}, u32[]{:S(2)}, u32[]{:S(2)}) collective-permute-start(bf16[64,4224]{1,0:T(8,128)(2,1)S(1)} %collective-permute-done.1), channel_id=1, source_target_pairs={{0,2},{2,4},{4,6},{6,7},{7,5},{5,3},{3,1},{1,0},{8,10},{10,12},{12... | collective-permute-start | bytes 1622024 | tf_op jit(solution)/shard_map/ppermute | solution.py:60
  34.8 0.8 %fusion.2 = f32[256]{0:T(256)S(1)} fusion(bf16[256,4096]{1,0:T(8,128)(2,1)S(1)} %pad_maximum_fusion, bf16[64,4224]{1,0:T(8,128)(2,1)S(1)} %collective-permute-done.1, f32[256]{0:T(256)S(1)} %get-tuple-element.30, f32[256]{0:T(256)S(1)} %get-tuple-element.29, f32[64]{0:T(128)S(1)} %add_reduce_fusion.4, f32[64]{0:T(128)S(1)} %multiply_floor_fusion.6), kind=kOutput, calls=%fused_computation.13 | convolution fusion | flops 134299392 | bytes 2625536 | tf_op jit(solution)/shard_map/id,jd->ij/dot_general | solution.py:26
  35.6 0.8 %fusion.4 = f32[256]{0:T(256)S(1)} fusion(bf16[256,4096]{1,0:T(8,128)(2,1)S(1)} %pad_maximum_fusion, bf16[64,4224]{1,0:T(8,128)(2,1)S(1)} %collective-permute-done.7, f32[256]{0:T(256)S(1)} %get-tuple-element.30, f32[256]{0:T(256)S(1)} %get-tuple-element.29, f32[64]{0:T(128)S(1)} %add_reduce_fusion.2, f32[64]{0:T(128)S(1)} %multiply_floor_fusion.3), kind=kOutput, calls=%fused_computation.15 | convolution fusion | flops 134299392 | bytes 2625536 | tf_op jit(solution)/shard_map/id,jd->ij/dot_general | solution.py:26
  36.4 0.3 collective-permute-start.9
  36.7 0.2 add_reduce_fusion.1
  36.9 0.8 %fusion.5 = f32[256]{0:T(256)S(1)} fusion(bf16[256,4096]{1,0:T(8,128)(2,1)S(1)} %pad_maximum_fusion, bf16[64,4224]{1,0:T(8,128)(2,1)S(1)} %collective-permute-done.8, f32[256]{0:T(256)S(1)} %get-tuple-element.30, f32[256]{0:T(256)S(1)} %get-tuple-element.29, f32[64]{0:T(128)S(1)} %add_reduce_fusion.1, f32[64]{0:T(128)S(1)} %multiply_floor_fusion.2), kind=kOutput, calls=%fused_computation.16 | convolution fusion | flops 134299392 | bytes 2625536 | tf_op jit(solution)/shard_map/id,jd->ij/dot_general | solution.py:26
  37.6 7.9 %collective-permute-done.5 = bf16[64,4224]{1,0:T(8,128)(2,1)S(1)} collective-permute-done((bf16[64,4224]{1,0:T(8,128)(2,1)S(1)}, bf16[64,4224]{1,0:T(8,128)(2,1)S(1)}, u32[]{:S(2)}, u32[]{:S(2)}) %collective-permute-start.5) | collective-permute-done | bytes 540704 | tf_op jit(solution)/shard_map/ppermute | solution.py:60
  45.6 0.2 add_reduce_fusion.3
  45.8 3.0 %collective-permute-done.9 = bf16[64,4224]{1,0:T(8,128)(2,1)S(1)} collective-permute-done((bf16[64,4224]{1,0:T(8,128)(2,1)S(1)}, bf16[64,4224]{1,0:T(8,128)(2,1)S(1)}, u32[]{:S(2)}, u32[]{:S(2)}) %collective-permute-start.9) | collective-permute-done | bytes 540704 | tf_op jit(solution)/shard_map/ppermute | solution.py:60
  48.7 0.2 add_reduce_fusion
  49.0 0.8 %fusion.3 = f32[256]{0:T(256)S(1)} fusion(bf16[256,4096]{1,0:T(8,128)(2,1)S(1)} %pad_maximum_fusion, bf16[64,4224]{1,0:T(8,128)(2,1)S(1)} %collective-permute-done.5, f32[256]{0:T(256)S(1)} %get-tuple-element.30, f32[256]{0:T(256)S(1)} %get-tuple-element.29, f32[64]{0:T(128)S(1)} %add_reduce_fusion.3, f32[64]{0:T(128)S(1)} %multiply_floor_fusion.5), kind=kOutput, calls=%fused_computation.14 | convolution fusion | flops 134299392 | bytes 2625536 | tf_op jit(solution)/shard_map/id,jd->ij/dot_general | solution.py:26
  49.7 1.6 %collective-permute-start.6 = (bf16[40,4224]{1,0:T(8,128)(2,1)S(1)}, bf16[40,4224]{1,0:T(8,128)(2,1)S(1)}, u32[]{:S(2)}, u32[]{:S(2)}) collective-permute-start(bf16[40,4224]{1,0:T(8,128)(2,1)S(1)} %slice.124), channel_id=1, source_target_pairs={{0,2},{2,4},{4,6},{6,7},{7,5},{5,3},{3,1},{1,0},{8,10},{10,12},{12... | collective-permute-start | bytes 1013768 | tf_op jit(solution)/shard_map/ppermute | solution.py:60
  51.4 0.4 collective-permute-start.10
  51.8 0.8 %fusion.6 = f32[256]{0:T(256)S(1)} fusion(bf16[256,4096]{1,0:T(8,128)(2,1)S(1)} %pad_maximum_fusion, bf16[64,4224]{1,0:T(8,128)(2,1)S(1)} %collective-permute-done.9, f32[256]{0:T(256)S(1)} %get-tuple-element.30, f32[256]{0:T(256)S(1)} %get-tuple-element.29, f32[64]{0:T(128)S(1)} %add_reduce_fusion, f32[64]{0:T(128)S(1)} %multiply_floor_fusion.1), kind=kOutput, calls=%fused_computation.17 | convolution fusion | flops 134299392 | bytes 2625536 | tf_op jit(solution)/shard_map/id,jd->ij/dot_general | solution.py:26
  52.6 4.5 %collective-permute-done.10 = bf16[24,4224]{1,0:T(8,128)(2,1)S(1)} collective-permute-done((bf16[24,4224]{1,0:T(8,128)(2,1)S(1)}, bf16[24,4224]{1,0:T(8,128)(2,1)S(1)}, u32[]{:S(2)}, u32[]{:S(2)}) %collective-permute-start.10) | collective-permute-done | bytes 202784 | tf_op jit(solution)/shard_map/ppermute | solution.py:60
  57.1 0.2 add_reduce_fusion.8
  57.3 0.7 %fusion.8 = f32[256]{0:T(256)S(1)} fusion(bf16[256,4096]{1,0:T(8,128)(2,1)S(1)} %pad_maximum_fusion, bf16[24,4224]{1,0:T(8,128)(2,1)S(1)} %collective-permute-done.10, f32[256]{0:T(256)S(1)} %get-tuple-element.30, f32[256]{0:T(256)S(1)} %get-tuple-element.29, f32[24]{0:T(128)S(1)} %add_reduce_fusion.8, f32[24]{0:T(128)S(1)} %multiply_floor_fusion), kind=kOutput, calls=%fused_computation.20 | convolution fusion | flops 50362112 | bytes 2297856 | tf_op jit(solution)/shard_map/id,jd->ij/dot_general | solution.py:26
  58.0 0.2 add_reduce_fusion.7
  58.2 0.8 %fusion.7 = f32[256]{0:T(256)S(1)} fusion(bf16[256,4096]{1,0:T(8,128)(2,1)S(1)} %pad_maximum_fusion, bf16[40,4224]{1,0:T(8,128)(2,1)S(1)} %collective-permute-done.6, f32[256]{0:T(256)S(1)} %get-tuple-element.30, f32[256]{0:T(256)S(1)} %get-tuple-element.29, f32[40]{0:T(128)S(1)} %add_reduce_fusion.7, f32[40]{0:T(128)S(1)} %multiply_floor_fusion.4), kind=kOutput, calls=%fused_computation.19 | convolution fusion | flops 83937024 | bytes 2428928 | tf_op jit(solution)/shard_map/id,jd->ij/dot_general | solution.py:26
  59.0 0.1 fusion.20
  59.1 0.0 collective-permute-start.11
  59.1 2.6 %collective-permute-start.12 = (f32[64]{0:T(128)S(1)}, f32[64]{0:T(128)S(1)}, u32[]{:S(2)}, u32[]{:S(2)}) collective-permute-start(f32[64]{0:T(128)S(1)} %get-tuple-element.35), channel_id=1, source_target_pairs={{0,16},{8,24},{16,0},{24,8},{1,17},{9,25},{17,1},{25,9},{2,18},{10... | collective-permute-start | bytes 776 | tf_op jit(solution)/shard_map/ppermute | solution.py:104
  61.7 0.0 collective-permute-start.13
  61.7 1.5 %collective-permute-done.12 = f32[64]{0:T(128)S(1)} collective-permute-done((f32[64]{0:T(128)S(1)}, f32[64]{0:T(128)S(1)}, u32[]{:S(2)}, u32[]{:S(2)}) %collective-permute-start.12) | collective-permute-done | bytes 288 | tf_op jit(solution)/shard_map/ppermute | solution.py:104
  63.2 1.4 %collective-permute-done.13 = f32[64]{0:T(128)S(1)} collective-permute-done((f32[64]{0:T(128)S(1)}, f32[64]{0:T(128)S(1)}, u32[]{:S(2)}, u32[]{:S(2)}) %collective-permute-start.13) | collective-permute-done | bytes 288 | tf_op jit(solution)/shard_map/ppermute | solution.py:104
  64.7 0.5 maximum_maximum_fusion.1
  (31 shorter events, 0.2 us)
Async XLA Ops:
  0.0 2.4 %copy-start = (s32[64]{0:T(128)S(1)}, s32[64]{0:T(128)}, u32[]{:S(2)}) copy-start(s32[64]{0:T(128)} %param.4) | copy-start | bytes 772
  0.0 2.4 %copy-start.1 = (s32[64]{0:T(128)S(1)}, s32[64]{0:T(128)}, u32[]{:S(2)}) copy-start(s32[64]{0:T(128)} %param.5) | copy-start | bytes 772
  2.7 15.3 %collective-permute-start.3 = (bf16[64,4224]{1,0:T(8,128)(2,1)S(1)}, bf16[64,4224]{1,0:T(8,128)(2,1)S(1)}, u32[]{:S(2)}, u32[]{:S(2)}) collective-permute-start(bf16[64,4224]{1,0:T(8,128)(2,1)S(1)} %select_convert_fusion), channel_id=1, source_target_pairs={{0,16},{8,24},{16,0},{24,8},{1,17},{9,25},{17,1},{25,9},{2,18},{10... | collective-permute-start | bytes 1622024 | tf_op jit(solution)/shard_map/ppermute | solution.py:69
  5.8 13.7 %collective-permute-start = (bf16[64,4224]{1,0:T(8,128)(2,1)S(1)}, bf16[64,4224]{1,0:T(8,128)(2,1)S(1)}, u32[]{:S(2)}, u32[]{:S(2)}) collective-permute-start(bf16[64,4224]{1,0:T(8,128)(2,1)S(1)} %select_convert_fusion), channel_id=1, source_target_pairs={{0,2},{2,4},{4,6},{6,7},{7,5},{5,3},{3,1},{1,0},{8,10},{10,12},{12... | collective-permute-start | bytes 1622024 | tf_op jit(solution)/shard_map/ppermute | solution.py:60
  7.4 13.9 %collective-permute-start.7 = (bf16[64,4224]{1,0:T(8,128)(2,1)S(1)}, bf16[64,4224]{1,0:T(8,128)(2,1)S(1)}, u32[]{:S(2)}, u32[]{:S(2)}) collective-permute-start(bf16[64,4224]{1,0:T(8,128)(2,1)S(1)} %select_convert_fusion), channel_id=1, source_target_pairs={{2,0},{4,2},{6,4},{7,6},{5,7},{3,5},{1,3},{0,1},{10,8},{12,10},{14... | collective-permute-start | bytes 1622024 | tf_op jit(solution)/shard_map/ppermute | solution.py:60
  7.8 14.2 %collective-permute-start.2 = (bf16[64,4224]{1,0:T(8,128)(2,1)S(1)}, bf16[64,4224]{1,0:T(8,128)(2,1)S(1)}, u32[]{:S(2)}, u32[]{:S(2)}) collective-permute-start(bf16[64,4224]{1,0:T(8,128)(2,1)S(1)} %select_convert_fusion), channel_id=1, source_target_pairs={{0,8},{8,0},{16,24},{24,16},{1,9},{9,1},{17,25},{25,17},{2,10},{10... | collective-permute-start | bytes 1622024 | tf_op jit(solution)/shard_map/ppermute | solution.py:70
  18.1 3.9 %collective-permute-start.4 = (bf16[64,4224]{1,0:T(8,128)(2,1)S(1)}, bf16[64,4224]{1,0:T(8,128)(2,1)S(1)}, u32[]{:S(2)}, u32[]{:S(2)}) collective-permute-start(bf16[64,4224]{1,0:T(8,128)(2,1)S(1)} %collective-permute-done.3), channel_id=1, source_target_pairs={{0,8},{8,0},{16,24},{24,16},{1,9},{9,1},{17,25},{25,17},{2,10},{10... | collective-permute-start | bytes 1622024 | tf_op jit(solution)/shard_map/ppermute | solution.py:71
  19.5 13.2 %collective-permute-start.1 = (bf16[64,4224]{1,0:T(8,128)(2,1)S(1)}, bf16[64,4224]{1,0:T(8,128)(2,1)S(1)}, u32[]{:S(2)}, u32[]{:S(2)}) collective-permute-start(bf16[64,4224]{1,0:T(8,128)(2,1)S(1)} %collective-permute-done), channel_id=1, source_target_pairs={{0,2},{2,4},{4,6},{6,7},{7,5},{5,3},{3,1},{1,0},{8,10},{10,12},{12... | collective-permute-start | bytes 1622024 | tf_op jit(solution)/shard_map/ppermute | solution.py:60
  21.3 15.1 %collective-permute-start.8 = (bf16[64,4224]{1,0:T(8,128)(2,1)S(1)}, bf16[64,4224]{1,0:T(8,128)(2,1)S(1)}, u32[]{:S(2)}, u32[]{:S(2)}) collective-permute-start(bf16[64,4224]{1,0:T(8,128)(2,1)S(1)} %collective-permute-done.7), channel_id=1, source_target_pairs={{2,0},{4,2},{6,4},{7,6},{5,7},{3,5},{1,3},{0,1},{10,8},{12,10},{14... | collective-permute-start | bytes 1622024 | tf_op jit(solution)/shard_map/ppermute | solution.py:60
  33.0 12.6 %collective-permute-start.5 = (bf16[64,4224]{1,0:T(8,128)(2,1)S(1)}, bf16[64,4224]{1,0:T(8,128)(2,1)S(1)}, u32[]{:S(2)}, u32[]{:S(2)}) collective-permute-start(bf16[64,4224]{1,0:T(8,128)(2,1)S(1)} %collective-permute-done.1), channel_id=1, source_target_pairs={{0,2},{2,4},{4,6},{6,7},{7,5},{5,3},{3,1},{1,0},{8,10},{10,12},{12... | collective-permute-start | bytes 1622024 | tf_op jit(solution)/shard_map/ppermute | solution.py:60
  36.4 12.4 %collective-permute-start.9 = (bf16[64,4224]{1,0:T(8,128)(2,1)S(1)}, bf16[64,4224]{1,0:T(8,128)(2,1)S(1)}, u32[]{:S(2)}, u32[]{:S(2)}) collective-permute-start(bf16[64,4224]{1,0:T(8,128)(2,1)S(1)} %collective-permute-done.8), channel_id=1, source_target_pairs={{2,0},{4,2},{6,4},{7,6},{5,7},{3,5},{1,3},{0,1},{10,8},{12,10},{14... | collective-permute-start | bytes 1622024 | tf_op jit(solution)/shard_map/ppermute | solution.py:60
  49.7 8.3 %collective-permute-start.6 = (bf16[40,4224]{1,0:T(8,128)(2,1)S(1)}, bf16[40,4224]{1,0:T(8,128)(2,1)S(1)}, u32[]{:S(2)}, u32[]{:S(2)}) collective-permute-start(bf16[40,4224]{1,0:T(8,128)(2,1)S(1)} %slice.124), channel_id=1, source_target_pairs={{0,2},{2,4},{4,6},{6,7},{7,5},{5,3},{3,1},{1,0},{8,10},{10,12},{12... | collective-permute-start | bytes 1013768 | tf_op jit(solution)/shard_map/ppermute | solution.py:60
  51.4 5.7 %collective-permute-start.10 = (bf16[24,4224]{1,0:T(8,128)(2,1)S(1)}, bf16[24,4224]{1,0:T(8,128)(2,1)S(1)}, u32[]{:S(2)}, u32[]{:S(2)}) collective-permute-start(bf16[24,4224]{1,0:T(8,128)(2,1)S(1)} %slice.137), channel_id=1, source_target_pairs={{2,0},{4,2},{6,4},{7,6},{5,7},{3,5},{1,3},{0,1},{10,8},{12,10},{14... | collective-permute-start | bytes 608264 | tf_op jit(solution)/shard_map/ppermute | solution.py:60
  59.1 2.7 %collective-permute-start.11 = (f32[64]{0:T(128)S(1)}, f32[64]{0:T(128)S(1)}, u32[]{:S(2)}, u32[]{:S(2)}) collective-permute-start(f32[64]{0:T(128)S(1)} %get-tuple-element.33), channel_id=1, source_target_pairs={{0,8},{8,0},{16,24},{24,16},{1,9},{9,1},{17,25},{25,17},{2,10},{10... | collective-permute-start | bytes 776 | tf_op jit(solution)/shard_map/ppermute | solution.py:104
  59.1 4.2 %collective-permute-start.12 = (f32[64]{0:T(128)S(1)}, f32[64]{0:T(128)S(1)}, u32[]{:S(2)}, u32[]{:S(2)}) collective-permute-start(f32[64]{0:T(128)S(1)} %get-tuple-element.35), channel_id=1, source_target_pairs={{0,16},{8,24},{16,0},{24,8},{1,17},{9,25},{17,1},{25,9},{2,18},{10... | collective-permute-start | bytes 776 | tf_op jit(solution)/shard_map/ppermute | solution.py:104
  61.7 3.0 %collective-permute-start.13 = (f32[64]{0:T(128)S(1)}, f32[64]{0:T(128)S(1)}, u32[]{:S(2)}, u32[]{:S(2)}) collective-permute-start(f32[64]{0:T(128)S(1)} %get-tuple-element.34), channel_id=1, source_target_pairs={{0,24},{8,16},{16,8},{24,0},{1,25},{9,17},{17,9},{25,1},{2,26},{10... | collective-permute-start | bytes 776 | tf_op jit(solution)/shard_map/ppermute | solution.py:104

commit v12 on v1

v12 whole, which is shorter than its diff:
```python
import math

import jax
import jax.numpy as jnp
from jax import lax
from jax.sharding import PartitionSpec as P

D = 4096
TAG_WIDTH = 128
ORDER_SPAN = 8192.0


def tag_labels(payload):
    high = payload[:, D].astype(jnp.float32)
    low = payload[:, D + 1].astype(jnp.float32)
    return high * 128.0 + low


def block_best(left_rows, left_labels, payload):
    scores = jnp.einsum("id,jd->ij", left_rows, payload[:, :D], preferred_element_type=jnp.float32)
    right_labels = tag_labels(payload)
    same_cluster = jnp.floor(left_labels[:, None] / ORDER_SPAN) == jnp.floor(right_labels[None, :] / ORDER_SPAN)
    earlier = same_cluster & (right_labels[None, :] < left_labels[:, None])
    return jnp.max(jnp.where(earlier, scores, jnp.float32(-1.0)), axis=1)


def per_device(embeddings, cluster_ids, row_index):
    group_count = lax.axis_size("grp")
    block_count = lax.axis_size("blk")
    rows_here = embeddings.shape[0]
    widened = embeddings.astype(jnp.float32)
    square_sum = jnp.sum(widened * widened, axis=1, keepdims=True)
    scale = lax.rsqrt(square_sum / D + 1e-06)
    high = (cluster_ids * 64 + row_index // 128).astype(jnp.float32)[:, None]
    low = (row_index % 128).astype(jnp.float32)[:, None]
    column = jnp.arange(D + TAG_WIDTH)[None, :]
    padded = jnp.pad(widened, ((0, 0), (0, TAG_WIDTH)))
    tags = jnp.where(column == D, high, jnp.where(column == D + 1, low, 0.0))
    payload = jnp.where(column < D, padded * scale / math.sqrt(D), tags).astype(jnp.bfloat16)

    lo = 2 if block_count % 2 == 0 else 1
    line_count = block_count // lo
    mesh_axes = ("grp", "blk")

    def xor_pairs(dg, dl):
        return [(g * block_count + b, (g ^ dg) * block_count + (b ^ dl))
                for g in range(group_count) for b in range(block_count)]

    def line_pairs(step, up):
        pairs = []
        for part in range(lo):
            for h in range(line_count):
                if up and step - 1 <= h <= line_count - 2:
                    pairs.append((h * lo + part, (h + 1) * lo + part))
                if not up and 1 <= h <= line_count - step:
                    pairs.append((h * lo + part, (h - 1) * lo + part))
        return pairs

    chains = [[payload, None, [], True], [payload, None, [], False]]
    line_steps = line_count - 1
    my_line = lax.axis_index("blk") // lo
    if line_steps >= 1:
        for chain in chains:
            chain[0] = lax.ppermute(chain[0], "blk", line_pairs(1, chain[3]))
            chain[2].append((chain[0], 1))

    if group_count == 4 and lo == 2:
        half = rows_here // 2
        beside_x = lax.ppermute(payload, "blk", [(b, b ^ 1) for b in range(block_count)])
        beside_y = lax.ppermute(payload, "grp", [(g, g ^ 2) for g in range(group_count)])
        far_top = lax.ppermute(beside_x[:half], "grp", [(g, g ^ 2) for g in range(group_count)])
        far_bottom = lax.ppermute(beside_y[half:], "blk", [(b, b ^ 1) for b in range(block_count)])
        far = jnp.concatenate([far_top, far_bottom], axis=0)
        same_core = [payload, beside_x, beside_y, far]
        other_core = [lax.ppermute(block, "grp", [(g, g ^ 1) for g in range(group_count)]) for block in same_core]
        offsets = [(0, 0), (0, 1), (2, 0), (2, 1), (1, 0), (1, 1), (3, 0), (3, 1)]
        left_payload = jnp.concatenate(same_core + other_core, axis=0)
    else:
        offsets = [(dg, dl) for dg in range(group_count) for dl in range(lo)]
        blocks = []
        for dg, dl in offsets:
            if dg == 0 and dl == 0:
                blocks.append(payload)
            else:
                pairs = [(((g + dg) % group_count) * block_count + (b ^ dl), g * block_count + b)
                         for g in range(group_count) for b in range(block_count)]
                blocks.append(lax.ppermute(payload, mesh_axes, pairs))
        left_payload = jnp.concatenate(blocks, axis=0)
    left_labels = tag_labels(left_payload)
    left_rows = left_payload[:, :D]

    def fold(best, blocks, up):
        for block, step in blocks:
            tile = block_best(left_rows, left_labels, block)
            if step:
                valid = my_line >= step if up else my_line + step <= line_count - 1
                tile = jnp.where(valid, tile, jnp.float32(-1.0))
            best = tile if best is None else jnp.maximum(best, tile)
        return best

    best = block_best(left_rows, left_labels, payload)
    for step in range(2, line_steps + 1):
        for chain in chains:
            visiting, chain_best, pending, up = chain
            visiting = lax.ppermute(visiting, "blk", line_pairs(step, up))
            chain_best = fold(chain_best, pending, up)
            visiting, chain_best = lax.optimization_barrier((visiting, chain_best))
            chain[0], chain[1], chain[2] = visiting, chain_best, [(visiting, step)]
    for visiting, chain_best, pending, up in chains:
        chain_best = fold(chain_best, pending, up)
        if chain_best is not None:
            best = jnp.maximum(best, chain_best)

    best = best.reshape(len(offsets), rows_here)
    result = best[0]
    for k in range(1, len(offsets)):
        dg, dl = offsets[k]
        if group_count == 4 and lo == 2:
            pairs = xor_pairs(dg, dl)
        else:
            pairs = [(g * block_count + b, ((g + dg) % group_count) * block_count + (b ^ dl))
                     for g in range(group_count) for b in range(block_count)]
        result = jnp.maximum(result, lax.ppermute(best[k], mesh_axes, pairs))
    return result


def solution(mesh):
    return jax.shard_map(
        per_device,
        mesh=mesh,
        in_specs=(P(("grp", "blk"), None), P(("grp", "blk")), P(("grp", "blk"))),
        out_specs=P(("grp", "blk")),
        check_vma=False,
    )
```

time: 129 us -> 76 us (0.59)
  waiting for transfers between devices: 77.5 us -> 25.1 us
  blocking collectives: 24.5 us -> 0 us
  starting transfers between devices: 0.04 us -> 24.1 us
  between operations: 14.8 us -> 0.33 us
  matrix products: 4.21 us -> 12.1 us
  local copies, waits for them, and re-layouts: 2.65 us -> 6.6 us
  other arithmetic: 4.62 us -> 7.51 us
    all_gather x2 -> x0, waiting for transfers between devices: 76.8 us -> none  [the longest x1 75 us: per_device(): right_rows = lax.all_gather(unit_rows, 'blk', axis=0, tiled=True)]
    ppermute x0 -> x21, waiting for transfers between devices: none -> 25.1 us  [the longest x4 14.1 us: per_device(): visiting = lax.ppermute(visiting, 'blk', line_pairs(step, up))]
    ppermute x0 -> x21, starting transfers between devices: none -> 24.1 us  [the longest x7 6.82 us: per_device(): result = jnp.maximum(result, lax.ppermute(best[k], mesh_axes, pairs))]
    unnamed x2 -> x0, blocking collectives: 18.2 us -> none
    dot_general x1 -> x7, matrix products: 4.21 us -> 12.1 us  [block_best(): jnp.einsum('id,jd->ij', left_rows, payload[:, :D], preferred_element_type...]
    all_to_all x1 -> x0, blocking collectives: 6.31 us -> none  [per_device(): lax.all_to_all(partial, 'grp', split_axis=0, concat_axis=0, tiled=True)]
    unnamed x4 -> x11, local copies, waits for them, and re-layouts: 2.57 us -> 5.66 us
    floor x0 -> x8, other arithmetic: none -> 1.45 us  [the longest x1 1.41 us: block_best(): jnp.floor(left_labels[:, None] / ORDER_SPAN)]
  transfers between devices with their start and end apart: 2 -> 21, of which waited for: 2 -> 7; matrix products, arithmetic and copies ran while one was open for 3% -> 26% of each run, Pallas kernels for 0% -> 0%
where the time goes in v12:
time: 76 us; the launch traced here: 75.7 us
  waiting for transfers between devices  25.1 us (33%)
  starting transfers between devices  24.1 us (32%)
  matrix products  12.1 us (16%)
  other arithmetic  7.51 us (10%)
  local copies, waits for them, and re-layouts  6.6 us (9%)
    ppermute x4, waiting for transfers between devices, per_device(): visiting = lax.ppermute(visiting, 'blk', line_pairs(step, up))  14.1 us
    dot_general x7, matrix products, block_best(): jnp.einsum('id,jd->ij', left_rows, payload[:, :D], preferred_element_type...  12.1 us
    ppermute x7, starting transfers between devices, per_device(): result = jnp.maximum(result, lax.ppermute(best[k], mesh_axes, pairs))  6.82 us
    unnamed x11, local copies, waits for them, and re-layouts  5.66 us
    ppermute x1, waiting for transfers between devices, per_device(): lax.ppermute(payload, 'blk', [(b, b ^ 1) for b in range(block_count)])  5.65 us
    ppermute x2, starting transfers between devices, per_device(): chain[0] = lax.ppermute(chain[0], 'blk', line_pairs(1, chain[3]))  4.79 us
    ppermute x2, waiting for transfers between devices, per_device(): chain[0] = lax.ppermute(chain[0], 'blk', line_pairs(1, chain[3]))  3.99 us
    ppermute x4, starting transfers between devices, per_device(): visiting = lax.ppermute(visiting, 'blk', line_pairs(step, up))  3.96 us
  transfers between devices with their start and end apart: 21, of which 7 were waited for; matrix products, arithmetic and copies ran while one was open for 26% of the time, Pallas kernels for 0%

profile of v12, /device:TPU:0, one launch (start us, length us, event | category | flops | bytes accessed | tf_op | source)
XLA Modules:
  0.0 75.7 jit_solution(5438189748762416108)
XLA Ops:
  0.0 1.1 %convert_element_type.178 = f32[64,4096]{1,0:T(8,128)S(1)} convert(bf16[64,4096]{1,0:T(8,128)(2,1)} %param.3) | non-fusion elementwise | flops 262144 | bytes 1572864 | tf_op jit(solution)/shard_map/convert_element_type | solution.py:31
  1.1 1.2 %multiply_reduce_fusion = f32[64]{0:T(128)S(1)} fusion(bf16[64,4096]{1,0:T(8,128)(2,1)} %param.3), kind=kLoop, calls=%fused_computation.29 | loop fusion | flops 786368 | bytes 524544 | tf_op jit(solution)/shard_map/reduce_sum | solution.py:32
  2.4 0.7 add_convert_fusion
  3.1 1.2 %constant_dynamic-update-slice_fusion.8 = (bf16[512,4224]{1,0:T(8,128)(2,1)}, bf16[64,4224]{1,0:T(8,128)(2,1)S(1)}) fusion(bf16[64]{0:T(256)(128)(2,1)S(1)} %get-tuple-element.33, pred[4224]{0:T(1024)(128)(4,1)S(1)} %get-tuple-element.34, bf16[64]{0:T(256)(128)(2,1)S(1)} %get-tuple-element.32, pred[4224]{0:T(1024)(128)(4,1)S(1)} %get-tuple-element.35, ...), kind=kLoop, calls=%fused_computation.56 | loop fusion | flops 1351679 | bytes 2143104
  4.3 3.0 %collective-permute-start = (bf16[64,4224]{1,0:T(8,128)(2,1)S(1)}, bf16[64,4224]{1,0:T(8,128)(2,1)S(1)}, u32[]{:S(2)}, u32[]{:S(2)}) collective-permute-start(bf16[64,4224]{1,0:T(8,128)(2,1)S(1)} %get-tuple-element.24), channel_id=1, source_target_pairs={{0,1},{1,0},{2,3},{3,2},{4,5},{5,4},{6,7},{7,6},{8,9},{9,8},{10,11... | collective-permute-start | bytes 1622024 | tf_op jit(solution)/shard_map/ppermute | solution.py:69
  7.2 1.5 %collective-permute-start.1 = (bf16[64,4224]{1,0:T(8,128)(2,1)S(1)}, bf16[64,4224]{1,0:T(8,128)(2,1)S(1)}, u32[]{:S(2)}, u32[]{:S(2)}) collective-permute-start(bf16[64,4224]{1,0:T(8,128)(2,1)S(1)} %get-tuple-element.24), channel_id=1, source_target_pairs={{0,16},{8,24},{16,0},{24,8},{1,17},{9,25},{17,1},{25,9},{2,18},{10... | collective-permute-start | bytes 1622024 | tf_op jit(solution)/shard_map/ppermute | solution.py:70
  8.8 3.5 %collective-permute-start.8 = (bf16[64,4224]{1,0:T(8,128)(2,1)S(1)}, bf16[64,4224]{1,0:T(8,128)(2,1)S(1)}, u32[]{:S(2)}, u32[]{:S(2)}) collective-permute-start(bf16[64,4224]{1,0:T(8,128)(2,1)S(1)} %get-tuple-element.24), channel_id=1, source_target_pairs={{0,2},{2,4},{4,6},{1,3},{3,5},{5,7},{8,10},{10,12},{12,14},{9,11},... | collective-permute-start | bytes 1622024 | tf_op jit(solution)/shard_map/ppermute | solution.py:64
  12.3 1.3 %collective-permute-start.11 = (bf16[64,4224]{1,0:T(8,128)(2,1)S(1)}, bf16[64,4224]{1,0:T(8,128)(2,1)S(1)}, u32[]{:S(2)}, u32[]{:S(2)}) collective-permute-start(bf16[64,4224]{1,0:T(8,128)(2,1)S(1)} %get-tuple-element.24), channel_id=1, source_target_pairs={{2,0},{4,2},{6,4},{3,1},{5,3},{7,5},{10,8},{12,10},{14,12},{11,9},... | collective-permute-start | bytes 1622024 | tf_op jit(solution)/shard_map/ppermute | solution.py:64
  13.7 0.2 add_reduce_fusion.6
  13.9 5.6 %collective-permute-done = bf16[64,4224]{1,0:T(8,128)(2,1)S(1)} collective-permute-done((bf16[64,4224]{1,0:T(8,128)(2,1)S(1)}, bf16[64,4224]{1,0:T(8,128)(2,1)S(1)}, u32[]{:S(2)}, u32[]{:S(2)}) %collective-permute-start) | collective-permute-done | bytes 540704 | tf_op jit(solution)/shard_map/ppermute | solution.py:69
  19.5 1.8 %collective-permute-start.2 = (bf16[32,4224]{1,0:T(8,128)(2,1)S(1)}, bf16[32,4224]{1,0:T(8,128)(2,1)S(1)}, u32[]{:S(2)}, u32[]{:S(2)}) collective-permute-start(bf16[32,4224]{1,0:T(8,128)(2,1)S(1)} %slice.144), channel_id=1, source_target_pairs={{0,16},{8,24},{16,0},{24,8},{1,17},{9,25},{17,1},{25,9},{2,18},{10... | collective-permute-start | bytes 811016 | tf_op jit(solution)/shard_map/ppermute | solution.py:71
  21.4 1.6 %collective-permute-start.3 = (bf16[32,4224]{1,0:T(8,128)(2,1)S(1)}, bf16[32,4224]{1,0:T(8,128)(2,1)S(1)}, u32[]{:S(2)}, u32[]{:S(2)}) collective-permute-start(bf16[32,4224]{1,0:T(8,128)(2,1)S(1)} %slice.145), channel_id=1, source_target_pairs={{0,1},{1,0},{2,3},{3,2},{4,5},{5,4},{6,7},{7,6},{8,9},{9,8},{10,11... | collective-permute-start | bytes 811016 | tf_op jit(solution)/shard_map/ppermute | solution.py:72
  22.9 0.2 collective-permute-done.8
  23.5 0.8 %constant_dynamic-update-slice_fusion.7 = bf16[512,4224]{1,0:T(8,128)(2,1)} fusion(bf16[512,4224]{1,0:T(8,128)(2,1)} %get-tuple-element.23, bf16[64,4224]{1,0:T(8,128)(2,1)S(1)} %collective-permute-done), kind=kLoop, calls=%fused_computation.55 | loop fusion | bytes 1081344
  24.3 0.8 %constant_dynamic-update-slice_fusion.6 = bf16[512,4224]{1,0:T(8,128)(2,1)} fusion(bf16[512,4224]{1,0:T(8,128)(2,1)} %constant_dynamic-update-slice_fusion.7, bf16[64,4224]{1,0:T(8,128)(2,1)S(1)} %collective-permute-done.1), kind=kLoop, calls=%fused_computation.54 | loop fusion | bytes 1081344
  25.1 3.8 %collective-permute-done.11 = bf16[64,4224]{1,0:T(8,128)(2,1)S(1)} collective-permute-done((bf16[64,4224]{1,0:T(8,128)(2,1)S(1)}, bf16[64,4224]{1,0:T(8,128)(2,1)S(1)}, u32[]{:S(2)}, u32[]{:S(2)}) %collective-permute-start.11) | collective-permute-done | bytes 540704 | tf_op jit(solution)/shard_map/ppermute | solution.py:64
  28.9 0.2 add_reduce_fusion.2
  29.1 0.7 collective-permute-start.9
  29.8 0.7 constant_dynamic-update-slice_fusion.5
  30.5 1.3 %collective-permute-start.12 = (bf16[64,4224]{1,0:T(8,128)(2,1)S(1)}, bf16[64,4224]{1,0:T(8,128)(2,1)S(1)}, u32[]{:S(2)}, u32[]{:S(2)}) collective-permute-start(bf16[64,4224]{1,0:T(8,128)(2,1)S(1)} %collective-permute-done.11), channel_id=1, source_target_pairs={{2,0},{4,2},{3,1},{5,3},{10,8},{12,10},{11,9},{13,11},{18,16},{20,... | collective-permute-start | bytes 1622024 | tf_op jit(solution)/shard_map/ppermute | solution.py:105
  31.9 0.7 constant_dynamic-update-slice_fusion.4
  32.6 0.5 collective-permute-start.7
  33.1 0.8 %constant_dynamic-update-slice_fusion.3 = bf16[512,4224]{1,0:T(8,128)(2,1)} fusion(bf16[512,4224]{1,0:T(8,128)(2,1)} %constant_dynamic-update-slice_fusion.4, bf16[64,4224]{1,0:T(8,128)(2,1)S(1)} %collective-permute-done.4), kind=kLoop, calls=%fused_computation.51 | loop fusion | bytes 1081344
  33.9 0.8 %constant_dynamic-update-slice_fusion.2 = bf16[512,4224]{1,0:T(8,128)(2,1)} fusion(bf16[512,4224]{1,0:T(8,128)(2,1)} %constant_dynamic-update-slice_fusion.3, bf16[64,4224]{1,0:T(8,128)(2,1)S(1)} %collective-permute-done.5), kind=kLoop, calls=%fused_computation.50 | loop fusion | bytes 1081344
  34.8 0.8 %constant_dynamic-update-slice_fusion.1 = bf16[512,4224]{1,0:T(8,128)(2,1)} fusion(bf16[512,4224]{1,0:T(8,128)(2,1)} %constant_dynamic-update-slice_fusion.2, bf16[64,4224]{1,0:T(8,128)(2,1)S(1)} %collective-permute-done.6), kind=kLoop, calls=%fused_computation.49 | loop fusion | bytes 1081344
  35.6 0.8 %constant_dynamic-update-slice_fusion = bf16[512,4224]{1,0:T(8,128)(2,1)} fusion(bf16[512,4224]{1,0:T(8,128)(2,1)} %constant_dynamic-update-slice_fusion.1, bf16[64,4224]{1,0:T(8,128)(2,1)S(1)} %collective-permute-done.7), kind=kLoop, calls=%fused_computation.48 | loop fusion | bytes 1081344 | tf_op jit(solution)/shard_map/concatenate | solution.py:77
  36.5 1.4 %floor_reduce_fusion = (f32[512]{0:T(512)S(1)}, f32[512]{0:T(512)S(1)}) fusion(bf16[512,4224]{1,0:T(8,128)(2,1)} %constant_dynamic-update-slice_fusion), kind=kLoop, calls=%fused_computation.38 | loop fusion | flops 3072 | bytes 6144 | tf_op jit(solution)/shard_map/floor | solution.py:22
  37.9 3.7 %fusion.50 = f32[512]{0:T(512)S(1)} fusion(bf16[512,4224]{1,0:T(8,128)(2,1)} %constant_dynamic-update-slice_fusion, bf16[64,4224]{1,0:T(8,128)(2,1)S(1)} %collective-permute-done.8, f32[512]{0:T(512)S(1)} %get-tuple-element.22, f32[512]{0:T(512)S(1)} %get-tuple-element.21, f32[64]{0:T(128)S(1)} %add_reduce_fusion.5, f32[64]{0:T(128)S(1)} %multiply_floor_fusion.5), kind=kOutput, calls=%fused_computation.26 | convolution fusion | flops 268598784 | bytes 4725760 | tf_op jit(solution)/shard_map/id,jd->ij/dot_general | solution.py:20
  41.6 0.2 add_reduce_fusion.4
  41.8 0.7 collective-permute-start.10
  42.5 1.4 %fusion.41 = f32[512]{0:T(512)S(1)} fusion(bf16[512,4224]{1,0:T(8,128)(2,1)S(1)} %bitcast.1, bf16[64,4224]{1,0:T(8,128)(2,1)S(1)} %collective-permute-done.11, f32[512]{0:T(512)S(1)} %get-tuple-element.22, f32[512]{0:T(512)S(1)} %get-tuple-element.21, f32[64]{0:T(128)S(1)} %add_reduce_fusion.2, f32[64]{0:T(128)S(1)} %multiply_floor_fusion.2), kind=kOutput, calls=%fused_computation.23 | convolution fusion | flops 268598784 | bytes 4725760 | tf_op jit(solution)/shard_map/id,jd->ij/dot_general | solution.py:20
  43.9 5.5 %collective-permute-done.12 = bf16[64,4224]{1,0:T(8,128)(2,1)S(1)} collective-permute-done((bf16[64,4224]{1,0:T(8,128)(2,1)S(1)}, bf16[64,4224]{1,0:T(8,128)(2,1)S(1)}, u32[]{:S(2)}, u32[]{:S(2)}) %collective-permute-start.12) | collective-permute-done | bytes 540704 | tf_op jit(solution)/shard_map/ppermute | solution.py:105
  49.6 1.3 %collective-permute-start.13 = (bf16[64,4224]{1,0:T(8,128)(2,1)S(1)}, bf16[64,4224]{1,0:T(8,128)(2,1)S(1)}, u32[]{:S(2)}, u32[]{:S(2)}) collective-permute-start(bf16[64,4224]{1,0:T(8,128)(2,1)S(1)} %collective-permute-done.12), channel_id=1, source_target_pairs={{2,0},{3,1},{10,8},{11,9},{18,16},{19,17},{26,24},{27,25}} | collective-permute-start | bytes 1622024 | tf_op jit(solution)/shard_map/ppermute | solution.py:105
  50.9 1.4 %fusion.47 = f32[512]{0:T(512)S(1)} fusion(bf16[512,4224]{1,0:T(8,128)(2,1)S(1)} %bitcast.1, bf16[64,4224]{1,0:T(8,128)(2,1)S(1)} %collective-permute-done.9, f32[512]{0:T(512)S(1)} %get-tuple-element.22, f32[512]{0:T(512)S(1)} %get-tuple-element.21, f32[64]{0:T(128)S(1)} %add_reduce_fusion.4, f32[64]{0:T(128)S(1)} %multiply_floor_fusion.4), kind=kOutput, calls=%fused_computation.25 | convolution fusion | flops 268598784 | bytes 4725760 | tf_op jit(solution)/shard_map/id,jd->ij/dot_general | solution.py:20
  52.4 1.4 %fusion.38 = f32[512]{0:T(512)S(1)} fusion(bf16[512,4224]{1,0:T(8,128)(2,1)S(1)} %bitcast.1, bf16[64,4224]{1,0:T(8,128)(2,1)S(1)} %collective-permute-done.12, f32[512]{0:T(512)S(1)} %get-tuple-element.22, f32[512]{0:T(512)S(1)} %get-tuple-element.21, f32[64]{0:T(128)S(1)} %add_reduce_fusion.1, f32[64]{0:T(128)S(1)} %multiply_floor_fusion.1), kind=kOutput, calls=%fused_computation.22 | convolution fusion | flops 268598784 | bytes 4725760 | tf_op jit(solution)/shard_map/id,jd->ij/dot_general | solution.py:20
  53.8 1.4 %fusion.53 = f32[512]{0:T(512)S(1)} fusion(bf16[512,4224]{1,0:T(8,128)(2,1)S(1)} %bitcast.1, bf16[64,4224]{1,0:T(8,128)(2,1)S(1)} %get-tuple-element.24, f32[512]{0:T(512)S(1)} %get-tuple-element.22, f32[512]{0:T(512)S(1)} %get-tuple-element.21, f32[64]{0:T(128)S(1)} %add_reduce_fusion.6, f32[64]{0:T(128)S(1)} %multiply_floor_fusion.6), kind=kOutput, calls=%fused_computation.27 | convolution fusion | flops 268598784 | bytes 4725760 | tf_op jit(solution)/shard_map/id,jd->ij/dot_general | solution.py:20
  55.2 0.2 add_reduce_fusion.3
  55.4 1.4 %fusion.44 = f32[512]{0:T(512)S(1)} fusion(bf16[512,4224]{1,0:T(8,128)(2,1)S(1)} %bitcast.1, bf16[64,4224]{1,0:T(8,128)(2,1)S(1)} %collective-permute-done.10, f32[512]{0:T(512)S(1)} %get-tuple-element.22, f32[512]{0:T(512)S(1)} %get-tuple-element.21, f32[64]{0:T(128)S(1)} %add_reduce_fusion.3, f32[64]{0:T(128)S(1)} %multiply_floor_fusion.3), kind=kOutput, calls=%fused_computation.24 | convolution fusion | flops 268598784 | bytes 4725760 | tf_op jit(solution)/shard_map/id,jd->ij/dot_general | solution.py:20
  56.8 8.6 %collective-permute-done.13 = bf16[64,4224]{1,0:T(8,128)(2,1)S(1)} collective-permute-done((bf16[64,4224]{1,0:T(8,128)(2,1)S(1)}, bf16[64,4224]{1,0:T(8,128)(2,1)S(1)}, u32[]{:S(2)}, u32[]{:S(2)}) %collective-permute-start.13) | collective-permute-done | bytes 540704 | tf_op jit(solution)/shard_map/ppermute | solution.py:105
  65.5 1.4 %fusion.35 = f32[512]{0:T(512)S(1)} fusion(bf16[512,4224]{1,0:T(8,128)(2,1)S(1)} %bitcast.1, bf16[64,4224]{1,0:T(8,128)(2,1)S(1)} %collective-permute-done.13, f32[512]{0:T(512)S(1)} %get-tuple-element.22, f32[512]{0:T(512)S(1)} %get-tuple-element.21, f32[64]{0:T(128)S(1)} %add_reduce_fusion, f32[64]{0:T(128)S(1)} %multiply_floor_fusion), kind=kOutput, calls=%fused_computation.21 | convolution fusion | flops 268598784 | bytes 4725760 | tf_op jit(solution)/shard_map/id,jd->ij/dot_general | solution.py:20
  67.0 0.5 collective-permute-start.14
  67.6 0.4 collective-permute-start.15
  68.0 2.5 %collective-permute-start.16 = (f32[64]{0:T(128)S(1)}, f32[64]{0:T(128)S(1)}, u32[]{:S(2)}, u32[]{:S(2)}) collective-permute-start(f32[64]{0:T(128)S(1)} %get-tuple-element.30), channel_id=1, source_target_pairs={{0,17},{1,16},{2,19},{3,18},{4,21},{5,20},{6,23},{7,22},{8,25},{9,... | collective-permute-start | bytes 776 | tf_op jit(solution)/shard_map/ppermute | solution.py:123
  70.5 0.6 collective-permute-start.18
  71.2 2.7 %collective-permute-start.20 = (f32[64]{0:T(128)S(1)}, f32[64]{0:T(128)S(1)}, u32[]{:S(2)}, u32[]{:S(2)}) collective-permute-start(f32[64]{0:T(128)S(1)} %get-tuple-element.26), channel_id=1, source_target_pairs={{0,25},{1,24},{2,27},{3,26},{4,29},{5,28},{6,31},{7,30},{8,17},{9,... | collective-permute-start | bytes 776 | tf_op jit(solution)/shard_map/ppermute | solution.py:123
  73.9 0.3 collective-permute-done.19
  74.2 1.0 %collective-permute-done.20 = f32[64]{0:T(128)S(1)} collective-permute-done((f32[64]{0:T(128)S(1)}, f32[64]{0:T(128)S(1)}, u32[]{:S(2)}, u32[]{:S(2)}) %collective-permute-start.20) | collective-permute-done | bytes 288 | tf_op jit(solution)/shard_map/ppermute | solution.py:123
  75.2 0.5 maximum_maximum_fusion.1
  (46 shorter events, 1.0 us)
Async XLA Ops:
  4.3 15.2 %collective-permute-start = (bf16[64,4224]{1,0:T(8,128)(2,1)S(1)}, bf16[64,4224]{1,0:T(8,128)(2,1)S(1)}, u32[]{:S(2)}, u32[]{:S(2)}) collective-permute-start(bf16[64,4224]{1,0:T(8,128)(2,1)S(1)} %get-tuple-element.24), channel_id=1, source_target_pairs={{0,1},{1,0},{2,3},{3,2},{4,5},{5,4},{6,7},{7,6},{8,9},{9,8},{10,11... | collective-permute-start | bytes 1622024 | tf_op jit(solution)/shard_map/ppermute | solution.py:69
  7.2 14.1 %collective-permute-start.1 = (bf16[64,4224]{1,0:T(8,128)(2,1)S(1)}, bf16[64,4224]{1,0:T(8,128)(2,1)S(1)}, u32[]{:S(2)}, u32[]{:S(2)}) collective-permute-start(bf16[64,4224]{1,0:T(8,128)(2,1)S(1)} %get-tuple-element.24), channel_id=1, source_target_pairs={{0,16},{8,24},{16,0},{24,8},{1,17},{9,25},{17,1},{25,9},{2,18},{10... | collective-permute-start | bytes 1622024 | tf_op jit(solution)/shard_map/ppermute | solution.py:70
  8.8 14.4 %collective-permute-start.8 = (bf16[64,4224]{1,0:T(8,128)(2,1)S(1)}, bf16[64,4224]{1,0:T(8,128)(2,1)S(1)}, u32[]{:S(2)}, u32[]{:S(2)}) collective-permute-start(bf16[64,4224]{1,0:T(8,128)(2,1)S(1)} %get-tuple-element.24), channel_id=1, source_target_pairs={{0,2},{2,4},{4,6},{1,3},{3,5},{5,7},{8,10},{10,12},{12,14},{9,11},... | collective-permute-start | bytes 1622024 | tf_op jit(solution)/shard_map/ppermute | solution.py:64
  12.3 20.3 %collective-permute-start.4 = (bf16[64,4224]{1,0:T(8,128)(2,1)S(1)}, bf16[64,4224]{1,0:T(8,128)(2,1)S(1)}, u32[]{:S(2)}, u32[]{:S(2)}) collective-permute-start(bf16[64,4224]{1,0:T(8,128)(2,1)S(1)} %get-tuple-element.24), channel_id=1, source_target_pairs={{0,8},{8,0},{16,24},{24,16},{1,9},{9,1},{17,25},{25,17},{2,10},{10... | collective-permute-start | bytes 1622024 | tf_op jit(solution)/shard_map/ppermute | solution.py:75
  12.3 16.6 %collective-permute-start.11 = (bf16[64,4224]{1,0:T(8,128)(2,1)S(1)}, bf16[64,4224]{1,0:T(8,128)(2,1)S(1)}, u32[]{:S(2)}, u32[]{:S(2)}) collective-permute-start(bf16[64,4224]{1,0:T(8,128)(2,1)S(1)} %get-tuple-element.24), channel_id=1, source_target_pairs={{2,0},{4,2},{6,4},{3,1},{5,3},{7,5},{10,8},{12,10},{14,12},{11,9},... | collective-permute-start | bytes 1622024 | tf_op jit(solution)/shard_map/ppermute | solution.py:64
  19.5 9.6 %collective-permute-start.2 = (bf16[32,4224]{1,0:T(8,128)(2,1)S(1)}, bf16[32,4224]{1,0:T(8,128)(2,1)S(1)}, u32[]{:S(2)}, u32[]{:S(2)}) collective-permute-start(bf16[32,4224]{1,0:T(8,128)(2,1)S(1)} %slice.144), channel_id=1, source_target_pairs={{0,16},{8,24},{16,0},{24,8},{1,17},{9,25},{17,1},{25,9},{2,18},{10... | collective-permute-start | bytes 811016 | tf_op jit(solution)/shard_map/ppermute | solution.py:71
  21.4 9.1 %collective-permute-start.3 = (bf16[32,4224]{1,0:T(8,128)(2,1)S(1)}, bf16[32,4224]{1,0:T(8,128)(2,1)S(1)}, u32[]{:S(2)}, u32[]{:S(2)}) collective-permute-start(bf16[32,4224]{1,0:T(8,128)(2,1)S(1)} %slice.145), channel_id=1, source_target_pairs={{0,1},{1,0},{2,3},{3,2},{4,5},{5,4},{6,7},{7,6},{8,9},{9,8},{10,11... | collective-permute-start | bytes 811016 | tf_op jit(solution)/shard_map/ppermute | solution.py:72
  23.4 10.6 %collective-permute-start.5 = (bf16[64,4224]{1,0:T(8,128)(2,1)S(1)}, bf16[64,4224]{1,0:T(8,128)(2,1)S(1)}, u32[]{:S(2)}, u32[]{:S(2)}) collective-permute-start(bf16[64,4224]{1,0:T(8,128)(2,1)S(1)} %collective-permute-done), channel_id=1, source_target_pairs={{0,8},{8,0},{16,24},{24,16},{1,9},{9,1},{17,25},{25,17},{2,10},{10... | collective-permute-start | bytes 1622024 | tf_op jit(solution)/shard_map/ppermute | solution.py:75
  28.9 5.9 %collective-permute-start.6 = (bf16[64,4224]{1,0:T(8,128)(2,1)S(1)}, bf16[64,4224]{1,0:T(8,128)(2,1)S(1)}, u32[]{:S(2)}, u32[]{:S(2)}) collective-permute-start(bf16[64,4224]{1,0:T(8,128)(2,1)S(1)} %collective-permute-done.1), channel_id=1, source_target_pairs={{0,8},{8,0},{16,24},{24,16},{1,9},{9,1},{17,25},{25,17},{2,10},{10... | collective-permute-start | bytes 1622024 | tf_op jit(solution)/shard_map/ppermute | solution.py:75
  29.1 12.5 %collective-permute-start.9 = (bf16[64,4224]{1,0:T(8,128)(2,1)S(1)}, bf16[64,4224]{1,0:T(8,128)(2,1)S(1)}, u32[]{:S(2)}, u32[]{:S(2)}) collective-permute-start(bf16[64,4224]{1,0:T(8,128)(2,1)S(1)} %collective-permute-done.8), channel_id=1, source_target_pairs={{2,4},{4,6},{3,5},{5,7},{10,12},{12,14},{11,13},{13,15},{18,20},{2... | collective-permute-start | bytes 1622024 | tf_op jit(solution)/shard_map/ppermute | solution.py:105
  30.5 18.9 %collective-permute-start.12 = (bf16[64,4224]{1,0:T(8,128)(2,1)S(1)}, bf16[64,4224]{1,0:T(8,128)(2,1)S(1)}, u32[]{:S(2)}, u32[]{:S(2)}) collective-permute-start(bf16[64,4224]{1,0:T(8,128)(2,1)S(1)} %collective-permute-done.11), channel_id=1, source_target_pairs={{2,0},{4,2},{3,1},{5,3},{10,8},{12,10},{11,9},{13,11},{18,16},{20,... | collective-permute-start | bytes 1622024 | tf_op jit(solution)/shard_map/ppermute | solution.py:105
  32.6 3.0 %collective-permute-start.7 = (bf16[64,4224]{1,0:T(8,128)(2,1)S(1)}, bf16[64,4224]{1,0:T(8,128)(2,1)S(1)}, u32[]{:S(2)}, u32[]{:S(2)}) collective-permute-start(bf16[64,4224]{1,0:T(8,128)(2,1)S(1)} %pad_maximum_fusion), channel_id=1, source_target_pairs={{0,8},{8,0},{16,24},{24,16},{1,9},{9,1},{17,25},{25,17},{2,10},{10... | collective-permute-start | bytes 1622024 | tf_op jit(solution)/shard_map/ppermute | solution.py:75
  36.5 6.0 %slice-start = ((s8[4325376]{0:T(1024)(128)(4,1)}), s8[4194304]{0:T(1024)(128)(4,1)S(1)}, s32[]{:S(2)}) async-start(s8[4325376]{0:T(1024)(128)(4,1)} %bitcast), calls=%async_computation | async-start | bytes 8388608
  37.9 4.6 %slice-start.1 = ((s8[4325376]{0:T(1024)(128)(4,1)}), s8[131072]{0:T(1024)(128)(4,1)S(1)}, s32[]{:S(2)}) async-start(s8[4325376]{0:T(1024)(128)(4,1)} %bitcast), calls=%async_computation.1 | async-start | bytes 262144
  41.8 13.4 %collective-permute-start.10 = (bf16[64,4224]{1,0:T(8,128)(2,1)S(1)}, bf16[64,4224]{1,0:T(8,128)(2,1)S(1)}, u32[]{:S(2)}, u32[]{:S(2)}) collective-permute-start(bf16[64,4224]{1,0:T(8,128)(2,1)S(1)} %collective-permute-done.9), channel_id=1, source_target_pairs={{4,6},{5,7},{12,14},{13,15},{20,22},{21,23},{28,30},{29,31}} | collective-permute-start | bytes 1622024 | tf_op jit(solution)/shard_map/ppermute | solution.py:105
  49.6 15.7 %collective-permute-start.13 = (bf16[64,4224]{1,0:T(8,128)(2,1)S(1)}, bf16[64,4224]{1,0:T(8,128)(2,1)S(1)}, u32[]{:S(2)}, u32[]{:S(2)}) collective-permute-start(bf16[64,4224]{1,0:T(8,128)(2,1)S(1)} %collective-permute-done.12), channel_id=1, source_target_pairs={{2,0},{3,1},{10,8},{11,9},{18,16},{19,17},{26,24},{27,25}} | collective-permute-start | bytes 1622024 | tf_op jit(solution)/shard_map/ppermute | solution.py:105
  67.0 4.2 %collective-permute-start.14 = (f32[64]{0:T(128)S(1)}, f32[64]{0:T(128)S(1)}, u32[]{:S(2)}, u32[]{:S(2)}) collective-permute-start(f32[64]{0:T(128)S(1)} %get-tuple-element.25), channel_id=1, source_target_pairs={{0,1},{1,0},{2,3},{3,2},{4,5},{5,4},{6,7},{7,6},{8,9},{9,8},{10,11... | collective-permute-start | bytes 776 | tf_op jit(solution)/shard_map/ppermute | solution.py:123
  67.6 3.6 %collective-permute-start.15 = (f32[64]{0:T(128)S(1)}, f32[64]{0:T(128)S(1)}, u32[]{:S(2)}, u32[]{:S(2)}) collective-permute-start(f32[64]{0:T(128)S(1)} %get-tuple-element.31), channel_id=1, source_target_pairs={{0,16},{1,17},{2,18},{3,19},{4,20},{5,21},{6,22},{7,23},{8,24},{9,... | collective-permute-start | bytes 776 | tf_op jit(solution)/shard_map/ppermute | solution.py:123
  68.0 5.9 %collective-permute-start.16 = (f32[64]{0:T(128)S(1)}, f32[64]{0:T(128)S(1)}, u32[]{:S(2)}, u32[]{:S(2)}) collective-permute-start(f32[64]{0:T(128)S(1)} %get-tuple-element.30), channel_id=1, source_target_pairs={{0,17},{1,16},{2,19},{3,18},{4,21},{5,20},{6,23},{7,22},{8,25},{9,... | collective-permute-start | bytes 776 | tf_op jit(solution)/shard_map/ppermute | solution.py:123
  70.5 3.3 %collective-permute-start.17 = (f32[64]{0:T(128)S(1)}, f32[64]{0:T(128)S(1)}, u32[]{:S(2)}, u32[]{:S(2)}) collective-permute-start(f32[64]{0:T(128)S(1)} %get-tuple-element.29), channel_id=1, source_target_pairs={{0,8},{1,9},{2,10},{3,11},{4,12},{5,13},{6,14},{7,15},{8,0},{9,1},... | collective-permute-start | bytes 776 | tf_op jit(solution)/shard_map/ppermute | solution.py:123
  70.5 3.3 %collective-permute-start.18 = (f32[64]{0:T(128)S(1)}, f32[64]{0:T(128)S(1)}, u32[]{:S(2)}, u32[]{:S(2)}) collective-permute-start(f32[64]{0:T(128)S(1)} %get-tuple-element.28), channel_id=1, source_target_pairs={{0,9},{1,8},{2,11},{3,10},{4,13},{5,12},{6,15},{7,14},{8,1},{9,0},... | collective-permute-start | bytes 776 | tf_op jit(solution)/shard_map/ppermute | solution.py:123
  71.2 3.0 %collective-permute-start.19 = (f32[64]{0:T(128)S(1)}, f32[64]{0:T(128)S(1)}, u32[]{:S(2)}, u32[]{:S(2)}) collective-permute-start(f32[64]{0:T(128)S(1)} %get-tuple-element.27), channel_id=1, source_target_pairs={{0,24},{1,25},{2,26},{3,27},{4,28},{5,29},{6,30},{7,31},{8,16},{9,... | collective-permute-start | bytes 776 | tf_op jit(solution)/shard_map/ppermute | solution.py:123
  71.2 3.9 %collective-permute-start.20 = (f32[64]{0:T(128)S(1)}, f32[64]{0:T(128)S(1)}, u32[]{:S(2)}, u32[]{:S(2)}) collective-permute-start(f32[64]{0:T(128)S(1)} %get-tuple-element.26), channel_id=1, source_target_pairs={{0,25},{1,24},{2,27},{3,26},{4,29},{5,28},{6,31},{7,30},{8,17},{9,... | collective-permute-start | bytes 776 | tf_op jit(solution)/shard_map/ppermute | solution.py:123

commit v13 on v7

--- a/solution.py
+++ b/solution.py
@@ -90,7 +90,6 @@
             visiting, best, pending = chain
             visiting = send(which, visiting, step)
             best = fold(best, pending)
-            visiting, best = lax.optimization_barrier((visiting, best))
             chain[0], chain[1], chain[2] = visiting, best, [visiting]
     best = None
     for _, chain_best, pending in chains:

time: 63 us -> 63 us (level)
  transfers between devices with their start and end apart: 14 -> 14, of which waited for: 9 -> 9; matrix products, arithmetic and copies ran while one was open for 13% -> 12% of each run, Pallas kernels for 0% -> 0%
where the time goes in v13:
time: 63 us; the launch traced here: 62.8 us
  waiting for transfers between devices  35.9 us (57%)
  starting transfers between devices  14.2 us (23%)
  matrix products  6.96 us (11%)
  other arithmetic  5.32 us (8%)
    ppermute x8, waiting for transfers between devices, send(): return lax.ppermute(visiting, 'blk', forward if which == 0 else backward)  22.9 us
    ppermute x1, waiting for transfers between devices, per_device(): across = lax.ppermute(payload, 'grp', partner_pairs(group_count, 2))  10.1 us
    ppermute x8, starting transfers between devices, send(): return lax.ppermute(visiting, 'blk', forward if which == 0 else backward)  8.35 us
    dot_general x9, matrix products, block_best(): jnp.einsum('id,jd->ij', left_rows, payload[:, :D], preferred_element_type...  6.96 us
    ppermute x1, starting transfers between devices, per_device(): across = lax.ppermute(payload, 'grp', partner_pairs(group_count, 2))  3.06 us
    ppermute x3, waiting for transfers between devices, per_device(): result = jnp.maximum(result, lax.ppermute(best[k], 'grp', pairs))  2.95 us
    ppermute x3, starting transfers between devices, per_device(): result = jnp.maximum(result, lax.ppermute(best[k], 'grp', pairs))  2.81 us
    add x9, other arithmetic, tag_labels(): return high * 128.0 + low  1.57 us
  transfers between devices with their start and end apart: 14, of which 9 were waited for; matrix products, arithmetic and copies ran while one was open for 12% of the time, Pallas kernels for 0%

profile of v13, /device:TPU:0, one launch (start us, length us, event | category | flops | bytes accessed | tf_op | source)
XLA Modules:
  0.0 62.8 jit_solution(9804441262036341182)
XLA Ops:
  0.0 1.1 %convert_element_type.222 = f32[64,4096]{1,0:T(8,128)S(1)} convert(bf16[64,4096]{1,0:T(8,128)(2,1)} %param.3) | non-fusion elementwise | flops 262144 | bytes 1572864 | tf_op jit(solution)/shard_map/convert_element_type | solution.py:41
  1.1 1.2 %multiply_reduce_fusion = f32[64]{0:T(128)S(1)} fusion(bf16[64,4096]{1,0:T(8,128)(2,1)} %param.3), kind=kLoop, calls=%fused_computation.22 | loop fusion | flops 786368 | bytes 524544 | tf_op jit(solution)/shard_map/reduce_sum | solution.py:42
  2.4 0.3 select_convert_fusion
  2.7 3.1 %collective-permute-start.1 = (bf16[64,4224]{1,0:T(8,128)(2,1)S(1)}, bf16[64,4224]{1,0:T(8,128)(2,1)S(1)}, u32[]{:S(2)}, u32[]{:S(2)}) collective-permute-start(bf16[64,4224]{1,0:T(8,128)(2,1)S(1)} %select_convert_fusion), channel_id=1, source_target_pairs={{0,16},{8,24},{16,0},{24,8},{1,17},{9,25},{17,1},{25,9},{2,18},{10... | collective-permute-start | bytes 1622024 | tf_op jit(solution)/shard_map/ppermute | solution.py:69
  5.8 1.6 %collective-permute-start.3 = (bf16[64,4224]{1,0:T(8,128)(2,1)S(1)}, bf16[64,4224]{1,0:T(8,128)(2,1)S(1)}, u32[]{:S(2)}, u32[]{:S(2)}) collective-permute-start(bf16[64,4224]{1,0:T(8,128)(2,1)S(1)} %select_convert_fusion), channel_id=1, source_target_pairs={{0,2},{2,4},{4,6},{6,7},{7,5},{5,3},{3,1},{1,0},{8,10},{10,12},{12... | collective-permute-start | bytes 1622024 | tf_op jit(solution)/shard_map/ppermute | solution.py:60
  7.4 0.4 collective-permute-start.7
  7.8 0.0 collective-permute-start
  7.8 0.2 add_reduce_fusion.6
  8.0 10.1 %collective-permute-done.1 = bf16[64,4224]{1,0:T(8,128)(2,1)S(1)} collective-permute-done((bf16[64,4224]{1,0:T(8,128)(2,1)S(1)}, bf16[64,4224]{1,0:T(8,128)(2,1)S(1)}, u32[]{:S(2)}, u32[]{:S(2)}) %collective-permute-start.1) | collective-permute-done | bytes 540704 | tf_op jit(solution)/shard_map/ppermute | solution.py:69
  18.1 1.5 %collective-permute-done.3 = bf16[64,4224]{1,0:T(8,128)(2,1)S(1)} collective-permute-done((bf16[64,4224]{1,0:T(8,128)(2,1)S(1)}, bf16[64,4224]{1,0:T(8,128)(2,1)S(1)}, u32[]{:S(2)}, u32[]{:S(2)}) %collective-permute-start.3) | collective-permute-done | bytes 540704 | tf_op jit(solution)/shard_map/ppermute | solution.py:60
  19.5 1.6 %collective-permute-start.4 = (bf16[64,4224]{1,0:T(8,128)(2,1)S(1)}, bf16[64,4224]{1,0:T(8,128)(2,1)S(1)}, u32[]{:S(2)}, u32[]{:S(2)}) collective-permute-start(bf16[64,4224]{1,0:T(8,128)(2,1)S(1)} %collective-permute-done.3), channel_id=1, source_target_pairs={{0,2},{2,4},{4,6},{6,7},{7,5},{5,3},{3,1},{1,0},{8,10},{10,12},{12... | collective-permute-start | bytes 1622024 | tf_op jit(solution)/shard_map/ppermute | solution.py:60
  21.1 0.2 add_reduce_fusion.5
  21.3 0.5 collective-permute-start.8
  21.8 0.2 add_reduce_fusion.2
  22.0 0.1 pad_maximum_fusion.4
  22.1 0.2 floor_reduce_fusion
  22.3 0.2 pad_maximum_fusion
  22.5 10.2 %collective-permute-done.4 = bf16[64,4224]{1,0:T(8,128)(2,1)S(1)} collective-permute-done((bf16[64,4224]{1,0:T(8,128)(2,1)S(1)}, bf16[64,4224]{1,0:T(8,128)(2,1)S(1)}, u32[]{:S(2)}, u32[]{:S(2)}) %collective-permute-start.4) | collective-permute-done | bytes 540704 | tf_op jit(solution)/shard_map/ppermute | solution.py:60
  32.8 1.8 %collective-permute-start.5 = (bf16[64,4224]{1,0:T(8,128)(2,1)S(1)}, bf16[64,4224]{1,0:T(8,128)(2,1)S(1)}, u32[]{:S(2)}, u32[]{:S(2)}) collective-permute-start(bf16[64,4224]{1,0:T(8,128)(2,1)S(1)} %collective-permute-done.4), channel_id=1, source_target_pairs={{0,2},{2,4},{4,6},{6,7},{7,5},{5,3},{3,1},{1,0},{8,10},{10,12},{12... | collective-permute-start | bytes 1622024 | tf_op jit(solution)/shard_map/ppermute | solution.py:60
  34.6 0.2 add_reduce_fusion.4
  34.8 0.8 %fusion = f32[256]{0:T(256)S(1)} fusion(bf16[256,4096]{1,0:T(8,128)(2,1)S(1)} %pad_maximum_fusion, bf16[64,4224]{1,0:T(8,128)(2,1)S(1)} %select_convert_fusion, f32[256]{0:T(256)S(1)} %get-tuple-element.6, f32[256]{0:T(256)S(1)} %get-tuple-element.5, f32[64]{0:T(128)S(1)} %add_reduce_fusion.6, f32[64]{0:T(128)S(1)} %multiply_floor_fusion.8), kind=kOutput, calls=%fused_computation.10 | convolution fusion | flops 134299392 | bytes 2625536 | tf_op jit(solution)/shard_map/id,jd->ij/dot_general | solution.py:26
  35.6 0.2 add_reduce_fusion.1
  35.7 0.3 collective-permute-start.9
  36.0 0.8 %fusion.1 = f32[256]{0:T(256)S(1)} fusion(bf16[256,4096]{1,0:T(8,128)(2,1)S(1)} %pad_maximum_fusion, bf16[64,4224]{1,0:T(8,128)(2,1)S(1)} %collective-permute-done.3, f32[256]{0:T(256)S(1)} %get-tuple-element.6, f32[256]{0:T(256)S(1)} %get-tuple-element.5, f32[64]{0:T(128)S(1)} %add_reduce_fusion.5, f32[64]{0:T(128)S(1)} %multiply_floor_fusion.7), kind=kOutput, calls=%fused_computation.11 | convolution fusion | flops 134299392 | bytes 2625536 | tf_op jit(solution)/shard_map/id,jd->ij/dot_general | solution.py:26
  36.8 0.8 %fusion.2 = f32[256]{0:T(256)S(1)} fusion(bf16[256,4096]{1,0:T(8,128)(2,1)S(1)} %pad_maximum_fusion, bf16[64,4224]{1,0:T(8,128)(2,1)S(1)} %collective-permute-done.4, f32[256]{0:T(256)S(1)} %get-tuple-element.6, f32[256]{0:T(256)S(1)} %get-tuple-element.5, f32[64]{0:T(128)S(1)} %add_reduce_fusion.4, f32[64]{0:T(128)S(1)} %multiply_floor_fusion.6), kind=kOutput, calls=%fused_computation.12 | convolution fusion | flops 134299392 | bytes 2625536 | tf_op jit(solution)/shard_map/id,jd->ij/dot_general | solution.py:26
  37.6 0.8 %fusion.5 = f32[256]{0:T(256)S(1)} fusion(bf16[256,4096]{1,0:T(8,128)(2,1)S(1)} %pad_maximum_fusion, bf16[64,4224]{1,0:T(8,128)(2,1)S(1)} %collective-permute-done.8, f32[256]{0:T(256)S(1)} %get-tuple-element.6, f32[256]{0:T(256)S(1)} %get-tuple-element.5, f32[64]{0:T(128)S(1)} %add_reduce_fusion.1, f32[64]{0:T(128)S(1)} %multiply_floor_fusion.2), kind=kOutput, calls=%fused_computation.15 | convolution fusion | flops 134299392 | bytes 2625536 | tf_op jit(solution)/shard_map/id,jd->ij/dot_general | solution.py:26
  38.4 0.8 %fusion.4 = f32[256]{0:T(256)S(1)} fusion(bf16[256,4096]{1,0:T(8,128)(2,1)S(1)} %pad_maximum_fusion, bf16[64,4224]{1,0:T(8,128)(2,1)S(1)} %collective-permute-done.7, f32[256]{0:T(256)S(1)} %get-tuple-element.6, f32[256]{0:T(256)S(1)} %get-tuple-element.5, f32[64]{0:T(128)S(1)} %add_reduce_fusion.2, f32[64]{0:T(128)S(1)} %multiply_floor_fusion.3), kind=kOutput, calls=%fused_computation.14 | convolution fusion | flops 134299392 | bytes 2625536 | tf_op jit(solution)/shard_map/id,jd->ij/dot_general | solution.py:26
  39.2 6.2 %collective-permute-done.5 = bf16[64,4224]{1,0:T(8,128)(2,1)S(1)} collective-permute-done((bf16[64,4224]{1,0:T(8,128)(2,1)S(1)}, bf16[64,4224]{1,0:T(8,128)(2,1)S(1)}, u32[]{:S(2)}, u32[]{:S(2)}) %collective-permute-start.5) | collective-permute-done | bytes 540704 | tf_op jit(solution)/shard_map/ppermute | solution.py:60
  45.4 1.9 %collective-permute-start.6 = (bf16[32,4224]{1,0:T(8,128)(2,1)S(1)}, bf16[32,4224]{1,0:T(8,128)(2,1)S(1)}, u32[]{:S(2)}, u32[]{:S(2)}) collective-permute-start(bf16[32,4224]{1,0:T(8,128)(2,1)S(1)} %slice.160), channel_id=1, source_target_pairs={{0,2},{2,4},{4,6},{6,7},{7,5},{5,3},{3,1},{1,0},{8,10},{10,12},{12... | collective-permute-start | bytes 811016 | tf_op jit(solution)/shard_map/ppermute | solution.py:60
  47.2 0.2 add_reduce_fusion.3
  47.4 0.7 %collective-permute-done.9 = bf16[64,4224]{1,0:T(8,128)(2,1)S(1)} collective-permute-done((bf16[64,4224]{1,0:T(8,128)(2,1)S(1)}, bf16[64,4224]{1,0:T(8,128)(2,1)S(1)}, u32[]{:S(2)}, u32[]{:S(2)}) %collective-permute-start.9) | collective-permute-done | bytes 540704 | tf_op jit(solution)/shard_map/ppermute | solution.py:60
  48.2 0.3 collective-permute-start.10
  48.5 0.2 add_reduce_fusion
  48.6 0.8 %fusion.3 = f32[256]{0:T(256)S(1)} fusion(bf16[256,4096]{1,0:T(8,128)(2,1)S(1)} %pad_maximum_fusion, bf16[64,4224]{1,0:T(8,128)(2,1)S(1)} %collective-permute-done.5, f32[256]{0:T(256)S(1)} %get-tuple-element.6, f32[256]{0:T(256)S(1)} %get-tuple-element.5, f32[64]{0:T(128)S(1)} %add_reduce_fusion.3, f32[64]{0:T(128)S(1)} %multiply_floor_fusion.5), kind=kOutput, calls=%fused_computation.13 | convolution fusion | flops 134299392 | bytes 2625536 | tf_op jit(solution)/shard_map/id,jd->ij/dot_general | solution.py:26
  49.4 0.8 %fusion.6 = f32[256]{0:T(256)S(1)} fusion(bf16[256,4096]{1,0:T(8,128)(2,1)S(1)} %pad_maximum_fusion, bf16[64,4224]{1,0:T(8,128)(2,1)S(1)} %collective-permute-done.9, f32[256]{0:T(256)S(1)} %get-tuple-element.6, f32[256]{0:T(256)S(1)} %get-tuple-element.5, f32[64]{0:T(128)S(1)} %add_reduce_fusion, f32[64]{0:T(128)S(1)} %multiply_floor_fusion.1), kind=kOutput, calls=%fused_computation.16 | convolution fusion | flops 134299392 | bytes 2625536 | tf_op jit(solution)/shard_map/id,jd->ij/dot_general | solution.py:26
  50.2 1.7 %collective-permute-done.6 = bf16[32,4224]{1,0:T(8,128)(2,1)S(1)} collective-permute-done((bf16[32,4224]{1,0:T(8,128)(2,1)S(1)}, bf16[32,4224]{1,0:T(8,128)(2,1)S(1)}, u32[]{:S(2)}, u32[]{:S(2)}) %collective-permute-start.6) | collective-permute-done | bytes 270368 | tf_op jit(solution)/shard_map/ppermute | solution.py:60
  51.9 0.2 add_reduce_fusion.8
  52.1 2.6 %collective-permute-done.10 = bf16[32,4224]{1,0:T(8,128)(2,1)S(1)} collective-permute-done((bf16[32,4224]{1,0:T(8,128)(2,1)S(1)}, bf16[32,4224]{1,0:T(8,128)(2,1)S(1)}, u32[]{:S(2)}, u32[]{:S(2)}) %collective-permute-start.10) | collective-permute-done | bytes 270368 | tf_op jit(solution)/shard_map/ppermute | solution.py:60
  54.7 0.2 add_reduce_fusion.7
  54.9 0.8 %fusion.7 = f32[256]{0:T(256)S(1)} fusion(bf16[256,4096]{1,0:T(8,128)(2,1)S(1)} %pad_maximum_fusion, bf16[32,4224]{1,0:T(8,128)(2,1)S(1)} %collective-permute-done.6, f32[256]{0:T(256)S(1)} %get-tuple-element.6, f32[256]{0:T(256)S(1)} %get-tuple-element.5, f32[32]{0:T(128)S(1)} %add_reduce_fusion.8, f32[32]{0:T(128)S(1)} %multiply_floor_fusion.4), kind=kOutput, calls=%fused_computation.19 | convolution fusion | flops 67149568 | bytes 2363392 | tf_op jit(solution)/shard_map/id,jd->ij/dot_general | solution.py:26
  55.6 0.8 %fusion.8 = f32[256]{0:T(256)S(1)} fusion(bf16[256,4096]{1,0:T(8,128)(2,1)S(1)} %pad_maximum_fusion, bf16[32,4224]{1,0:T(8,128)(2,1)S(1)} %collective-permute-done.10, f32[256]{0:T(256)S(1)} %get-tuple-element.6, f32[256]{0:T(256)S(1)} %get-tuple-element.5, f32[32]{0:T(128)S(1)} %add_reduce_fusion.7, f32[32]{0:T(128)S(1)} %multiply_floor_fusion), kind=kOutput, calls=%fused_computation.20 | convolution fusion | flops 67149568 | bytes 2363392 | tf_op jit(solution)/shard_map/id,jd->ij/dot_general | solution.py:26
  56.4 0.1 fusion.20
  56.5 0.0 collective-permute-start.11
  56.5 2.8 %collective-permute-start.12 = (f32[64]{0:T(128)S(1)}, f32[64]{0:T(128)S(1)}, u32[]{:S(2)}, u32[]{:S(2)}) collective-permute-start(f32[64]{0:T(128)S(1)} %get-tuple-element.11), channel_id=1, source_target_pairs={{0,16},{8,24},{16,0},{24,8},{1,17},{9,25},{17,1},{25,9},{2,18},{10... | collective-permute-start | bytes 776 | tf_op jit(solution)/shard_map/ppermute | solution.py:103
  59.3 0.0 collective-permute-start.13
  59.3 1.5 %collective-permute-done.12 = f32[64]{0:T(128)S(1)} collective-permute-done((f32[64]{0:T(128)S(1)}, f32[64]{0:T(128)S(1)}, u32[]{:S(2)}, u32[]{:S(2)}) %collective-permute-start.12) | collective-permute-done | bytes 288 | tf_op jit(solution)/shard_map/ppermute | solution.py:103
  60.8 1.4 %collective-permute-done.13 = f32[64]{0:T(128)S(1)} collective-permute-done((f32[64]{0:T(128)S(1)}, f32[64]{0:T(128)S(1)}, u32[]{:S(2)}, u32[]{:S(2)}) %collective-permute-start.13) | collective-permute-done | bytes 288 | tf_op jit(solution)/shard_map/ppermute | solution.py:103
  62.3 0.5 maximum_maximum_fusion.1
  (26 shorter events, 0.2 us)
Async XLA Ops:
  0.0 2.4 %copy-start = (s32[64]{0:T(128)S(1)}, s32[64]{0:T(128)}, u32[]{:S(2)}) copy-start(s32[64]{0:T(128)} %param.4) | copy-start | bytes 772
  0.0 2.4 %copy-start.1 = (s32[64]{0:T(128)S(1)}, s32[64]{0:T(128)}, u32[]{:S(2)}) copy-start(s32[64]{0:T(128)} %param.5) | copy-start | bytes 772
  2.7 15.3 %collective-permute-start.1 = (bf16[64,4224]{1,0:T(8,128)(2,1)S(1)}, bf16[64,4224]{1,0:T(8,128)(2,1)S(1)}, u32[]{:S(2)}, u32[]{:S(2)}) collective-permute-start(bf16[64,4224]{1,0:T(8,128)(2,1)S(1)} %select_convert_fusion), channel_id=1, source_target_pairs={{0,16},{8,24},{16,0},{24,8},{1,17},{9,25},{17,1},{25,9},{2,18},{10... | collective-permute-start | bytes 1622024 | tf_op jit(solution)/shard_map/ppermute | solution.py:69
  5.8 13.7 %collective-permute-start.3 = (bf16[64,4224]{1,0:T(8,128)(2,1)S(1)}, bf16[64,4224]{1,0:T(8,128)(2,1)S(1)}, u32[]{:S(2)}, u32[]{:S(2)}) collective-permute-start(bf16[64,4224]{1,0:T(8,128)(2,1)S(1)} %select_convert_fusion), channel_id=1, source_target_pairs={{0,2},{2,4},{4,6},{6,7},{7,5},{5,3},{3,1},{1,0},{8,10},{10,12},{12... | collective-permute-start | bytes 1622024 | tf_op jit(solution)/shard_map/ppermute | solution.py:60
  7.4 13.9 %collective-permute-start.7 = (bf16[64,4224]{1,0:T(8,128)(2,1)S(1)}, bf16[64,4224]{1,0:T(8,128)(2,1)S(1)}, u32[]{:S(2)}, u32[]{:S(2)}) collective-permute-start(bf16[64,4224]{1,0:T(8,128)(2,1)S(1)} %select_convert_fusion), channel_id=1, source_target_pairs={{2,0},{4,2},{6,4},{7,6},{5,7},{3,5},{1,3},{0,1},{10,8},{12,10},{14... | collective-permute-start | bytes 1622024 | tf_op jit(solution)/shard_map/ppermute | solution.py:60
  7.8 14.2 %collective-permute-start = (bf16[64,4224]{1,0:T(8,128)(2,1)S(1)}, bf16[64,4224]{1,0:T(8,128)(2,1)S(1)}, u32[]{:S(2)}, u32[]{:S(2)}) collective-permute-start(bf16[64,4224]{1,0:T(8,128)(2,1)S(1)} %select_convert_fusion), channel_id=1, source_target_pairs={{0,8},{8,0},{16,24},{24,16},{1,9},{9,1},{17,25},{25,17},{2,10},{10... | collective-permute-start | bytes 1622024 | tf_op jit(solution)/shard_map/ppermute | solution.py:70
  18.1 3.9 %collective-permute-start.2 = (bf16[64,4224]{1,0:T(8,128)(2,1)S(1)}, bf16[64,4224]{1,0:T(8,128)(2,1)S(1)}, u32[]{:S(2)}, u32[]{:S(2)}) collective-permute-start(bf16[64,4224]{1,0:T(8,128)(2,1)S(1)} %collective-permute-done.1), channel_id=1, source_target_pairs={{0,8},{8,0},{16,24},{24,16},{1,9},{9,1},{17,25},{25,17},{2,10},{10... | collective-permute-start | bytes 1622024 | tf_op jit(solution)/shard_map/ppermute | solution.py:71
  19.5 13.2 %collective-permute-start.4 = (bf16[64,4224]{1,0:T(8,128)(2,1)S(1)}, bf16[64,4224]{1,0:T(8,128)(2,1)S(1)}, u32[]{:S(2)}, u32[]{:S(2)}) collective-permute-start(bf16[64,4224]{1,0:T(8,128)(2,1)S(1)} %collective-permute-done.3), channel_id=1, source_target_pairs={{0,2},{2,4},{4,6},{6,7},{7,5},{5,3},{3,1},{1,0},{8,10},{10,12},{12... | collective-permute-start | bytes 1622024 | tf_op jit(solution)/shard_map/ppermute | solution.py:60
  21.3 14.2 %collective-permute-start.8 = (bf16[64,4224]{1,0:T(8,128)(2,1)S(1)}, bf16[64,4224]{1,0:T(8,128)(2,1)S(1)}, u32[]{:S(2)}, u32[]{:S(2)}) collective-permute-start(bf16[64,4224]{1,0:T(8,128)(2,1)S(1)} %collective-permute-done.7), channel_id=1, source_target_pairs={{2,0},{4,2},{6,4},{7,6},{5,7},{3,5},{1,3},{0,1},{10,8},{12,10},{14... | collective-permute-start | bytes 1622024 | tf_op jit(solution)/shard_map/ppermute | solution.py:60
  32.8 12.6 %collective-permute-start.5 = (bf16[64,4224]{1,0:T(8,128)(2,1)S(1)}, bf16[64,4224]{1,0:T(8,128)(2,1)S(1)}, u32[]{:S(2)}, u32[]{:S(2)}) collective-permute-start(bf16[64,4224]{1,0:T(8,128)(2,1)S(1)} %collective-permute-done.4), channel_id=1, source_target_pairs={{0,2},{2,4},{4,6},{6,7},{7,5},{5,3},{3,1},{1,0},{8,10},{10,12},{12... | collective-permute-start | bytes 1622024 | tf_op jit(solution)/shard_map/ppermute | solution.py:60
  35.7 12.4 %collective-permute-start.9 = (bf16[64,4224]{1,0:T(8,128)(2,1)S(1)}, bf16[64,4224]{1,0:T(8,128)(2,1)S(1)}, u32[]{:S(2)}, u32[]{:S(2)}) collective-permute-start(bf16[64,4224]{1,0:T(8,128)(2,1)S(1)} %collective-permute-done.8), channel_id=1, source_target_pairs={{2,0},{4,2},{6,4},{7,6},{5,7},{3,5},{1,3},{0,1},{10,8},{12,10},{14... | collective-permute-start | bytes 1622024 | tf_op jit(solution)/shard_map/ppermute | solution.py:60
  45.4 6.5 %collective-permute-start.6 = (bf16[32,4224]{1,0:T(8,128)(2,1)S(1)}, bf16[32,4224]{1,0:T(8,128)(2,1)S(1)}, u32[]{:S(2)}, u32[]{:S(2)}) collective-permute-start(bf16[32,4224]{1,0:T(8,128)(2,1)S(1)} %slice.160), channel_id=1, source_target_pairs={{0,2},{2,4},{4,6},{6,7},{7,5},{5,3},{3,1},{1,0},{8,10},{10,12},{12... | collective-permute-start | bytes 811016 | tf_op jit(solution)/shard_map/ppermute | solution.py:60
  48.2 6.5 %collective-permute-start.10 = (bf16[32,4224]{1,0:T(8,128)(2,1)S(1)}, bf16[32,4224]{1,0:T(8,128)(2,1)S(1)}, u32[]{:S(2)}, u32[]{:S(2)}) collective-permute-start(bf16[32,4224]{1,0:T(8,128)(2,1)S(1)} %slice.173), channel_id=1, source_target_pairs={{2,0},{4,2},{6,4},{7,6},{5,7},{3,5},{1,3},{0,1},{10,8},{12,10},{14... | collective-permute-start | bytes 811016 | tf_op jit(solution)/shard_map/ppermute | solution.py:60
  56.5 2.8 %collective-permute-start.11 = (f32[64]{0:T(128)S(1)}, f32[64]{0:T(128)S(1)}, u32[]{:S(2)}, u32[]{:S(2)}) collective-permute-start(f32[64]{0:T(128)S(1)} %get-tuple-element.9), channel_id=1, source_target_pairs={{0,8},{8,0},{16,24},{24,16},{1,9},{9,1},{17,25},{25,17},{2,10},{10... | collective-permute-start | bytes 776 | tf_op jit(solution)/shard_map/ppermute | solution.py:103
  56.5 4.3 %collective-permute-start.12 = (f32[64]{0:T(128)S(1)}, f32[64]{0:T(128)S(1)}, u32[]{:S(2)}, u32[]{:S(2)}) collective-permute-start(f32[64]{0:T(128)S(1)} %get-tuple-element.11), channel_id=1, source_target_pairs={{0,16},{8,24},{16,0},{24,8},{1,17},{9,25},{17,1},{25,9},{2,18},{10... | collective-permute-start | bytes 776 | tf_op jit(solution)/shard_map/ppermute | solution.py:103
  59.3 3.0 %collective-permute-start.13 = (f32[64]{0:T(128)S(1)}, f32[64]{0:T(128)S(1)}, u32[]{:S(2)}, u32[]{:S(2)}) collective-permute-start(f32[64]{0:T(128)S(1)} %get-tuple-element.10), channel_id=1, source_target_pairs={{0,24},{8,16},{16,8},{24,0},{1,25},{9,17},{17,9},{25,1},{2,26},{10... | collective-permute-start | bytes 776 | tf_op jit(solution)/shard_map/ppermute | solution.py:103

commit v14 on v13

--- a/solution.py
+++ b/solution.py
@@ -91,6 +91,9 @@
             visiting = send(which, visiting, step)
             best = fold(best, pending)
             chain[0], chain[1], chain[2] = visiting, best, [visiting]
+    if steps >= 1 and block_count % 2 == 0:
+        chains[0][2] = [jnp.concatenate([chains[0][2][-1], chains[1][2][-1]], axis=0)] + chains[0][2][:-1]
+        chains[1][2] = chains[1][2][:-1]
     best = None
     for _, chain_best, pending in chains:
         chain_best = fold(chain_best, pending)

time: 63 us -> 62.1 us (0.986)
  matrix products: 6.96 us -> 6.25 us
    dot_general x9 -> x8, matrix products: 6.96 us -> 6.25 us  [block_best(): jnp.einsum('id,jd->ij', left_rows, payload[:, :D], preferred_element_type...]
    add x9 -> x8, other arithmetic: 1.57 us -> 1.39 us  [tag_labels(): return high * 128.0 + low]
where the time goes in v14:
time: 62.1 us; the launch traced here: 61.9 us
  waiting for transfers between devices  35.9 us (58%)
  starting transfers between devices  14.2 us (23%)
  matrix products  6.25 us (10%)
  other arithmetic  5.13 us (8%)
    ppermute x8, waiting for transfers between devices, send(): return lax.ppermute(visiting, 'blk', forward if which == 0 else backward)  22.9 us
    ppermute x1, waiting for transfers between devices, per_device(): across = lax.ppermute(payload, 'grp', partner_pairs(group_count, 2))  10.1 us
    ppermute x8, starting transfers between devices, send(): return lax.ppermute(visiting, 'blk', forward if which == 0 else backward)  8.35 us
    dot_general x8, matrix products, block_best(): jnp.einsum('id,jd->ij', left_rows, payload[:, :D], preferred_element_type...  6.25 us
    ppermute x1, starting transfers between devices, per_device(): across = lax.ppermute(payload, 'grp', partner_pairs(group_count, 2))  3.06 us
    ppermute x3, waiting for transfers between devices, per_device(): result = jnp.maximum(result, lax.ppermute(best[k], 'grp', pairs))  2.95 us
    ppermute x3, starting transfers between devices, per_device(): result = jnp.maximum(result, lax.ppermute(best[k], 'grp', pairs))  2.81 us
    add x8, other arithmetic, tag_labels(): return high * 128.0 + low  1.39 us
  transfers between devices with their start and end apart: 14, of which 9 were waited for; matrix products, arithmetic and copies ran while one was open for 12% of the time, Pallas kernels for 0%

profile of v14, /device:TPU:0, one launch (start us, length us, event | category | flops | bytes accessed | tf_op | source)
XLA Modules:
  0.0 61.9 jit_solution(12007710879498205036)
XLA Ops:
  0.0 1.1 %convert_element_type.200 = f32[64,4096]{1,0:T(8,128)S(1)} convert(bf16[64,4096]{1,0:T(8,128)(2,1)} %param.3) | non-fusion elementwise | flops 262144 | bytes 1572864 | tf_op jit(solution)/shard_map/convert_element_type | solution.py:41
  1.1 1.2 %multiply_reduce_fusion = f32[64]{0:T(128)S(1)} fusion(bf16[64,4096]{1,0:T(8,128)(2,1)} %param.3), kind=kLoop, calls=%fused_computation.20 | loop fusion | flops 786368 | bytes 524544 | tf_op jit(solution)/shard_map/reduce_sum | solution.py:42
  2.4 0.3 select_convert_fusion
  2.7 3.1 %collective-permute-start.1 = (bf16[64,4224]{1,0:T(8,128)(2,1)S(1)}, bf16[64,4224]{1,0:T(8,128)(2,1)S(1)}, u32[]{:S(2)}, u32[]{:S(2)}) collective-permute-start(bf16[64,4224]{1,0:T(8,128)(2,1)S(1)} %select_convert_fusion), channel_id=1, source_target_pairs={{0,16},{8,24},{16,0},{24,8},{1,17},{9,25},{17,1},{25,9},{2,18},{10... | collective-permute-start | bytes 1622024 | tf_op jit(solution)/shard_map/ppermute | solution.py:69
  5.8 1.6 %collective-permute-start.3 = (bf16[64,4224]{1,0:T(8,128)(2,1)S(1)}, bf16[64,4224]{1,0:T(8,128)(2,1)S(1)}, u32[]{:S(2)}, u32[]{:S(2)}) collective-permute-start(bf16[64,4224]{1,0:T(8,128)(2,1)S(1)} %select_convert_fusion), channel_id=1, source_target_pairs={{0,2},{2,4},{4,6},{6,7},{7,5},{5,3},{3,1},{1,0},{8,10},{10,12},{12... | collective-permute-start | bytes 1622024 | tf_op jit(solution)/shard_map/ppermute | solution.py:60
  7.4 0.4 collective-permute-start.7
  7.8 0.0 collective-permute-start
  7.8 0.2 add_reduce_fusion.7
  8.0 10.1 %collective-permute-done.1 = bf16[64,4224]{1,0:T(8,128)(2,1)S(1)} collective-permute-done((bf16[64,4224]{1,0:T(8,128)(2,1)S(1)}, bf16[64,4224]{1,0:T(8,128)(2,1)S(1)}, u32[]{:S(2)}, u32[]{:S(2)}) %collective-permute-start.1) | collective-permute-done | bytes 540704 | tf_op jit(solution)/shard_map/ppermute | solution.py:69
  18.1 0.0 collective-permute-start.2
  18.1 1.5 %collective-permute-done.3 = bf16[64,4224]{1,0:T(8,128)(2,1)S(1)} collective-permute-done((bf16[64,4224]{1,0:T(8,128)(2,1)S(1)}, bf16[64,4224]{1,0:T(8,128)(2,1)S(1)}, u32[]{:S(2)}, u32[]{:S(2)}) %collective-permute-start.3) | collective-permute-done | bytes 540704 | tf_op jit(solution)/shard_map/ppermute | solution.py:60
  19.5 1.6 %collective-permute-start.4 = (bf16[64,4224]{1,0:T(8,128)(2,1)S(1)}, bf16[64,4224]{1,0:T(8,128)(2,1)S(1)}, u32[]{:S(2)}, u32[]{:S(2)}) collective-permute-start(bf16[64,4224]{1,0:T(8,128)(2,1)S(1)} %collective-permute-done.3), channel_id=1, source_target_pairs={{0,2},{2,4},{4,6},{6,7},{7,5},{5,3},{3,1},{1,0},{8,10},{10,12},{12... | collective-permute-start | bytes 1622024 | tf_op jit(solution)/shard_map/ppermute | solution.py:60
  21.1 0.2 add_reduce_fusion.6
  21.3 0.0 collective-permute-done.7
  21.3 0.5 collective-permute-start.8
  21.8 0.2 add_reduce_fusion.2
  22.0 0.1 pad_maximum_fusion.4
  22.1 0.2 floor_reduce_fusion
  22.3 0.2 pad_maximum_fusion
  22.5 10.2 %collective-permute-done.4 = bf16[64,4224]{1,0:T(8,128)(2,1)S(1)} collective-permute-done((bf16[64,4224]{1,0:T(8,128)(2,1)S(1)}, bf16[64,4224]{1,0:T(8,128)(2,1)S(1)}, u32[]{:S(2)}, u32[]{:S(2)}) %collective-permute-start.4) | collective-permute-done | bytes 540704 | tf_op jit(solution)/shard_map/ppermute | solution.py:60
  32.8 1.8 %collective-permute-start.5 = (bf16[64,4224]{1,0:T(8,128)(2,1)S(1)}, bf16[64,4224]{1,0:T(8,128)(2,1)S(1)}, u32[]{:S(2)}, u32[]{:S(2)}) collective-permute-start(bf16[64,4224]{1,0:T(8,128)(2,1)S(1)} %collective-permute-done.4), channel_id=1, source_target_pairs={{0,2},{2,4},{4,6},{6,7},{7,5},{5,3},{3,1},{1,0},{8,10},{10,12},{12... | collective-permute-start | bytes 1622024 | tf_op jit(solution)/shard_map/ppermute | solution.py:60
  34.6 0.2 add_reduce_fusion.5
  34.8 0.8 %fusion = f32[256]{0:T(256)S(1)} fusion(bf16[256,4096]{1,0:T(8,128)(2,1)S(1)} %pad_maximum_fusion, bf16[64,4224]{1,0:T(8,128)(2,1)S(1)} %select_convert_fusion, f32[256]{0:T(256)S(1)} %get-tuple-element.6, f32[256]{0:T(256)S(1)} %get-tuple-element.5, f32[64]{0:T(128)S(1)} %add_reduce_fusion.7, f32[64]{0:T(128)S(1)} %multiply_floor_fusion.7), kind=kOutput, calls=%fused_computation.11 | convolution fusion | flops 134299392 | bytes 2625536 | tf_op jit(solution)/shard_map/id,jd->ij/dot_general | solution.py:26
  35.6 0.3 collective-permute-start.9
  35.8 0.2 add_reduce_fusion.1
  36.0 0.8 %fusion.1 = f32[256]{0:T(256)S(1)} fusion(bf16[256,4096]{1,0:T(8,128)(2,1)S(1)} %pad_maximum_fusion, bf16[64,4224]{1,0:T(8,128)(2,1)S(1)} %collective-permute-done.3, f32[256]{0:T(256)S(1)} %get-tuple-element.6, f32[256]{0:T(256)S(1)} %get-tuple-element.5, f32[64]{0:T(128)S(1)} %add_reduce_fusion.6, f32[64]{0:T(128)S(1)} %multiply_floor_fusion.6), kind=kOutput, calls=%fused_computation.12 | convolution fusion | flops 134299392 | bytes 2625536 | tf_op jit(solution)/shard_map/id,jd->ij/dot_general | solution.py:26
  36.8 0.8 %fusion.2 = f32[256]{0:T(256)S(1)} fusion(bf16[256,4096]{1,0:T(8,128)(2,1)S(1)} %pad_maximum_fusion, bf16[64,4224]{1,0:T(8,128)(2,1)S(1)} %collective-permute-done.4, f32[256]{0:T(256)S(1)} %get-tuple-element.6, f32[256]{0:T(256)S(1)} %get-tuple-element.5, f32[64]{0:T(128)S(1)} %add_reduce_fusion.5, f32[64]{0:T(128)S(1)} %multiply_floor_fusion.5), kind=kOutput, calls=%fused_computation.13 | convolution fusion | flops 134299392 | bytes 2625536 | tf_op jit(solution)/shard_map/id,jd->ij/dot_general | solution.py:26
  37.6 0.8 %fusion.6 = f32[256]{0:T(256)S(1)} fusion(bf16[256,4096]{1,0:T(8,128)(2,1)S(1)} %pad_maximum_fusion, bf16[64,4224]{1,0:T(8,128)(2,1)S(1)} %collective-permute-done.8, f32[256]{0:T(256)S(1)} %get-tuple-element.6, f32[256]{0:T(256)S(1)} %get-tuple-element.5, f32[64]{0:T(128)S(1)} %add_reduce_fusion.1, f32[64]{0:T(128)S(1)} %multiply_floor_fusion.1), kind=kOutput, calls=%fused_computation.17 | convolution fusion | flops 134299392 | bytes 2625536 | tf_op jit(solution)/shard_map/id,jd->ij/dot_general | solution.py:26
  38.4 0.8 %fusion.5 = f32[256]{0:T(256)S(1)} fusion(bf16[256,4096]{1,0:T(8,128)(2,1)S(1)} %pad_maximum_fusion, bf16[64,4224]{1,0:T(8,128)(2,1)S(1)} %collective-permute-done.7, f32[256]{0:T(256)S(1)} %get-tuple-element.6, f32[256]{0:T(256)S(1)} %get-tuple-element.5, f32[64]{0:T(128)S(1)} %add_reduce_fusion.2, f32[64]{0:T(128)S(1)} %multiply_floor_fusion.2), kind=kOutput, calls=%fused_computation.16 | convolution fusion | flops 134299392 | bytes 2625536 | tf_op jit(solution)/shard_map/id,jd->ij/dot_general | solution.py:26
  39.2 6.2 %collective-permute-done.5 = bf16[64,4224]{1,0:T(8,128)(2,1)S(1)} collective-permute-done((bf16[64,4224]{1,0:T(8,128)(2,1)S(1)}, bf16[64,4224]{1,0:T(8,128)(2,1)S(1)}, u32[]{:S(2)}, u32[]{:S(2)}) %collective-permute-start.5) | collective-permute-done | bytes 540704 | tf_op jit(solution)/shard_map/ppermute | solution.py:60
  45.4 1.9 %collective-permute-start.6 = (bf16[32,4224]{1,0:T(8,128)(2,1)S(1)}, bf16[32,4224]{1,0:T(8,128)(2,1)S(1)}, u32[]{:S(2)}, u32[]{:S(2)}) collective-permute-start(bf16[32,4224]{1,0:T(8,128)(2,1)S(1)} %slice.148), channel_id=1, source_target_pairs={{0,2},{2,4},{4,6},{6,7},{7,5},{5,3},{3,1},{1,0},{8,10},{10,12},{12... | collective-permute-start | bytes 811016 | tf_op jit(solution)/shard_map/ppermute | solution.py:60
  47.2 0.2 add_reduce_fusion.4
  47.4 0.5 collective-permute-done.9
  48.0 0.3 collective-permute-start.10
  48.3 0.2 add_reduce_fusion
  48.5 0.8 %fusion.3 = f32[256]{0:T(256)S(1)} fusion(bf16[256,4096]{1,0:T(8,128)(2,1)S(1)} %pad_maximum_fusion, bf16[64,4224]{1,0:T(8,128)(2,1)S(1)} %collective-permute-done.5, f32[256]{0:T(256)S(1)} %get-tuple-element.6, f32[256]{0:T(256)S(1)} %get-tuple-element.5, f32[64]{0:T(128)S(1)} %add_reduce_fusion.4, f32[64]{0:T(128)S(1)} %multiply_floor_fusion.4), kind=kOutput, calls=%fused_computation.14 | convolution fusion | flops 134299392 | bytes 2625536 | tf_op jit(solution)/shard_map/id,jd->ij/dot_general | solution.py:26
  49.3 0.8 %fusion.7 = f32[256]{0:T(256)S(1)} fusion(bf16[256,4096]{1,0:T(8,128)(2,1)S(1)} %pad_maximum_fusion, bf16[64,4224]{1,0:T(8,128)(2,1)S(1)} %collective-permute-done.9, f32[256]{0:T(256)S(1)} %get-tuple-element.6, f32[256]{0:T(256)S(1)} %get-tuple-element.5, f32[64]{0:T(128)S(1)} %add_reduce_fusion, f32[64]{0:T(128)S(1)} %multiply_floor_fusion), kind=kOutput, calls=%fused_computation.18 | convolution fusion | flops 134299392 | bytes 2625536 | tf_op jit(solution)/shard_map/id,jd->ij/dot_general | solution.py:26
  50.0 1.8 %collective-permute-done.6 = bf16[32,4224]{1,0:T(8,128)(2,1)S(1)} collective-permute-done((bf16[32,4224]{1,0:T(8,128)(2,1)S(1)}, bf16[32,4224]{1,0:T(8,128)(2,1)S(1)}, u32[]{:S(2)}, u32[]{:S(2)}) %collective-permute-start.6) | collective-permute-done | bytes 270368 | tf_op jit(solution)/shard_map/ppermute | solution.py:60
  51.9 2.6 %collective-permute-done.10 = bf16[32,4224]{1,0:T(8,128)(2,1)S(1)} collective-permute-done((bf16[32,4224]{1,0:T(8,128)(2,1)S(1)}, bf16[32,4224]{1,0:T(8,128)(2,1)S(1)}, u32[]{:S(2)}, u32[]{:S(2)}) %collective-permute-start.10) | collective-permute-done | bytes 270368 | tf_op jit(solution)/shard_map/ppermute | solution.py:60
  54.5 0.2 add_reduce_fusion.3
  54.7 0.8 %fusion.4 = f32[256]{0:T(256)S(1)} fusion(bf16[256,4096]{1,0:T(8,128)(2,1)S(1)} %pad_maximum_fusion, bf16[64,4224]{1,0:T(8,128)(2,1)S(1)} %constant_dynamic-update-slice_fusion, f32[256]{0:T(256)S(1)} %get-tuple-element.6, f32[256]{0:T(256)S(1)} %get-tuple-element.5, f32[64]{0:T(128)S(1)} %add_reduce_fusion.3, f32[64]{0:T(128)S(1)} %multiply_floor_fusion.3), kind=kOutput, calls=%fused_computation.15 | convolution fusion | flops 134299392 | bytes 2625536 | tf_op jit(solution)/shard_map/id,jd->ij/dot_general | solution.py:26
  55.5 0.1 fusion.18
  55.6 0.0 collective-permute-start.11
  55.6 2.8 %collective-permute-start.12 = (f32[64]{0:T(128)S(1)}, f32[64]{0:T(128)S(1)}, u32[]{:S(2)}, u32[]{:S(2)}) collective-permute-start(f32[64]{0:T(128)S(1)} %get-tuple-element.11), channel_id=1, source_target_pairs={{0,16},{8,24},{16,0},{24,8},{1,17},{9,25},{17,1},{25,9},{2,18},{10... | collective-permute-start | bytes 776 | tf_op jit(solution)/shard_map/ppermute | solution.py:106
  58.4 0.0 collective-permute-start.13
  58.4 1.5 %collective-permute-done.12 = f32[64]{0:T(128)S(1)} collective-permute-done((f32[64]{0:T(128)S(1)}, f32[64]{0:T(128)S(1)}, u32[]{:S(2)}, u32[]{:S(2)}) %collective-permute-start.12) | collective-permute-done | bytes 288 | tf_op jit(solution)/shard_map/ppermute | solution.py:106
  59.9 1.4 %collective-permute-done.13 = f32[64]{0:T(128)S(1)} collective-permute-done((f32[64]{0:T(128)S(1)}, f32[64]{0:T(128)S(1)}, u32[]{:S(2)}, u32[]{:S(2)}) %collective-permute-start.13) | collective-permute-done | bytes 288 | tf_op jit(solution)/shard_map/ppermute | solution.py:106
  61.4 0.5 maximum_maximum_fusion.1
  (25 shorter events, 0.2 us)
Async XLA Ops:
  0.0 2.4 %copy-start = (s32[64]{0:T(128)S(1)}, s32[64]{0:T(128)}, u32[]{:S(2)}) copy-start(s32[64]{0:T(128)} %param.4) | copy-start | bytes 772
  0.0 2.4 %copy-start.1 = (s32[64]{0:T(128)S(1)}, s32[64]{0:T(128)}, u32[]{:S(2)}) copy-start(s32[64]{0:T(128)} %param.5) | copy-start | bytes 772
  2.7 15.3 %collective-permute-start.1 = (bf16[64,4224]{1,0:T(8,128)(2,1)S(1)}, bf16[64,4224]{1,0:T(8,128)(2,1)S(1)}, u32[]{:S(2)}, u32[]{:S(2)}) collective-permute-start(bf16[64,4224]{1,0:T(8,128)(2,1)S(1)} %select_convert_fusion), channel_id=1, source_target_pairs={{0,16},{8,24},{16,0},{24,8},{1,17},{9,25},{17,1},{25,9},{2,18},{10... | collective-permute-start | bytes 1622024 | tf_op jit(solution)/shard_map/ppermute | solution.py:69
  5.8 13.7 %collective-permute-start.3 = (bf16[64,4224]{1,0:T(8,128)(2,1)S(1)}, bf16[64,4224]{1,0:T(8,128)(2,1)S(1)}, u32[]{:S(2)}, u32[]{:S(2)}) collective-permute-start(bf16[64,4224]{1,0:T(8,128)(2,1)S(1)} %select_convert_fusion), channel_id=1, source_target_pairs={{0,2},{2,4},{4,6},{6,7},{7,5},{5,3},{3,1},{1,0},{8,10},{10,12},{12... | collective-permute-start | bytes 1622024 | tf_op jit(solution)/shard_map/ppermute | solution.py:60
  7.4 13.9 %collective-permute-start.7 = (bf16[64,4224]{1,0:T(8,128)(2,1)S(1)}, bf16[64,4224]{1,0:T(8,128)(2,1)S(1)}, u32[]{:S(2)}, u32[]{:S(2)}) collective-permute-start(bf16[64,4224]{1,0:T(8,128)(2,1)S(1)} %select_convert_fusion), channel_id=1, source_target_pairs={{2,0},{4,2},{6,4},{7,6},{5,7},{3,5},{1,3},{0,1},{10,8},{12,10},{14... | collective-permute-start | bytes 1622024 | tf_op jit(solution)/shard_map/ppermute | solution.py:60
  7.8 14.2 %collective-permute-start = (bf16[64,4224]{1,0:T(8,128)(2,1)S(1)}, bf16[64,4224]{1,0:T(8,128)(2,1)S(1)}, u32[]{:S(2)}, u32[]{:S(2)}) collective-permute-start(bf16[64,4224]{1,0:T(8,128)(2,1)S(1)} %select_convert_fusion), channel_id=1, source_target_pairs={{0,8},{8,0},{16,24},{24,16},{1,9},{9,1},{17,25},{25,17},{2,10},{10... | collective-permute-start | bytes 1622024 | tf_op jit(solution)/shard_map/ppermute | solution.py:70
  18.1 3.9 %collective-permute-start.2 = (bf16[64,4224]{1,0:T(8,128)(2,1)S(1)}, bf16[64,4224]{1,0:T(8,128)(2,1)S(1)}, u32[]{:S(2)}, u32[]{:S(2)}) collective-permute-start(bf16[64,4224]{1,0:T(8,128)(2,1)S(1)} %collective-permute-done.1), channel_id=1, source_target_pairs={{0,8},{8,0},{16,24},{24,16},{1,9},{9,1},{17,25},{25,17},{2,10},{10... | collective-permute-start | bytes 1622024 | tf_op jit(solution)/shard_map/ppermute | solution.py:71
  19.5 13.2 %collective-permute-start.4 = (bf16[64,4224]{1,0:T(8,128)(2,1)S(1)}, bf16[64,4224]{1,0:T(8,128)(2,1)S(1)}, u32[]{:S(2)}, u32[]{:S(2)}) collective-permute-start(bf16[64,4224]{1,0:T(8,128)(2,1)S(1)} %collective-permute-done.3), channel_id=1, source_target_pairs={{0,2},{2,4},{4,6},{6,7},{7,5},{5,3},{3,1},{1,0},{8,10},{10,12},{12... | collective-permute-start | bytes 1622024 | tf_op jit(solution)/shard_map/ppermute | solution.py:60
  21.3 14.2 %collective-permute-start.8 = (bf16[64,4224]{1,0:T(8,128)(2,1)S(1)}, bf16[64,4224]{1,0:T(8,128)(2,1)S(1)}, u32[]{:S(2)}, u32[]{:S(2)}) collective-permute-start(bf16[64,4224]{1,0:T(8,128)(2,1)S(1)} %collective-permute-done.7), channel_id=1, source_target_pairs={{2,0},{4,2},{6,4},{7,6},{5,7},{3,5},{1,3},{0,1},{10,8},{12,10},{14... | collective-permute-start | bytes 1622024 | tf_op jit(solution)/shard_map/ppermute | solution.py:60
  32.8 12.6 %collective-permute-start.5 = (bf16[64,4224]{1,0:T(8,128)(2,1)S(1)}, bf16[64,4224]{1,0:T(8,128)(2,1)S(1)}, u32[]{:S(2)}, u32[]{:S(2)}) collective-permute-start(bf16[64,4224]{1,0:T(8,128)(2,1)S(1)} %collective-permute-done.4), channel_id=1, source_target_pairs={{0,2},{2,4},{4,6},{6,7},{7,5},{5,3},{3,1},{1,0},{8,10},{10,12},{12... | collective-permute-start | bytes 1622024 | tf_op jit(solution)/shard_map/ppermute | solution.py:60
  35.6 12.4 %collective-permute-start.9 = (bf16[64,4224]{1,0:T(8,128)(2,1)S(1)}, bf16[64,4224]{1,0:T(8,128)(2,1)S(1)}, u32[]{:S(2)}, u32[]{:S(2)}) collective-permute-start(bf16[64,4224]{1,0:T(8,128)(2,1)S(1)} %collective-permute-done.8), channel_id=1, source_target_pairs={{2,0},{4,2},{6,4},{7,6},{5,7},{3,5},{1,3},{0,1},{10,8},{12,10},{14... | collective-permute-start | bytes 1622024 | tf_op jit(solution)/shard_map/ppermute | solution.py:60
  45.4 6.5 %collective-permute-start.6 = (bf16[32,4224]{1,0:T(8,128)(2,1)S(1)}, bf16[32,4224]{1,0:T(8,128)(2,1)S(1)}, u32[]{:S(2)}, u32[]{:S(2)}) collective-permute-start(bf16[32,4224]{1,0:T(8,128)(2,1)S(1)} %slice.148), channel_id=1, source_target_pairs={{0,2},{2,4},{4,6},{6,7},{7,5},{5,3},{3,1},{1,0},{8,10},{10,12},{12... | collective-permute-start | bytes 811016 | tf_op jit(solution)/shard_map/ppermute | solution.py:60
  48.0 6.5 %collective-permute-start.10 = (bf16[32,4224]{1,0:T(8,128)(2,1)S(1)}, bf16[32,4224]{1,0:T(8,128)(2,1)S(1)}, u32[]{:S(2)}, u32[]{:S(2)}) collective-permute-start(bf16[32,4224]{1,0:T(8,128)(2,1)S(1)} %slice.149), channel_id=1, source_target_pairs={{2,0},{4,2},{6,4},{7,6},{5,7},{3,5},{1,3},{0,1},{10,8},{12,10},{14... | collective-permute-start | bytes 811016 | tf_op jit(solution)/shard_map/ppermute | solution.py:60
  55.6 2.8 %collective-permute-start.11 = (f32[64]{0:T(128)S(1)}, f32[64]{0:T(128)S(1)}, u32[]{:S(2)}, u32[]{:S(2)}) collective-permute-start(f32[64]{0:T(128)S(1)} %get-tuple-element.9), channel_id=1, source_target_pairs={{0,8},{8,0},{16,24},{24,16},{1,9},{9,1},{17,25},{25,17},{2,10},{10... | collective-permute-start | bytes 776 | tf_op jit(solution)/shard_map/ppermute | solution.py:106
  55.6 4.3 %collective-permute-start.12 = (f32[64]{0:T(128)S(1)}, f32[64]{0:T(128)S(1)}, u32[]{:S(2)}, u32[]{:S(2)}) collective-permute-start(f32[64]{0:T(128)S(1)} %get-tuple-element.11), channel_id=1, source_target_pairs={{0,16},{8,24},{16,0},{24,8},{1,17},{9,25},{17,1},{25,9},{2,18},{10... | collective-permute-start | bytes 776 | tf_op jit(solution)/shard_map/ppermute | solution.py:106
  58.4 3.0 %collective-permute-start.13 = (f32[64]{0:T(128)S(1)}, f32[64]{0:T(128)S(1)}, u32[]{:S(2)}, u32[]{:S(2)}) collective-permute-start(f32[64]{0:T(128)S(1)} %get-tuple-element.10), channel_id=1, source_target_pairs={{0,24},{8,16},{16,8},{24,0},{1,25},{9,17},{17,9},{25,1},{2,26},{10... | collective-permute-start | bytes 776 | tf_op jit(solution)/shard_map/ppermute | solution.py:106

commit v15 on v14

--- a/solution.py
+++ b/solution.py
@@ -39,7 +39,9 @@
     block_count = lax.axis_size("blk")
     rows_here = embeddings.shape[0]
     widened = embeddings.astype(jnp.float32)
-    square_sum = jnp.sum(widened * widened, axis=1, keepdims=True)
+    squares = (widened * widened).reshape(rows_here, -1, 128)
+    partial_sums = lax.optimization_barrier(jnp.sum(squares, axis=1))
+    square_sum = jnp.sum(partial_sums, axis=1, keepdims=True)
     scale = lax.rsqrt(square_sum / D + 1e-06)
     high = (cluster_ids * 64 + row_index // 128).astype(jnp.float32)[:, None]
     low = (row_index % 128).astype(jnp.float32)[:, None]

time: 62.1 us -> 62.4 us (level)
    unnamed x0 -> x1, other arithmetic: none -> 1.11 us
    reduce_sum x1 -> x2, other arithmetic: 1.25 us -> 0.2 us  [the longest x1 0.11 us: per_device(): square_sum = jnp.sum(partial_sums, axis=1, keepdims=True)]
where the time goes in v15:
time: 62.4 us; the launch traced here: 62.2 us
  waiting for transfers between devices  35.9 us (58%)
  starting transfers between devices  14.2 us (23%)
  matrix products  6.25 us (10%)
  other arithmetic  5.2 us (8%)
    ppermute x8, waiting for transfers between devices, send(): return lax.ppermute(visiting, 'blk', forward if which == 0 else backward)  22.9 us
    ppermute x1, waiting for transfers between devices, per_device(): across = lax.ppermute(payload, 'grp', partner_pairs(group_count, 2))  10.1 us
    ppermute x8, starting transfers between devices, send(): return lax.ppermute(visiting, 'blk', forward if which == 0 else backward)  8.35 us
    dot_general x8, matrix products, block_best(): jnp.einsum('id,jd->ij', left_rows, payload[:, :D], preferred_element_type...  6.25 us
    ppermute x1, starting transfers between devices, per_device(): across = lax.ppermute(payload, 'grp', partner_pairs(group_count, 2))  3.07 us
    ppermute x3, waiting for transfers between devices, per_device(): result = jnp.maximum(result, lax.ppermute(best[k], 'grp', pairs))  2.95 us
    ppermute x3, starting transfers between devices, per_device(): result = jnp.maximum(result, lax.ppermute(best[k], 'grp', pairs))  2.81 us
    add x8, other arithmetic, tag_labels(): return high * 128.0 + low  1.39 us
  transfers between devices with their start and end apart: 14, of which 9 were waited for; matrix products, arithmetic and copies ran while one was open for 12% of the time, Pallas kernels for 0%

profile of v15, /device:TPU:0, one launch (start us, length us, event | category | flops | bytes accessed | tf_op | source)
XLA Modules:
  0.0 62.2 jit_solution(9361222752306620372)
XLA Ops:
  0.0 1.1 %multiply_bitcast_fusion = f32[8,8,32,128]{3,1,2,0:T(8,128)S(1)} fusion(bf16[64,4096]{1,0:T(8,128)(2,1)} %param.3), kind=kLoop, calls=%fused_computation.21 | loop fusion | flops 524288 | bytes 1572864
  1.1 1.1 %convert_element_type.200 = f32[64,4096]{1,0:T(8,128)S(1)} convert(bf16[64,4096]{1,0:T(8,128)(2,1)} %param.3) | non-fusion elementwise | flops 262144 | bytes 1572864 | tf_op jit(solution)/shard_map/convert_element_type | solution.py:41
  2.3 0.2 copy.4
  2.5 0.1 bitcast_reduce_fusion
  2.6 0.1 reduce_sum.19
  2.7 0.3 select_convert_fusion
  3.0 3.1 %collective-permute-start.1 = (bf16[64,4224]{1,0:T(8,128)(2,1)S(1)}, bf16[64,4224]{1,0:T(8,128)(2,1)S(1)}, u32[]{:S(2)}, u32[]{:S(2)}) collective-permute-start(bf16[64,4224]{1,0:T(8,128)(2,1)S(1)} %select_convert_fusion), channel_id=1, source_target_pairs={{0,16},{8,24},{16,0},{24,8},{1,17},{9,25},{17,1},{25,9},{2,18},{10... | collective-permute-start | bytes 1622024 | tf_op jit(solution)/shard_map/ppermute | solution.py:71
  6.1 1.6 %collective-permute-start.3 = (bf16[64,4224]{1,0:T(8,128)(2,1)S(1)}, bf16[64,4224]{1,0:T(8,128)(2,1)S(1)}, u32[]{:S(2)}, u32[]{:S(2)}) collective-permute-start(bf16[64,4224]{1,0:T(8,128)(2,1)S(1)} %select_convert_fusion), channel_id=1, source_target_pairs={{0,2},{2,4},{4,6},{6,7},{7,5},{5,3},{3,1},{1,0},{8,10},{10,12},{12... | collective-permute-start | bytes 1622024 | tf_op jit(solution)/shard_map/ppermute | solution.py:62
  7.7 0.4 collective-permute-start.7
  8.1 0.2 add_reduce_fusion.7
  8.3 10.1 %collective-permute-done.1 = bf16[64,4224]{1,0:T(8,128)(2,1)S(1)} collective-permute-done((bf16[64,4224]{1,0:T(8,128)(2,1)S(1)}, bf16[64,4224]{1,0:T(8,128)(2,1)S(1)}, u32[]{:S(2)}, u32[]{:S(2)}) %collective-permute-start.1) | collective-permute-done | bytes 540704 | tf_op jit(solution)/shard_map/ppermute | solution.py:71
  18.4 1.5 %collective-permute-done.3 = bf16[64,4224]{1,0:T(8,128)(2,1)S(1)} collective-permute-done((bf16[64,4224]{1,0:T(8,128)(2,1)S(1)}, bf16[64,4224]{1,0:T(8,128)(2,1)S(1)}, u32[]{:S(2)}, u32[]{:S(2)}) %collective-permute-start.3) | collective-permute-done | bytes 540704 | tf_op jit(solution)/shard_map/ppermute | solution.py:62
  19.8 1.6 %collective-permute-start.4 = (bf16[64,4224]{1,0:T(8,128)(2,1)S(1)}, bf16[64,4224]{1,0:T(8,128)(2,1)S(1)}, u32[]{:S(2)}, u32[]{:S(2)}) collective-permute-start(bf16[64,4224]{1,0:T(8,128)(2,1)S(1)} %collective-permute-done.3), channel_id=1, source_target_pairs={{0,2},{2,4},{4,6},{6,7},{7,5},{5,3},{3,1},{1,0},{8,10},{10,12},{12... | collective-permute-start | bytes 1622024 | tf_op jit(solution)/shard_map/ppermute | solution.py:62
  21.4 0.2 add_reduce_fusion.6
  21.6 0.5 collective-permute-start.8
  22.1 0.2 add_reduce_fusion.2
  22.3 0.1 pad_maximum_fusion.4
  22.4 0.2 floor_reduce_fusion
  22.6 0.2 pad_maximum_fusion
  22.8 10.2 %collective-permute-done.4 = bf16[64,4224]{1,0:T(8,128)(2,1)S(1)} collective-permute-done((bf16[64,4224]{1,0:T(8,128)(2,1)S(1)}, bf16[64,4224]{1,0:T(8,128)(2,1)S(1)}, u32[]{:S(2)}, u32[]{:S(2)}) %collective-permute-start.4) | collective-permute-done | bytes 540704 | tf_op jit(solution)/shard_map/ppermute | solution.py:62
  33.1 1.8 %collective-permute-start.5 = (bf16[64,4224]{1,0:T(8,128)(2,1)S(1)}, bf16[64,4224]{1,0:T(8,128)(2,1)S(1)}, u32[]{:S(2)}, u32[]{:S(2)}) collective-permute-start(bf16[64,4224]{1,0:T(8,128)(2,1)S(1)} %collective-permute-done.4), channel_id=1, source_target_pairs={{0,2},{2,4},{4,6},{6,7},{7,5},{5,3},{3,1},{1,0},{8,10},{10,12},{12... | collective-permute-start | bytes 1622024 | tf_op jit(solution)/shard_map/ppermute | solution.py:62
  34.9 0.2 add_reduce_fusion.5
  35.1 0.8 %fusion = f32[256]{0:T(256)S(1)} fusion(bf16[256,4096]{1,0:T(8,128)(2,1)S(1)} %pad_maximum_fusion, bf16[64,4224]{1,0:T(8,128)(2,1)S(1)} %select_convert_fusion, f32[256]{0:T(256)S(1)} %get-tuple-element.6, f32[256]{0:T(256)S(1)} %get-tuple-element.5, f32[64]{0:T(128)S(1)} %add_reduce_fusion.7, f32[64]{0:T(128)S(1)} %multiply_floor_fusion.7), kind=kOutput, calls=%fused_computation.11 | convolution fusion | flops 134299392 | bytes 2625536 | tf_op jit(solution)/shard_map/id,jd->ij/dot_general | solution.py:26
  35.9 0.3 collective-permute-start.9
  36.1 0.2 add_reduce_fusion.1
  36.3 0.8 %fusion.1 = f32[256]{0:T(256)S(1)} fusion(bf16[256,4096]{1,0:T(8,128)(2,1)S(1)} %pad_maximum_fusion, bf16[64,4224]{1,0:T(8,128)(2,1)S(1)} %collective-permute-done.3, f32[256]{0:T(256)S(1)} %get-tuple-element.6, f32[256]{0:T(256)S(1)} %get-tuple-element.5, f32[64]{0:T(128)S(1)} %add_reduce_fusion.6, f32[64]{0:T(128)S(1)} %multiply_floor_fusion.6), kind=kOutput, calls=%fused_computation.12 | convolution fusion | flops 134299392 | bytes 2625536 | tf_op jit(solution)/shard_map/id,jd->ij/dot_general | solution.py:26
  37.1 0.8 %fusion.2 = f32[256]{0:T(256)S(1)} fusion(bf16[256,4096]{1,0:T(8,128)(2,1)S(1)} %pad_maximum_fusion, bf16[64,4224]{1,0:T(8,128)(2,1)S(1)} %collective-permute-done.4, f32[256]{0:T(256)S(1)} %get-tuple-element.6, f32[256]{0:T(256)S(1)} %get-tuple-element.5, f32[64]{0:T(128)S(1)} %add_reduce_fusion.5, f32[64]{0:T(128)S(1)} %multiply_floor_fusion.5), kind=kOutput, calls=%fused_computation.13 | convolution fusion | flops 134299392 | bytes 2625536 | tf_op jit(solution)/shard_map/id,jd->ij/dot_general | solution.py:26
  37.9 0.8 %fusion.6 = f32[256]{0:T(256)S(1)} fusion(bf16[256,4096]{1,0:T(8,128)(2,1)S(1)} %pad_maximum_fusion, bf16[64,4224]{1,0:T(8,128)(2,1)S(1)} %collective-permute-done.8, f32[256]{0:T(256)S(1)} %get-tuple-element.6, f32[256]{0:T(256)S(1)} %get-tuple-element.5, f32[64]{0:T(128)S(1)} %add_reduce_fusion.1, f32[64]{0:T(128)S(1)} %multiply_floor_fusion.1), kind=kOutput, calls=%fused_computation.17 | convolution fusion | flops 134299392 | bytes 2625536 | tf_op jit(solution)/shard_map/id,jd->ij/dot_general | solution.py:26
  38.7 0.8 %fusion.5 = f32[256]{0:T(256)S(1)} fusion(bf16[256,4096]{1,0:T(8,128)(2,1)S(1)} %pad_maximum_fusion, bf16[64,4224]{1,0:T(8,128)(2,1)S(1)} %collective-permute-done.7, f32[256]{0:T(256)S(1)} %get-tuple-element.6, f32[256]{0:T(256)S(1)} %get-tuple-element.5, f32[64]{0:T(128)S(1)} %add_reduce_fusion.2, f32[64]{0:T(128)S(1)} %multiply_floor_fusion.2), kind=kOutput, calls=%fused_computation.16 | convolution fusion | flops 134299392 | bytes 2625536 | tf_op jit(solution)/shard_map/id,jd->ij/dot_general | solution.py:26
  39.5 6.2 %collective-permute-done.5 = bf16[64,4224]{1,0:T(8,128)(2,1)S(1)} collective-permute-done((bf16[64,4224]{1,0:T(8,128)(2,1)S(1)}, bf16[64,4224]{1,0:T(8,128)(2,1)S(1)}, u32[]{:S(2)}, u32[]{:S(2)}) %collective-permute-start.5) | collective-permute-done | bytes 540704 | tf_op jit(solution)/shard_map/ppermute | solution.py:62
  45.7 1.9 %collective-permute-start.6 = (bf16[32,4224]{1,0:T(8,128)(2,1)S(1)}, bf16[32,4224]{1,0:T(8,128)(2,1)S(1)}, u32[]{:S(2)}, u32[]{:S(2)}) collective-permute-start(bf16[32,4224]{1,0:T(8,128)(2,1)S(1)} %slice.148), channel_id=1, source_target_pairs={{0,2},{2,4},{4,6},{6,7},{7,5},{5,3},{3,1},{1,0},{8,10},{10,12},{12... | collective-permute-start | bytes 811016 | tf_op jit(solution)/shard_map/ppermute | solution.py:62
  47.5 0.2 add_reduce_fusion.4
  47.7 0.5 collective-permute-done.9
  48.3 0.3 collective-permute-start.10
  48.6 0.2 add_reduce_fusion
  48.8 0.8 %fusion.3 = f32[256]{0:T(256)S(1)} fusion(bf16[256,4096]{1,0:T(8,128)(2,1)S(1)} %pad_maximum_fusion, bf16[64,4224]{1,0:T(8,128)(2,1)S(1)} %collective-permute-done.5, f32[256]{0:T(256)S(1)} %get-tuple-element.6, f32[256]{0:T(256)S(1)} %get-tuple-element.5, f32[64]{0:T(128)S(1)} %add_reduce_fusion.4, f32[64]{0:T(128)S(1)} %multiply_floor_fusion.4), kind=kOutput, calls=%fused_computation.14 | convolution fusion | flops 134299392 | bytes 2625536 | tf_op jit(solution)/shard_map/id,jd->ij/dot_general | solution.py:26
  49.6 0.8 %fusion.7 = f32[256]{0:T(256)S(1)} fusion(bf16[256,4096]{1,0:T(8,128)(2,1)S(1)} %pad_maximum_fusion, bf16[64,4224]{1,0:T(8,128)(2,1)S(1)} %collective-permute-done.9, f32[256]{0:T(256)S(1)} %get-tuple-element.6, f32[256]{0:T(256)S(1)} %get-tuple-element.5, f32[64]{0:T(128)S(1)} %add_reduce_fusion, f32[64]{0:T(128)S(1)} %multiply_floor_fusion), kind=kOutput, calls=%fused_computation.18 | convolution fusion | flops 134299392 | bytes 2625536 | tf_op jit(solution)/shard_map/id,jd->ij/dot_general | solution.py:26
  50.3 1.8 %collective-permute-done.6 = bf16[32,4224]{1,0:T(8,128)(2,1)S(1)} collective-permute-done((bf16[32,4224]{1,0:T(8,128)(2,1)S(1)}, bf16[32,4224]{1,0:T(8,128)(2,1)S(1)}, u32[]{:S(2)}, u32[]{:S(2)}) %collective-permute-start.6) | collective-permute-done | bytes 270368 | tf_op jit(solution)/shard_map/ppermute | solution.py:62
  52.2 2.6 %collective-permute-done.10 = bf16[32,4224]{1,0:T(8,128)(2,1)S(1)} collective-permute-done((bf16[32,4224]{1,0:T(8,128)(2,1)S(1)}, bf16[32,4224]{1,0:T(8,128)(2,1)S(1)}, u32[]{:S(2)}, u32[]{:S(2)}) %collective-permute-start.10) | collective-permute-done | bytes 270368 | tf_op jit(solution)/shard_map/ppermute | solution.py:62
  54.8 0.2 add_reduce_fusion.3
  55.0 0.8 %fusion.4 = f32[256]{0:T(256)S(1)} fusion(bf16[256,4096]{1,0:T(8,128)(2,1)S(1)} %pad_maximum_fusion, bf16[64,4224]{1,0:T(8,128)(2,1)S(1)} %constant_dynamic-update-slice_fusion, f32[256]{0:T(256)S(1)} %get-tuple-element.6, f32[256]{0:T(256)S(1)} %get-tuple-element.5, f32[64]{0:T(128)S(1)} %add_reduce_fusion.3, f32[64]{0:T(128)S(1)} %multiply_floor_fusion.3), kind=kOutput, calls=%fused_computation.15 | convolution fusion | flops 134299392 | bytes 2625536 | tf_op jit(solution)/shard_map/id,jd->ij/dot_general | solution.py:26
  55.8 0.1 fusion.18
  55.9 0.0 collective-permute-start.11
  55.9 2.8 %collective-permute-start.12 = (f32[64]{0:T(128)S(1)}, f32[64]{0:T(128)S(1)}, u32[]{:S(2)}, u32[]{:S(2)}) collective-permute-start(f32[64]{0:T(128)S(1)} %get-tuple-element.11), channel_id=1, source_target_pairs={{0,16},{8,24},{16,0},{24,8},{1,17},{9,25},{17,1},{25,9},{2,18},{10... | collective-permute-start | bytes 776 | tf_op jit(solution)/shard_map/ppermute | solution.py:108
  58.7 0.0 collective-permute-start.13
  58.7 1.5 %collective-permute-done.12 = f32[64]{0:T(128)S(1)} collective-permute-done((f32[64]{0:T(128)S(1)}, f32[64]{0:T(128)S(1)}, u32[]{:S(2)}, u32[]{:S(2)}) %collective-permute-start.12) | collective-permute-done | bytes 288 | tf_op jit(solution)/shard_map/ppermute | solution.py:108
  60.2 1.4 %collective-permute-done.13 = f32[64]{0:T(128)S(1)} collective-permute-done((f32[64]{0:T(128)S(1)}, f32[64]{0:T(128)S(1)}, u32[]{:S(2)}, u32[]{:S(2)}) %collective-permute-start.13) | collective-permute-done | bytes 288 | tf_op jit(solution)/shard_map/ppermute | solution.py:108
  61.7 0.5 maximum_maximum_fusion.1
  (28 shorter events, 0.2 us)
Async XLA Ops:
  1.1 1.6 %copy-start = (s32[64]{0:T(128)S(1)}, s32[64]{0:T(128)}, u32[]{:S(2)}) copy-start(s32[64]{0:T(128)} %param.4) | copy-start | bytes 772
  1.1 1.6 %copy-start.1 = (s32[64]{0:T(128)S(1)}, s32[64]{0:T(128)}, u32[]{:S(2)}) copy-start(s32[64]{0:T(128)} %param.5) | copy-start | bytes 772
  3.0 15.3 %collective-permute-start.1 = (bf16[64,4224]{1,0:T(8,128)(2,1)S(1)}, bf16[64,4224]{1,0:T(8,128)(2,1)S(1)}, u32[]{:S(2)}, u32[]{:S(2)}) collective-permute-start(bf16[64,4224]{1,0:T(8,128)(2,1)S(1)} %select_convert_fusion), channel_id=1, source_target_pairs={{0,16},{8,24},{16,0},{24,8},{1,17},{9,25},{17,1},{25,9},{2,18},{10... | collective-permute-start | bytes 1622024 | tf_op jit(solution)/shard_map/ppermute | solution.py:71
  6.1 13.7 %collective-permute-start.3 = (bf16[64,4224]{1,0:T(8,128)(2,1)S(1)}, bf16[64,4224]{1,0:T(8,128)(2,1)S(1)}, u32[]{:S(2)}, u32[]{:S(2)}) collective-permute-start(bf16[64,4224]{1,0:T(8,128)(2,1)S(1)} %select_convert_fusion), channel_id=1, source_target_pairs={{0,2},{2,4},{4,6},{6,7},{7,5},{5,3},{3,1},{1,0},{8,10},{10,12},{12... | collective-permute-start | bytes 1622024 | tf_op jit(solution)/shard_map/ppermute | solution.py:62
  7.7 13.9 %collective-permute-start.7 = (bf16[64,4224]{1,0:T(8,128)(2,1)S(1)}, bf16[64,4224]{1,0:T(8,128)(2,1)S(1)}, u32[]{:S(2)}, u32[]{:S(2)}) collective-permute-start(bf16[64,4224]{1,0:T(8,128)(2,1)S(1)} %select_convert_fusion), channel_id=1, source_target_pairs={{2,0},{4,2},{6,4},{7,6},{5,7},{3,5},{1,3},{0,1},{10,8},{12,10},{14... | collective-permute-start | bytes 1622024 | tf_op jit(solution)/shard_map/ppermute | solution.py:62
  8.1 14.2 %collective-permute-start = (bf16[64,4224]{1,0:T(8,128)(2,1)S(1)}, bf16[64,4224]{1,0:T(8,128)(2,1)S(1)}, u32[]{:S(2)}, u32[]{:S(2)}) collective-permute-start(bf16[64,4224]{1,0:T(8,128)(2,1)S(1)} %select_convert_fusion), channel_id=1, source_target_pairs={{0,8},{8,0},{16,24},{24,16},{1,9},{9,1},{17,25},{25,17},{2,10},{10... | collective-permute-start | bytes 1622024 | tf_op jit(solution)/shard_map/ppermute | solution.py:72
  18.4 3.9 %collective-permute-start.2 = (bf16[64,4224]{1,0:T(8,128)(2,1)S(1)}, bf16[64,4224]{1,0:T(8,128)(2,1)S(1)}, u32[]{:S(2)}, u32[]{:S(2)}) collective-permute-start(bf16[64,4224]{1,0:T(8,128)(2,1)S(1)} %collective-permute-done.1), channel_id=1, source_target_pairs={{0,8},{8,0},{16,24},{24,16},{1,9},{9,1},{17,25},{25,17},{2,10},{10... | collective-permute-start | bytes 1622024 | tf_op jit(solution)/shard_map/ppermute | solution.py:73
  19.8 13.2 %collective-permute-start.4 = (bf16[64,4224]{1,0:T(8,128)(2,1)S(1)}, bf16[64,4224]{1,0:T(8,128)(2,1)S(1)}, u32[]{:S(2)}, u32[]{:S(2)}) collective-permute-start(bf16[64,4224]{1,0:T(8,128)(2,1)S(1)} %collective-permute-done.3), channel_id=1, source_target_pairs={{0,2},{2,4},{4,6},{6,7},{7,5},{5,3},{3,1},{1,0},{8,10},{10,12},{12... | collective-permute-start | bytes 1622024 | tf_op jit(solution)/shard_map/ppermute | solution.py:62
  21.6 14.2 %collective-permute-start.8 = (bf16[64,4224]{1,0:T(8,128)(2,1)S(1)}, bf16[64,4224]{1,0:T(8,128)(2,1)S(1)}, u32[]{:S(2)}, u32[]{:S(2)}) collective-permute-start(bf16[64,4224]{1,0:T(8,128)(2,1)S(1)} %collective-permute-done.7), channel_id=1, source_target_pairs={{2,0},{4,2},{6,4},{7,6},{5,7},{3,5},{1,3},{0,1},{10,8},{12,10},{14... | collective-permute-start | bytes 1622024 | tf_op jit(solution)/shard_map/ppermute | solution.py:62
  33.1 12.6 %collective-permute-start.5 = (bf16[64,4224]{1,0:T(8,128)(2,1)S(1)}, bf16[64,4224]{1,0:T(8,128)(2,1)S(1)}, u32[]{:S(2)}, u32[]{:S(2)}) collective-permute-start(bf16[64,4224]{1,0:T(8,128)(2,1)S(1)} %collective-permute-done.4), channel_id=1, source_target_pairs={{0,2},{2,4},{4,6},{6,7},{7,5},{5,3},{3,1},{1,0},{8,10},{10,12},{12... | collective-permute-start | bytes 1622024 | tf_op jit(solution)/shard_map/ppermute | solution.py:62
  35.9 12.4 %collective-permute-start.9 = (bf16[64,4224]{1,0:T(8,128)(2,1)S(1)}, bf16[64,4224]{1,0:T(8,128)(2,1)S(1)}, u32[]{:S(2)}, u32[]{:S(2)}) collective-permute-start(bf16[64,4224]{1,0:T(8,128)(2,1)S(1)} %collective-permute-done.8), channel_id=1, source_target_pairs={{2,0},{4,2},{6,4},{7,6},{5,7},{3,5},{1,3},{0,1},{10,8},{12,10},{14... | collective-permute-start | bytes 1622024 | tf_op jit(solution)/shard_map/ppermute | solution.py:62
  45.7 6.5 %collective-permute-start.6 = (bf16[32,4224]{1,0:T(8,128)(2,1)S(1)}, bf16[32,4224]{1,0:T(8,128)(2,1)S(1)}, u32[]{:S(2)}, u32[]{:S(2)}) collective-permute-start(bf16[32,4224]{1,0:T(8,128)(2,1)S(1)} %slice.148), channel_id=1, source_target_pairs={{0,2},{2,4},{4,6},{6,7},{7,5},{5,3},{3,1},{1,0},{8,10},{10,12},{12... | collective-permute-start | bytes 811016 | tf_op jit(solution)/shard_map/ppermute | solution.py:62
  48.3 6.5 %collective-permute-start.10 = (bf16[32,4224]{1,0:T(8,128)(2,1)S(1)}, bf16[32,4224]{1,0:T(8,128)(2,1)S(1)}, u32[]{:S(2)}, u32[]{:S(2)}) collective-permute-start(bf16[32,4224]{1,0:T(8,128)(2,1)S(1)} %slice.149), channel_id=1, source_target_pairs={{2,0},{4,2},{6,4},{7,6},{5,7},{3,5},{1,3},{0,1},{10,8},{12,10},{14... | collective-permute-start | bytes 811016 | tf_op jit(solution)/shard_map/ppermute | solution.py:62
  55.9 2.8 %collective-permute-start.11 = (f32[64]{0:T(128)S(1)}, f32[64]{0:T(128)S(1)}, u32[]{:S(2)}, u32[]{:S(2)}) collective-permute-start(f32[64]{0:T(128)S(1)} %get-tuple-element.9), channel_id=1, source_target_pairs={{0,8},{8,0},{16,24},{24,16},{1,9},{9,1},{17,25},{25,17},{2,10},{10... | collective-permute-start | bytes 776 | tf_op jit(solution)/shard_map/ppermute | solution.py:108
  55.9 4.3 %collective-permute-start.12 = (f32[64]{0:T(128)S(1)}, f32[64]{0:T(128)S(1)}, u32[]{:S(2)}, u32[]{:S(2)}) collective-permute-start(f32[64]{0:T(128)S(1)} %get-tuple-element.11), channel_id=1, source_target_pairs={{0,16},{8,24},{16,0},{24,8},{1,17},{9,25},{17,1},{25,9},{2,18},{10... | collective-permute-start | bytes 776 | tf_op jit(solution)/shard_map/ppermute | solution.py:108
  58.7 3.0 %collective-permute-start.13 = (f32[64]{0:T(128)S(1)}, f32[64]{0:T(128)S(1)}, u32[]{:S(2)}, u32[]{:S(2)}) collective-permute-start(f32[64]{0:T(128)S(1)} %get-tuple-element.10), channel_id=1, source_target_pairs={{0,24},{8,16},{16,8},{24,0},{1,25},{9,17},{17,9},{25,1},{2,26},{10... | collective-permute-start | bytes 776 | tf_op jit(solution)/shard_map/ppermute | solution.py:108

commit v16 on v14

--- a/solution.py
+++ b/solution.py
@@ -66,7 +66,10 @@
             chain[2].append(chain[0])
 
     if group_count == 4:
-        across = lax.ppermute(payload, "grp", partner_pairs(group_count, 2))
+        later = payload
+        if steps >= 1:
+            later, _ = lax.optimization_barrier((payload, chains[0][0]))
+        across = lax.ppermute(later, "grp", partner_pairs(group_count, 2))
         beside = lax.ppermute(payload, "grp", partner_pairs(group_count, 1))
         diagonal = lax.ppermute(across, "grp", partner_pairs(group_count, 1))
         segment_pairs = [partner_pairs(group_count, k) for k in range(1, 4)]
@@ -90,6 +93,8 @@
             visiting, best, pending = chain
             visiting = send(which, visiting, step)
             best = fold(best, pending)
+            if step >= 3:
+                visiting, best = lax.optimization_barrier((visiting, best))
             chain[0], chain[1], chain[2] = visiting, best, [visiting]
     if steps >= 1 and block_count % 2 == 0:
         chains[0][2] = [jnp.concatenate([chains[0][2][-1], chains[1][2][-1]], axis=0)] + chains[0][2][:-1]

time: 62.1 us -> 64.5 us (1.039)
  waiting for transfers between devices: 35.9 us -> 38.7 us
    ppermute x8, waiting for transfers between devices: 22.9 us -> 26.6 us  [send(): return lax.ppermute(visiting, 'blk', forward if which == 0 else backward)]
    ppermute x1, starting transfers between devices: 3.06 us -> 1.77 us  [per_device(): across = lax.ppermute(later, 'grp', partner_pairs(group_count, 2))]
    ppermute x8, starting transfers between devices: 8.35 us -> 9.39 us  [send(): return lax.ppermute(visiting, 'blk', forward if which == 0 else backward)]
    ppermute x1, waiting for transfers between devices: 10.1 us -> 9.21 us  [per_device(): across = lax.ppermute(later, 'grp', partner_pairs(group_count, 2))]
  transfers between devices with their start and end apart: 14 -> 14, of which waited for: 9 -> 8; matrix products, arithmetic and copies ran while one was open for 12% -> 11% of each run, Pallas kernels for 0% -> 0%
where the time goes in v16:
time: 64.5 us; the launch traced here: 64.4 us
  waiting for transfers between devices  38.7 us (60%)
  starting transfers between devices  13.8 us (21%)
  matrix products  6.24 us (10%)
  other arithmetic  5.15 us (8%)
    ppermute x8, waiting for transfers between devices, send(): return lax.ppermute(visiting, 'blk', forward if which == 0 else backward)  26.6 us
    ppermute x8, starting transfers between devices, send(): return lax.ppermute(visiting, 'blk', forward if which == 0 else backward)  9.39 us
    ppermute x1, waiting for transfers between devices, per_device(): across = lax.ppermute(later, 'grp', partner_pairs(group_count, 2))  9.21 us
    dot_general x8, matrix products, block_best(): jnp.einsum('id,jd->ij', left_rows, payload[:, :D], preferred_element_type...  6.24 us
    ppermute x3, waiting for transfers between devices, per_device(): result = jnp.maximum(result, lax.ppermute(best[k], 'grp', pairs))  2.95 us
    ppermute x3, starting transfers between devices, per_device(): result = jnp.maximum(result, lax.ppermute(best[k], 'grp', pairs))  2.65 us
    ppermute x1, starting transfers between devices, per_device(): across = lax.ppermute(later, 'grp', partner_pairs(group_count, 2))  1.77 us
    add x8, other arithmetic, tag_labels(): return high * 128.0 + low  1.39 us
  transfers between devices with their start and end apart: 14, of which 8 were waited for; matrix products, arithmetic and copies ran while one was open for 11% of the time, Pallas kernels for 0%

profile of v16, /device:TPU:0, one launch (start us, length us, event | category | flops | bytes accessed | tf_op | source)
XLA Modules:
  0.0 64.4 jit_solution(10873313054136577629)
XLA Ops:
  0.0 1.1 %convert_element_type.200 = f32[64,4096]{1,0:T(8,128)S(1)} convert(bf16[64,4096]{1,0:T(8,128)(2,1)} %param.3) | non-fusion elementwise | flops 262144 | bytes 1572864 | tf_op jit(solution)/shard_map/convert_element_type | solution.py:41
  1.1 1.2 %multiply_reduce_fusion = f32[64]{0:T(128)S(1)} fusion(bf16[64,4096]{1,0:T(8,128)(2,1)} %param.3), kind=kLoop, calls=%fused_computation.20 | loop fusion | flops 786368 | bytes 524544 | tf_op jit(solution)/shard_map/reduce_sum | solution.py:42
  2.4 0.3 select_convert_fusion
  2.7 3.1 %collective-permute-start = (bf16[64,4224]{1,0:T(8,128)(2,1)S(1)}, bf16[64,4224]{1,0:T(8,128)(2,1)S(1)}, u32[]{:S(2)}, u32[]{:S(2)}) collective-permute-start(bf16[64,4224]{1,0:T(8,128)(2,1)S(1)} %select_convert_fusion), channel_id=1, source_target_pairs={{0,2},{2,4},{4,6},{6,7},{7,5},{5,3},{3,1},{1,0},{8,10},{10,12},{12... | collective-permute-start | bytes 1622024 | tf_op jit(solution)/shard_map/ppermute | solution.py:60
  5.9 0.0 collective-permute-start.3
  5.9 0.2 add_reduce_fusion.7
  6.0 12.0 %collective-permute-done = bf16[64,4224]{1,0:T(8,128)(2,1)S(1)} collective-permute-done((bf16[64,4224]{1,0:T(8,128)(2,1)S(1)}, bf16[64,4224]{1,0:T(8,128)(2,1)S(1)}, u32[]{:S(2)}, u32[]{:S(2)}) %collective-permute-start) | collective-permute-done | bytes 540704 | tf_op jit(solution)/shard_map/ppermute | solution.py:60
  18.0 1.8 %collective-permute-start.4 = (bf16[64,4224]{1,0:T(8,128)(2,1)S(1)}, bf16[64,4224]{1,0:T(8,128)(2,1)S(1)}, u32[]{:S(2)}, u32[]{:S(2)}) collective-permute-start(bf16[64,4224]{1,0:T(8,128)(2,1)S(1)} %select_convert_fusion), channel_id=1, source_target_pairs={{0,16},{8,24},{16,0},{24,8},{1,17},{9,25},{17,1},{25,9},{2,18},{10... | collective-permute-start | bytes 1622024 | tf_op jit(solution)/shard_map/ppermute | solution.py:72
  19.8 1.6 %collective-permute-start.1 = (bf16[64,4224]{1,0:T(8,128)(2,1)S(1)}, bf16[64,4224]{1,0:T(8,128)(2,1)S(1)}, u32[]{:S(2)}, u32[]{:S(2)}) collective-permute-start(bf16[64,4224]{1,0:T(8,128)(2,1)S(1)} %collective-permute-done), channel_id=1, source_target_pairs={{0,2},{2,4},{4,6},{6,7},{7,5},{5,3},{3,1},{1,0},{8,10},{10,12},{12... | collective-permute-start | bytes 1622024 | tf_op jit(solution)/shard_map/ppermute | solution.py:60
  21.4 0.2 add_reduce_fusion.6
  21.6 0.0 collective-permute-done.7
  21.6 0.5 collective-permute-start.8
  22.1 0.2 add_reduce_fusion.3
  22.3 9.2 %collective-permute-done.4 = bf16[64,4224]{1,0:T(8,128)(2,1)S(1)} collective-permute-done((bf16[64,4224]{1,0:T(8,128)(2,1)S(1)}, bf16[64,4224]{1,0:T(8,128)(2,1)S(1)}, u32[]{:S(2)}, u32[]{:S(2)}) %collective-permute-start.4) | collective-permute-done | bytes 540704 | tf_op jit(solution)/shard_map/ppermute | solution.py:72
  31.5 0.0 collective-permute-start.5
  31.5 1.2 %collective-permute-done.1 = bf16[64,4224]{1,0:T(8,128)(2,1)S(1)} collective-permute-done((bf16[64,4224]{1,0:T(8,128)(2,1)S(1)}, bf16[64,4224]{1,0:T(8,128)(2,1)S(1)}, u32[]{:S(2)}, u32[]{:S(2)}) %collective-permute-start.1) | collective-permute-done | bytes 540704 | tf_op jit(solution)/shard_map/ppermute | solution.py:60
  32.7 1.6 %collective-permute-start.2 = (bf16[64,4224]{1,0:T(8,128)(2,1)S(1)}, bf16[64,4224]{1,0:T(8,128)(2,1)S(1)}, u32[]{:S(2)}, u32[]{:S(2)}) collective-permute-start(bf16[64,4224]{1,0:T(8,128)(2,1)S(1)} %collective-permute-done.1), channel_id=1, source_target_pairs={{0,2},{2,4},{4,6},{6,7},{7,5},{5,3},{3,1},{1,0},{8,10},{10,12},{12... | collective-permute-start | bytes 1622024 | tf_op jit(solution)/shard_map/ppermute | solution.py:60
  34.3 0.2 add_reduce_fusion.5
  34.4 0.0 collective-permute-done.8
  34.5 0.5 collective-permute-start.9
  35.0 0.2 add_reduce_fusion.2
  35.2 0.0 collective-permute-done.3
  35.2 0.1 pad_maximum_fusion.4
  35.3 0.2 floor_reduce_fusion
  35.4 0.3 pad_maximum_fusion
  35.7 0.8 %fusion = f32[256]{0:T(256)S(1)} fusion(bf16[256,4096]{1,0:T(8,128)(2,1)S(1)} %pad_maximum_fusion, bf16[64,4224]{1,0:T(8,128)(2,1)S(1)} %select_convert_fusion, f32[256]{0:T(256)S(1)} %get-tuple-element.24, f32[256]{0:T(256)S(1)} %get-tuple-element.23, f32[64]{0:T(128)S(1)} %add_reduce_fusion.7, f32[64]{0:T(128)S(1)} %multiply_floor_fusion.7), kind=kOutput, calls=%fused_computation.11 | convolution fusion | flops 134299392 | bytes 2625536 | tf_op jit(solution)/shard_map/id,jd->ij/dot_general | solution.py:26
  36.5 0.8 %fusion.1 = f32[256]{0:T(256)S(1)} fusion(bf16[256,4096]{1,0:T(8,128)(2,1)S(1)} %pad_maximum_fusion, bf16[64,4224]{1,0:T(8,128)(2,1)S(1)} %collective-permute-done, f32[256]{0:T(256)S(1)} %get-tuple-element.24, f32[256]{0:T(256)S(1)} %get-tuple-element.23, f32[64]{0:T(128)S(1)} %add_reduce_fusion.6, f32[64]{0:T(128)S(1)} %multiply_floor_fusion.6), kind=kOutput, calls=%fused_computation.12 | convolution fusion | flops 134299392 | bytes 2625536 | tf_op jit(solution)/shard_map/id,jd->ij/dot_general | solution.py:26
  37.2 0.8 %fusion.2 = f32[256]{0:T(256)S(1)} fusion(bf16[256,4096]{1,0:T(8,128)(2,1)S(1)} %pad_maximum_fusion, bf16[64,4224]{1,0:T(8,128)(2,1)S(1)} %collective-permute-done.1, f32[256]{0:T(256)S(1)} %get-tuple-element.24, f32[256]{0:T(256)S(1)} %get-tuple-element.23, f32[64]{0:T(128)S(1)} %add_reduce_fusion.5, f32[64]{0:T(128)S(1)} %multiply_floor_fusion.5), kind=kOutput, calls=%fused_computation.13 | convolution fusion | flops 134299392 | bytes 2625536 | tf_op jit(solution)/shard_map/id,jd->ij/dot_general | solution.py:26
  38.0 8.1 %collective-permute-done.2 = bf16[64,4224]{1,0:T(8,128)(2,1)S(1)} collective-permute-done((bf16[64,4224]{1,0:T(8,128)(2,1)S(1)}, bf16[64,4224]{1,0:T(8,128)(2,1)S(1)}, u32[]{:S(2)}, u32[]{:S(2)}) %collective-permute-start.2) | collective-permute-done | bytes 540704 | tf_op jit(solution)/shard_map/ppermute | solution.py:60
  46.2 1.6 %collective-permute-start.6 = (bf16[32,4224]{1,0:T(8,128)(2,1)S(1)}, bf16[32,4224]{1,0:T(8,128)(2,1)S(1)}, u32[]{:S(2)}, u32[]{:S(2)}) collective-permute-start(bf16[32,4224]{1,0:T(8,128)(2,1)S(1)} %slice.115), channel_id=1, source_target_pairs={{0,2},{2,4},{4,6},{6,7},{7,5},{5,3},{3,1},{1,0},{8,10},{10,12},{12... | collective-permute-start | bytes 811016 | tf_op jit(solution)/shard_map/ppermute | solution.py:60
  47.8 0.8 %fusion.5 = f32[256]{0:T(256)S(1)} fusion(bf16[256,4096]{1,0:T(8,128)(2,1)S(1)} %pad_maximum_fusion, bf16[64,4224]{1,0:T(8,128)(2,1)S(1)} %collective-permute-done.8, f32[256]{0:T(256)S(1)} %get-tuple-element.24, f32[256]{0:T(256)S(1)} %get-tuple-element.23, f32[64]{0:T(128)S(1)} %add_reduce_fusion.2, f32[64]{0:T(128)S(1)} %multiply_floor_fusion.2), kind=kOutput, calls=%fused_computation.16 | convolution fusion | flops 134299392 | bytes 2625536 | tf_op jit(solution)/shard_map/id,jd->ij/dot_general | solution.py:26
  48.6 0.8 %fusion.4 = f32[256]{0:T(256)S(1)} fusion(bf16[256,4096]{1,0:T(8,128)(2,1)S(1)} %pad_maximum_fusion, bf16[64,4224]{1,0:T(8,128)(2,1)S(1)} %collective-permute-done.7, f32[256]{0:T(256)S(1)} %get-tuple-element.24, f32[256]{0:T(256)S(1)} %get-tuple-element.23, f32[64]{0:T(128)S(1)} %add_reduce_fusion.3, f32[64]{0:T(128)S(1)} %multiply_floor_fusion.3), kind=kOutput, calls=%fused_computation.15 | convolution fusion | flops 134299392 | bytes 2625536 | tf_op jit(solution)/shard_map/id,jd->ij/dot_general | solution.py:26
  49.4 0.2 add_reduce_fusion.4
  49.6 0.8 %fusion.3 = f32[256]{0:T(256)S(1)} fusion(bf16[256,4096]{1,0:T(8,128)(2,1)S(1)} %pad_maximum_fusion, bf16[64,4224]{1,0:T(8,128)(2,1)S(1)} %collective-permute-done.2, f32[256]{0:T(256)S(1)} %get-tuple-element.24, f32[256]{0:T(256)S(1)} %get-tuple-element.23, f32[64]{0:T(128)S(1)} %add_reduce_fusion.4, f32[64]{0:T(128)S(1)} %multiply_floor_fusion.4), kind=kOutput, calls=%fused_computation.14 | convolution fusion | flops 134299392 | bytes 2625536 | tf_op jit(solution)/shard_map/id,jd->ij/dot_general | solution.py:26
  50.4 0.2 add_reduce_fusion.1
  50.6 0.5 collective-permute-start.10
  51.1 0.8 %fusion.6 = f32[256]{0:T(256)S(1)} fusion(bf16[256,4096]{1,0:T(8,128)(2,1)S(1)} %pad_maximum_fusion, bf16[64,4224]{1,0:T(8,128)(2,1)S(1)} %collective-permute-done.9, f32[256]{0:T(256)S(1)} %get-tuple-element.24, f32[256]{0:T(256)S(1)} %get-tuple-element.23, f32[64]{0:T(128)S(1)} %add_reduce_fusion.1, f32[64]{0:T(128)S(1)} %multiply_floor_fusion.1), kind=kOutput, calls=%fused_computation.17 | convolution fusion | flops 134299392 | bytes 2625536 | tf_op jit(solution)/shard_map/id,jd->ij/dot_general | solution.py:26
  51.9 1.2 %collective-permute-done.6 = bf16[32,4224]{1,0:T(8,128)(2,1)S(1)} collective-permute-done((bf16[32,4224]{1,0:T(8,128)(2,1)S(1)}, bf16[32,4224]{1,0:T(8,128)(2,1)S(1)}, u32[]{:S(2)}, u32[]{:S(2)}) %collective-permute-start.6) | collective-permute-done | bytes 270368 | tf_op jit(solution)/shard_map/ppermute | solution.py:60
  53.1 4.0 %collective-permute-done.10 = bf16[32,4224]{1,0:T(8,128)(2,1)S(1)} collective-permute-done((bf16[32,4224]{1,0:T(8,128)(2,1)S(1)}, bf16[32,4224]{1,0:T(8,128)(2,1)S(1)}, u32[]{:S(2)}, u32[]{:S(2)}) %collective-permute-start.10) | collective-permute-done | bytes 270368 | tf_op jit(solution)/shard_map/ppermute | solution.py:60
  57.2 0.2 add_reduce_fusion
  57.4 0.8 %fusion.7 = f32[256]{0:T(256)S(1)} fusion(bf16[256,4096]{1,0:T(8,128)(2,1)S(1)} %pad_maximum_fusion, bf16[64,4224]{1,0:T(8,128)(2,1)S(1)} %constant_dynamic-update-slice_fusion, f32[256]{0:T(256)S(1)} %get-tuple-element.24, f32[256]{0:T(256)S(1)} %get-tuple-element.23, f32[64]{0:T(128)S(1)} %add_reduce_fusion, f32[64]{0:T(128)S(1)} %multiply_floor_fusion), kind=kOutput, calls=%fused_computation.18 | convolution fusion | flops 134299392 | bytes 2625536 | tf_op jit(solution)/shard_map/id,jd->ij/dot_general | solution.py:26
  58.2 0.1 fusion.18
  58.2 0.0 collective-permute-start.11
  58.3 2.6 %collective-permute-start.12 = (f32[64]{0:T(128)S(1)}, f32[64]{0:T(128)S(1)}, u32[]{:S(2)}, u32[]{:S(2)}) collective-permute-start(f32[64]{0:T(128)S(1)} %get-tuple-element.29), channel_id=1, source_target_pairs={{0,16},{8,24},{16,0},{24,8},{1,17},{9,25},{17,1},{25,9},{2,18},{10... | collective-permute-start | bytes 776 | tf_op jit(solution)/shard_map/ppermute | solution.py:111
  60.9 0.0 collective-permute-start.13
  60.9 1.5 %collective-permute-done.12 = f32[64]{0:T(128)S(1)} collective-permute-done((f32[64]{0:T(128)S(1)}, f32[64]{0:T(128)S(1)}, u32[]{:S(2)}, u32[]{:S(2)}) %collective-permute-start.12) | collective-permute-done | bytes 288 | tf_op jit(solution)/shard_map/ppermute | solution.py:111
  62.4 1.4 %collective-permute-done.13 = f32[64]{0:T(128)S(1)} collective-permute-done((f32[64]{0:T(128)S(1)}, f32[64]{0:T(128)S(1)}, u32[]{:S(2)}, u32[]{:S(2)}) %collective-permute-start.13) | collective-permute-done | bytes 288 | tf_op jit(solution)/shard_map/ppermute | solution.py:111
  63.8 0.5 maximum_maximum_fusion.2
  (29 shorter events, 0.2 us)
Async XLA Ops:
  0.0 2.4 %copy-start = (s32[64]{0:T(128)S(1)}, s32[64]{0:T(128)}, u32[]{:S(2)}) copy-start(s32[64]{0:T(128)} %param.4) | copy-start | bytes 772
  0.0 2.4 %copy-start.1 = (s32[64]{0:T(128)S(1)}, s32[64]{0:T(128)}, u32[]{:S(2)}) copy-start(s32[64]{0:T(128)} %param.5) | copy-start | bytes 772
  2.7 15.3 %collective-permute-start = (bf16[64,4224]{1,0:T(8,128)(2,1)S(1)}, bf16[64,4224]{1,0:T(8,128)(2,1)S(1)}, u32[]{:S(2)}, u32[]{:S(2)}) collective-permute-start(bf16[64,4224]{1,0:T(8,128)(2,1)S(1)} %select_convert_fusion), channel_id=1, source_target_pairs={{0,2},{2,4},{4,6},{6,7},{7,5},{5,3},{3,1},{1,0},{8,10},{10,12},{12... | collective-permute-start | bytes 1622024 | tf_op jit(solution)/shard_map/ppermute | solution.py:60
  5.9 15.7 %collective-permute-start.7 = (bf16[64,4224]{1,0:T(8,128)(2,1)S(1)}, bf16[64,4224]{1,0:T(8,128)(2,1)S(1)}, u32[]{:S(2)}, u32[]{:S(2)}) collective-permute-start(bf16[64,4224]{1,0:T(8,128)(2,1)S(1)} %select_convert_fusion), channel_id=1, source_target_pairs={{2,0},{4,2},{6,4},{7,6},{5,7},{3,5},{1,3},{0,1},{10,8},{12,10},{14... | collective-permute-start | bytes 1622024 | tf_op jit(solution)/shard_map/ppermute | solution.py:60
  5.9 29.3 %collective-permute-start.3 = (bf16[64,4224]{1,0:T(8,128)(2,1)S(1)}, bf16[64,4224]{1,0:T(8,128)(2,1)S(1)}, u32[]{:S(2)}, u32[]{:S(2)}) collective-permute-start(bf16[64,4224]{1,0:T(8,128)(2,1)S(1)} %select_convert_fusion), channel_id=1, source_target_pairs={{0,8},{8,0},{16,24},{24,16},{1,9},{9,1},{17,25},{25,17},{2,10},{10... | collective-permute-start | bytes 1622024 | tf_op jit(solution)/shard_map/ppermute | solution.py:73
  18.0 13.4 %collective-permute-start.4 = (bf16[64,4224]{1,0:T(8,128)(2,1)S(1)}, bf16[64,4224]{1,0:T(8,128)(2,1)S(1)}, u32[]{:S(2)}, u32[]{:S(2)}) collective-permute-start(bf16[64,4224]{1,0:T(8,128)(2,1)S(1)} %select_convert_fusion), channel_id=1, source_target_pairs={{0,16},{8,24},{16,0},{24,8},{1,17},{9,25},{17,1},{25,9},{2,18},{10... | collective-permute-start | bytes 1622024 | tf_op jit(solution)/shard_map/ppermute | solution.py:72
  19.8 12.9 %collective-permute-start.1 = (bf16[64,4224]{1,0:T(8,128)(2,1)S(1)}, bf16[64,4224]{1,0:T(8,128)(2,1)S(1)}, u32[]{:S(2)}, u32[]{:S(2)}) collective-permute-start(bf16[64,4224]{1,0:T(8,128)(2,1)S(1)} %collective-permute-done), channel_id=1, source_target_pairs={{0,2},{2,4},{4,6},{6,7},{7,5},{5,3},{3,1},{1,0},{8,10},{10,12},{12... | collective-permute-start | bytes 1622024 | tf_op jit(solution)/shard_map/ppermute | solution.py:60
  21.6 12.9 %collective-permute-start.8 = (bf16[64,4224]{1,0:T(8,128)(2,1)S(1)}, bf16[64,4224]{1,0:T(8,128)(2,1)S(1)}, u32[]{:S(2)}, u32[]{:S(2)}) collective-permute-start(bf16[64,4224]{1,0:T(8,128)(2,1)S(1)} %collective-permute-done.7), channel_id=1, source_target_pairs={{2,0},{4,2},{6,4},{7,6},{5,7},{3,5},{1,3},{0,1},{10,8},{12,10},{14... | collective-permute-start | bytes 1622024 | tf_op jit(solution)/shard_map/ppermute | solution.py:60
  31.5 3.7 %collective-permute-start.5 = (bf16[64,4224]{1,0:T(8,128)(2,1)S(1)}, bf16[64,4224]{1,0:T(8,128)(2,1)S(1)}, u32[]{:S(2)}, u32[]{:S(2)}) collective-permute-start(bf16[64,4224]{1,0:T(8,128)(2,1)S(1)} %collective-permute-done.4), channel_id=1, source_target_pairs={{0,8},{8,0},{16,24},{24,16},{1,9},{9,1},{17,25},{25,17},{2,10},{10... | collective-permute-start | bytes 1622024 | tf_op jit(solution)/shard_map/ppermute | solution.py:74
  32.7 13.5 %collective-permute-start.2 = (bf16[64,4224]{1,0:T(8,128)(2,1)S(1)}, bf16[64,4224]{1,0:T(8,128)(2,1)S(1)}, u32[]{:S(2)}, u32[]{:S(2)}) collective-permute-start(bf16[64,4224]{1,0:T(8,128)(2,1)S(1)} %collective-permute-done.1), channel_id=1, source_target_pairs={{0,2},{2,4},{4,6},{6,7},{7,5},{5,3},{3,1},{1,0},{8,10},{10,12},{12... | collective-permute-start | bytes 1622024 | tf_op jit(solution)/shard_map/ppermute | solution.py:60
  34.5 15.9 %collective-permute-start.9 = (bf16[64,4224]{1,0:T(8,128)(2,1)S(1)}, bf16[64,4224]{1,0:T(8,128)(2,1)S(1)}, u32[]{:S(2)}, u32[]{:S(2)}) collective-permute-start(bf16[64,4224]{1,0:T(8,128)(2,1)S(1)} %collective-permute-done.8), channel_id=1, source_target_pairs={{2,0},{4,2},{6,4},{7,6},{5,7},{3,5},{1,3},{0,1},{10,8},{12,10},{14... | collective-permute-start | bytes 1622024 | tf_op jit(solution)/shard_map/ppermute | solution.py:60
  46.2 6.9 %collective-permute-start.6 = (bf16[32,4224]{1,0:T(8,128)(2,1)S(1)}, bf16[32,4224]{1,0:T(8,128)(2,1)S(1)}, u32[]{:S(2)}, u32[]{:S(2)}) collective-permute-start(bf16[32,4224]{1,0:T(8,128)(2,1)S(1)} %slice.115), channel_id=1, source_target_pairs={{0,2},{2,4},{4,6},{6,7},{7,5},{5,3},{3,1},{1,0},{8,10},{10,12},{12... | collective-permute-start | bytes 811016 | tf_op jit(solution)/shard_map/ppermute | solution.py:60
  50.6 6.6 %collective-permute-start.10 = (bf16[32,4224]{1,0:T(8,128)(2,1)S(1)}, bf16[32,4224]{1,0:T(8,128)(2,1)S(1)}, u32[]{:S(2)}, u32[]{:S(2)}) collective-permute-start(bf16[32,4224]{1,0:T(8,128)(2,1)S(1)} %slice.125), channel_id=1, source_target_pairs={{2,0},{4,2},{6,4},{7,6},{5,7},{3,5},{1,3},{0,1},{10,8},{12,10},{14... | collective-permute-start | bytes 811016 | tf_op jit(solution)/shard_map/ppermute | solution.py:60
  58.2 2.7 %collective-permute-start.11 = (f32[64]{0:T(128)S(1)}, f32[64]{0:T(128)S(1)}, u32[]{:S(2)}, u32[]{:S(2)}) collective-permute-start(f32[64]{0:T(128)S(1)} %get-tuple-element.27), channel_id=1, source_target_pairs={{0,8},{8,0},{16,24},{24,16},{1,9},{9,1},{17,25},{25,17},{2,10},{10... | collective-permute-start | bytes 776 | tf_op jit(solution)/shard_map/ppermute | solution.py:111
  58.3 4.1 %collective-permute-start.12 = (f32[64]{0:T(128)S(1)}, f32[64]{0:T(128)S(1)}, u32[]{:S(2)}, u32[]{:S(2)}) collective-permute-start(f32[64]{0:T(128)S(1)} %get-tuple-element.29), channel_id=1, source_target_pairs={{0,16},{8,24},{16,0},{24,8},{1,17},{9,25},{17,1},{25,9},{2,18},{10... | collective-permute-start | bytes 776 | tf_op jit(solution)/shard_map/ppermute | solution.py:111
  60.9 3.0 %collective-permute-start.13 = (f32[64]{0:T(128)S(1)}, f32[64]{0:T(128)S(1)}, u32[]{:S(2)}, u32[]{:S(2)}) collective-permute-start(f32[64]{0:T(128)S(1)} %get-tuple-element.28), channel_id=1, source_target_pairs={{0,24},{8,16},{16,8},{24,0},{1,25},{9,17},{17,9},{25,1},{2,26},{10... | collective-permute-start | bytes 776 | tf_op jit(solution)/shard_map/ppermute | solution.py:111

commit v17 on v14

--- a/solution.py
+++ b/solution.py
@@ -3,6 +3,8 @@
 import jax
 import jax.numpy as jnp
 from jax import lax
+from jax.experimental import pallas as pl
+from jax.experimental.pallas import tpu as pltpu
 from jax.sharding import PartitionSpec as P
 
 D = 4096
@@ -30,6 +32,31 @@
     return jnp.max(jnp.where(earlier, scores, jnp.float32(-1.0)), axis=1)
 
 
+def payload_kernel(rows_ref, cluster_ref, index_ref, out_ref):
+    widened = rows_ref[...].astype(jnp.float32)
+    square_sum = jnp.sum(widened * widened, axis=1, keepdims=True)
+    scale = lax.rsqrt(square_sum / D + 1e-06)
+    out_ref[:, :D] = (widened * scale / math.sqrt(D)).astype(jnp.bfloat16)
+    index = index_ref[...]
+    high = (cluster_ref[...] * 64 + index // 128).astype(jnp.float32)
+    low = (index % 128).astype(jnp.float32)
+    column = lax.broadcasted_iota(jnp.int32, (out_ref.shape[0], TAG_WIDTH), 1)
+    tags = jnp.where(column == 0, high, jnp.where(column == 1, low, 0.0))
+    out_ref[:, D:] = tags.astype(jnp.bfloat16)
+
+
+def build_payload(embeddings, cluster_ids, row_index):
+    rows = embeddings.shape[0]
+    return pl.pallas_call(
+        payload_kernel,
+        out_shape=jax.ShapeDtypeStruct((rows, D + TAG_WIDTH), jnp.bfloat16),
+        in_specs=[pl.BlockSpec(memory_space=pltpu.VMEM)] * 3,
+        out_specs=pl.BlockSpec(memory_space=pltpu.VMEM),
+        cost_estimate=pl.CostEstimate(flops=4 * rows * D, bytes_accessed=4 * rows * D + 2 * rows * TAG_WIDTH,
+                                      transcendentals=rows),
+    )(embeddings, cluster_ids.reshape(rows, 1), row_index.reshape(rows, 1))
+
+
 def partner_pairs(group_count, mask):
     return [(g, g ^ mask) for g in range(group_count)]
 
@@ -38,15 +65,7 @@
     group_count = lax.axis_size("grp")
     block_count = lax.axis_size("blk")
     rows_here = embeddings.shape[0]
-    widened = embeddings.astype(jnp.float32)
-    square_sum = jnp.sum(widened * widened, axis=1, keepdims=True)
-    scale = lax.rsqrt(square_sum / D + 1e-06)
-    high = (cluster_ids * 64 + row_index // 128).astype(jnp.float32)[:, None]
-    low = (row_index % 128).astype(jnp.float32)[:, None]
-    column = jnp.arange(D + TAG_WIDTH)[None, :]
-    padded = jnp.pad(widened, ((0, 0), (0, TAG_WIDTH)))
-    tags = jnp.where(column == D, high, jnp.where(column == D + 1, low, 0.0))
-    payload = jnp.where(column < D, padded * scale / math.sqrt(D), tags).astype(jnp.bfloat16)
+    payload = build_payload(embeddings, cluster_ids, row_index)
 
     order = ring_order(block_count)
     forward = [(order[i], order[(i + 1) % block_count]) for i in range(block_count)]

time: 62.1 us -> 64.4 us (1.037)
  local copies, waits for them, and re-layouts: 0.16 us -> 2.87 us
  Pallas kernels: 0 us -> 2.13 us
  waiting for transfers between devices: 35.9 us -> 34.5 us
  other arithmetic: 5.13 us -> 4.02 us
    reshape x0 -> x2, local copies, waits for them, and re-layouts: none -> 2.71 us  [the longest x1 1.36 us: build_payload(): row_index.reshape(rows, 1)]
    pallas_call x0 -> x1, Pallas kernels: none -> 2.13 us  [build_payload(): pl.pallas_call(payload_kernel, out_shape=jax.ShapeDtypeStruct((rows, D +...]
    convert_element_type x3 -> x0, other arithmetic: 1.42 us -> none  [the longest x1 1.12 us: per_device(): widened = embeddings.astype(jnp.float32)]
    reduce_sum x1 -> x0, other arithmetic: 1.25 us -> none  [per_device(): square_sum = jnp.sum(widened * widened, axis=1, keepdims=True)]
    ppermute x8, waiting for transfers between devices: 22.9 us -> 22 us  [send(): return lax.ppermute(visiting, 'blk', forward if which == 0 else backward)]
    slice x1, other arithmetic: 0.09 us -> 0.88 us  [tag_labels(): high = payload[:, D].astype(jnp.float32)]
    add x8, other arithmetic: 1.39 us -> 2.17 us  [tag_labels(): return high * 128.0 + low]
  transfers between devices with their start and end apart: 14 -> 14, of which waited for: 9 -> 9; matrix products, arithmetic and copies ran while one was open for 12% -> 14% of each run, Pallas kernels for 0% -> 0%
where the time goes in v17:
time: 64.4 us; the launch traced here: 64.1 us
  waiting for transfers between devices  34.5 us (54%)
  starting transfers between devices  14.2 us (22%)
  matrix products  6.25 us (10%)
  other arithmetic  4.02 us (6%)
  local copies, waits for them, and re-layouts  2.87 us (4%)
  Pallas kernels  2.13 us (3%)
    ppermute x8, waiting for transfers between devices, send(): return lax.ppermute(visiting, 'blk', forward if which == 0 else backward)  22 us
    ppermute x1, waiting for transfers between devices, per_device(): across = lax.ppermute(payload, 'grp', partner_pairs(group_count, 2))  9.55 us
    ppermute x8, starting transfers between devices, send(): return lax.ppermute(visiting, 'blk', forward if which == 0 else backward)  8.4 us
    dot_general x8, matrix products, block_best(): jnp.einsum('id,jd->ij', left_rows, payload[:, :D], preferred_element_type...  6.25 us
    ppermute x1, starting transfers between devices, per_device(): across = lax.ppermute(payload, 'grp', partner_pairs(group_count, 2))  3 us
    ppermute x3, waiting for transfers between devices, per_device(): result = jnp.maximum(result, lax.ppermute(best[k], 'grp', pairs))  2.95 us
    ppermute x3, starting transfers between devices, per_device(): result = jnp.maximum(result, lax.ppermute(best[k], 'grp', pairs))  2.82 us
    add x8, other arithmetic, tag_labels(): return high * 128.0 + low  2.17 us
  transfers between devices with their start and end apart: 14, of which 9 were waited for; matrix products, arithmetic and copies ran while one was open for 14% of the time, Pallas kernels for 0%

profile of v17, /device:TPU:0, one launch (start us, length us, event | category | flops | bytes accessed | tf_op | source)
XLA Modules:
  0.0 64.1 jit_solution(18001115998702701163)
XLA Ops:
  0.0 1.4 %copy.6.cluster_ref = s32[64,1]{1,0:T(8,128)} copy(s32[64,1]{0,1:T(1,128)} %bitcast.10) | data formatting | bytes 512 | tf_op jit(solution)/shard_map/reshape | solution.py:57
  1.4 1.4 %copy.7.index_ref = s32[64,1]{1,0:T(8,128)} copy(s32[64,1]{0,1:T(1,128)} %bitcast.11) | data formatting | bytes 512 | tf_op jit(solution)/shard_map/reshape | solution.py:57
  2.7 2.1 %shard_map.37 = bf16[64,4224]{1,0:T(8,128)(2,1)} custom-call(bf16[64,4096]{1,0:T(8,128)(2,1)} %rows_ref.1, s32[64,1]{1,0:T(8,128)} %copy.6.cluster_ref, s32[64,1]{1,0:T(8,128)} %copy.7.index_ref), custom_call_target="tpu_custom_call" | custom-call | flops 1048576 | bytes 1064960 | tf_op jit(solution)/shard_map/pallas_call | solution.py:50
  4.8 3.0 %collective-permute-start.1 = (bf16[64,4224]{1,0:T(8,128)(2,1)}, bf16[64,4224]{1,0:T(8,128)(2,1)S(1)}, u32[]{:S(2)}, u32[]{:S(2)}) collective-permute-start(bf16[64,4224]{1,0:T(8,128)(2,1)} %shard_map.37), channel_id=1, source_target_pairs={{0,16},{8,24},{16,0},{24,8},{1,17},{9,25},{17,1},{25,9},{2,18},{10... | collective-permute-start | bytes 1622024 | tf_op jit(solution)/shard_map/ppermute | solution.py:88
  7.8 1.6 %collective-permute-start.3 = (bf16[64,4224]{1,0:T(8,128)(2,1)}, bf16[64,4224]{1,0:T(8,128)(2,1)S(1)}, u32[]{:S(2)}, u32[]{:S(2)}) collective-permute-start(bf16[64,4224]{1,0:T(8,128)(2,1)} %shard_map.37), channel_id=1, source_target_pairs={{0,2},{2,4},{4,6},{6,7},{7,5},{5,3},{3,1},{1,0},{8,10},{10,12},{12... | collective-permute-start | bytes 1622024 | tf_op jit(solution)/shard_map/ppermute | solution.py:79
  9.4 0.4 collective-permute-start.7
  9.9 1.0 %add_reduce_fusion.7 = f32[64]{0:T(128)S(1)} fusion(bf16[64,4224]{1,0:T(8,128)(2,1)} %shard_map.37), kind=kLoop, calls=%fused_computation.39 | loop fusion | flops 256 | bytes 512 | tf_op jit(solution)/shard_map/add | solution.py:24
  10.8 9.6 %collective-permute-done.1 = bf16[64,4224]{1,0:T(8,128)(2,1)S(1)} collective-permute-done((bf16[64,4224]{1,0:T(8,128)(2,1)}, bf16[64,4224]{1,0:T(8,128)(2,1)S(1)}, u32[]{:S(2)}, u32[]{:S(2)}) %collective-permute-start.1) | collective-permute-done | bytes 540704 | tf_op jit(solution)/shard_map/ppermute | solution.py:88
  20.4 1.4 %collective-permute-done.3 = bf16[64,4224]{1,0:T(8,128)(2,1)S(1)} collective-permute-done((bf16[64,4224]{1,0:T(8,128)(2,1)}, bf16[64,4224]{1,0:T(8,128)(2,1)S(1)}, u32[]{:S(2)}, u32[]{:S(2)}) %collective-permute-start.3) | collective-permute-done | bytes 540704 | tf_op jit(solution)/shard_map/ppermute | solution.py:79
  21.8 1.6 %collective-permute-start.4 = (bf16[64,4224]{1,0:T(8,128)(2,1)S(1)}, bf16[64,4224]{1,0:T(8,128)(2,1)S(1)}, u32[]{:S(2)}, u32[]{:S(2)}) collective-permute-start(bf16[64,4224]{1,0:T(8,128)(2,1)S(1)} %collective-permute-done.3), channel_id=1, source_target_pairs={{0,2},{2,4},{4,6},{6,7},{7,5},{5,3},{3,1},{1,0},{8,10},{10,12},{12... | collective-permute-start | bytes 1622024 | tf_op jit(solution)/shard_map/ppermute | solution.py:79
  23.4 0.2 add_reduce_fusion.6
  23.5 0.5 collective-permute-start.8
  24.1 0.2 add_reduce_fusion.2
  24.3 0.0 collective-permute-done.2
  24.3 0.9 %pad_maximum_fusion.4 = (bf16[256,1]{1,0:T(8,128)(2,1)S(1)}, bf16[256,1]{1,0:T(8,128)(2,1)S(1)}) fusion(bf16[64,4224]{1,0:T(8,128)(2,1)S(1)} %collective-permute-done.2, bf16[64,4224]{1,0:T(8,128)(2,1)S(1)} %collective-permute-done.1, bf16[64,4224]{1,0:T(8,128)(2,1)S(1)} %collective-permute-done, bf16[64,4224]{1,0:T(8,128)(2,1)} %shard_map.37), kind=kLoop, calls=%fused_computation.31 | loop fusion | flops 4096 | bytes 2163712 | tf_op jit(solution)/shard_map/slice | solution.py:22
  25.2 0.2 floor_reduce_fusion
  25.3 0.2 pad_maximum_fusion
  25.6 9.5 %collective-permute-done.4 = bf16[64,4224]{1,0:T(8,128)(2,1)S(1)} collective-permute-done((bf16[64,4224]{1,0:T(8,128)(2,1)S(1)}, bf16[64,4224]{1,0:T(8,128)(2,1)S(1)}, u32[]{:S(2)}, u32[]{:S(2)}) %collective-permute-start.4) | collective-permute-done | bytes 540704 | tf_op jit(solution)/shard_map/ppermute | solution.py:79
  35.1 1.7 %collective-permute-start.5 = (bf16[64,4224]{1,0:T(8,128)(2,1)S(1)}, bf16[64,4224]{1,0:T(8,128)(2,1)S(1)}, u32[]{:S(2)}, u32[]{:S(2)}) collective-permute-start(bf16[64,4224]{1,0:T(8,128)(2,1)S(1)} %collective-permute-done.4), channel_id=1, source_target_pairs={{0,2},{2,4},{4,6},{6,7},{7,5},{5,3},{3,1},{1,0},{8,10},{10,12},{12... | collective-permute-start | bytes 1622024 | tf_op jit(solution)/shard_map/ppermute | solution.py:79
  36.8 0.2 add_reduce_fusion.5
  37.0 0.8 %fusion = f32[256]{0:T(256)S(1)} fusion(bf16[256,4096]{1,0:T(8,128)(2,1)S(1)} %pad_maximum_fusion, bf16[64,4224]{1,0:T(8,128)(2,1)S(1)} %copy-done, f32[256]{0:T(256)S(1)} %get-tuple-element.6, f32[256]{0:T(256)S(1)} %get-tuple-element.5, f32[64]{0:T(128)S(1)} %add_reduce_fusion.7, f32[64]{0:T(128)S(1)} %multiply_floor_fusion.7), kind=kOutput, calls=%fused_computation.11 | convolution fusion | flops 134299392 | bytes 2625536 | tf_op jit(solution)/shard_map/id,jd->ij/dot_general | solution.py:28
  37.8 0.0 collective-permute-done.8
  37.8 0.3 collective-permute-start.9
  38.1 0.2 add_reduce_fusion.1
  38.3 0.8 %fusion.1 = f32[256]{0:T(256)S(1)} fusion(bf16[256,4096]{1,0:T(8,128)(2,1)S(1)} %pad_maximum_fusion, bf16[64,4224]{1,0:T(8,128)(2,1)S(1)} %collective-permute-done.3, f32[256]{0:T(256)S(1)} %get-tuple-element.6, f32[256]{0:T(256)S(1)} %get-tuple-element.5, f32[64]{0:T(128)S(1)} %add_reduce_fusion.6, f32[64]{0:T(128)S(1)} %multiply_floor_fusion.6), kind=kOutput, calls=%fused_computation.12 | convolution fusion | flops 134299392 | bytes 2625536 | tf_op jit(solution)/shard_map/id,jd->ij/dot_general | solution.py:28
  39.1 0.8 %fusion.2 = f32[256]{0:T(256)S(1)} fusion(bf16[256,4096]{1,0:T(8,128)(2,1)S(1)} %pad_maximum_fusion, bf16[64,4224]{1,0:T(8,128)(2,1)S(1)} %collective-permute-done.4, f32[256]{0:T(256)S(1)} %get-tuple-element.6, f32[256]{0:T(256)S(1)} %get-tuple-element.5, f32[64]{0:T(128)S(1)} %add_reduce_fusion.5, f32[64]{0:T(128)S(1)} %multiply_floor_fusion.5), kind=kOutput, calls=%fused_computation.13 | convolution fusion | flops 134299392 | bytes 2625536 | tf_op jit(solution)/shard_map/id,jd->ij/dot_general | solution.py:28
  39.9 0.8 %fusion.6 = f32[256]{0:T(256)S(1)} fusion(bf16[256,4096]{1,0:T(8,128)(2,1)S(1)} %pad_maximum_fusion, bf16[64,4224]{1,0:T(8,128)(2,1)S(1)} %collective-permute-done.8, f32[256]{0:T(256)S(1)} %get-tuple-element.6, f32[256]{0:T(256)S(1)} %get-tuple-element.5, f32[64]{0:T(128)S(1)} %add_reduce_fusion.1, f32[64]{0:T(128)S(1)} %multiply_floor_fusion.1), kind=kOutput, calls=%fused_computation.17 | convolution fusion | flops 134299392 | bytes 2625536 | tf_op jit(solution)/shard_map/id,jd->ij/dot_general | solution.py:28
  40.7 0.8 %fusion.5 = f32[256]{0:T(256)S(1)} fusion(bf16[256,4096]{1,0:T(8,128)(2,1)S(1)} %pad_maximum_fusion, bf16[64,4224]{1,0:T(8,128)(2,1)S(1)} %collective-permute-done.7, f32[256]{0:T(256)S(1)} %get-tuple-element.6, f32[256]{0:T(256)S(1)} %get-tuple-element.5, f32[64]{0:T(128)S(1)} %add_reduce_fusion.2, f32[64]{0:T(128)S(1)} %multiply_floor_fusion.2), kind=kOutput, calls=%fused_computation.16 | convolution fusion | flops 134299392 | bytes 2625536 | tf_op jit(solution)/shard_map/id,jd->ij/dot_general | solution.py:28
  41.5 6.1 %collective-permute-done.5 = bf16[64,4224]{1,0:T(8,128)(2,1)S(1)} collective-permute-done((bf16[64,4224]{1,0:T(8,128)(2,1)S(1)}, bf16[64,4224]{1,0:T(8,128)(2,1)S(1)}, u32[]{:S(2)}, u32[]{:S(2)}) %collective-permute-start.5) | collective-permute-done | bytes 540704 | tf_op jit(solution)/shard_map/ppermute | solution.py:79
  47.6 1.9 %collective-permute-start.6 = (bf16[32,4224]{1,0:T(8,128)(2,1)S(1)}, bf16[32,4224]{1,0:T(8,128)(2,1)S(1)}, u32[]{:S(2)}, u32[]{:S(2)}) collective-permute-start(bf16[32,4224]{1,0:T(8,128)(2,1)S(1)} %slice.148), channel_id=1, source_target_pairs={{0,2},{2,4},{4,6},{6,7},{7,5},{5,3},{3,1},{1,0},{8,10},{10,12},{12... | collective-permute-start | bytes 811016 | tf_op jit(solution)/shard_map/ppermute | solution.py:79
  49.5 0.2 add_reduce_fusion.4
  49.7 0.5 collective-permute-done.9
  50.2 0.3 collective-permute-start.10
  50.6 0.2 add_reduce_fusion
  50.8 0.8 %fusion.3 = f32[256]{0:T(256)S(1)} fusion(bf16[256,4096]{1,0:T(8,128)(2,1)S(1)} %pad_maximum_fusion, bf16[64,4224]{1,0:T(8,128)(2,1)S(1)} %collective-permute-done.5, f32[256]{0:T(256)S(1)} %get-tuple-element.6, f32[256]{0:T(256)S(1)} %get-tuple-element.5, f32[64]{0:T(128)S(1)} %add_reduce_fusion.4, f32[64]{0:T(128)S(1)} %multiply_floor_fusion.4), kind=kOutput, calls=%fused_computation.14 | convolution fusion | flops 134299392 | bytes 2625536 | tf_op jit(solution)/shard_map/id,jd->ij/dot_general | solution.py:28
  51.6 0.8 %fusion.7 = f32[256]{0:T(256)S(1)} fusion(bf16[256,4096]{1,0:T(8,128)(2,1)S(1)} %pad_maximum_fusion, bf16[64,4224]{1,0:T(8,128)(2,1)S(1)} %collective-permute-done.9, f32[256]{0:T(256)S(1)} %get-tuple-element.6, f32[256]{0:T(256)S(1)} %get-tuple-element.5, f32[64]{0:T(128)S(1)} %add_reduce_fusion, f32[64]{0:T(128)S(1)} %multiply_floor_fusion), kind=kOutput, calls=%fused_computation.18 | convolution fusion | flops 134299392 | bytes 2625536 | tf_op jit(solution)/shard_map/id,jd->ij/dot_general | solution.py:28
  52.3 1.8 %collective-permute-done.6 = bf16[32,4224]{1,0:T(8,128)(2,1)S(1)} collective-permute-done((bf16[32,4224]{1,0:T(8,128)(2,1)S(1)}, bf16[32,4224]{1,0:T(8,128)(2,1)S(1)}, u32[]{:S(2)}, u32[]{:S(2)}) %collective-permute-start.6) | collective-permute-done | bytes 270368 | tf_op jit(solution)/shard_map/ppermute | solution.py:79
  54.1 2.6 %collective-permute-done.10 = bf16[32,4224]{1,0:T(8,128)(2,1)S(1)} collective-permute-done((bf16[32,4224]{1,0:T(8,128)(2,1)S(1)}, bf16[32,4224]{1,0:T(8,128)(2,1)S(1)}, u32[]{:S(2)}, u32[]{:S(2)}) %collective-permute-start.10) | collective-permute-done | bytes 270368 | tf_op jit(solution)/shard_map/ppermute | solution.py:79
  56.8 0.2 add_reduce_fusion.3
  57.0 0.8 %fusion.4 = f32[256]{0:T(256)S(1)} fusion(bf16[256,4096]{1,0:T(8,128)(2,1)S(1)} %pad_maximum_fusion, bf16[64,4224]{1,0:T(8,128)(2,1)S(1)} %constant_dynamic-update-slice_fusion, f32[256]{0:T(256)S(1)} %get-tuple-element.6, f32[256]{0:T(256)S(1)} %get-tuple-element.5, f32[64]{0:T(128)S(1)} %add_reduce_fusion.3, f32[64]{0:T(128)S(1)} %multiply_floor_fusion.3), kind=kOutput, calls=%fused_computation.15 | convolution fusion | flops 134299392 | bytes 2625536 | tf_op jit(solution)/shard_map/id,jd->ij/dot_general | solution.py:28
  57.8 0.1 fusion.17
  57.8 0.0 collective-permute-start.11
  57.9 2.8 %collective-permute-start.12 = (f32[64]{0:T(128)S(1)}, f32[64]{0:T(128)S(1)}, u32[]{:S(2)}, u32[]{:S(2)}) collective-permute-start(f32[64]{0:T(128)S(1)} %get-tuple-element.11), channel_id=1, source_target_pairs={{0,16},{8,24},{16,0},{24,8},{1,17},{9,25},{17,1},{25,9},{2,18},{10... | collective-permute-start | bytes 776 | tf_op jit(solution)/shard_map/ppermute | solution.py:125
  60.6 0.0 collective-permute-start.13
  60.7 0.0 collective-permute-done.11
  60.7 1.5 %collective-permute-done.12 = f32[64]{0:T(128)S(1)} collective-permute-done((f32[64]{0:T(128)S(1)}, f32[64]{0:T(128)S(1)}, u32[]{:S(2)}, u32[]{:S(2)}) %collective-permute-start.12) | collective-permute-done | bytes 288 | tf_op jit(solution)/shard_map/ppermute | solution.py:125
  62.2 1.4 %collective-permute-done.13 = f32[64]{0:T(128)S(1)} collective-permute-done((f32[64]{0:T(128)S(1)}, f32[64]{0:T(128)S(1)}, u32[]{:S(2)}, u32[]{:S(2)}) %collective-permute-start.13) | collective-permute-done | bytes 288 | tf_op jit(solution)/shard_map/ppermute | solution.py:125
  63.6 0.5 maximum_maximum_fusion.1
  (19 shorter events, 0.1 us)
Async XLA Ops:
  4.8 20.5 %copy-start = (bf16[64,4224]{1,0:T(8,128)(2,1)S(1)}, bf16[64,4224]{1,0:T(8,128)(2,1)}, u32[]{:S(2)}) copy-start(bf16[64,4224]{1,0:T(8,128)(2,1)} %shard_map.37) | copy-start | bytes 1622020
  4.8 15.5 %collective-permute-start.1 = (bf16[64,4224]{1,0:T(8,128)(2,1)}, bf16[64,4224]{1,0:T(8,128)(2,1)S(1)}, u32[]{:S(2)}, u32[]{:S(2)}) collective-permute-start(bf16[64,4224]{1,0:T(8,128)(2,1)} %shard_map.37), channel_id=1, source_target_pairs={{0,16},{8,24},{16,0},{24,8},{1,17},{9,25},{17,1},{25,9},{2,18},{10... | collective-permute-start | bytes 1622024 | tf_op jit(solution)/shard_map/ppermute | solution.py:88
  7.8 13.9 %collective-permute-start.3 = (bf16[64,4224]{1,0:T(8,128)(2,1)}, bf16[64,4224]{1,0:T(8,128)(2,1)S(1)}, u32[]{:S(2)}, u32[]{:S(2)}) collective-permute-start(bf16[64,4224]{1,0:T(8,128)(2,1)} %shard_map.37), channel_id=1, source_target_pairs={{0,2},{2,4},{4,6},{6,7},{7,5},{5,3},{3,1},{1,0},{8,10},{10,12},{12... | collective-permute-start | bytes 1622024 | tf_op jit(solution)/shard_map/ppermute | solution.py:79
  9.4 14.1 %collective-permute-start.7 = (bf16[64,4224]{1,0:T(8,128)(2,1)}, bf16[64,4224]{1,0:T(8,128)(2,1)S(1)}, u32[]{:S(2)}, u32[]{:S(2)}) collective-permute-start(bf16[64,4224]{1,0:T(8,128)(2,1)} %shard_map.37), channel_id=1, source_target_pairs={{2,0},{4,2},{6,4},{7,6},{5,7},{3,5},{1,3},{0,1},{10,8},{12,10},{14... | collective-permute-start | bytes 1622024 | tf_op jit(solution)/shard_map/ppermute | solution.py:79
  9.9 14.4 %collective-permute-start = (bf16[64,4224]{1,0:T(8,128)(2,1)}, bf16[64,4224]{1,0:T(8,128)(2,1)S(1)}, u32[]{:S(2)}, u32[]{:S(2)}) collective-permute-start(bf16[64,4224]{1,0:T(8,128)(2,1)} %shard_map.37), channel_id=1, source_target_pairs={{0,8},{8,0},{16,24},{24,16},{1,9},{9,1},{17,25},{25,17},{2,10},{10... | collective-permute-start | bytes 1622024 | tf_op jit(solution)/shard_map/ppermute | solution.py:89
  20.4 3.9 %collective-permute-start.2 = (bf16[64,4224]{1,0:T(8,128)(2,1)S(1)}, bf16[64,4224]{1,0:T(8,128)(2,1)S(1)}, u32[]{:S(2)}, u32[]{:S(2)}) collective-permute-start(bf16[64,4224]{1,0:T(8,128)(2,1)S(1)} %collective-permute-done.1), channel_id=1, source_target_pairs={{0,8},{8,0},{16,24},{24,16},{1,9},{9,1},{17,25},{25,17},{2,10},{10... | collective-permute-start | bytes 1622024 | tf_op jit(solution)/shard_map/ppermute | solution.py:90
  21.8 13.3 %collective-permute-start.4 = (bf16[64,4224]{1,0:T(8,128)(2,1)S(1)}, bf16[64,4224]{1,0:T(8,128)(2,1)S(1)}, u32[]{:S(2)}, u32[]{:S(2)}) collective-permute-start(bf16[64,4224]{1,0:T(8,128)(2,1)S(1)} %collective-permute-done.3), channel_id=1, source_target_pairs={{0,2},{2,4},{4,6},{6,7},{7,5},{5,3},{3,1},{1,0},{8,10},{10,12},{12... | collective-permute-start | bytes 1622024 | tf_op jit(solution)/shard_map/ppermute | solution.py:79
  23.5 14.2 %collective-permute-start.8 = (bf16[64,4224]{1,0:T(8,128)(2,1)S(1)}, bf16[64,4224]{1,0:T(8,128)(2,1)S(1)}, u32[]{:S(2)}, u32[]{:S(2)}) collective-permute-start(bf16[64,4224]{1,0:T(8,128)(2,1)S(1)} %collective-permute-done.7), channel_id=1, source_target_pairs={{2,0},{4,2},{6,4},{7,6},{5,7},{3,5},{1,3},{0,1},{10,8},{12,10},{14... | collective-permute-start | bytes 1622024 | tf_op jit(solution)/shard_map/ppermute | solution.py:79
  35.1 12.5 %collective-permute-start.5 = (bf16[64,4224]{1,0:T(8,128)(2,1)S(1)}, bf16[64,4224]{1,0:T(8,128)(2,1)S(1)}, u32[]{:S(2)}, u32[]{:S(2)}) collective-permute-start(bf16[64,4224]{1,0:T(8,128)(2,1)S(1)} %collective-permute-done.4), channel_id=1, source_target_pairs={{0,2},{2,4},{4,6},{6,7},{7,5},{5,3},{3,1},{1,0},{8,10},{10,12},{12... | collective-permute-start | bytes 1622024 | tf_op jit(solution)/shard_map/ppermute | solution.py:79
  37.8 12.4 %collective-permute-start.9 = (bf16[64,4224]{1,0:T(8,128)(2,1)S(1)}, bf16[64,4224]{1,0:T(8,128)(2,1)S(1)}, u32[]{:S(2)}, u32[]{:S(2)}) collective-permute-start(bf16[64,4224]{1,0:T(8,128)(2,1)S(1)} %collective-permute-done.8), channel_id=1, source_target_pairs={{2,0},{4,2},{6,4},{7,6},{5,7},{3,5},{1,3},{0,1},{10,8},{12,10},{14... | collective-permute-start | bytes 1622024 | tf_op jit(solution)/shard_map/ppermute | solution.py:79
  47.6 6.5 %collective-permute-start.6 = (bf16[32,4224]{1,0:T(8,128)(2,1)S(1)}, bf16[32,4224]{1,0:T(8,128)(2,1)S(1)}, u32[]{:S(2)}, u32[]{:S(2)}) collective-permute-start(bf16[32,4224]{1,0:T(8,128)(2,1)S(1)} %slice.148), channel_id=1, source_target_pairs={{0,2},{2,4},{4,6},{6,7},{7,5},{5,3},{3,1},{1,0},{8,10},{10,12},{12... | collective-permute-start | bytes 811016 | tf_op jit(solution)/shard_map/ppermute | solution.py:79
  50.2 6.5 %collective-permute-start.10 = (bf16[32,4224]{1,0:T(8,128)(2,1)S(1)}, bf16[32,4224]{1,0:T(8,128)(2,1)S(1)}, u32[]{:S(2)}, u32[]{:S(2)}) collective-permute-start(bf16[32,4224]{1,0:T(8,128)(2,1)S(1)} %slice.149), channel_id=1, source_target_pairs={{2,0},{4,2},{6,4},{7,6},{5,7},{3,5},{1,3},{0,1},{10,8},{12,10},{14... | collective-permute-start | bytes 811016 | tf_op jit(solution)/shard_map/ppermute | solution.py:79
  57.8 2.8 %collective-permute-start.11 = (f32[64]{0:T(128)S(1)}, f32[64]{0:T(128)S(1)}, u32[]{:S(2)}, u32[]{:S(2)}) collective-permute-start(f32[64]{0:T(128)S(1)} %get-tuple-element.9), channel_id=1, source_target_pairs={{0,8},{8,0},{16,24},{24,16},{1,9},{9,1},{17,25},{25,17},{2,10},{10... | collective-permute-start | bytes 776 | tf_op jit(solution)/shard_map/ppermute | solution.py:125
  57.9 4.3 %collective-permute-start.12 = (f32[64]{0:T(128)S(1)}, f32[64]{0:T(128)S(1)}, u32[]{:S(2)}, u32[]{:S(2)}) collective-permute-start(f32[64]{0:T(128)S(1)} %get-tuple-element.11), channel_id=1, source_target_pairs={{0,16},{8,24},{16,0},{24,8},{1,17},{9,25},{17,1},{25,9},{2,18},{10... | collective-permute-start | bytes 776 | tf_op jit(solution)/shard_map/ppermute | solution.py:125
  60.6 3.0 %collective-permute-start.13 = (f32[64]{0:T(128)S(1)}, f32[64]{0:T(128)S(1)}, u32[]{:S(2)}, u32[]{:S(2)}) collective-permute-start(f32[64]{0:T(128)S(1)} %get-tuple-element.10), channel_id=1, source_target_pairs={{0,24},{8,16},{16,8},{24,0},{1,25},{9,17},{17,9},{25,1},{2,26},{10... | collective-permute-start | bytes 776 | tf_op jit(solution)/shard_map/ppermute | solution.py:125

commit v18 on v14

--- a/solution.py
+++ b/solution.py
@@ -101,6 +101,11 @@
             best = chain_best if best is None else jnp.maximum(best, chain_best)
 
     best = best.reshape(group_count, rows_here)
+    if group_count == 4:
+        swapped = lax.ppermute(jnp.stack([best[1], best[3]]), "grp", partner_pairs(group_count, 1))
+        mine = jnp.maximum(best[0], swapped[0])
+        across = jnp.maximum(best[2], swapped[1])
+        return jnp.maximum(mine, lax.ppermute(across, "grp", partner_pairs(group_count, 2)))
     result = best[0]
     for k, pairs in enumerate(segment_pairs, start=1):
         result = jnp.maximum(result, lax.ppermute(best[k], "grp", pairs))

time: 62.1 us -> 61.8 us (level)
    ppermute x3 -> x2, waiting for transfers between devices: 2.95 us -> 2.69 us  [the longest x1 1.55 us: per_device(): lax.ppermute(across, 'grp', partner_pairs(group_count, 2))]
    ppermute x3 -> x2, starting transfers between devices: 2.81 us -> 2.76 us  [the longest x1 2.7 us: per_device(): lax.ppermute(across, 'grp', partner_pairs(group_count, 2))]
  transfers between devices with their start and end apart: 14 -> 13, of which waited for: 9 -> 9; matrix products, arithmetic and copies ran while one was open for 12% -> 12% of each run, Pallas kernels for 0% -> 0%
where the time goes in v18:
time: 61.8 us; the launch traced here: 61.6 us
  waiting for transfers between devices  35.6 us (58%)
  starting transfers between devices  14.2 us (23%)
  matrix products  6.25 us (10%)
  other arithmetic  5.14 us (8%)
    ppermute x8, waiting for transfers between devices, send(): return lax.ppermute(visiting, 'blk', forward if which == 0 else backward)  22.9 us
    ppermute x1, waiting for transfers between devices, per_device(): across = lax.ppermute(payload, 'grp', partner_pairs(group_count, 2))  10.1 us
    ppermute x8, starting transfers between devices, send(): return lax.ppermute(visiting, 'blk', forward if which == 0 else backward)  8.35 us
    dot_general x8, matrix products, block_best(): jnp.einsum('id,jd->ij', left_rows, payload[:, :D], preferred_element_type...  6.25 us
    ppermute x1, starting transfers between devices, per_device(): across = lax.ppermute(payload, 'grp', partner_pairs(group_count, 2))  3.06 us
    ppermute x1, starting transfers between devices, per_device(): lax.ppermute(across, 'grp', partner_pairs(group_count, 2))  2.7 us
    ppermute x1, waiting for transfers between devices, per_device(): lax.ppermute(across, 'grp', partner_pairs(group_count, 2))  1.55 us
    add x8, other arithmetic, tag_labels(): return high * 128.0 + low  1.39 us
  transfers between devices with their start and end apart: 13, of which 9 were waited for; matrix products, arithmetic and copies ran while one was open for 12% of the time, Pallas kernels for 0%

profile of v18, /device:TPU:0, one launch (start us, length us, event | category | flops | bytes accessed | tf_op | source)
XLA Modules:
  0.0 61.6 jit_solution(3867749111016560535)
XLA Ops:
  0.0 1.1 %convert_element_type.200 = f32[64,4096]{1,0:T(8,128)S(1)} convert(bf16[64,4096]{1,0:T(8,128)(2,1)} %param.3) | non-fusion elementwise | flops 262144 | bytes 1572864 | tf_op jit(solution)/shard_map/convert_element_type | solution.py:41
  1.1 1.2 %multiply_reduce_fusion = f32[64]{0:T(128)S(1)} fusion(bf16[64,4096]{1,0:T(8,128)(2,1)} %param.3), kind=kLoop, calls=%fused_computation.20 | loop fusion | flops 786368 | bytes 524544 | tf_op jit(solution)/shard_map/reduce_sum | solution.py:42
  2.4 0.3 select_convert_fusion
  2.7 3.1 %collective-permute-start.1 = (bf16[64,4224]{1,0:T(8,128)(2,1)S(1)}, bf16[64,4224]{1,0:T(8,128)(2,1)S(1)}, u32[]{:S(2)}, u32[]{:S(2)}) collective-permute-start(bf16[64,4224]{1,0:T(8,128)(2,1)S(1)} %select_convert_fusion), channel_id=1, source_target_pairs={{0,16},{8,24},{16,0},{24,8},{1,17},{9,25},{17,1},{25,9},{2,18},{10... | collective-permute-start | bytes 1622024 | tf_op jit(solution)/shard_map/ppermute | solution.py:69
  5.8 1.6 %collective-permute-start.3 = (bf16[64,4224]{1,0:T(8,128)(2,1)S(1)}, bf16[64,4224]{1,0:T(8,128)(2,1)S(1)}, u32[]{:S(2)}, u32[]{:S(2)}) collective-permute-start(bf16[64,4224]{1,0:T(8,128)(2,1)S(1)} %select_convert_fusion), channel_id=1, source_target_pairs={{0,2},{2,4},{4,6},{6,7},{7,5},{5,3},{3,1},{1,0},{8,10},{10,12},{12... | collective-permute-start | bytes 1622024 | tf_op jit(solution)/shard_map/ppermute | solution.py:60
  7.4 0.4 collective-permute-start.7
  7.8 0.0 collective-permute-start
  7.8 0.2 add_reduce_fusion.7
  8.0 10.1 %collective-permute-done.1 = bf16[64,4224]{1,0:T(8,128)(2,1)S(1)} collective-permute-done((bf16[64,4224]{1,0:T(8,128)(2,1)S(1)}, bf16[64,4224]{1,0:T(8,128)(2,1)S(1)}, u32[]{:S(2)}, u32[]{:S(2)}) %collective-permute-start.1) | collective-permute-done | bytes 540704 | tf_op jit(solution)/shard_map/ppermute | solution.py:69
  18.1 0.0 collective-permute-start.2
  18.1 1.5 %collective-permute-done.3 = bf16[64,4224]{1,0:T(8,128)(2,1)S(1)} collective-permute-done((bf16[64,4224]{1,0:T(8,128)(2,1)S(1)}, bf16[64,4224]{1,0:T(8,128)(2,1)S(1)}, u32[]{:S(2)}, u32[]{:S(2)}) %collective-permute-start.3) | collective-permute-done | bytes 540704 | tf_op jit(solution)/shard_map/ppermute | solution.py:60
  19.5 1.6 %collective-permute-start.4 = (bf16[64,4224]{1,0:T(8,128)(2,1)S(1)}, bf16[64,4224]{1,0:T(8,128)(2,1)S(1)}, u32[]{:S(2)}, u32[]{:S(2)}) collective-permute-start(bf16[64,4224]{1,0:T(8,128)(2,1)S(1)} %collective-permute-done.3), channel_id=1, source_target_pairs={{0,2},{2,4},{4,6},{6,7},{7,5},{5,3},{3,1},{1,0},{8,10},{10,12},{12... | collective-permute-start | bytes 1622024 | tf_op jit(solution)/shard_map/ppermute | solution.py:60
  21.1 0.2 add_reduce_fusion.6
  21.3 0.0 collective-permute-done.7
  21.3 0.5 collective-permute-start.8
  21.8 0.2 add_reduce_fusion.2
  22.0 0.0 collective-permute-done.2
  22.0 0.1 pad_maximum_fusion.4
  22.1 0.2 floor_reduce_fusion
  22.3 0.2 pad_maximum_fusion
  22.5 10.2 %collective-permute-done.4 = bf16[64,4224]{1,0:T(8,128)(2,1)S(1)} collective-permute-done((bf16[64,4224]{1,0:T(8,128)(2,1)S(1)}, bf16[64,4224]{1,0:T(8,128)(2,1)S(1)}, u32[]{:S(2)}, u32[]{:S(2)}) %collective-permute-start.4) | collective-permute-done | bytes 540704 | tf_op jit(solution)/shard_map/ppermute | solution.py:60
  32.8 1.8 %collective-permute-start.5 = (bf16[64,4224]{1,0:T(8,128)(2,1)S(1)}, bf16[64,4224]{1,0:T(8,128)(2,1)S(1)}, u32[]{:S(2)}, u32[]{:S(2)}) collective-permute-start(bf16[64,4224]{1,0:T(8,128)(2,1)S(1)} %collective-permute-done.4), channel_id=1, source_target_pairs={{0,2},{2,4},{4,6},{6,7},{7,5},{5,3},{3,1},{1,0},{8,10},{10,12},{12... | collective-permute-start | bytes 1622024 | tf_op jit(solution)/shard_map/ppermute | solution.py:60
  34.6 0.2 add_reduce_fusion.5
  34.8 0.8 %fusion = f32[256]{0:T(256)S(1)} fusion(bf16[256,4096]{1,0:T(8,128)(2,1)S(1)} %pad_maximum_fusion, bf16[64,4224]{1,0:T(8,128)(2,1)S(1)} %select_convert_fusion, f32[256]{0:T(256)S(1)} %get-tuple-element.6, f32[256]{0:T(256)S(1)} %get-tuple-element.5, f32[64]{0:T(128)S(1)} %add_reduce_fusion.7, f32[64]{0:T(128)S(1)} %multiply_floor_fusion.7), kind=kOutput, calls=%fused_computation.11 | convolution fusion | flops 134299392 | bytes 2625536 | tf_op jit(solution)/shard_map/id,jd->ij/dot_general | solution.py:26
  35.6 0.3 collective-permute-start.9
  35.8 0.2 add_reduce_fusion.1
  36.0 0.8 %fusion.1 = f32[256]{0:T(256)S(1)} fusion(bf16[256,4096]{1,0:T(8,128)(2,1)S(1)} %pad_maximum_fusion, bf16[64,4224]{1,0:T(8,128)(2,1)S(1)} %collective-permute-done.3, f32[256]{0:T(256)S(1)} %get-tuple-element.6, f32[256]{0:T(256)S(1)} %get-tuple-element.5, f32[64]{0:T(128)S(1)} %add_reduce_fusion.6, f32[64]{0:T(128)S(1)} %multiply_floor_fusion.6), kind=kOutput, calls=%fused_computation.12 | convolution fusion | flops 134299392 | bytes 2625536 | tf_op jit(solution)/shard_map/id,jd->ij/dot_general | solution.py:26
  36.8 0.8 %fusion.2 = f32[256]{0:T(256)S(1)} fusion(bf16[256,4096]{1,0:T(8,128)(2,1)S(1)} %pad_maximum_fusion, bf16[64,4224]{1,0:T(8,128)(2,1)S(1)} %collective-permute-done.4, f32[256]{0:T(256)S(1)} %get-tuple-element.6, f32[256]{0:T(256)S(1)} %get-tuple-element.5, f32[64]{0:T(128)S(1)} %add_reduce_fusion.5, f32[64]{0:T(128)S(1)} %multiply_floor_fusion.5), kind=kOutput, calls=%fused_computation.13 | convolution fusion | flops 134299392 | bytes 2625536 | tf_op jit(solution)/shard_map/id,jd->ij/dot_general | solution.py:26
  37.6 0.8 %fusion.6 = f32[256]{0:T(256)S(1)} fusion(bf16[256,4096]{1,0:T(8,128)(2,1)S(1)} %pad_maximum_fusion, bf16[64,4224]{1,0:T(8,128)(2,1)S(1)} %collective-permute-done.8, f32[256]{0:T(256)S(1)} %get-tuple-element.6, f32[256]{0:T(256)S(1)} %get-tuple-element.5, f32[64]{0:T(128)S(1)} %add_reduce_fusion.1, f32[64]{0:T(128)S(1)} %multiply_floor_fusion.1), kind=kOutput, calls=%fused_computation.17 | convolution fusion | flops 134299392 | bytes 2625536 | tf_op jit(solution)/shard_map/id,jd->ij/dot_general | solution.py:26
  38.4 0.8 %fusion.5 = f32[256]{0:T(256)S(1)} fusion(bf16[256,4096]{1,0:T(8,128)(2,1)S(1)} %pad_maximum_fusion, bf16[64,4224]{1,0:T(8,128)(2,1)S(1)} %collective-permute-done.7, f32[256]{0:T(256)S(1)} %get-tuple-element.6, f32[256]{0:T(256)S(1)} %get-tuple-element.5, f32[64]{0:T(128)S(1)} %add_reduce_fusion.2, f32[64]{0:T(128)S(1)} %multiply_floor_fusion.2), kind=kOutput, calls=%fused_computation.16 | convolution fusion | flops 134299392 | bytes 2625536 | tf_op jit(solution)/shard_map/id,jd->ij/dot_general | solution.py:26
  39.2 6.2 %collective-permute-done.5 = bf16[64,4224]{1,0:T(8,128)(2,1)S(1)} collective-permute-done((bf16[64,4224]{1,0:T(8,128)(2,1)S(1)}, bf16[64,4224]{1,0:T(8,128)(2,1)S(1)}, u32[]{:S(2)}, u32[]{:S(2)}) %collective-permute-start.5) | collective-permute-done | bytes 540704 | tf_op jit(solution)/shard_map/ppermute | solution.py:60
  45.4 1.9 %collective-permute-start.6 = (bf16[32,4224]{1,0:T(8,128)(2,1)S(1)}, bf16[32,4224]{1,0:T(8,128)(2,1)S(1)}, u32[]{:S(2)}, u32[]{:S(2)}) collective-permute-start(bf16[32,4224]{1,0:T(8,128)(2,1)S(1)} %slice.162), channel_id=1, source_target_pairs={{0,2},{2,4},{4,6},{6,7},{7,5},{5,3},{3,1},{1,0},{8,10},{10,12},{12... | collective-permute-start | bytes 811016 | tf_op jit(solution)/shard_map/ppermute | solution.py:60
  47.2 0.2 add_reduce_fusion.4
  47.4 0.5 collective-permute-done.9
  48.0 0.3 collective-permute-start.10
  48.3 0.2 add_reduce_fusion
  48.5 0.8 %fusion.3 = f32[256]{0:T(256)S(1)} fusion(bf16[256,4096]{1,0:T(8,128)(2,1)S(1)} %pad_maximum_fusion, bf16[64,4224]{1,0:T(8,128)(2,1)S(1)} %collective-permute-done.5, f32[256]{0:T(256)S(1)} %get-tuple-element.6, f32[256]{0:T(256)S(1)} %get-tuple-element.5, f32[64]{0:T(128)S(1)} %add_reduce_fusion.4, f32[64]{0:T(128)S(1)} %multiply_floor_fusion.4), kind=kOutput, calls=%fused_computation.14 | convolution fusion | flops 134299392 | bytes 2625536 | tf_op jit(solution)/shard_map/id,jd->ij/dot_general | solution.py:26
  49.3 0.8 %fusion.7 = f32[256]{0:T(256)S(1)} fusion(bf16[256,4096]{1,0:T(8,128)(2,1)S(1)} %pad_maximum_fusion, bf16[64,4224]{1,0:T(8,128)(2,1)S(1)} %collective-permute-done.9, f32[256]{0:T(256)S(1)} %get-tuple-element.6, f32[256]{0:T(256)S(1)} %get-tuple-element.5, f32[64]{0:T(128)S(1)} %add_reduce_fusion, f32[64]{0:T(128)S(1)} %multiply_floor_fusion), kind=kOutput, calls=%fused_computation.18 | convolution fusion | flops 134299392 | bytes 2625536 | tf_op jit(solution)/shard_map/id,jd->ij/dot_general | solution.py:26
  50.0 1.8 %collective-permute-done.6 = bf16[32,4224]{1,0:T(8,128)(2,1)S(1)} collective-permute-done((bf16[32,4224]{1,0:T(8,128)(2,1)S(1)}, bf16[32,4224]{1,0:T(8,128)(2,1)S(1)}, u32[]{:S(2)}, u32[]{:S(2)}) %collective-permute-start.6) | collective-permute-done | bytes 270368 | tf_op jit(solution)/shard_map/ppermute | solution.py:60
  51.9 2.6 %collective-permute-done.10 = bf16[32,4224]{1,0:T(8,128)(2,1)S(1)} collective-permute-done((bf16[32,4224]{1,0:T(8,128)(2,1)S(1)}, bf16[32,4224]{1,0:T(8,128)(2,1)S(1)}, u32[]{:S(2)}, u32[]{:S(2)}) %collective-permute-start.10) | collective-permute-done | bytes 270368 | tf_op jit(solution)/shard_map/ppermute | solution.py:60
  54.5 0.2 add_reduce_fusion.3
  54.7 0.8 %fusion.4 = f32[256]{0:T(256)S(1)} fusion(bf16[256,4096]{1,0:T(8,128)(2,1)S(1)} %pad_maximum_fusion, bf16[64,4224]{1,0:T(8,128)(2,1)S(1)} %constant_dynamic-update-slice_fusion, f32[256]{0:T(256)S(1)} %get-tuple-element.6, f32[256]{0:T(256)S(1)} %get-tuple-element.5, f32[64]{0:T(128)S(1)} %add_reduce_fusion.3, f32[64]{0:T(128)S(1)} %multiply_floor_fusion.3), kind=kOutput, calls=%fused_computation.15 | convolution fusion | flops 134299392 | bytes 2625536 | tf_op jit(solution)/shard_map/id,jd->ij/dot_general | solution.py:26
  55.5 0.1 slice_bitcast_fusion.1
  55.6 0.1 collective-permute-start.11
  55.7 1.1 %collective-permute-done.11 = f32[2,64]{1,0:T(2,128)S(1)} collective-permute-done((f32[2,64]{1,0:T(2,128)S(1)}, f32[2,64]{1,0:T(2,128)S(1)}, u32[]{:S(2)}, u32[]{:S(2)}) %collective-permute-start.11) | collective-permute-done | bytes 544 | tf_op jit(solution)/shard_map/ppermute | solution.py:105
  56.8 2.7 %collective-permute-start.12 = (f32[64]{0:T(128)S(1)}, f32[64]{0:T(128)S(1)}, u32[]{:S(2)}, u32[]{:S(2)}) collective-permute-start(f32[64]{0:T(128)S(1)} %bitcast_maximum_fusion), channel_id=1, source_target_pairs={{0,16},{8,24},{16,0},{24,8},{1,17},{9,25},{17,1},{25,9},{2,18},{10... | collective-permute-start | bytes 776 | tf_op jit(solution)/shard_map/ppermute | solution.py:108
  59.5 1.5 %collective-permute-done.12 = f32[64]{0:T(128)S(1)} collective-permute-done((f32[64]{0:T(128)S(1)}, f32[64]{0:T(128)S(1)}, u32[]{:S(2)}, u32[]{:S(2)}) %collective-permute-start.12) | collective-permute-done | bytes 288 | tf_op jit(solution)/shard_map/ppermute | solution.py:108
  61.1 0.5 fusion.18
  (25 shorter events, 0.2 us)
Async XLA Ops:
  0.0 2.4 %copy-start = (s32[64]{0:T(128)S(1)}, s32[64]{0:T(128)}, u32[]{:S(2)}) copy-start(s32[64]{0:T(128)} %param.4) | copy-start | bytes 772
  0.0 2.4 %copy-start.1 = (s32[64]{0:T(128)S(1)}, s32[64]{0:T(128)}, u32[]{:S(2)}) copy-start(s32[64]{0:T(128)} %param.5) | copy-start | bytes 772
  2.7 15.3 %collective-permute-start.1 = (bf16[64,4224]{1,0:T(8,128)(2,1)S(1)}, bf16[64,4224]{1,0:T(8,128)(2,1)S(1)}, u32[]{:S(2)}, u32[]{:S(2)}) collective-permute-start(bf16[64,4224]{1,0:T(8,128)(2,1)S(1)} %select_convert_fusion), channel_id=1, source_target_pairs={{0,16},{8,24},{16,0},{24,8},{1,17},{9,25},{17,1},{25,9},{2,18},{10... | collective-permute-start | bytes 1622024 | tf_op jit(solution)/shard_map/ppermute | solution.py:69
  5.8 13.7 %collective-permute-start.3 = (bf16[64,4224]{1,0:T(8,128)(2,1)S(1)}, bf16[64,4224]{1,0:T(8,128)(2,1)S(1)}, u32[]{:S(2)}, u32[]{:S(2)}) collective-permute-start(bf16[64,4224]{1,0:T(8,128)(2,1)S(1)} %select_convert_fusion), channel_id=1, source_target_pairs={{0,2},{2,4},{4,6},{6,7},{7,5},{5,3},{3,1},{1,0},{8,10},{10,12},{12... | collective-permute-start | bytes 1622024 | tf_op jit(solution)/shard_map/ppermute | solution.py:60
  7.4 13.9 %collective-permute-start.7 = (bf16[64,4224]{1,0:T(8,128)(2,1)S(1)}, bf16[64,4224]{1,0:T(8,128)(2,1)S(1)}, u32[]{:S(2)}, u32[]{:S(2)}) collective-permute-start(bf16[64,4224]{1,0:T(8,128)(2,1)S(1)} %select_convert_fusion), channel_id=1, source_target_pairs={{2,0},{4,2},{6,4},{7,6},{5,7},{3,5},{1,3},{0,1},{10,8},{12,10},{14... | collective-permute-start | bytes 1622024 | tf_op jit(solution)/shard_map/ppermute | solution.py:60
  7.8 14.2 %collective-permute-start = (bf16[64,4224]{1,0:T(8,128)(2,1)S(1)}, bf16[64,4224]{1,0:T(8,128)(2,1)S(1)}, u32[]{:S(2)}, u32[]{:S(2)}) collective-permute-start(bf16[64,4224]{1,0:T(8,128)(2,1)S(1)} %select_convert_fusion), channel_id=1, source_target_pairs={{0,8},{8,0},{16,24},{24,16},{1,9},{9,1},{17,25},{25,17},{2,10},{10... | collective-permute-start | bytes 1622024 | tf_op jit(solution)/shard_map/ppermute | solution.py:70
  18.1 3.9 %collective-permute-start.2 = (bf16[64,4224]{1,0:T(8,128)(2,1)S(1)}, bf16[64,4224]{1,0:T(8,128)(2,1)S(1)}, u32[]{:S(2)}, u32[]{:S(2)}) collective-permute-start(bf16[64,4224]{1,0:T(8,128)(2,1)S(1)} %collective-permute-done.1), channel_id=1, source_target_pairs={{0,8},{8,0},{16,24},{24,16},{1,9},{9,1},{17,25},{25,17},{2,10},{10... | collective-permute-start | bytes 1622024 | tf_op jit(solution)/shard_map/ppermute | solution.py:71
  19.5 13.2 %collective-permute-start.4 = (bf16[64,4224]{1,0:T(8,128)(2,1)S(1)}, bf16[64,4224]{1,0:T(8,128)(2,1)S(1)}, u32[]{:S(2)}, u32[]{:S(2)}) collective-permute-start(bf16[64,4224]{1,0:T(8,128)(2,1)S(1)} %collective-permute-done.3), channel_id=1, source_target_pairs={{0,2},{2,4},{4,6},{6,7},{7,5},{5,3},{3,1},{1,0},{8,10},{10,12},{12... | collective-permute-start | bytes 1622024 | tf_op jit(solution)/shard_map/ppermute | solution.py:60
  21.3 14.2 %collective-permute-start.8 = (bf16[64,4224]{1,0:T(8,128)(2,1)S(1)}, bf16[64,4224]{1,0:T(8,128)(2,1)S(1)}, u32[]{:S(2)}, u32[]{:S(2)}) collective-permute-start(bf16[64,4224]{1,0:T(8,128)(2,1)S(1)} %collective-permute-done.7), channel_id=1, source_target_pairs={{2,0},{4,2},{6,4},{7,6},{5,7},{3,5},{1,3},{0,1},{10,8},{12,10},{14... | collective-permute-start | bytes 1622024 | tf_op jit(solution)/shard_map/ppermute | solution.py:60
  32.8 12.6 %collective-permute-start.5 = (bf16[64,4224]{1,0:T(8,128)(2,1)S(1)}, bf16[64,4224]{1,0:T(8,128)(2,1)S(1)}, u32[]{:S(2)}, u32[]{:S(2)}) collective-permute-start(bf16[64,4224]{1,0:T(8,128)(2,1)S(1)} %collective-permute-done.4), channel_id=1, source_target_pairs={{0,2},{2,4},{4,6},{6,7},{7,5},{5,3},{3,1},{1,0},{8,10},{10,12},{12... | collective-permute-start | bytes 1622024 | tf_op jit(solution)/shard_map/ppermute | solution.py:60
  35.6 12.4 %collective-permute-start.9 = (bf16[64,4224]{1,0:T(8,128)(2,1)S(1)}, bf16[64,4224]{1,0:T(8,128)(2,1)S(1)}, u32[]{:S(2)}, u32[]{:S(2)}) collective-permute-start(bf16[64,4224]{1,0:T(8,128)(2,1)S(1)} %collective-permute-done.8), channel_id=1, source_target_pairs={{2,0},{4,2},{6,4},{7,6},{5,7},{3,5},{1,3},{0,1},{10,8},{12,10},{14... | collective-permute-start | bytes 1622024 | tf_op jit(solution)/shard_map/ppermute | solution.py:60
  45.4 6.5 %collective-permute-start.6 = (bf16[32,4224]{1,0:T(8,128)(2,1)S(1)}, bf16[32,4224]{1,0:T(8,128)(2,1)S(1)}, u32[]{:S(2)}, u32[]{:S(2)}) collective-permute-start(bf16[32,4224]{1,0:T(8,128)(2,1)S(1)} %slice.162), channel_id=1, source_target_pairs={{0,2},{2,4},{4,6},{6,7},{7,5},{5,3},{3,1},{1,0},{8,10},{10,12},{12... | collective-permute-start | bytes 811016 | tf_op jit(solution)/shard_map/ppermute | solution.py:60
  48.0 6.5 %collective-permute-start.10 = (bf16[32,4224]{1,0:T(8,128)(2,1)S(1)}, bf16[32,4224]{1,0:T(8,128)(2,1)S(1)}, u32[]{:S(2)}, u32[]{:S(2)}) collective-permute-start(bf16[32,4224]{1,0:T(8,128)(2,1)S(1)} %slice.163), channel_id=1, source_target_pairs={{2,0},{4,2},{6,4},{7,6},{5,7},{3,5},{1,3},{0,1},{10,8},{12,10},{14... | collective-permute-start | bytes 811016 | tf_op jit(solution)/shard_map/ppermute | solution.py:60
  55.6 1.2 %collective-permute-start.11 = (f32[2,64]{1,0:T(2,128)S(1)}, f32[2,64]{1,0:T(2,128)S(1)}, u32[]{:S(2)}, u32[]{:S(2)}) collective-permute-start(f32[2,64]{1,0:T(2,128)S(1)} %pad_maximum_fusion.5), channel_id=1, source_target_pairs={{0,8},{8,0},{16,24},{24,16},{1,9},{9,1},{17,25},{25,17},{2,10},{10... | collective-permute-start | bytes 1544 | tf_op jit(solution)/shard_map/ppermute | solution.py:105
  56.8 4.2 %collective-permute-start.12 = (f32[64]{0:T(128)S(1)}, f32[64]{0:T(128)S(1)}, u32[]{:S(2)}, u32[]{:S(2)}) collective-permute-start(f32[64]{0:T(128)S(1)} %bitcast_maximum_fusion), channel_id=1, source_target_pairs={{0,16},{8,24},{16,0},{24,8},{1,17},{9,25},{17,1},{25,9},{2,18},{10... | collective-permute-start | bytes 776 | tf_op jit(solution)/shard_map/ppermute | solution.py:108

commit v19 on v18

--- a/solution.py
+++ b/solution.py
@@ -39,7 +39,9 @@
     block_count = lax.axis_size("blk")
     rows_here = embeddings.shape[0]
     widened = embeddings.astype(jnp.float32)
-    square_sum = jnp.sum(widened * widened, axis=1, keepdims=True)
+    gram = jnp.einsum("id,jd->ij", embeddings, embeddings, preferred_element_type=jnp.float32)
+    diagonal = lax.broadcasted_iota(jnp.int32, gram.shape, 0) == lax.broadcasted_iota(jnp.int32, gram.shape, 1)
+    square_sum = jnp.sum(jnp.where(diagonal, gram, 0.0), axis=1, keepdims=True)
     scale = lax.rsqrt(square_sum / D + 1e-06)
     high = (cluster_ids * 64 + row_index // 128).astype(jnp.float32)[:, None]
     low = (row_index % 128).astype(jnp.float32)[:, None]

time: 61.8 us -> 62.6 us (1.013)
  matrix products: 6.25 us -> 7.75 us
    dot_general x0 -> x1, matrix products: none -> 1.5 us  [per_device(): jnp.einsum('id,jd->ij', embeddings, embeddings, preferred_element_type=jn...]
    reduce_sum x1 -> x0, other arithmetic: 1.25 us -> none  [per_device(): square_sum = jnp.sum(widened * widened, axis=1, keepdims=True)]
    convert_element_type x1 -> x0, other arithmetic: 1.12 us -> none  [per_device(): widened = embeddings.astype(jnp.float32)]
    convert_element_type x1, other arithmetic: 0.29 us -> 1.36 us  [per_device(): jnp.where(column < D, padded * scale / math.sqrt(D), tags)]
    convert_element_type x1, other arithmetic: 0.01 us -> 0.69 us  [per_device(): high = (cluster_ids * 64 + row_index // 128).astype(jnp.float32)[:, None]]
where the time goes in v19:
time: 62.6 us; the launch traced here: 62.5 us
  waiting for transfers between devices  35.6 us (57%)
  starting transfers between devices  14.2 us (23%)
  matrix products  7.75 us (12%)
  other arithmetic  4.53 us (7%)
    ppermute x8, waiting for transfers between devices, send(): return lax.ppermute(visiting, 'blk', forward if which == 0 else backward)  22.9 us
    ppermute x1, waiting for transfers between devices, per_device(): across = lax.ppermute(payload, 'grp', partner_pairs(group_count, 2))  10.1 us
    ppermute x8, starting transfers between devices, send(): return lax.ppermute(visiting, 'blk', forward if which == 0 else backward)  8.34 us
    dot_general x8, matrix products, block_best(): jnp.einsum('id,jd->ij', left_rows, payload[:, :D], preferred_element_type...  6.25 us
    ppermute x1, starting transfers between devices, per_device(): across = lax.ppermute(payload, 'grp', partner_pairs(group_count, 2))  3.06 us
    ppermute x1, starting transfers between devices, per_device(): lax.ppermute(across, 'grp', partner_pairs(group_count, 2))  2.72 us
    ppermute x1, waiting for transfers between devices, per_device(): lax.ppermute(across, 'grp', partner_pairs(group_count, 2))  1.55 us
    dot_general x1, matrix products, per_device(): jnp.einsum('id,jd->ij', embeddings, embeddings, preferred_element_type=jn...  1.5 us
  transfers between devices with their start and end apart: 13, of which 9 were waited for; matrix products, arithmetic and copies ran while one was open for 12% of the time, Pallas kernels for 0%

profile of v19, /device:TPU:0, one launch (start us, length us, event | category | flops | bytes accessed | tf_op | source)
XLA Modules:
  0.0 62.5 jit_solution(4484877109285396325)
XLA Ops:
  0.0 1.5 %fusion.8 = f32[64]{0:T(128)S(1)} fusion(bf16[64,4096]{1,0:T(8,128)(2,1)} %param.3), kind=kOutput, calls=%fused_computation.20 | convolution fusion | flops 33566656 | bytes 524544 | tf_op jit(solution)/shard_map/id,jd->ij/dot_general | solution.py:42
  1.5 0.7 %add_convert_fusion = (bf16[64]{0:T(256)(128)(2,1)S(1)}, bf16[64]{0:T(256)(128)(2,1)S(1)}) fusion(s32[64]{0:T(128)} %param.4, s32[64]{0:T(128)} %param.5), kind=kLoop, calls=%fused_computation.70 | loop fusion | flops 1472 | bytes 768 | tf_op jit(solution)/shard_map/convert_element_type | solution.py:46
  2.2 1.4 %select_convert_fusion = bf16[64,4224]{1,0:T(8,128)(2,1)S(1)} fusion(bf16[64]{0:T(256)(128)(2,1)S(1)} %get-tuple-element.12, bf16[64]{0:T(256)(128)(2,1)S(1)} %get-tuple-element.11, f32[64]{0:T(128)S(1)} %add_rsqrt_fusion, bf16[64,4096]{1,0:T(8,128)(2,1)} %param.3, pred[4224]{0:T(1024)(128)(4,1)S(1)} %get-tuple-element.13, ...), kind=kLoop, calls=%fused_computation.21 | loop fusion | flops 1622016 | bytes 1078144 | tf_op jit(solution)/shard_map/convert_element_type | solution.py:51
  3.6 3.1 %collective-permute-start.1 = (bf16[64,4224]{1,0:T(8,128)(2,1)S(1)}, bf16[64,4224]{1,0:T(8,128)(2,1)S(1)}, u32[]{:S(2)}, u32[]{:S(2)}) collective-permute-start(bf16[64,4224]{1,0:T(8,128)(2,1)S(1)} %select_convert_fusion), channel_id=1, source_target_pairs={{0,16},{8,24},{16,0},{24,8},{1,17},{9,25},{17,1},{25,9},{2,18},{10... | collective-permute-start | bytes 1622024 | tf_op jit(solution)/shard_map/ppermute | solution.py:71
  6.7 1.6 %collective-permute-start.3 = (bf16[64,4224]{1,0:T(8,128)(2,1)S(1)}, bf16[64,4224]{1,0:T(8,128)(2,1)S(1)}, u32[]{:S(2)}, u32[]{:S(2)}) collective-permute-start(bf16[64,4224]{1,0:T(8,128)(2,1)S(1)} %select_convert_fusion), channel_id=1, source_target_pairs={{0,2},{2,4},{4,6},{6,7},{7,5},{5,3},{3,1},{1,0},{8,10},{10,12},{12... | collective-permute-start | bytes 1622024 | tf_op jit(solution)/shard_map/ppermute | solution.py:62
  8.2 0.4 collective-permute-start.7
  8.7 0.0 collective-permute-start
  8.7 0.2 add_reduce_fusion.7
  8.9 10.1 %collective-permute-done.1 = bf16[64,4224]{1,0:T(8,128)(2,1)S(1)} collective-permute-done((bf16[64,4224]{1,0:T(8,128)(2,1)S(1)}, bf16[64,4224]{1,0:T(8,128)(2,1)S(1)}, u32[]{:S(2)}, u32[]{:S(2)}) %collective-permute-start.1) | collective-permute-done | bytes 540704 | tf_op jit(solution)/shard_map/ppermute | solution.py:71
  18.9 0.0 collective-permute-start.2
  18.9 1.5 %collective-permute-done.3 = bf16[64,4224]{1,0:T(8,128)(2,1)S(1)} collective-permute-done((bf16[64,4224]{1,0:T(8,128)(2,1)S(1)}, bf16[64,4224]{1,0:T(8,128)(2,1)S(1)}, u32[]{:S(2)}, u32[]{:S(2)}) %collective-permute-start.3) | collective-permute-done | bytes 540704 | tf_op jit(solution)/shard_map/ppermute | solution.py:62
  20.4 1.6 %collective-permute-start.4 = (bf16[64,4224]{1,0:T(8,128)(2,1)S(1)}, bf16[64,4224]{1,0:T(8,128)(2,1)S(1)}, u32[]{:S(2)}, u32[]{:S(2)}) collective-permute-start(bf16[64,4224]{1,0:T(8,128)(2,1)S(1)} %collective-permute-done.3), channel_id=1, source_target_pairs={{0,2},{2,4},{4,6},{6,7},{7,5},{5,3},{3,1},{1,0},{8,10},{10,12},{12... | collective-permute-start | bytes 1622024 | tf_op jit(solution)/shard_map/ppermute | solution.py:62
  22.0 0.2 add_reduce_fusion.6
  22.1 0.0 collective-permute-done.7
  22.2 0.5 collective-permute-start.8
  22.7 0.2 add_reduce_fusion.2
  22.9 0.0 collective-permute-done.2
  22.9 0.1 pad_maximum_fusion.4
  23.0 0.2 floor_reduce_fusion
  23.1 0.2 pad_maximum_fusion
  23.4 10.2 %collective-permute-done.4 = bf16[64,4224]{1,0:T(8,128)(2,1)S(1)} collective-permute-done((bf16[64,4224]{1,0:T(8,128)(2,1)S(1)}, bf16[64,4224]{1,0:T(8,128)(2,1)S(1)}, u32[]{:S(2)}, u32[]{:S(2)}) %collective-permute-start.4) | collective-permute-done | bytes 540704 | tf_op jit(solution)/shard_map/ppermute | solution.py:62
  33.6 1.8 %collective-permute-start.5 = (bf16[64,4224]{1,0:T(8,128)(2,1)S(1)}, bf16[64,4224]{1,0:T(8,128)(2,1)S(1)}, u32[]{:S(2)}, u32[]{:S(2)}) collective-permute-start(bf16[64,4224]{1,0:T(8,128)(2,1)S(1)} %collective-permute-done.4), channel_id=1, source_target_pairs={{0,2},{2,4},{4,6},{6,7},{7,5},{5,3},{3,1},{1,0},{8,10},{10,12},{12... | collective-permute-start | bytes 1622024 | tf_op jit(solution)/shard_map/ppermute | solution.py:62
  35.4 0.2 add_reduce_fusion.5
  35.6 0.8 %fusion = f32[256]{0:T(256)S(1)} fusion(bf16[256,4096]{1,0:T(8,128)(2,1)S(1)} %pad_maximum_fusion, bf16[64,4224]{1,0:T(8,128)(2,1)S(1)} %select_convert_fusion, f32[256]{0:T(256)S(1)} %get-tuple-element.6, f32[256]{0:T(256)S(1)} %get-tuple-element.5, f32[64]{0:T(128)S(1)} %add_reduce_fusion.7, f32[64]{0:T(128)S(1)} %multiply_floor_fusion.7), kind=kOutput, calls=%fused_computation.11 | convolution fusion | flops 134299392 | bytes 2625536 | tf_op jit(solution)/shard_map/id,jd->ij/dot_general | solution.py:26
  36.4 0.3 collective-permute-start.9
  36.7 0.2 add_reduce_fusion.1
  36.9 0.8 %fusion.1 = f32[256]{0:T(256)S(1)} fusion(bf16[256,4096]{1,0:T(8,128)(2,1)S(1)} %pad_maximum_fusion, bf16[64,4224]{1,0:T(8,128)(2,1)S(1)} %collective-permute-done.3, f32[256]{0:T(256)S(1)} %get-tuple-element.6, f32[256]{0:T(256)S(1)} %get-tuple-element.5, f32[64]{0:T(128)S(1)} %add_reduce_fusion.6, f32[64]{0:T(128)S(1)} %multiply_floor_fusion.6), kind=kOutput, calls=%fused_computation.12 | convolution fusion | flops 134299392 | bytes 2625536 | tf_op jit(solution)/shard_map/id,jd->ij/dot_general | solution.py:26
  37.6 0.8 %fusion.2 = f32[256]{0:T(256)S(1)} fusion(bf16[256,4096]{1,0:T(8,128)(2,1)S(1)} %pad_maximum_fusion, bf16[64,4224]{1,0:T(8,128)(2,1)S(1)} %collective-permute-done.4, f32[256]{0:T(256)S(1)} %get-tuple-element.6, f32[256]{0:T(256)S(1)} %get-tuple-element.5, f32[64]{0:T(128)S(1)} %add_reduce_fusion.5, f32[64]{0:T(128)S(1)} %multiply_floor_fusion.5), kind=kOutput, calls=%fused_computation.13 | convolution fusion | flops 134299392 | bytes 2625536 | tf_op jit(solution)/shard_map/id,jd->ij/dot_general | solution.py:26
  38.4 0.8 %fusion.6 = f32[256]{0:T(256)S(1)} fusion(bf16[256,4096]{1,0:T(8,128)(2,1)S(1)} %pad_maximum_fusion, bf16[64,4224]{1,0:T(8,128)(2,1)S(1)} %collective-permute-done.8, f32[256]{0:T(256)S(1)} %get-tuple-element.6, f32[256]{0:T(256)S(1)} %get-tuple-element.5, f32[64]{0:T(128)S(1)} %add_reduce_fusion.1, f32[64]{0:T(128)S(1)} %multiply_floor_fusion.1), kind=kOutput, calls=%fused_computation.17 | convolution fusion | flops 134299392 | bytes 2625536 | tf_op jit(solution)/shard_map/id,jd->ij/dot_general | solution.py:26
  39.2 0.8 %fusion.5 = f32[256]{0:T(256)S(1)} fusion(bf16[256,4096]{1,0:T(8,128)(2,1)S(1)} %pad_maximum_fusion, bf16[64,4224]{1,0:T(8,128)(2,1)S(1)} %collective-permute-done.7, f32[256]{0:T(256)S(1)} %get-tuple-element.6, f32[256]{0:T(256)S(1)} %get-tuple-element.5, f32[64]{0:T(128)S(1)} %add_reduce_fusion.2, f32[64]{0:T(128)S(1)} %multiply_floor_fusion.2), kind=kOutput, calls=%fused_computation.16 | convolution fusion | flops 134299392 | bytes 2625536 | tf_op jit(solution)/shard_map/id,jd->ij/dot_general | solution.py:26
  40.0 6.2 %collective-permute-done.5 = bf16[64,4224]{1,0:T(8,128)(2,1)S(1)} collective-permute-done((bf16[64,4224]{1,0:T(8,128)(2,1)S(1)}, bf16[64,4224]{1,0:T(8,128)(2,1)S(1)}, u32[]{:S(2)}, u32[]{:S(2)}) %collective-permute-start.5) | collective-permute-done | bytes 540704 | tf_op jit(solution)/shard_map/ppermute | solution.py:62
  46.2 1.9 %collective-permute-start.6 = (bf16[32,4224]{1,0:T(8,128)(2,1)S(1)}, bf16[32,4224]{1,0:T(8,128)(2,1)S(1)}, u32[]{:S(2)}, u32[]{:S(2)}) collective-permute-start(bf16[32,4224]{1,0:T(8,128)(2,1)S(1)} %slice.162), channel_id=1, source_target_pairs={{0,2},{2,4},{4,6},{6,7},{7,5},{5,3},{3,1},{1,0},{8,10},{10,12},{12... | collective-permute-start | bytes 811016 | tf_op jit(solution)/shard_map/ppermute | solution.py:62
  48.1 0.2 add_reduce_fusion.4
  48.3 0.5 collective-permute-done.9
  48.8 0.3 collective-permute-start.10
  49.1 0.2 add_reduce_fusion
  49.3 0.8 %fusion.3 = f32[256]{0:T(256)S(1)} fusion(bf16[256,4096]{1,0:T(8,128)(2,1)S(1)} %pad_maximum_fusion, bf16[64,4224]{1,0:T(8,128)(2,1)S(1)} %collective-permute-done.5, f32[256]{0:T(256)S(1)} %get-tuple-element.6, f32[256]{0:T(256)S(1)} %get-tuple-element.5, f32[64]{0:T(128)S(1)} %add_reduce_fusion.4, f32[64]{0:T(128)S(1)} %multiply_floor_fusion.4), kind=kOutput, calls=%fused_computation.14 | convolution fusion | flops 134299392 | bytes 2625536 | tf_op jit(solution)/shard_map/id,jd->ij/dot_general | solution.py:26
  50.1 0.8 %fusion.7 = f32[256]{0:T(256)S(1)} fusion(bf16[256,4096]{1,0:T(8,128)(2,1)S(1)} %pad_maximum_fusion, bf16[64,4224]{1,0:T(8,128)(2,1)S(1)} %collective-permute-done.9, f32[256]{0:T(256)S(1)} %get-tuple-element.6, f32[256]{0:T(256)S(1)} %get-tuple-element.5, f32[64]{0:T(128)S(1)} %add_reduce_fusion, f32[64]{0:T(128)S(1)} %multiply_floor_fusion), kind=kOutput, calls=%fused_computation.18 | convolution fusion | flops 134299392 | bytes 2625536 | tf_op jit(solution)/shard_map/id,jd->ij/dot_general | solution.py:26
  50.9 1.8 %collective-permute-done.6 = bf16[32,4224]{1,0:T(8,128)(2,1)S(1)} collective-permute-done((bf16[32,4224]{1,0:T(8,128)(2,1)S(1)}, bf16[32,4224]{1,0:T(8,128)(2,1)S(1)}, u32[]{:S(2)}, u32[]{:S(2)}) %collective-permute-start.6) | collective-permute-done | bytes 270368 | tf_op jit(solution)/shard_map/ppermute | solution.py:62
  52.7 2.6 %collective-permute-done.10 = bf16[32,4224]{1,0:T(8,128)(2,1)S(1)} collective-permute-done((bf16[32,4224]{1,0:T(8,128)(2,1)S(1)}, bf16[32,4224]{1,0:T(8,128)(2,1)S(1)}, u32[]{:S(2)}, u32[]{:S(2)}) %collective-permute-start.10) | collective-permute-done | bytes 270368 | tf_op jit(solution)/shard_map/ppermute | solution.py:62
  55.4 0.2 add_reduce_fusion.3
  55.6 0.8 %fusion.4 = f32[256]{0:T(256)S(1)} fusion(bf16[256,4096]{1,0:T(8,128)(2,1)S(1)} %pad_maximum_fusion, bf16[64,4224]{1,0:T(8,128)(2,1)S(1)} %constant_dynamic-update-slice_fusion, f32[256]{0:T(256)S(1)} %get-tuple-element.6, f32[256]{0:T(256)S(1)} %get-tuple-element.5, f32[64]{0:T(128)S(1)} %add_reduce_fusion.3, f32[64]{0:T(128)S(1)} %multiply_floor_fusion.3), kind=kOutput, calls=%fused_computation.15 | convolution fusion | flops 134299392 | bytes 2625536 | tf_op jit(solution)/shard_map/id,jd->ij/dot_general | solution.py:26
  56.4 0.1 slice_bitcast_fusion.1
  56.5 0.1 collective-permute-start.11
  56.5 1.1 %collective-permute-done.11 = f32[2,64]{1,0:T(2,128)S(1)} collective-permute-done((f32[2,64]{1,0:T(2,128)S(1)}, f32[2,64]{1,0:T(2,128)S(1)}, u32[]{:S(2)}, u32[]{:S(2)}) %collective-permute-start.11) | collective-permute-done | bytes 544 | tf_op jit(solution)/shard_map/ppermute | solution.py:107
  57.7 2.7 %collective-permute-start.12 = (f32[64]{0:T(128)S(1)}, f32[64]{0:T(128)S(1)}, u32[]{:S(2)}, u32[]{:S(2)}) collective-permute-start(f32[64]{0:T(128)S(1)} %bitcast_maximum_fusion), channel_id=1, source_target_pairs={{0,16},{8,24},{16,0},{24,8},{1,17},{9,25},{17,1},{25,9},{2,18},{10... | collective-permute-start | bytes 776 | tf_op jit(solution)/shard_map/ppermute | solution.py:110
  60.4 1.5 %collective-permute-done.12 = f32[64]{0:T(128)S(1)} collective-permute-done((f32[64]{0:T(128)S(1)}, f32[64]{0:T(128)S(1)}, u32[]{:S(2)}, u32[]{:S(2)}) %collective-permute-start.12) | collective-permute-done | bytes 288 | tf_op jit(solution)/shard_map/ppermute | solution.py:110
  61.9 0.5 fusion.19
  (20 shorter events, 0.2 us)
Async XLA Ops:
  3.6 15.3 %collective-permute-start.1 = (bf16[64,4224]{1,0:T(8,128)(2,1)S(1)}, bf16[64,4224]{1,0:T(8,128)(2,1)S(1)}, u32[]{:S(2)}, u32[]{:S(2)}) collective-permute-start(bf16[64,4224]{1,0:T(8,128)(2,1)S(1)} %select_convert_fusion), channel_id=1, source_target_pairs={{0,16},{8,24},{16,0},{24,8},{1,17},{9,25},{17,1},{25,9},{2,18},{10... | collective-permute-start | bytes 1622024 | tf_op jit(solution)/shard_map/ppermute | solution.py:71
  6.7 13.7 %collective-permute-start.3 = (bf16[64,4224]{1,0:T(8,128)(2,1)S(1)}, bf16[64,4224]{1,0:T(8,128)(2,1)S(1)}, u32[]{:S(2)}, u32[]{:S(2)}) collective-permute-start(bf16[64,4224]{1,0:T(8,128)(2,1)S(1)} %select_convert_fusion), channel_id=1, source_target_pairs={{0,2},{2,4},{4,6},{6,7},{7,5},{5,3},{3,1},{1,0},{8,10},{10,12},{12... | collective-permute-start | bytes 1622024 | tf_op jit(solution)/shard_map/ppermute | solution.py:62
  8.2 13.9 %collective-permute-start.7 = (bf16[64,4224]{1,0:T(8,128)(2,1)S(1)}, bf16[64,4224]{1,0:T(8,128)(2,1)S(1)}, u32[]{:S(2)}, u32[]{:S(2)}) collective-permute-start(bf16[64,4224]{1,0:T(8,128)(2,1)S(1)} %select_convert_fusion), channel_id=1, source_target_pairs={{2,0},{4,2},{6,4},{7,6},{5,7},{3,5},{1,3},{0,1},{10,8},{12,10},{14... | collective-permute-start | bytes 1622024 | tf_op jit(solution)/shard_map/ppermute | solution.py:62
  8.7 14.2 %collective-permute-start = (bf16[64,4224]{1,0:T(8,128)(2,1)S(1)}, bf16[64,4224]{1,0:T(8,128)(2,1)S(1)}, u32[]{:S(2)}, u32[]{:S(2)}) collective-permute-start(bf16[64,4224]{1,0:T(8,128)(2,1)S(1)} %select_convert_fusion), channel_id=1, source_target_pairs={{0,8},{8,0},{16,24},{24,16},{1,9},{9,1},{17,25},{25,17},{2,10},{10... | collective-permute-start | bytes 1622024 | tf_op jit(solution)/shard_map/ppermute | solution.py:72
  18.9 3.9 %collective-permute-start.2 = (bf16[64,4224]{1,0:T(8,128)(2,1)S(1)}, bf16[64,4224]{1,0:T(8,128)(2,1)S(1)}, u32[]{:S(2)}, u32[]{:S(2)}) collective-permute-start(bf16[64,4224]{1,0:T(8,128)(2,1)S(1)} %collective-permute-done.1), channel_id=1, source_target_pairs={{0,8},{8,0},{16,24},{24,16},{1,9},{9,1},{17,25},{25,17},{2,10},{10... | collective-permute-start | bytes 1622024 | tf_op jit(solution)/shard_map/ppermute | solution.py:73
  20.4 13.2 %collective-permute-start.4 = (bf16[64,4224]{1,0:T(8,128)(2,1)S(1)}, bf16[64,4224]{1,0:T(8,128)(2,1)S(1)}, u32[]{:S(2)}, u32[]{:S(2)}) collective-permute-start(bf16[64,4224]{1,0:T(8,128)(2,1)S(1)} %collective-permute-done.3), channel_id=1, source_target_pairs={{0,2},{2,4},{4,6},{6,7},{7,5},{5,3},{3,1},{1,0},{8,10},{10,12},{12... | collective-permute-start | bytes 1622024 | tf_op jit(solution)/shard_map/ppermute | solution.py:62
  22.2 14.2 %collective-permute-start.8 = (bf16[64,4224]{1,0:T(8,128)(2,1)S(1)}, bf16[64,4224]{1,0:T(8,128)(2,1)S(1)}, u32[]{:S(2)}, u32[]{:S(2)}) collective-permute-start(bf16[64,4224]{1,0:T(8,128)(2,1)S(1)} %collective-permute-done.7), channel_id=1, source_target_pairs={{2,0},{4,2},{6,4},{7,6},{5,7},{3,5},{1,3},{0,1},{10,8},{12,10},{14... | collective-permute-start | bytes 1622024 | tf_op jit(solution)/shard_map/ppermute | solution.py:62
  33.6 12.6 %collective-permute-start.5 = (bf16[64,4224]{1,0:T(8,128)(2,1)S(1)}, bf16[64,4224]{1,0:T(8,128)(2,1)S(1)}, u32[]{:S(2)}, u32[]{:S(2)}) collective-permute-start(bf16[64,4224]{1,0:T(8,128)(2,1)S(1)} %collective-permute-done.4), channel_id=1, source_target_pairs={{0,2},{2,4},{4,6},{6,7},{7,5},{5,3},{3,1},{1,0},{8,10},{10,12},{12... | collective-permute-start | bytes 1622024 | tf_op jit(solution)/shard_map/ppermute | solution.py:62
  36.4 12.4 %collective-permute-start.9 = (bf16[64,4224]{1,0:T(8,128)(2,1)S(1)}, bf16[64,4224]{1,0:T(8,128)(2,1)S(1)}, u32[]{:S(2)}, u32[]{:S(2)}) collective-permute-start(bf16[64,4224]{1,0:T(8,128)(2,1)S(1)} %collective-permute-done.8), channel_id=1, source_target_pairs={{2,0},{4,2},{6,4},{7,6},{5,7},{3,5},{1,3},{0,1},{10,8},{12,10},{14... | collective-permute-start | bytes 1622024 | tf_op jit(solution)/shard_map/ppermute | solution.py:62
  46.2 6.5 %collective-permute-start.6 = (bf16[32,4224]{1,0:T(8,128)(2,1)S(1)}, bf16[32,4224]{1,0:T(8,128)(2,1)S(1)}, u32[]{:S(2)}, u32[]{:S(2)}) collective-permute-start(bf16[32,4224]{1,0:T(8,128)(2,1)S(1)} %slice.162), channel_id=1, source_target_pairs={{0,2},{2,4},{4,6},{6,7},{7,5},{5,3},{3,1},{1,0},{8,10},{10,12},{12... | collective-permute-start | bytes 811016 | tf_op jit(solution)/shard_map/ppermute | solution.py:62
  48.8 6.5 %collective-permute-start.10 = (bf16[32,4224]{1,0:T(8,128)(2,1)S(1)}, bf16[32,4224]{1,0:T(8,128)(2,1)S(1)}, u32[]{:S(2)}, u32[]{:S(2)}) collective-permute-start(bf16[32,4224]{1,0:T(8,128)(2,1)S(1)} %slice.163), channel_id=1, source_target_pairs={{2,0},{4,2},{6,4},{7,6},{5,7},{3,5},{1,3},{0,1},{10,8},{12,10},{14... | collective-permute-start | bytes 811016 | tf_op jit(solution)/shard_map/ppermute | solution.py:62
  56.5 1.2 %collective-permute-start.11 = (f32[2,64]{1,0:T(2,128)S(1)}, f32[2,64]{1,0:T(2,128)S(1)}, u32[]{:S(2)}, u32[]{:S(2)}) collective-permute-start(f32[2,64]{1,0:T(2,128)S(1)} %pad_maximum_fusion.5), channel_id=1, source_target_pairs={{0,8},{8,0},{16,24},{24,16},{1,9},{9,1},{17,25},{25,17},{2,10},{10... | collective-permute-start | bytes 1544 | tf_op jit(solution)/shard_map/ppermute | solution.py:107
  57.7 4.3 %collective-permute-start.12 = (f32[64]{0:T(128)S(1)}, f32[64]{0:T(128)S(1)}, u32[]{:S(2)}, u32[]{:S(2)}) collective-permute-start(f32[64]{0:T(128)S(1)} %bitcast_maximum_fusion), channel_id=1, source_target_pairs={{0,16},{8,24},{16,0},{24,8},{1,17},{9,25},{17,1},{25,9},{2,18},{10... | collective-permute-start | bytes 776 | tf_op jit(solution)/shard_map/ppermute | solution.py:110

commit v20 on v18

--- a/solution.py
+++ b/solution.py
@@ -85,20 +85,27 @@
             best = tile if best is None else jnp.maximum(best, tile)
         return best
 
+    def fold_joined(best, blocks):
+        if not blocks:
+            return best
+        joined = blocks[0] if len(blocks) == 1 else jnp.concatenate(blocks, axis=0)
+        tile = block_best(left_rows, left_labels, joined)
+        return tile if best is None else jnp.maximum(best, tile)
+
+    best = None
     for step in range(2, steps + 1):
+        pending = chains[0][2] + chains[1][2]
         for which, chain in enumerate(chains):
-            visiting, best, pending = chain
-            visiting = send(which, visiting, step)
-            best = fold(best, pending)
-            chain[0], chain[1], chain[2] = visiting, best, [visiting]
+            chain[0] = send(which, chain[0], step)
+            chain[2] = [chain[0]]
+        best = fold_joined(best, pending)
     if steps >= 1 and block_count % 2 == 0:
-        chains[0][2] = [jnp.concatenate([chains[0][2][-1], chains[1][2][-1]], axis=0)] + chains[0][2][:-1]
-        chains[1][2] = chains[1][2][:-1]
-    best = None
-    for _, chain_best, pending in chains:
-        chain_best = fold(chain_best, pending)
-        if chain_best is not None:
-            best = chain_best if best is None else jnp.maximum(best, chain_best)
+        last = [chains[0][2][-1], chains[1][2][-1]]
+        rest = chains[0][2][:-1] + chains[1][2][:-1]
+    else:
+        last, rest = chains[0][2] + chains[1][2], []
+    best = fold_joined(best, rest)
+    best = fold_joined(best, last)
 
     best = best.reshape(group_count, rows_here)
     if group_count == 4:

time: 61.8 us -> 63.1 us (1.021)
  waiting for transfers between devices: 35.6 us -> 41.6 us
  matrix products: 6.25 us -> 3.27 us
  other arithmetic: 5.14 us -> 4.19 us
  starting transfers between devices: 14.2 us -> 13.3 us
    ppermute x8, waiting for transfers between devices: 22.9 us -> 38.4 us  [send(): return lax.ppermute(visiting, 'blk', forward if which == 0 else backward)]
    ppermute x1, waiting for transfers between devices: 10.1 us -> 0.01 us  [per_device(): across = lax.ppermute(payload, 'grp', partner_pairs(group_count, 2))]
    dot_general x8 -> x4, matrix products: 6.25 us -> 3.27 us  [block_best(): jnp.einsum('id,jd->ij', left_rows, payload[:, :D], preferred_element_type...]
    ppermute x1, starting transfers between devices: 2.7 us -> 1.52 us  [per_device(): lax.ppermute(across, 'grp', partner_pairs(group_count, 2))]
    ppermute x1, starting transfers between devices: 3.06 us -> 1.97 us  [per_device(): across = lax.ppermute(payload, 'grp', partner_pairs(group_count, 2))]
    ppermute x8, starting transfers between devices: 8.35 us -> 9.34 us  [send(): return lax.ppermute(visiting, 'blk', forward if which == 0 else backward)]
    add x8 -> x4, other arithmetic: 1.39 us -> 0.69 us  [tag_labels(): return high * 128.0 + low]
  transfers between devices with their start and end apart: 13 -> 13, of which waited for: 9 -> 7; matrix products, arithmetic and copies ran while one was open for 12% -> 5% of each run, Pallas kernels for 0% -> 0%
where the time goes in v20:
time: 63.1 us; the launch traced here: 62.9 us
  waiting for transfers between devices  41.6 us (66%)
  starting transfers between devices  13.3 us (21%)
  other arithmetic  4.19 us (7%)
  matrix products  3.27 us (5%)
    ppermute x8, waiting for transfers between devices, send(): return lax.ppermute(visiting, 'blk', forward if which == 0 else backward)  38.4 us
    ppermute x8, starting transfers between devices, send(): return lax.ppermute(visiting, 'blk', forward if which == 0 else backward)  9.34 us
    dot_general x4, matrix products, block_best(): jnp.einsum('id,jd->ij', left_rows, payload[:, :D], preferred_element_type...  3.27 us
    ppermute x1, waiting for transfers between devices, per_device(): lax.ppermute(across, 'grp', partner_pairs(group_count, 2))  2.05 us
    ppermute x1, starting transfers between devices, per_device(): across = lax.ppermute(payload, 'grp', partner_pairs(group_count, 2))  1.97 us
    ppermute x1, starting transfers between devices, per_device(): lax.ppermute(across, 'grp', partner_pairs(group_count, 2))  1.52 us
  transfers between devices with their start and end apart: 13, of which 7 were waited for; matrix products, arithmetic and copies ran while one was open for 5% of the time, Pallas kernels for 0%

profile of v20, /device:TPU:0, one launch (start us, length us, event | category | flops | bytes accessed | tf_op | source)
XLA Modules:
  0.0 62.9 jit_solution(13660076209187141801)
XLA Ops:
  0.0 0.0 copy-start.1
  0.0 0.0 copy-start
  0.0 1.3 %multiply_reduce_fusion = f32[64]{0:T(128)S(1)} fusion(bf16[64,4096]{1,0:T(8,128)(2,1)} %param.3), kind=kLoop, calls=%fused_computation.18 | loop fusion | flops 786368 | bytes 524544 | tf_op jit(solution)/shard_map/reduce_sum | solution.py:42
  1.3 1.1 %convert_element_type.112 = f32[64,4096]{1,0:T(8,128)S(1)} convert(bf16[64,4096]{1,0:T(8,128)(2,1)} %param.3) | non-fusion elementwise | flops 262144 | bytes 1572864 | tf_op jit(solution)/shard_map/convert_element_type | solution.py:41
  2.4 0.0 copy-done.1
  2.4 0.0 copy-done
  2.5 0.3 select_convert_fusion
  2.8 3.1 %collective-permute-start.3 = (bf16[64,4224]{1,0:T(8,128)(2,1)S(1)}, bf16[64,4224]{1,0:T(8,128)(2,1)S(1)}, u32[]{:S(2)}, u32[]{:S(2)}) collective-permute-start(bf16[64,4224]{1,0:T(8,128)(2,1)S(1)} %select_convert_fusion), channel_id=1, source_target_pairs={{0,2},{2,4},{4,6},{6,7},{7,5},{5,3},{3,1},{1,0},{8,10},{10,12},{12... | collective-permute-start | bytes 1622024 | tf_op jit(solution)/shard_map/ppermute | solution.py:60
  5.9 0.0 collective-permute-start.4
  5.9 2.0 %collective-permute-start.1 = (bf16[64,4224]{1,0:T(8,128)(2,1)S(1)}, bf16[64,4224]{1,0:T(8,128)(2,1)S(1)}, u32[]{:S(2)}, u32[]{:S(2)}) collective-permute-start(bf16[64,4224]{1,0:T(8,128)(2,1)S(1)} %select_convert_fusion), channel_id=1, source_target_pairs={{0,16},{8,24},{16,0},{24,8},{1,17},{9,25},{17,1},{25,9},{2,18},{10... | collective-permute-start | bytes 1622024 | tf_op jit(solution)/shard_map/ppermute | solution.py:69
  7.8 10.2 %collective-permute-done.3 = bf16[64,4224]{1,0:T(8,128)(2,1)S(1)} collective-permute-done((bf16[64,4224]{1,0:T(8,128)(2,1)S(1)}, bf16[64,4224]{1,0:T(8,128)(2,1)S(1)}, u32[]{:S(2)}, u32[]{:S(2)}) %collective-permute-start.3) | collective-permute-done | bytes 540704 | tf_op jit(solution)/shard_map/ppermute | solution.py:60
  18.0 1.8 %collective-permute-start.5 = (bf16[64,4224]{1,0:T(8,128)(2,1)S(1)}, bf16[64,4224]{1,0:T(8,128)(2,1)S(1)}, u32[]{:S(2)}, u32[]{:S(2)}) collective-permute-start(bf16[64,4224]{1,0:T(8,128)(2,1)S(1)} %collective-permute-done.3), channel_id=1, source_target_pairs={{0,2},{2,4},{4,6},{6,7},{7,5},{5,3},{3,1},{1,0},{8,10},{10,12},{12... | collective-permute-start | bytes 1622024 | tf_op jit(solution)/shard_map/ppermute | solution.py:60
  19.9 0.0 collective-permute-start
  19.9 0.0 collective-permute-done.4
  19.9 0.2 collective-permute-start.6
  20.1 0.0 collective-permute-done.1
  20.1 0.4 collective-permute-start.2
  20.5 0.2 add_reduce_fusion
  20.6 10.8 %collective-permute-done.5 = bf16[64,4224]{1,0:T(8,128)(2,1)S(1)} collective-permute-done((bf16[64,4224]{1,0:T(8,128)(2,1)S(1)}, bf16[64,4224]{1,0:T(8,128)(2,1)S(1)}, u32[]{:S(2)}, u32[]{:S(2)}) %collective-permute-start.5) | collective-permute-done | bytes 540704 | tf_op jit(solution)/shard_map/ppermute | solution.py:60
  31.5 3.0 %collective-permute-done.6 = bf16[64,4224]{1,0:T(8,128)(2,1)S(1)} collective-permute-done((bf16[64,4224]{1,0:T(8,128)(2,1)S(1)}, bf16[64,4224]{1,0:T(8,128)(2,1)S(1)}, u32[]{:S(2)}, u32[]{:S(2)}) %collective-permute-start.6) | collective-permute-done | bytes 540704 | tf_op jit(solution)/shard_map/ppermute | solution.py:60
  34.6 0.2 add_reduce_fusion.2
  34.8 0.0 collective-permute-done
  34.8 0.0 collective-permute-done.2
  34.8 0.1 pad_maximum_fusion.12
  34.9 0.2 floor_reduce_fusion
  35.1 0.3 collective-permute-start.8
  35.4 1.7 %collective-permute-start.7 = (bf16[64,4224]{1,0:T(8,128)(2,1)S(1)}, bf16[64,4224]{1,0:T(8,128)(2,1)S(1)}, u32[]{:S(2)}, u32[]{:S(2)}) collective-permute-start(bf16[64,4224]{1,0:T(8,128)(2,1)S(1)} %collective-permute-done.5), channel_id=1, source_target_pairs={{0,2},{2,4},{4,6},{6,7},{7,5},{5,3},{3,1},{1,0},{8,10},{10,12},{12... | collective-permute-start | bytes 1622024 | tf_op jit(solution)/shard_map/ppermute | solution.py:60
  37.2 0.8 %fusion.4 = f32[256]{0:T(256)S(1)} fusion(bf16[128,4224]{1,0:T(8,128)(2,1)S(1)} %constant_dynamic-update-slice_fusion, f32[256]{0:T(256)S(1)} %get-tuple-element.6, f32[256]{0:T(256)S(1)} %get-tuple-element.5, f32[128]{0:T(128)S(1)} %add_reduce_fusion.2, f32[128]{0:T(128)S(1)} %multiply_floor_fusion.3, bf16[64,4224]{1,0:T(8,128)(2,1)S(1)} %collective-permute-done.2, ...), kind=kOutput, calls=%fused_computation.11 | convolution fusion | flops 276987648 | bytes 3215360 | tf_op jit(solution)/shard_map/id,jd->ij/dot_general | solution.py:26
  38.0 0.9 %fusion.3 = f32[256]{0:T(256)S(1)} fusion(bf16[64,4224]{1,0:T(8,128)(2,1)S(1)} %collective-permute-done.4, bf16[64,4224]{1,0:T(8,128)(2,1)S(1)} %collective-permute-done.3, bf16[64,4224]{1,0:T(8,128)(2,1)S(1)} %select_convert_fusion, f32[256]{0:T(256)S(1)} %get-tuple-element.6, f32[256]{0:T(256)S(1)} %get-tuple-element.5, f32[192]{0:T(256)S(1)} %add_reduce_fusion, ...), kind=kOutput, calls=%fused_computation.10 | convolution fusion | flops 416005888 | bytes 3248640 | tf_op jit(solution)/shard_map/id,jd->ij/dot_general | solution.py:26
  38.8 10.1 %collective-permute-done.8 = bf16[64,4224]{1,0:T(8,128)(2,1)S(1)} collective-permute-done((bf16[64,4224]{1,0:T(8,128)(2,1)S(1)}, bf16[64,4224]{1,0:T(8,128)(2,1)S(1)}, u32[]{:S(2)}, u32[]{:S(2)}) %collective-permute-start.8) | collective-permute-done | bytes 540704 | tf_op jit(solution)/shard_map/ppermute | solution.py:60
  49.0 0.4 collective-permute-start.10
  49.4 0.0 collective-permute-done.7
  49.4 1.7 %collective-permute-start.9 = (bf16[32,4224]{1,0:T(8,128)(2,1)S(1)}, bf16[32,4224]{1,0:T(8,128)(2,1)S(1)}, u32[]{:S(2)}, u32[]{:S(2)}) collective-permute-start(bf16[32,4224]{1,0:T(8,128)(2,1)S(1)} %slice.108), channel_id=1, source_target_pairs={{0,2},{2,4},{4,6},{6,7},{7,5},{5,3},{3,1},{1,0},{8,10},{10,12},{12... | collective-permute-start | bytes 811016 | tf_op jit(solution)/shard_map/ppermute | solution.py:60
  51.2 0.1 constant_dynamic-update-slice_fusion.2
  51.2 0.2 add_reduce_fusion.1
  51.4 0.8 %fusion.5 = f32[256]{0:T(256)S(1)} fusion(bf16[128,4224]{1,0:T(8,128)(2,1)S(1)} %constant_dynamic-update-slice_fusion.2, f32[256]{0:T(256)S(1)} %get-tuple-element.6, f32[256]{0:T(256)S(1)} %get-tuple-element.5, f32[128]{0:T(128)S(1)} %add_reduce_fusion.1, f32[128]{0:T(128)S(1)} %multiply_floor_fusion.2, bf16[64,4224]{1,0:T(8,128)(2,1)S(1)} %collective-permute-done.2, ...), kind=kOutput, calls=%fused_computation.12 | convolution fusion | flops 276987648 | bytes 3215360 | tf_op jit(solution)/shard_map/id,jd->ij/dot_general | solution.py:26
  52.2 4.2 %collective-permute-done.9 = bf16[32,4224]{1,0:T(8,128)(2,1)S(1)} collective-permute-done((bf16[32,4224]{1,0:T(8,128)(2,1)S(1)}, bf16[32,4224]{1,0:T(8,128)(2,1)S(1)}, u32[]{:S(2)}, u32[]{:S(2)}) %collective-permute-start.9) | collective-permute-done | bytes 270368 | tf_op jit(solution)/shard_map/ppermute | solution.py:60
  56.5 0.0 collective-permute-done.10
  56.5 0.2 add_reduce_fusion.3
  56.7 0.8 %fusion.6 = f32[256]{0:T(256)S(1)} fusion(bf16[64,4224]{1,0:T(8,128)(2,1)S(1)} %constant_dynamic-update-slice_fusion.4, f32[256]{0:T(256)S(1)} %get-tuple-element.6, f32[256]{0:T(256)S(1)} %get-tuple-element.5, f32[64]{0:T(128)S(1)} %add_reduce_fusion.3, f32[64]{0:T(128)S(1)} %multiply_floor_fusion.1, bf16[64,4224]{1,0:T(8,128)(2,1)S(1)} %collective-permute-done.2, ...), kind=kOutput, calls=%fused_computation.14 | convolution fusion | flops 142688000 | bytes 2691072 | tf_op jit(solution)/shard_map/id,jd->ij/dot_general | solution.py:26
  57.5 0.1 slice_bitcast_fusion.1
  57.6 0.1 collective-permute-start.11
  57.7 1.1 %collective-permute-done.11 = f32[2,64]{1,0:T(2,128)S(1)} collective-permute-done((f32[2,64]{1,0:T(2,128)S(1)}, f32[2,64]{1,0:T(2,128)S(1)}, u32[]{:S(2)}, u32[]{:S(2)}) %collective-permute-start.11) | collective-permute-done | bytes 544 | tf_op jit(solution)/shard_map/ppermute | solution.py:112
  58.8 1.5 %collective-permute-start.12 = (f32[64]{0:T(128)S(1)}, f32[64]{0:T(128)S(1)}, u32[]{:S(2)}, u32[]{:S(2)}) collective-permute-start(f32[64]{0:T(128)S(1)} %bitcast_maximum_fusion), channel_id=1, source_target_pairs={{0,16},{8,24},{16,0},{24,8},{1,17},{9,25},{17,1},{25,9},{2,18},{10... | collective-permute-start | bytes 776 | tf_op jit(solution)/shard_map/ppermute | solution.py:115
  60.3 2.0 %collective-permute-done.12 = f32[64]{0:T(128)S(1)} collective-permute-done((f32[64]{0:T(128)S(1)}, f32[64]{0:T(128)S(1)}, u32[]{:S(2)}, u32[]{:S(2)}) %collective-permute-start.12) | collective-permute-done | bytes 288 | tf_op jit(solution)/shard_map/ppermute | solution.py:115
  62.4 0.5 fusion.12
  (18 shorter events, 0.3 us)
Async XLA Ops:
  0.0 2.4 %copy-start.1 = (s32[64]{0:T(128)S(1)}, s32[64]{0:T(128)}, u32[]{:S(2)}) copy-start(s32[64]{0:T(128)} %param.5) | copy-start | bytes 772
  0.0 2.4 %copy-start = (s32[64]{0:T(128)S(1)}, s32[64]{0:T(128)}, u32[]{:S(2)}) copy-start(s32[64]{0:T(128)} %param.4) | copy-start | bytes 772
  2.8 15.3 %collective-permute-start.3 = (bf16[64,4224]{1,0:T(8,128)(2,1)S(1)}, bf16[64,4224]{1,0:T(8,128)(2,1)S(1)}, u32[]{:S(2)}, u32[]{:S(2)}) collective-permute-start(bf16[64,4224]{1,0:T(8,128)(2,1)S(1)} %select_convert_fusion), channel_id=1, source_target_pairs={{0,2},{2,4},{4,6},{6,7},{7,5},{5,3},{3,1},{1,0},{8,10},{10,12},{12... | collective-permute-start | bytes 1622024 | tf_op jit(solution)/shard_map/ppermute | solution.py:60
  5.9 14.0 %collective-permute-start.4 = (bf16[64,4224]{1,0:T(8,128)(2,1)S(1)}, bf16[64,4224]{1,0:T(8,128)(2,1)S(1)}, u32[]{:S(2)}, u32[]{:S(2)}) collective-permute-start(bf16[64,4224]{1,0:T(8,128)(2,1)S(1)} %select_convert_fusion), channel_id=1, source_target_pairs={{2,0},{4,2},{6,4},{7,6},{5,7},{3,5},{1,3},{0,1},{10,8},{12,10},{14... | collective-permute-start | bytes 1622024 | tf_op jit(solution)/shard_map/ppermute | solution.py:60
  5.9 14.2 %collective-permute-start.1 = (bf16[64,4224]{1,0:T(8,128)(2,1)S(1)}, bf16[64,4224]{1,0:T(8,128)(2,1)S(1)}, u32[]{:S(2)}, u32[]{:S(2)}) collective-permute-start(bf16[64,4224]{1,0:T(8,128)(2,1)S(1)} %select_convert_fusion), channel_id=1, source_target_pairs={{0,16},{8,24},{16,0},{24,8},{1,17},{9,25},{17,1},{25,9},{2,18},{10... | collective-permute-start | bytes 1622024 | tf_op jit(solution)/shard_map/ppermute | solution.py:69
  18.0 13.4 %collective-permute-start.5 = (bf16[64,4224]{1,0:T(8,128)(2,1)S(1)}, bf16[64,4224]{1,0:T(8,128)(2,1)S(1)}, u32[]{:S(2)}, u32[]{:S(2)}) collective-permute-start(bf16[64,4224]{1,0:T(8,128)(2,1)S(1)} %collective-permute-done.3), channel_id=1, source_target_pairs={{0,2},{2,4},{4,6},{6,7},{7,5},{5,3},{3,1},{1,0},{8,10},{10,12},{12... | collective-permute-start | bytes 1622024 | tf_op jit(solution)/shard_map/ppermute | solution.py:60
  19.9 14.9 %collective-permute-start = (bf16[64,4224]{1,0:T(8,128)(2,1)S(1)}, bf16[64,4224]{1,0:T(8,128)(2,1)S(1)}, u32[]{:S(2)}, u32[]{:S(2)}) collective-permute-start(bf16[64,4224]{1,0:T(8,128)(2,1)S(1)} %select_convert_fusion), channel_id=1, source_target_pairs={{0,8},{8,0},{16,24},{24,16},{1,9},{9,1},{17,25},{25,17},{2,10},{10... | collective-permute-start | bytes 1622024 | tf_op jit(solution)/shard_map/ppermute | solution.py:70
  19.9 14.7 %collective-permute-start.6 = (bf16[64,4224]{1,0:T(8,128)(2,1)S(1)}, bf16[64,4224]{1,0:T(8,128)(2,1)S(1)}, u32[]{:S(2)}, u32[]{:S(2)}) collective-permute-start(bf16[64,4224]{1,0:T(8,128)(2,1)S(1)} %collective-permute-done.4), channel_id=1, source_target_pairs={{2,0},{4,2},{6,4},{7,6},{5,7},{3,5},{1,3},{0,1},{10,8},{12,10},{14... | collective-permute-start | bytes 1622024 | tf_op jit(solution)/shard_map/ppermute | solution.py:60
  20.1 14.7 %collective-permute-start.2 = (bf16[64,4224]{1,0:T(8,128)(2,1)S(1)}, bf16[64,4224]{1,0:T(8,128)(2,1)S(1)}, u32[]{:S(2)}, u32[]{:S(2)}) collective-permute-start(bf16[64,4224]{1,0:T(8,128)(2,1)S(1)} %collective-permute-done.1), channel_id=1, source_target_pairs={{0,8},{8,0},{16,24},{24,16},{1,9},{9,1},{17,25},{25,17},{2,10},{10... | collective-permute-start | bytes 1622024 | tf_op jit(solution)/shard_map/ppermute | solution.py:71
  35.1 13.9 %collective-permute-start.8 = (bf16[64,4224]{1,0:T(8,128)(2,1)S(1)}, bf16[64,4224]{1,0:T(8,128)(2,1)S(1)}, u32[]{:S(2)}, u32[]{:S(2)}) collective-permute-start(bf16[64,4224]{1,0:T(8,128)(2,1)S(1)} %collective-permute-done.6), channel_id=1, source_target_pairs={{2,0},{4,2},{6,4},{7,6},{5,7},{3,5},{1,3},{0,1},{10,8},{12,10},{14... | collective-permute-start | bytes 1622024 | tf_op jit(solution)/shard_map/ppermute | solution.py:60
  35.4 14.0 %collective-permute-start.7 = (bf16[64,4224]{1,0:T(8,128)(2,1)S(1)}, bf16[64,4224]{1,0:T(8,128)(2,1)S(1)}, u32[]{:S(2)}, u32[]{:S(2)}) collective-permute-start(bf16[64,4224]{1,0:T(8,128)(2,1)S(1)} %collective-permute-done.5), channel_id=1, source_target_pairs={{0,2},{2,4},{4,6},{6,7},{7,5},{5,3},{3,1},{1,0},{8,10},{10,12},{12... | collective-permute-start | bytes 1622024 | tf_op jit(solution)/shard_map/ppermute | solution.py:60
  49.0 7.5 %collective-permute-start.10 = (bf16[32,4224]{1,0:T(8,128)(2,1)S(1)}, bf16[32,4224]{1,0:T(8,128)(2,1)S(1)}, u32[]{:S(2)}, u32[]{:S(2)}) collective-permute-start(bf16[32,4224]{1,0:T(8,128)(2,1)S(1)} %slice.109), channel_id=1, source_target_pairs={{2,0},{4,2},{6,4},{7,6},{5,7},{3,5},{1,3},{0,1},{10,8},{12,10},{14... | collective-permute-start | bytes 811016 | tf_op jit(solution)/shard_map/ppermute | solution.py:60
  49.4 7.0 %collective-permute-start.9 = (bf16[32,4224]{1,0:T(8,128)(2,1)S(1)}, bf16[32,4224]{1,0:T(8,128)(2,1)S(1)}, u32[]{:S(2)}, u32[]{:S(2)}) collective-permute-start(bf16[32,4224]{1,0:T(8,128)(2,1)S(1)} %slice.108), channel_id=1, source_target_pairs={{0,2},{2,4},{4,6},{6,7},{7,5},{5,3},{3,1},{1,0},{8,10},{10,12},{12... | collective-permute-start | bytes 811016 | tf_op jit(solution)/shard_map/ppermute | solution.py:60
  57.6 1.2 %collective-permute-start.11 = (f32[2,64]{1,0:T(2,128)S(1)}, f32[2,64]{1,0:T(2,128)S(1)}, u32[]{:S(2)}, u32[]{:S(2)}) collective-permute-start(f32[2,64]{1,0:T(2,128)S(1)} %pad_maximum_fusion.13), channel_id=1, source_target_pairs={{0,8},{8,0},{16,24},{24,16},{1,9},{9,1},{17,25},{25,17},{2,10},{10... | collective-permute-start | bytes 1544 | tf_op jit(solution)/shard_map/ppermute | solution.py:112
  58.8 3.6 %collective-permute-start.12 = (f32[64]{0:T(128)S(1)}, f32[64]{0:T(128)S(1)}, u32[]{:S(2)}, u32[]{:S(2)}) collective-permute-start(f32[64]{0:T(128)S(1)} %bitcast_maximum_fusion), channel_id=1, source_target_pairs={{0,16},{8,24},{16,0},{24,8},{1,17},{9,25},{17,1},{25,9},{2,18},{10... | collective-permute-start | bytes 776 | tf_op jit(solution)/shard_map/ppermute | solution.py:115

commit v21 on v18

--- a/solution.py
+++ b/solution.py
@@ -51,7 +51,7 @@
     order = ring_order(block_count)
     forward = [(order[i], order[(i + 1) % block_count]) for i in range(block_count)]
     backward = [(dst, src) for src, dst in forward]
-    half = rows_here // 2
+    half = min(rows_here, (rows_here * 5 // 8) // 8 * 8)
     steps = block_count // 2
 
     def send(which, visiting, step):

time: 61.8 us -> 61.5 us (level)
  waiting for transfers between devices: 35.6 us -> 34.9 us
    ppermute x8, waiting for transfers between devices: 22.9 us -> 22.2 us  [send(): return lax.ppermute(visiting, 'blk', forward if which == 0 else backward)]
where the time goes in v21:
time: 61.5 us; the launch traced here: 61.4 us
  waiting for transfers between devices  34.9 us (57%)
  starting transfers between devices  14.7 us (24%)
  matrix products  6.25 us (10%)
  other arithmetic  5.14 us (8%)
    ppermute x8, waiting for transfers between devices, send(): return lax.ppermute(visiting, 'blk', forward if which == 0 else backward)  22.2 us
    ppermute x1, waiting for transfers between devices, per_device(): across = lax.ppermute(payload, 'grp', partner_pairs(group_count, 2))  10.1 us
    ppermute x8, starting transfers between devices, send(): return lax.ppermute(visiting, 'blk', forward if which == 0 else backward)  8.34 us
    dot_general x8, matrix products, block_best(): jnp.einsum('id,jd->ij', left_rows, payload[:, :D], preferred_element_type...  6.25 us
    ppermute x1, starting transfers between devices, per_device(): lax.ppermute(across, 'grp', partner_pairs(group_count, 2))  3.19 us
    ppermute x1, starting transfers between devices, per_device(): across = lax.ppermute(payload, 'grp', partner_pairs(group_count, 2))  3.06 us
    ppermute x1, waiting for transfers between devices, per_device(): lax.ppermute(across, 'grp', partner_pairs(group_count, 2))  1.55 us
    add x8, other arithmetic, tag_labels(): return high * 128.0 + low  1.39 us
  transfers between devices with their start and end apart: 13, of which 9 were waited for; matrix products, arithmetic and copies ran while one was open for 12% of the time, Pallas kernels for 0%

profile of v21, /device:TPU:0, one launch (start us, length us, event | category | flops | bytes accessed | tf_op | source)
XLA Modules:
  0.0 61.4 jit_solution(16802052923231313345)
XLA Ops:
  0.0 1.1 %convert_element_type.200 = f32[64,4096]{1,0:T(8,128)S(1)} convert(bf16[64,4096]{1,0:T(8,128)(2,1)} %param.3) | non-fusion elementwise | flops 262144 | bytes 1572864 | tf_op jit(solution)/shard_map/convert_element_type | solution.py:41
  1.1 1.2 %multiply_reduce_fusion = f32[64]{0:T(128)S(1)} fusion(bf16[64,4096]{1,0:T(8,128)(2,1)} %param.3), kind=kLoop, calls=%fused_computation.20 | loop fusion | flops 786368 | bytes 524544 | tf_op jit(solution)/shard_map/reduce_sum | solution.py:42
  2.4 0.3 select_convert_fusion
  2.7 3.1 %collective-permute-start.1 = (bf16[64,4224]{1,0:T(8,128)(2,1)S(1)}, bf16[64,4224]{1,0:T(8,128)(2,1)S(1)}, u32[]{:S(2)}, u32[]{:S(2)}) collective-permute-start(bf16[64,4224]{1,0:T(8,128)(2,1)S(1)} %select_convert_fusion), channel_id=1, source_target_pairs={{0,16},{8,24},{16,0},{24,8},{1,17},{9,25},{17,1},{25,9},{2,18},{10... | collective-permute-start | bytes 1622024 | tf_op jit(solution)/shard_map/ppermute | solution.py:69
  5.8 1.6 %collective-permute-start.3 = (bf16[64,4224]{1,0:T(8,128)(2,1)S(1)}, bf16[64,4224]{1,0:T(8,128)(2,1)S(1)}, u32[]{:S(2)}, u32[]{:S(2)}) collective-permute-start(bf16[64,4224]{1,0:T(8,128)(2,1)S(1)} %select_convert_fusion), channel_id=1, source_target_pairs={{0,2},{2,4},{4,6},{6,7},{7,5},{5,3},{3,1},{1,0},{8,10},{10,12},{12... | collective-permute-start | bytes 1622024 | tf_op jit(solution)/shard_map/ppermute | solution.py:60
  7.4 0.4 collective-permute-start.7
  7.8 0.0 collective-permute-start
  7.8 0.2 add_reduce_fusion.7
  8.0 10.1 %collective-permute-done.1 = bf16[64,4224]{1,0:T(8,128)(2,1)S(1)} collective-permute-done((bf16[64,4224]{1,0:T(8,128)(2,1)S(1)}, bf16[64,4224]{1,0:T(8,128)(2,1)S(1)}, u32[]{:S(2)}, u32[]{:S(2)}) %collective-permute-start.1) | collective-permute-done | bytes 540704 | tf_op jit(solution)/shard_map/ppermute | solution.py:69
  18.1 0.0 collective-permute-start.2
  18.1 1.5 %collective-permute-done.3 = bf16[64,4224]{1,0:T(8,128)(2,1)S(1)} collective-permute-done((bf16[64,4224]{1,0:T(8,128)(2,1)S(1)}, bf16[64,4224]{1,0:T(8,128)(2,1)S(1)}, u32[]{:S(2)}, u32[]{:S(2)}) %collective-permute-start.3) | collective-permute-done | bytes 540704 | tf_op jit(solution)/shard_map/ppermute | solution.py:60
  19.5 1.6 %collective-permute-start.4 = (bf16[64,4224]{1,0:T(8,128)(2,1)S(1)}, bf16[64,4224]{1,0:T(8,128)(2,1)S(1)}, u32[]{:S(2)}, u32[]{:S(2)}) collective-permute-start(bf16[64,4224]{1,0:T(8,128)(2,1)S(1)} %collective-permute-done.3), channel_id=1, source_target_pairs={{0,2},{2,4},{4,6},{6,7},{7,5},{5,3},{3,1},{1,0},{8,10},{10,12},{12... | collective-permute-start | bytes 1622024 | tf_op jit(solution)/shard_map/ppermute | solution.py:60
  21.1 0.2 add_reduce_fusion.6
  21.3 0.0 collective-permute-done.7
  21.3 0.5 collective-permute-start.8
  21.8 0.2 add_reduce_fusion.2
  22.0 0.0 collective-permute-done.2
  22.0 0.1 pad_maximum_fusion.4
  22.1 0.2 floor_reduce_fusion
  22.3 0.2 pad_maximum_fusion
  22.5 10.2 %collective-permute-done.4 = bf16[64,4224]{1,0:T(8,128)(2,1)S(1)} collective-permute-done((bf16[64,4224]{1,0:T(8,128)(2,1)S(1)}, bf16[64,4224]{1,0:T(8,128)(2,1)S(1)}, u32[]{:S(2)}, u32[]{:S(2)}) %collective-permute-start.4) | collective-permute-done | bytes 540704 | tf_op jit(solution)/shard_map/ppermute | solution.py:60
  32.8 1.8 %collective-permute-start.5 = (bf16[64,4224]{1,0:T(8,128)(2,1)S(1)}, bf16[64,4224]{1,0:T(8,128)(2,1)S(1)}, u32[]{:S(2)}, u32[]{:S(2)}) collective-permute-start(bf16[64,4224]{1,0:T(8,128)(2,1)S(1)} %collective-permute-done.4), channel_id=1, source_target_pairs={{0,2},{2,4},{4,6},{6,7},{7,5},{5,3},{3,1},{1,0},{8,10},{10,12},{12... | collective-permute-start | bytes 1622024 | tf_op jit(solution)/shard_map/ppermute | solution.py:60
  34.6 0.2 add_reduce_fusion.5
  34.8 0.8 %fusion = f32[256]{0:T(256)S(1)} fusion(bf16[256,4096]{1,0:T(8,128)(2,1)S(1)} %pad_maximum_fusion, bf16[64,4224]{1,0:T(8,128)(2,1)S(1)} %select_convert_fusion, f32[256]{0:T(256)S(1)} %get-tuple-element.6, f32[256]{0:T(256)S(1)} %get-tuple-element.5, f32[64]{0:T(128)S(1)} %add_reduce_fusion.7, f32[64]{0:T(128)S(1)} %multiply_floor_fusion.7), kind=kOutput, calls=%fused_computation.11 | convolution fusion | flops 134299392 | bytes 2625536 | tf_op jit(solution)/shard_map/id,jd->ij/dot_general | solution.py:26
  35.6 0.3 collective-permute-start.9
  35.8 0.2 add_reduce_fusion.1
  36.0 0.8 %fusion.1 = f32[256]{0:T(256)S(1)} fusion(bf16[256,4096]{1,0:T(8,128)(2,1)S(1)} %pad_maximum_fusion, bf16[64,4224]{1,0:T(8,128)(2,1)S(1)} %collective-permute-done.3, f32[256]{0:T(256)S(1)} %get-tuple-element.6, f32[256]{0:T(256)S(1)} %get-tuple-element.5, f32[64]{0:T(128)S(1)} %add_reduce_fusion.6, f32[64]{0:T(128)S(1)} %multiply_floor_fusion.6), kind=kOutput, calls=%fused_computation.12 | convolution fusion | flops 134299392 | bytes 2625536 | tf_op jit(solution)/shard_map/id,jd->ij/dot_general | solution.py:26
  36.8 0.8 %fusion.2 = f32[256]{0:T(256)S(1)} fusion(bf16[256,4096]{1,0:T(8,128)(2,1)S(1)} %pad_maximum_fusion, bf16[64,4224]{1,0:T(8,128)(2,1)S(1)} %collective-permute-done.4, f32[256]{0:T(256)S(1)} %get-tuple-element.6, f32[256]{0:T(256)S(1)} %get-tuple-element.5, f32[64]{0:T(128)S(1)} %add_reduce_fusion.5, f32[64]{0:T(128)S(1)} %multiply_floor_fusion.5), kind=kOutput, calls=%fused_computation.13 | convolution fusion | flops 134299392 | bytes 2625536 | tf_op jit(solution)/shard_map/id,jd->ij/dot_general | solution.py:26
  37.6 0.8 %fusion.6 = f32[256]{0:T(256)S(1)} fusion(bf16[256,4096]{1,0:T(8,128)(2,1)S(1)} %pad_maximum_fusion, bf16[64,4224]{1,0:T(8,128)(2,1)S(1)} %collective-permute-done.8, f32[256]{0:T(256)S(1)} %get-tuple-element.6, f32[256]{0:T(256)S(1)} %get-tuple-element.5, f32[64]{0:T(128)S(1)} %add_reduce_fusion.1, f32[64]{0:T(128)S(1)} %multiply_floor_fusion.1), kind=kOutput, calls=%fused_computation.17 | convolution fusion | flops 134299392 | bytes 2625536 | tf_op jit(solution)/shard_map/id,jd->ij/dot_general | solution.py:26
  38.4 0.8 %fusion.5 = f32[256]{0:T(256)S(1)} fusion(bf16[256,4096]{1,0:T(8,128)(2,1)S(1)} %pad_maximum_fusion, bf16[64,4224]{1,0:T(8,128)(2,1)S(1)} %collective-permute-done.7, f32[256]{0:T(256)S(1)} %get-tuple-element.6, f32[256]{0:T(256)S(1)} %get-tuple-element.5, f32[64]{0:T(128)S(1)} %add_reduce_fusion.2, f32[64]{0:T(128)S(1)} %multiply_floor_fusion.2), kind=kOutput, calls=%fused_computation.16 | convolution fusion | flops 134299392 | bytes 2625536 | tf_op jit(solution)/shard_map/id,jd->ij/dot_general | solution.py:26
  39.2 6.2 %collective-permute-done.5 = bf16[64,4224]{1,0:T(8,128)(2,1)S(1)} collective-permute-done((bf16[64,4224]{1,0:T(8,128)(2,1)S(1)}, bf16[64,4224]{1,0:T(8,128)(2,1)S(1)}, u32[]{:S(2)}, u32[]{:S(2)}) %collective-permute-start.5) | collective-permute-done | bytes 540704 | tf_op jit(solution)/shard_map/ppermute | solution.py:60
  45.4 1.9 %collective-permute-start.6 = (bf16[40,4224]{1,0:T(8,128)(2,1)S(1)}, bf16[40,4224]{1,0:T(8,128)(2,1)S(1)}, u32[]{:S(2)}, u32[]{:S(2)}) collective-permute-start(bf16[40,4224]{1,0:T(8,128)(2,1)S(1)} %slice.162), channel_id=1, source_target_pairs={{0,2},{2,4},{4,6},{6,7},{7,5},{5,3},{3,1},{1,0},{8,10},{10,12},{12... | collective-permute-start | bytes 1013768 | tf_op jit(solution)/shard_map/ppermute | solution.py:60
  47.2 0.2 add_reduce_fusion.4
  47.4 0.5 collective-permute-done.9
  48.0 0.3 collective-permute-start.10
  48.3 0.2 add_reduce_fusion
  48.5 0.8 %fusion.3 = f32[256]{0:T(256)S(1)} fusion(bf16[256,4096]{1,0:T(8,128)(2,1)S(1)} %pad_maximum_fusion, bf16[64,4224]{1,0:T(8,128)(2,1)S(1)} %collective-permute-done.5, f32[256]{0:T(256)S(1)} %get-tuple-element.6, f32[256]{0:T(256)S(1)} %get-tuple-element.5, f32[64]{0:T(128)S(1)} %add_reduce_fusion.4, f32[64]{0:T(128)S(1)} %multiply_floor_fusion.4), kind=kOutput, calls=%fused_computation.14 | convolution fusion | flops 134299392 | bytes 2625536 | tf_op jit(solution)/shard_map/id,jd->ij/dot_general | solution.py:26
  49.3 0.8 %fusion.7 = f32[256]{0:T(256)S(1)} fusion(bf16[256,4096]{1,0:T(8,128)(2,1)S(1)} %pad_maximum_fusion, bf16[64,4224]{1,0:T(8,128)(2,1)S(1)} %collective-permute-done.9, f32[256]{0:T(256)S(1)} %get-tuple-element.6, f32[256]{0:T(256)S(1)} %get-tuple-element.5, f32[64]{0:T(128)S(1)} %add_reduce_fusion, f32[64]{0:T(128)S(1)} %multiply_floor_fusion), kind=kOutput, calls=%fused_computation.18 | convolution fusion | flops 134299392 | bytes 2625536 | tf_op jit(solution)/shard_map/id,jd->ij/dot_general | solution.py:26
  50.0 2.8 %collective-permute-done.6 = bf16[40,4224]{1,0:T(8,128)(2,1)S(1)} collective-permute-done((bf16[40,4224]{1,0:T(8,128)(2,1)S(1)}, bf16[40,4224]{1,0:T(8,128)(2,1)S(1)}, u32[]{:S(2)}, u32[]{:S(2)}) %collective-permute-start.6) | collective-permute-done | bytes 337952 | tf_op jit(solution)/shard_map/ppermute | solution.py:60
  52.8 0.9 %collective-permute-done.10 = bf16[24,4224]{1,0:T(8,128)(2,1)S(1)} collective-permute-done((bf16[24,4224]{1,0:T(8,128)(2,1)S(1)}, bf16[24,4224]{1,0:T(8,128)(2,1)S(1)}, u32[]{:S(2)}, u32[]{:S(2)}) %collective-permute-start.10) | collective-permute-done | bytes 202784 | tf_op jit(solution)/shard_map/ppermute | solution.py:60
  53.8 0.2 add_reduce_fusion.3
  54.0 0.8 %fusion.4 = f32[256]{0:T(256)S(1)} fusion(bf16[256,4096]{1,0:T(8,128)(2,1)S(1)} %pad_maximum_fusion, bf16[64,4224]{1,0:T(8,128)(2,1)S(1)} %constant_dynamic-update-slice_fusion, f32[256]{0:T(256)S(1)} %get-tuple-element.6, f32[256]{0:T(256)S(1)} %get-tuple-element.5, f32[64]{0:T(128)S(1)} %add_reduce_fusion.3, f32[64]{0:T(128)S(1)} %multiply_floor_fusion.3), kind=kOutput, calls=%fused_computation.15 | convolution fusion | flops 134299392 | bytes 2625536 | tf_op jit(solution)/shard_map/id,jd->ij/dot_general | solution.py:26
  54.8 0.1 slice_bitcast_fusion.1
  54.9 0.1 collective-permute-start.11
  55.0 1.1 %collective-permute-done.11 = f32[2,64]{1,0:T(2,128)S(1)} collective-permute-done((f32[2,64]{1,0:T(2,128)S(1)}, f32[2,64]{1,0:T(2,128)S(1)}, u32[]{:S(2)}, u32[]{:S(2)}) %collective-permute-start.11) | collective-permute-done | bytes 544 | tf_op jit(solution)/shard_map/ppermute | solution.py:105
  56.1 3.2 %collective-permute-start.12 = (f32[64]{0:T(128)S(1)}, f32[64]{0:T(128)S(1)}, u32[]{:S(2)}, u32[]{:S(2)}) collective-permute-start(f32[64]{0:T(128)S(1)} %bitcast_maximum_fusion), channel_id=1, source_target_pairs={{0,16},{8,24},{16,0},{24,8},{1,17},{9,25},{17,1},{25,9},{2,18},{10... | collective-permute-start | bytes 776 | tf_op jit(solution)/shard_map/ppermute | solution.py:108
  59.3 1.5 %collective-permute-done.12 = f32[64]{0:T(128)S(1)} collective-permute-done((f32[64]{0:T(128)S(1)}, f32[64]{0:T(128)S(1)}, u32[]{:S(2)}, u32[]{:S(2)}) %collective-permute-start.12) | collective-permute-done | bytes 288 | tf_op jit(solution)/shard_map/ppermute | solution.py:108
  60.8 0.5 fusion.18
  (25 shorter events, 0.2 us)
Async XLA Ops:
  0.0 2.4 %copy-start = (s32[64]{0:T(128)S(1)}, s32[64]{0:T(128)}, u32[]{:S(2)}) copy-start(s32[64]{0:T(128)} %param.4) | copy-start | bytes 772
  0.0 2.4 %copy-start.1 = (s32[64]{0:T(128)S(1)}, s32[64]{0:T(128)}, u32[]{:S(2)}) copy-start(s32[64]{0:T(128)} %param.5) | copy-start | bytes 772
  2.7 15.3 %collective-permute-start.1 = (bf16[64,4224]{1,0:T(8,128)(2,1)S(1)}, bf16[64,4224]{1,0:T(8,128)(2,1)S(1)}, u32[]{:S(2)}, u32[]{:S(2)}) collective-permute-start(bf16[64,4224]{1,0:T(8,128)(2,1)S(1)} %select_convert_fusion), channel_id=1, source_target_pairs={{0,16},{8,24},{16,0},{24,8},{1,17},{9,25},{17,1},{25,9},{2,18},{10... | collective-permute-start | bytes 1622024 | tf_op jit(solution)/shard_map/ppermute | solution.py:69
  5.8 13.7 %collective-permute-start.3 = (bf16[64,4224]{1,0:T(8,128)(2,1)S(1)}, bf16[64,4224]{1,0:T(8,128)(2,1)S(1)}, u32[]{:S(2)}, u32[]{:S(2)}) collective-permute-start(bf16[64,4224]{1,0:T(8,128)(2,1)S(1)} %select_convert_fusion), channel_id=1, source_target_pairs={{0,2},{2,4},{4,6},{6,7},{7,5},{5,3},{3,1},{1,0},{8,10},{10,12},{12... | collective-permute-start | bytes 1622024 | tf_op jit(solution)/shard_map/ppermute | solution.py:60
  7.4 13.9 %collective-permute-start.7 = (bf16[64,4224]{1,0:T(8,128)(2,1)S(1)}, bf16[64,4224]{1,0:T(8,128)(2,1)S(1)}, u32[]{:S(2)}, u32[]{:S(2)}) collective-permute-start(bf16[64,4224]{1,0:T(8,128)(2,1)S(1)} %select_convert_fusion), channel_id=1, source_target_pairs={{2,0},{4,2},{6,4},{7,6},{5,7},{3,5},{1,3},{0,1},{10,8},{12,10},{14... | collective-permute-start | bytes 1622024 | tf_op jit(solution)/shard_map/ppermute | solution.py:60
  7.8 14.2 %collective-permute-start = (bf16[64,4224]{1,0:T(8,128)(2,1)S(1)}, bf16[64,4224]{1,0:T(8,128)(2,1)S(1)}, u32[]{:S(2)}, u32[]{:S(2)}) collective-permute-start(bf16[64,4224]{1,0:T(8,128)(2,1)S(1)} %select_convert_fusion), channel_id=1, source_target_pairs={{0,8},{8,0},{16,24},{24,16},{1,9},{9,1},{17,25},{25,17},{2,10},{10... | collective-permute-start | bytes 1622024 | tf_op jit(solution)/shard_map/ppermute | solution.py:70
  18.1 3.9 %collective-permute-start.2 = (bf16[64,4224]{1,0:T(8,128)(2,1)S(1)}, bf16[64,4224]{1,0:T(8,128)(2,1)S(1)}, u32[]{:S(2)}, u32[]{:S(2)}) collective-permute-start(bf16[64,4224]{1,0:T(8,128)(2,1)S(1)} %collective-permute-done.1), channel_id=1, source_target_pairs={{0,8},{8,0},{16,24},{24,16},{1,9},{9,1},{17,25},{25,17},{2,10},{10... | collective-permute-start | bytes 1622024 | tf_op jit(solution)/shard_map/ppermute | solution.py:71
  19.5 13.2 %collective-permute-start.4 = (bf16[64,4224]{1,0:T(8,128)(2,1)S(1)}, bf16[64,4224]{1,0:T(8,128)(2,1)S(1)}, u32[]{:S(2)}, u32[]{:S(2)}) collective-permute-start(bf16[64,4224]{1,0:T(8,128)(2,1)S(1)} %collective-permute-done.3), channel_id=1, source_target_pairs={{0,2},{2,4},{4,6},{6,7},{7,5},{5,3},{3,1},{1,0},{8,10},{10,12},{12... | collective-permute-start | bytes 1622024 | tf_op jit(solution)/shard_map/ppermute | solution.py:60
  21.3 14.2 %collective-permute-start.8 = (bf16[64,4224]{1,0:T(8,128)(2,1)S(1)}, bf16[64,4224]{1,0:T(8,128)(2,1)S(1)}, u32[]{:S(2)}, u32[]{:S(2)}) collective-permute-start(bf16[64,4224]{1,0:T(8,128)(2,1)S(1)} %collective-permute-done.7), channel_id=1, source_target_pairs={{2,0},{4,2},{6,4},{7,6},{5,7},{3,5},{1,3},{0,1},{10,8},{12,10},{14... | collective-permute-start | bytes 1622024 | tf_op jit(solution)/shard_map/ppermute | solution.py:60
  32.8 12.6 %collective-permute-start.5 = (bf16[64,4224]{1,0:T(8,128)(2,1)S(1)}, bf16[64,4224]{1,0:T(8,128)(2,1)S(1)}, u32[]{:S(2)}, u32[]{:S(2)}) collective-permute-start(bf16[64,4224]{1,0:T(8,128)(2,1)S(1)} %collective-permute-done.4), channel_id=1, source_target_pairs={{0,2},{2,4},{4,6},{6,7},{7,5},{5,3},{3,1},{1,0},{8,10},{10,12},{12... | collective-permute-start | bytes 1622024 | tf_op jit(solution)/shard_map/ppermute | solution.py:60
  35.6 12.4 %collective-permute-start.9 = (bf16[64,4224]{1,0:T(8,128)(2,1)S(1)}, bf16[64,4224]{1,0:T(8,128)(2,1)S(1)}, u32[]{:S(2)}, u32[]{:S(2)}) collective-permute-start(bf16[64,4224]{1,0:T(8,128)(2,1)S(1)} %collective-permute-done.8), channel_id=1, source_target_pairs={{2,0},{4,2},{6,4},{7,6},{5,7},{3,5},{1,3},{0,1},{10,8},{12,10},{14... | collective-permute-start | bytes 1622024 | tf_op jit(solution)/shard_map/ppermute | solution.py:60
  45.4 7.4 %collective-permute-start.6 = (bf16[40,4224]{1,0:T(8,128)(2,1)S(1)}, bf16[40,4224]{1,0:T(8,128)(2,1)S(1)}, u32[]{:S(2)}, u32[]{:S(2)}) collective-permute-start(bf16[40,4224]{1,0:T(8,128)(2,1)S(1)} %slice.162), channel_id=1, source_target_pairs={{0,2},{2,4},{4,6},{6,7},{7,5},{5,3},{3,1},{1,0},{8,10},{10,12},{12... | collective-permute-start | bytes 1013768 | tf_op jit(solution)/shard_map/ppermute | solution.py:60
  48.0 5.8 %collective-permute-start.10 = (bf16[24,4224]{1,0:T(8,128)(2,1)S(1)}, bf16[24,4224]{1,0:T(8,128)(2,1)S(1)}, u32[]{:S(2)}, u32[]{:S(2)}) collective-permute-start(bf16[24,4224]{1,0:T(8,128)(2,1)S(1)} %slice.163), channel_id=1, source_target_pairs={{2,0},{4,2},{6,4},{7,6},{5,7},{3,5},{1,3},{0,1},{10,8},{12,10},{14... | collective-permute-start | bytes 608264 | tf_op jit(solution)/shard_map/ppermute | solution.py:60
  54.9 1.2 %collective-permute-start.11 = (f32[2,64]{1,0:T(2,128)S(1)}, f32[2,64]{1,0:T(2,128)S(1)}, u32[]{:S(2)}, u32[]{:S(2)}) collective-permute-start(f32[2,64]{1,0:T(2,128)S(1)} %pad_maximum_fusion.5), channel_id=1, source_target_pairs={{0,8},{8,0},{16,24},{24,16},{1,9},{9,1},{17,25},{25,17},{2,10},{10... | collective-permute-start | bytes 1544 | tf_op jit(solution)/shard_map/ppermute | solution.py:105
  56.1 4.7 %collective-permute-start.12 = (f32[64]{0:T(128)S(1)}, f32[64]{0:T(128)S(1)}, u32[]{:S(2)}, u32[]{:S(2)}) collective-permute-start(f32[64]{0:T(128)S(1)} %bitcast_maximum_fusion), channel_id=1, source_target_pairs={{0,16},{8,24},{16,0},{24,8},{1,17},{9,25},{17,1},{25,9},{2,18},{10... | collective-permute-start | bytes 776 | tf_op jit(solution)/shard_map/ppermute | solution.py:108

commit v22 on v21

--- a/solution.py
+++ b/solution.py
@@ -38,13 +38,12 @@
     group_count = lax.axis_size("grp")
     block_count = lax.axis_size("blk")
     rows_here = embeddings.shape[0]
-    widened = embeddings.astype(jnp.float32)
-    square_sum = jnp.sum(widened * widened, axis=1, keepdims=True)
+    padded = jnp.pad(embeddings, ((0, 0), (0, TAG_WIDTH))).astype(jnp.float32)
+    square_sum = jnp.sum(padded * padded, axis=1, keepdims=True)
     scale = lax.rsqrt(square_sum / D + 1e-06)
     high = (cluster_ids * 64 + row_index // 128).astype(jnp.float32)[:, None]
     low = (row_index % 128).astype(jnp.float32)[:, None]
     column = jnp.arange(D + TAG_WIDTH)[None, :]
-    padded = jnp.pad(widened, ((0, 0), (0, TAG_WIDTH)))
     tags = jnp.where(column == D, high, jnp.where(column == D + 1, low, 0.0))
     payload = jnp.where(column < D, padded * scale / math.sqrt(D), tags).astype(jnp.bfloat16)
 

time: 61.5 us -> 62.2 us (1.011)
  other arithmetic: 5.14 us -> 5.77 us
    convert_element_type x1 -> x0, other arithmetic: 1.12 us -> none  [per_device(): widened = embeddings.astype(jnp.float32)]
    convert_element_type x1, other arithmetic: 0.29 us -> 1.36 us  [per_device(): jnp.where(column < D, padded * scale / math.sqrt(D), tags)]
    convert_element_type x1, other arithmetic: 0.01 us -> 0.69 us  [per_device(): high = (cluster_ids * 64 + row_index // 128).astype(jnp.float32)[:, None]]
where the time goes in v22:
time: 62.2 us; the launch traced here: 62 us
  waiting for transfers between devices  34.9 us (56%)
  starting transfers between devices  14.7 us (24%)
  matrix products  6.25 us (10%)
  other arithmetic  5.77 us (9%)
    ppermute x8, waiting for transfers between devices, send(): return lax.ppermute(visiting, 'blk', forward if which == 0 else backward)  22.2 us
    ppermute x1, waiting for transfers between devices, per_device(): across = lax.ppermute(payload, 'grp', partner_pairs(group_count, 2))  10.1 us
    ppermute x8, starting transfers between devices, send(): return lax.ppermute(visiting, 'blk', forward if which == 0 else backward)  8.34 us
    dot_general x8, matrix products, block_best(): jnp.einsum('id,jd->ij', left_rows, payload[:, :D], preferred_element_type...  6.25 us
    ppermute x1, starting transfers between devices, per_device(): lax.ppermute(across, 'grp', partner_pairs(group_count, 2))  3.19 us
    ppermute x1, starting transfers between devices, per_device(): across = lax.ppermute(payload, 'grp', partner_pairs(group_count, 2))  3.07 us
    ppermute x1, waiting for transfers between devices, per_device(): lax.ppermute(across, 'grp', partner_pairs(group_count, 2))  1.55 us
    add x8, other arithmetic, tag_labels(): return high * 128.0 + low  1.39 us
  transfers between devices with their start and end apart: 13, of which 9 were waited for; matrix products, arithmetic and copies ran while one was open for 12% of the time, Pallas kernels for 0%

profile of v22, /device:TPU:0, one launch (start us, length us, event | category | flops | bytes accessed | tf_op | source)
XLA Modules:
  0.0 62.0 jit_solution(6240938251902055798)
XLA Ops:
  0.0 1.2 %fusion.8 = f32[64]{0:T(128)S(1)} fusion(bf16[64,4096]{1,0:T(8,128)(2,1)} %param.3), kind=kLoop, calls=%fused_computation.21 | loop fusion | flops 810944 | bytes 524544 | tf_op jit(solution)/shard_map/reduce_sum | solution.py:42
  1.3 0.7 %add_convert_fusion = (bf16[64]{0:T(256)(128)(2,1)S(1)}, bf16[64]{0:T(256)(128)(2,1)S(1)}) fusion(s32[64]{0:T(128)} %param.4, s32[64]{0:T(128)} %param.5), kind=kLoop, calls=%fused_computation.72 | loop fusion | flops 1472 | bytes 768 | tf_op jit(solution)/shard_map/convert_element_type | solution.py:44
  2.0 1.4 %fusion.11 = bf16[64,4224]{1,0:T(8,128)(2,1)S(1)} fusion(bf16[64]{0:T(256)(128)(2,1)S(1)} %get-tuple-element.12, bf16[64]{0:T(256)(128)(2,1)S(1)} %get-tuple-element.11, f32[64]{0:T(128)S(1)} %add_rsqrt_fusion, pred[4224]{0:T(1024)(128)(4,1)S(1)} %get-tuple-element.13, pred[4224]{0:T(1024)(128)(4,1)S(1)} %get-tuple-element.14, ...), kind=kLoop, calls=%fused_computation.24 | loop fusion | flops 1622016 | bytes 1078144 | tf_op jit(solution)/shard_map/convert_element_type | solution.py:48
  3.3 3.1 %collective-permute-start.1 = (bf16[64,4224]{1,0:T(8,128)(2,1)S(1)}, bf16[64,4224]{1,0:T(8,128)(2,1)S(1)}, u32[]{:S(2)}, u32[]{:S(2)}) collective-permute-start(bf16[64,4224]{1,0:T(8,128)(2,1)S(1)} %fusion.11), channel_id=1, source_target_pairs={{0,16},{8,24},{16,0},{24,8},{1,17},{9,25},{17,1},{25,9},{2,18},{10... | collective-permute-start | bytes 1622024 | tf_op jit(solution)/shard_map/ppermute | solution.py:68
  6.4 1.6 %collective-permute-start.3 = (bf16[64,4224]{1,0:T(8,128)(2,1)S(1)}, bf16[64,4224]{1,0:T(8,128)(2,1)S(1)}, u32[]{:S(2)}, u32[]{:S(2)}) collective-permute-start(bf16[64,4224]{1,0:T(8,128)(2,1)S(1)} %fusion.11), channel_id=1, source_target_pairs={{0,2},{2,4},{4,6},{6,7},{7,5},{5,3},{3,1},{1,0},{8,10},{10,12},{12... | collective-permute-start | bytes 1622024 | tf_op jit(solution)/shard_map/ppermute | solution.py:59
  8.0 0.4 collective-permute-start.7
  8.4 0.0 collective-permute-start
  8.4 0.2 add_reduce_fusion.7
  8.6 10.1 %collective-permute-done.1 = bf16[64,4224]{1,0:T(8,128)(2,1)S(1)} collective-permute-done((bf16[64,4224]{1,0:T(8,128)(2,1)S(1)}, bf16[64,4224]{1,0:T(8,128)(2,1)S(1)}, u32[]{:S(2)}, u32[]{:S(2)}) %collective-permute-start.1) | collective-permute-done | bytes 540704 | tf_op jit(solution)/shard_map/ppermute | solution.py:68
  18.7 0.0 collective-permute-start.2
  18.7 1.5 %collective-permute-done.3 = bf16[64,4224]{1,0:T(8,128)(2,1)S(1)} collective-permute-done((bf16[64,4224]{1,0:T(8,128)(2,1)S(1)}, bf16[64,4224]{1,0:T(8,128)(2,1)S(1)}, u32[]{:S(2)}, u32[]{:S(2)}) %collective-permute-start.3) | collective-permute-done | bytes 540704 | tf_op jit(solution)/shard_map/ppermute | solution.py:59
  20.1 1.6 %collective-permute-start.4 = (bf16[64,4224]{1,0:T(8,128)(2,1)S(1)}, bf16[64,4224]{1,0:T(8,128)(2,1)S(1)}, u32[]{:S(2)}, u32[]{:S(2)}) collective-permute-start(bf16[64,4224]{1,0:T(8,128)(2,1)S(1)} %collective-permute-done.3), channel_id=1, source_target_pairs={{0,2},{2,4},{4,6},{6,7},{7,5},{5,3},{3,1},{1,0},{8,10},{10,12},{12... | collective-permute-start | bytes 1622024 | tf_op jit(solution)/shard_map/ppermute | solution.py:59
  21.7 0.2 add_reduce_fusion.6
  21.9 0.0 collective-permute-done.7
  21.9 0.5 collective-permute-start.8
  22.4 0.2 add_reduce_fusion.2
  22.6 0.0 collective-permute-done.2
  22.6 0.1 pad_maximum_fusion.4
  22.7 0.2 floor_reduce_fusion
  22.9 0.2 pad_maximum_fusion
  23.1 10.2 %collective-permute-done.4 = bf16[64,4224]{1,0:T(8,128)(2,1)S(1)} collective-permute-done((bf16[64,4224]{1,0:T(8,128)(2,1)S(1)}, bf16[64,4224]{1,0:T(8,128)(2,1)S(1)}, u32[]{:S(2)}, u32[]{:S(2)}) %collective-permute-start.4) | collective-permute-done | bytes 540704 | tf_op jit(solution)/shard_map/ppermute | solution.py:59
  33.4 1.8 %collective-permute-start.5 = (bf16[64,4224]{1,0:T(8,128)(2,1)S(1)}, bf16[64,4224]{1,0:T(8,128)(2,1)S(1)}, u32[]{:S(2)}, u32[]{:S(2)}) collective-permute-start(bf16[64,4224]{1,0:T(8,128)(2,1)S(1)} %collective-permute-done.4), channel_id=1, source_target_pairs={{0,2},{2,4},{4,6},{6,7},{7,5},{5,3},{3,1},{1,0},{8,10},{10,12},{12... | collective-permute-start | bytes 1622024 | tf_op jit(solution)/shard_map/ppermute | solution.py:59
  35.2 0.2 add_reduce_fusion.5
  35.4 0.8 %fusion = f32[256]{0:T(256)S(1)} fusion(bf16[256,4096]{1,0:T(8,128)(2,1)S(1)} %pad_maximum_fusion, bf16[64,4224]{1,0:T(8,128)(2,1)S(1)} %fusion.11, f32[256]{0:T(256)S(1)} %get-tuple-element.6, f32[256]{0:T(256)S(1)} %get-tuple-element.5, f32[64]{0:T(128)S(1)} %add_reduce_fusion.7, f32[64]{0:T(128)S(1)} %multiply_floor_fusion.7), kind=kOutput, calls=%fused_computation.13 | convolution fusion | flops 134299392 | bytes 2625536 | tf_op jit(solution)/shard_map/id,jd->ij/dot_general | solution.py:26
  36.2 0.3 collective-permute-start.9
  36.4 0.2 add_reduce_fusion.1
  36.6 0.8 %fusion.1 = f32[256]{0:T(256)S(1)} fusion(bf16[256,4096]{1,0:T(8,128)(2,1)S(1)} %pad_maximum_fusion, bf16[64,4224]{1,0:T(8,128)(2,1)S(1)} %collective-permute-done.3, f32[256]{0:T(256)S(1)} %get-tuple-element.6, f32[256]{0:T(256)S(1)} %get-tuple-element.5, f32[64]{0:T(128)S(1)} %add_reduce_fusion.6, f32[64]{0:T(128)S(1)} %multiply_floor_fusion.6), kind=kOutput, calls=%fused_computation.14 | convolution fusion | flops 134299392 | bytes 2625536 | tf_op jit(solution)/shard_map/id,jd->ij/dot_general | solution.py:26
  37.4 0.8 %fusion.2 = f32[256]{0:T(256)S(1)} fusion(bf16[256,4096]{1,0:T(8,128)(2,1)S(1)} %pad_maximum_fusion, bf16[64,4224]{1,0:T(8,128)(2,1)S(1)} %collective-permute-done.4, f32[256]{0:T(256)S(1)} %get-tuple-element.6, f32[256]{0:T(256)S(1)} %get-tuple-element.5, f32[64]{0:T(128)S(1)} %add_reduce_fusion.5, f32[64]{0:T(128)S(1)} %multiply_floor_fusion.5), kind=kOutput, calls=%fused_computation.15 | convolution fusion | flops 134299392 | bytes 2625536 | tf_op jit(solution)/shard_map/id,jd->ij/dot_general | solution.py:26
  38.2 0.8 %fusion.6 = f32[256]{0:T(256)S(1)} fusion(bf16[256,4096]{1,0:T(8,128)(2,1)S(1)} %pad_maximum_fusion, bf16[64,4224]{1,0:T(8,128)(2,1)S(1)} %collective-permute-done.8, f32[256]{0:T(256)S(1)} %get-tuple-element.6, f32[256]{0:T(256)S(1)} %get-tuple-element.5, f32[64]{0:T(128)S(1)} %add_reduce_fusion.1, f32[64]{0:T(128)S(1)} %multiply_floor_fusion.1), kind=kOutput, calls=%fused_computation.19 | convolution fusion | flops 134299392 | bytes 2625536 | tf_op jit(solution)/shard_map/id,jd->ij/dot_general | solution.py:26
  39.0 0.8 %fusion.5 = f32[256]{0:T(256)S(1)} fusion(bf16[256,4096]{1,0:T(8,128)(2,1)S(1)} %pad_maximum_fusion, bf16[64,4224]{1,0:T(8,128)(2,1)S(1)} %collective-permute-done.7, f32[256]{0:T(256)S(1)} %get-tuple-element.6, f32[256]{0:T(256)S(1)} %get-tuple-element.5, f32[64]{0:T(128)S(1)} %add_reduce_fusion.2, f32[64]{0:T(128)S(1)} %multiply_floor_fusion.2), kind=kOutput, calls=%fused_computation.18 | convolution fusion | flops 134299392 | bytes 2625536 | tf_op jit(solution)/shard_map/id,jd->ij/dot_general | solution.py:26
  39.8 6.2 %collective-permute-done.5 = bf16[64,4224]{1,0:T(8,128)(2,1)S(1)} collective-permute-done((bf16[64,4224]{1,0:T(8,128)(2,1)S(1)}, bf16[64,4224]{1,0:T(8,128)(2,1)S(1)}, u32[]{:S(2)}, u32[]{:S(2)}) %collective-permute-start.5) | collective-permute-done | bytes 540704 | tf_op jit(solution)/shard_map/ppermute | solution.py:59
  46.0 1.9 %collective-permute-start.6 = (bf16[40,4224]{1,0:T(8,128)(2,1)S(1)}, bf16[40,4224]{1,0:T(8,128)(2,1)S(1)}, u32[]{:S(2)}, u32[]{:S(2)}) collective-permute-start(bf16[40,4224]{1,0:T(8,128)(2,1)S(1)} %slice.162), channel_id=1, source_target_pairs={{0,2},{2,4},{4,6},{6,7},{7,5},{5,3},{3,1},{1,0},{8,10},{10,12},{12... | collective-permute-start | bytes 1013768 | tf_op jit(solution)/shard_map/ppermute | solution.py:59
  47.8 0.2 add_reduce_fusion.4
  48.0 0.5 collective-permute-done.9
  48.6 0.3 collective-permute-start.10
  48.9 0.2 add_reduce_fusion
  49.1 0.8 %fusion.3 = f32[256]{0:T(256)S(1)} fusion(bf16[256,4096]{1,0:T(8,128)(2,1)S(1)} %pad_maximum_fusion, bf16[64,4224]{1,0:T(8,128)(2,1)S(1)} %collective-permute-done.5, f32[256]{0:T(256)S(1)} %get-tuple-element.6, f32[256]{0:T(256)S(1)} %get-tuple-element.5, f32[64]{0:T(128)S(1)} %add_reduce_fusion.4, f32[64]{0:T(128)S(1)} %multiply_floor_fusion.4), kind=kOutput, calls=%fused_computation.16 | convolution fusion | flops 134299392 | bytes 2625536 | tf_op jit(solution)/shard_map/id,jd->ij/dot_general | solution.py:26
  49.9 0.8 %fusion.7 = f32[256]{0:T(256)S(1)} fusion(bf16[256,4096]{1,0:T(8,128)(2,1)S(1)} %pad_maximum_fusion, bf16[64,4224]{1,0:T(8,128)(2,1)S(1)} %collective-permute-done.9, f32[256]{0:T(256)S(1)} %get-tuple-element.6, f32[256]{0:T(256)S(1)} %get-tuple-element.5, f32[64]{0:T(128)S(1)} %add_reduce_fusion, f32[64]{0:T(128)S(1)} %multiply_floor_fusion), kind=kOutput, calls=%fused_computation.20 | convolution fusion | flops 134299392 | bytes 2625536 | tf_op jit(solution)/shard_map/id,jd->ij/dot_general | solution.py:26
  50.6 2.8 %collective-permute-done.6 = bf16[40,4224]{1,0:T(8,128)(2,1)S(1)} collective-permute-done((bf16[40,4224]{1,0:T(8,128)(2,1)S(1)}, bf16[40,4224]{1,0:T(8,128)(2,1)S(1)}, u32[]{:S(2)}, u32[]{:S(2)}) %collective-permute-start.6) | collective-permute-done | bytes 337952 | tf_op jit(solution)/shard_map/ppermute | solution.py:59
  53.4 0.9 %collective-permute-done.10 = bf16[24,4224]{1,0:T(8,128)(2,1)S(1)} collective-permute-done((bf16[24,4224]{1,0:T(8,128)(2,1)S(1)}, bf16[24,4224]{1,0:T(8,128)(2,1)S(1)}, u32[]{:S(2)}, u32[]{:S(2)}) %collective-permute-start.10) | collective-permute-done | bytes 202784 | tf_op jit(solution)/shard_map/ppermute | solution.py:59
  54.4 0.2 add_reduce_fusion.3
  54.6 0.8 %fusion.4 = f32[256]{0:T(256)S(1)} fusion(bf16[256,4096]{1,0:T(8,128)(2,1)S(1)} %pad_maximum_fusion, bf16[64,4224]{1,0:T(8,128)(2,1)S(1)} %constant_dynamic-update-slice_fusion, f32[256]{0:T(256)S(1)} %get-tuple-element.6, f32[256]{0:T(256)S(1)} %get-tuple-element.5, f32[64]{0:T(128)S(1)} %add_reduce_fusion.3, f32[64]{0:T(128)S(1)} %multiply_floor_fusion.3), kind=kOutput, calls=%fused_computation.17 | convolution fusion | flops 134299392 | bytes 2625536 | tf_op jit(solution)/shard_map/id,jd->ij/dot_general | solution.py:26
  55.4 0.1 slice_bitcast_fusion.1
  55.5 0.1 collective-permute-start.11
  55.6 1.1 %collective-permute-done.11 = f32[2,64]{1,0:T(2,128)S(1)} collective-permute-done((f32[2,64]{1,0:T(2,128)S(1)}, f32[2,64]{1,0:T(2,128)S(1)}, u32[]{:S(2)}, u32[]{:S(2)}) %collective-permute-start.11) | collective-permute-done | bytes 544 | tf_op jit(solution)/shard_map/ppermute | solution.py:104
  56.7 3.2 %collective-permute-start.12 = (f32[64]{0:T(128)S(1)}, f32[64]{0:T(128)S(1)}, u32[]{:S(2)}, u32[]{:S(2)}) collective-permute-start(f32[64]{0:T(128)S(1)} %bitcast_maximum_fusion), channel_id=1, source_target_pairs={{0,16},{8,24},{16,0},{24,8},{1,17},{9,25},{17,1},{25,9},{2,18},{10... | collective-permute-start | bytes 776 | tf_op jit(solution)/shard_map/ppermute | solution.py:107
  59.9 1.5 %collective-permute-done.12 = f32[64]{0:T(128)S(1)} collective-permute-done((f32[64]{0:T(128)S(1)}, f32[64]{0:T(128)S(1)}, u32[]{:S(2)}, u32[]{:S(2)}) %collective-permute-start.12) | collective-permute-done | bytes 288 | tf_op jit(solution)/shard_map/ppermute | solution.py:107
  61.4 0.5 fusion.22
  (20 shorter events, 0.2 us)
Async XLA Ops:
  3.3 15.3 %collective-permute-start.1 = (bf16[64,4224]{1,0:T(8,128)(2,1)S(1)}, bf16[64,4224]{1,0:T(8,128)(2,1)S(1)}, u32[]{:S(2)}, u32[]{:S(2)}) collective-permute-start(bf16[64,4224]{1,0:T(8,128)(2,1)S(1)} %fusion.11), channel_id=1, source_target_pairs={{0,16},{8,24},{16,0},{24,8},{1,17},{9,25},{17,1},{25,9},{2,18},{10... | collective-permute-start | bytes 1622024 | tf_op jit(solution)/shard_map/ppermute | solution.py:68
  6.4 13.7 %collective-permute-start.3 = (bf16[64,4224]{1,0:T(8,128)(2,1)S(1)}, bf16[64,4224]{1,0:T(8,128)(2,1)S(1)}, u32[]{:S(2)}, u32[]{:S(2)}) collective-permute-start(bf16[64,4224]{1,0:T(8,128)(2,1)S(1)} %fusion.11), channel_id=1, source_target_pairs={{0,2},{2,4},{4,6},{6,7},{7,5},{5,3},{3,1},{1,0},{8,10},{10,12},{12... | collective-permute-start | bytes 1622024 | tf_op jit(solution)/shard_map/ppermute | solution.py:59
  8.0 13.9 %collective-permute-start.7 = (bf16[64,4224]{1,0:T(8,128)(2,1)S(1)}, bf16[64,4224]{1,0:T(8,128)(2,1)S(1)}, u32[]{:S(2)}, u32[]{:S(2)}) collective-permute-start(bf16[64,4224]{1,0:T(8,128)(2,1)S(1)} %fusion.11), channel_id=1, source_target_pairs={{2,0},{4,2},{6,4},{7,6},{5,7},{3,5},{1,3},{0,1},{10,8},{12,10},{14... | collective-permute-start | bytes 1622024 | tf_op jit(solution)/shard_map/ppermute | solution.py:59
  8.4 14.2 %collective-permute-start = (bf16[64,4224]{1,0:T(8,128)(2,1)S(1)}, bf16[64,4224]{1,0:T(8,128)(2,1)S(1)}, u32[]{:S(2)}, u32[]{:S(2)}) collective-permute-start(bf16[64,4224]{1,0:T(8,128)(2,1)S(1)} %fusion.11), channel_id=1, source_target_pairs={{0,8},{8,0},{16,24},{24,16},{1,9},{9,1},{17,25},{25,17},{2,10},{10... | collective-permute-start | bytes 1622024 | tf_op jit(solution)/shard_map/ppermute | solution.py:69
  18.7 3.9 %collective-permute-start.2 = (bf16[64,4224]{1,0:T(8,128)(2,1)S(1)}, bf16[64,4224]{1,0:T(8,128)(2,1)S(1)}, u32[]{:S(2)}, u32[]{:S(2)}) collective-permute-start(bf16[64,4224]{1,0:T(8,128)(2,1)S(1)} %collective-permute-done.1), channel_id=1, source_target_pairs={{0,8},{8,0},{16,24},{24,16},{1,9},{9,1},{17,25},{25,17},{2,10},{10... | collective-permute-start | bytes 1622024 | tf_op jit(solution)/shard_map/ppermute | solution.py:70
  20.1 13.2 %collective-permute-start.4 = (bf16[64,4224]{1,0:T(8,128)(2,1)S(1)}, bf16[64,4224]{1,0:T(8,128)(2,1)S(1)}, u32[]{:S(2)}, u32[]{:S(2)}) collective-permute-start(bf16[64,4224]{1,0:T(8,128)(2,1)S(1)} %collective-permute-done.3), channel_id=1, source_target_pairs={{0,2},{2,4},{4,6},{6,7},{7,5},{5,3},{3,1},{1,0},{8,10},{10,12},{12... | collective-permute-start | bytes 1622024 | tf_op jit(solution)/shard_map/ppermute | solution.py:59
  21.9 14.2 %collective-permute-start.8 = (bf16[64,4224]{1,0:T(8,128)(2,1)S(1)}, bf16[64,4224]{1,0:T(8,128)(2,1)S(1)}, u32[]{:S(2)}, u32[]{:S(2)}) collective-permute-start(bf16[64,4224]{1,0:T(8,128)(2,1)S(1)} %collective-permute-done.7), channel_id=1, source_target_pairs={{2,0},{4,2},{6,4},{7,6},{5,7},{3,5},{1,3},{0,1},{10,8},{12,10},{14... | collective-permute-start | bytes 1622024 | tf_op jit(solution)/shard_map/ppermute | solution.py:59
  33.4 12.6 %collective-permute-start.5 = (bf16[64,4224]{1,0:T(8,128)(2,1)S(1)}, bf16[64,4224]{1,0:T(8,128)(2,1)S(1)}, u32[]{:S(2)}, u32[]{:S(2)}) collective-permute-start(bf16[64,4224]{1,0:T(8,128)(2,1)S(1)} %collective-permute-done.4), channel_id=1, source_target_pairs={{0,2},{2,4},{4,6},{6,7},{7,5},{5,3},{3,1},{1,0},{8,10},{10,12},{12... | collective-permute-start | bytes 1622024 | tf_op jit(solution)/shard_map/ppermute | solution.py:59
  36.2 12.4 %collective-permute-start.9 = (bf16[64,4224]{1,0:T(8,128)(2,1)S(1)}, bf16[64,4224]{1,0:T(8,128)(2,1)S(1)}, u32[]{:S(2)}, u32[]{:S(2)}) collective-permute-start(bf16[64,4224]{1,0:T(8,128)(2,1)S(1)} %collective-permute-done.8), channel_id=1, source_target_pairs={{2,0},{4,2},{6,4},{7,6},{5,7},{3,5},{1,3},{0,1},{10,8},{12,10},{14... | collective-permute-start | bytes 1622024 | tf_op jit(solution)/shard_map/ppermute | solution.py:59
  46.0 7.4 %collective-permute-start.6 = (bf16[40,4224]{1,0:T(8,128)(2,1)S(1)}, bf16[40,4224]{1,0:T(8,128)(2,1)S(1)}, u32[]{:S(2)}, u32[]{:S(2)}) collective-permute-start(bf16[40,4224]{1,0:T(8,128)(2,1)S(1)} %slice.162), channel_id=1, source_target_pairs={{0,2},{2,4},{4,6},{6,7},{7,5},{5,3},{3,1},{1,0},{8,10},{10,12},{12... | collective-permute-start | bytes 1013768 | tf_op jit(solution)/shard_map/ppermute | solution.py:59
  48.6 5.8 %collective-permute-start.10 = (bf16[24,4224]{1,0:T(8,128)(2,1)S(1)}, bf16[24,4224]{1,0:T(8,128)(2,1)S(1)}, u32[]{:S(2)}, u32[]{:S(2)}) collective-permute-start(bf16[24,4224]{1,0:T(8,128)(2,1)S(1)} %slice.163), channel_id=1, source_target_pairs={{2,0},{4,2},{6,4},{7,6},{5,7},{3,5},{1,3},{0,1},{10,8},{12,10},{14... | collective-permute-start | bytes 608264 | tf_op jit(solution)/shard_map/ppermute | solution.py:59
  55.5 1.2 %collective-permute-start.11 = (f32[2,64]{1,0:T(2,128)S(1)}, f32[2,64]{1,0:T(2,128)S(1)}, u32[]{:S(2)}, u32[]{:S(2)}) collective-permute-start(f32[2,64]{1,0:T(2,128)S(1)} %pad_maximum_fusion.5), channel_id=1, source_target_pairs={{0,8},{8,0},{16,24},{24,16},{1,9},{9,1},{17,25},{25,17},{2,10},{10... | collective-permute-start | bytes 1544 | tf_op jit(solution)/shard_map/ppermute | solution.py:104
  56.7 4.7 %collective-permute-start.12 = (f32[64]{0:T(128)S(1)}, f32[64]{0:T(128)S(1)}, u32[]{:S(2)}, u32[]{:S(2)}) collective-permute-start(f32[64]{0:T(128)S(1)} %bitcast_maximum_fusion), channel_id=1, source_target_pairs={{0,16},{8,24},{16,0},{24,8},{1,17},{9,25},{17,1},{25,9},{2,18},{10... | collective-permute-start | bytes 776 | tf_op jit(solution)/shard_map/ppermute | solution.py:107
